TPU v7x, 32 devices: a whole 2x2x4 slice. The times are simulated.
32 devices in a mesh: blk: 8 (over z, core), help: 4 (over y, x).
Axes of the slice: x: 2, y: 2, z: 4, core: 2. Of those that a mesh axis runs over, the one named last changes fastest.
Arguments:
- vectors: float32 [8, 16384], P(None, ('blk', 'help')), may hold values from -6 to 6
- tile_blocks: float32 [32, 5, 3, 256, 256], P(('blk', 'help')), may hold values from -0.1875 to 0.1875
- tile_row: int32 [32, 5, 3], P(('blk', 'help')), may hold values from 0 to 7
- tile_col: int32 [32, 5, 3], P(('blk', 'help')), may hold values from 0 to 7
- counts: int32 [32, 5], P(('blk', 'help')), may hold values from 1 to 3, as said below
Outputs:
- product: float32 [8, 16384], P(None, ('blk', 'help'))
- gram_energy: float32 [8, 8], replicated
- gram_correlation: float32 [8, 8], replicated
Inputs may be any that keep to these rules, and one draw needn't show every extreme that they name: `counts`: in every group of 4 helpers one helper has 3 live slots for every band offset; every other helper has fewer, and at least one, for each offset.
All inputs are finite; a program needn't handle non-finite values.
Results may differ from a plain program's by a relative error of at most 0.0003.
Values sent between devices are 32-bit elements; how exact they have to be, the bound alone decides.
No kernel may reach another device: no remote copies, remote signals or barrier semaphores. Data moves between devices by JAX's collectives and lax.ppermute only.
A program may use at most 64 MiB of HBM per device.

v0:
```python
import jax
import jax.numpy as jnp
from jax import lax
from jax.sharding import PartitionSpec as P

VEC = 8
TILE = 256
BAND = 2
SLOTS = 3
NOFF = 5


def shifted(value, axis, steps):
    count = lax.axis_size(axis)
    initial, last = (max(0, -steps), min(count, count - steps))
    return lax.ppermute(value, axis, [(source, source + steps) for source in range(initial, last)])


def neighbour_panels(source):
    lowers = []
    uppers = []
    current = source
    for hop_index in range(BAND):
        current = shifted(current, "blk", 1)
        lowers.append(current)
    current = source
    for hop_index in range(BAND):
        current = shifted(current, "blk", -1)
        uppers.append(current)
    return lowers[::-1] + [source] + uppers


def local(vectors, tile_blocks, tile_row, tile_col, counts):
    groups = lax.axis_size("blk")
    piece_width = vectors.shape[1]
    group_width = piece_width * lax.axis_size("help")
    group_rows = group_width // TILE
    full_panel = lax.all_gather(vectors, "help", axis=1, tiled=True)
    panels = neighbour_panels(full_panel)
    slot_ids = jnp.arange(SLOTS, dtype=jnp.int32)
    row_ids = jnp.arange(group_rows, dtype=jnp.int32)
    partial_value = jnp.zeros((VEC, group_rows, TILE), jnp.float32)
    for offset_index in range(NOFF):
        panel_tiles = panels[offset_index].reshape(VEC, group_rows, TILE)
        pieces = jnp.take(panel_tiles, tile_col[0, offset_index], axis=1)
        live = (slot_ids < counts[0, offset_index]).astype(jnp.float32)
        contribution = jnp.einsum(
            "ist,stu->isu", pieces, tile_blocks[0, offset_index], precision=lax.Precision.HIGHEST
        )
        one_hot = (tile_row[0, offset_index][:, None] == row_ids[None, :]).astype(
            jnp.float32
        ) * live[:, None]
        partial_value = partial_value + jnp.einsum(
            "isu,sr->iru", contribution, one_hot, precision=lax.Precision.HIGHEST
        )
    flattened = partial_value.reshape(VEC, group_width)
    basis_size = float(groups * group_width)
    correlation_term = jnp.dot(
        vectors, vectors.T, precision=lax.Precision.HIGHEST, preferred_element_type=jnp.float32
    )
    own_panel = panels[BAND]
    early_terms = (
        jnp.dot(
            own_panel,
            flattened.T,
            precision=lax.Precision.HIGHEST,
            preferred_element_type=jnp.float32,
        ),
        correlation_term,
    )
    gram_energy, gram_correlation = lax.psum((early_terms[0], early_terms[1]), ("blk", "help"))
    product = lax.psum_scatter(flattened, "help", scatter_dimension=1, tiled=True)
    return (product, gram_energy / basis_size, gram_correlation / basis_size)


def solution(mesh):
    placed = (
        P(None, ("blk", "help")),
        P(("blk", "help"), None, None, None, None),
        P(("blk", "help"), None, None),
        P(("blk", "help"), None, None),
        P(("blk", "help"), None),
    )
    return jax.shard_map(
        local,
        mesh=mesh,
        in_specs=placed,
        out_specs=(P(None, ("blk", "help")), P(), P()),
        check_vma=False,
    )
```

profile of v0, /device:TPU:0, one launch (start us, length us, event | category | flops | bytes accessed | tf_op | source)
XLA Modules:
  0.0 99.4 jit_solution(237913537589706720)
XLA Ops:
  7.2 0.0 reduce-scatter.2.cloned.1.call-start
  7.2 9.8 %all_gather.3 = f32[8,2048]{1,0:T(8,128)S(1)} all-gather(f32[8,512]{1,0:T(8,128)} %param.7), channel_id=1, replica_groups=mesh['blk'=8,'help'=4] {'help'}, dimensions={1}, use_global_device_ids=true | all-gather | bytes 81920 | tf_op jit(solution)/shard_map/all_gather | solution.py:38
  17.1 1.3 %collective-permute-start = (f32[8,2048]{1,0:T(8,128)S(1)}, f32[8,2048]{1,0:T(8,128)S(1)}, u32[]{:S(2)}, u32[]{:S(2)}) collective-permute-start(f32[8,2048]{1,0:T(8,128)S(1)} %all_gather.3), channel_id=1, source_target_pairs={{0,4},{4,8},{8,12},{12,16},{16,20},{20,24},{24,28},{1,5},{5,9},{9,... | collective-permute-start | bytes 196616 | tf_op jit(solution)/shard_map/ppermute | solution.py:16
  18.3 1.3 %collective-permute-start.2 = (f32[8,2048]{1,0:T(8,128)S(1)}, f32[8,2048]{1,0:T(8,128)S(1)}, u32[]{:S(2)}, u32[]{:S(2)}) collective-permute-start(f32[8,2048]{1,0:T(8,128)S(1)} %all_gather.3), channel_id=1, source_target_pairs={{4,0},{8,4},{12,8},{16,12},{20,16},{24,20},{28,24},{5,1},{9,5},{13... | collective-permute-start | bytes 196616 | tf_op jit(solution)/shard_map/ppermute | solution.py:16
  19.6 1.3 %slice_reduce_fusion = (s32[3]{0:T(128)S(1)}, s32[3]{0:T(128)S(1)}, s32[3]{0:T(128)S(1)}, s32[3]{0:T(128)S(1)}, s32[3]{0:T(128)S(1)}) fusion(s32[1,5,3]{1,0,2:T(1,128)} %param.10), kind=kLoop, calls=%fused_computation.94 | loop fusion | bytes 120 | tf_op jit(solution)/shard_map/slice | solution.py:45
  21.1 0.9 fusion.83
  22.0 1.4 %fusion.82 = (s32[1,1]{1,0:T(1,128)}, s32[1,1]{1,0:T(1,128)}, s32[1,1]{1,0:T(1,128)}, s32[1,1]{1,0:T(1,128)}, s32[1,1]{1,0:T(1,128)}) fusion(s32[1,5]{1,0:T(1,128)} %param.11), kind=kLoop, calls=%fused_computation.129 | loop fusion | bytes 40 | tf_op jit(solution)/shard_map/slice | solution.py:46
  23.5 0.7 compare_convert_fusion.4
  24.2 1.3 %slice_reduce_fusion.1 = (s32[3]{0:T(128)S(1)}, s32[3]{0:T(128)S(1)}, s32[3]{0:T(128)S(1)}, s32[3]{0:T(128)S(1)}, s32[3]{0:T(128)S(1)}) fusion(s32[1,5,3]{1,0,2:T(1,128)} %param.9), kind=kLoop, calls=%fused_computation.95 | loop fusion | bytes 120 | tf_op jit(solution)/shard_map/slice | solution.py:50
  25.5 0.7 compare_convert_fusion.3
  26.2 0.7 compare_convert_fusion.2
  26.8 0.6 compare_convert_fusion.1
  27.4 0.6 gather_fusion.2
  28.0 1.6 %fusion.5 = f32[3,8,256]{2,1,0:T(8,128)S(1)} fusion(f32[1,5,3,256,256]{4,3,2,1,0:T(8,128)} %param.8, f32[3,8,256]{2,1,0:T(8,128)S(1)} %gather_fusion.2, pred[3]{0:T(512)(128)(4,1)S(1)} %compare_and_fusion.2), kind=kOutput, calls=%fused_computation.15 | convolution fusion | flops 18880512 | bytes 835587 | tf_op jit(solution)/shard_map/ist,stu->isu/dot_general | solution.py:47
  29.6 0.7 compare_convert_fusion
  30.2 0.0 collective-permute-done
  30.3 0.6 gather_fusion.1
  30.8 1.6 %fusion.7 = f32[3,8,256]{2,1,0:T(8,128)S(1)} fusion(f32[1,5,3,256,256]{4,3,2,1,0:T(8,128)} %param.8, f32[3,8,256]{2,1,0:T(8,128)S(1)} %gather_fusion.1, pred[3]{0:T(512)(128)(4,1)S(1)} %compare_and_fusion.3), kind=kOutput, calls=%fused_computation.17 | convolution fusion | flops 18880512 | bytes 835587 | tf_op jit(solution)/shard_map/ist,stu->isu/dot_general | solution.py:47
  32.4 0.0 collective-permute-done.2
  32.4 0.6 gather_fusion.3
  33.0 4.8 %collective-permute-start.1 = (f32[8,2048]{1,0:T(8,128)S(1)}, f32[8,2048]{1,0:T(8,128)S(1)}, u32[]{:S(2)}, u32[]{:S(2)}) collective-permute-start(f32[8,2048]{1,0:T(8,128)S(1)} %collective-permute-done), channel_id=1, source_target_pairs={{0,4},{4,8},{8,12},{12,16},{16,20},{20,24},{24,28},{1,5},{5,9},{9,... | collective-permute-start | bytes 196616 | tf_op jit(solution)/shard_map/ppermute | solution.py:16
  37.8 1.6 %fusion.3 = f32[3,8,256]{2,1,0:T(8,128)S(1)} fusion(f32[1,5,3,256,256]{4,3,2,1,0:T(8,128)} %param.8, f32[3,8,256]{2,1,0:T(8,128)S(1)} %gather_fusion.3, pred[3]{0:T(512)(128)(4,1)S(1)} %compare_and_fusion.1), kind=kOutput, calls=%fused_computation.13 | convolution fusion | flops 18880512 | bytes 835587 | tf_op jit(solution)/shard_map/ist,stu->isu/dot_general | solution.py:47
  39.4 1.3 %collective-permute-start.3 = (f32[8,2048]{1,0:T(8,128)S(1)}, f32[8,2048]{1,0:T(8,128)S(1)}, u32[]{:S(2)}, u32[]{:S(2)}) collective-permute-start(f32[8,2048]{1,0:T(8,128)S(1)} %collective-permute-done.2), channel_id=1, source_target_pairs={{4,0},{8,4},{12,8},{16,12},{20,16},{24,20},{28,24},{5,1},{9,5},{13... | collective-permute-start | bytes 196616 | tf_op jit(solution)/shard_map/ppermute | solution.py:16
  40.8 0.0 collective-permute-done.1
  40.8 0.6 gather_fusion
  41.3 1.6 %fusion.9 = f32[3,8,256]{2,1,0:T(8,128)S(1)} fusion(f32[1,5,3,256,256]{4,3,2,1,0:T(8,128)} %param.8, f32[3,8,256]{2,1,0:T(8,128)S(1)} %gather_fusion, pred[3]{0:T(512)(128)(4,1)S(1)} %compare_and_fusion.4), kind=kOutput, calls=%fused_computation.19 | convolution fusion | flops 18880512 | bytes 835587 | tf_op jit(solution)/shard_map/ist,stu->isu/dot_general | solution.py:47
  42.9 0.9 collective-permute-done.3
  43.8 0.5 gather_fusion.4
  44.4 1.6 %fusion.1 = f32[3,8,256]{2,1,0:T(8,128)S(1)} fusion(f32[1,5,3,256,256]{4,3,2,1,0:T(8,128)} %param.8, f32[3,8,256]{2,1,0:T(8,128)S(1)} %gather_fusion.4, pred[3]{0:T(512)(128)(4,1)S(1)} %compare_and_fusion), kind=kOutput, calls=%fused_computation.11 | convolution fusion | flops 18880512 | bytes 835587 | tf_op jit(solution)/shard_map/ist,stu->isu/dot_general | solution.py:47
  46.0 0.4 fusion.20
  46.4 0.3 convolution_add_fusion.3
  46.7 0.3 convolution_add_fusion.2
  47.0 0.3 convolution_add_fusion.1
  47.3 0.3 fusion
  47.7 0.6 copy.20
  48.3 0.0 reduce-scatter.2.cloned.1.call-update
  48.3 1.0 %convolution_bitcast_fusion = f32[8,8]{0,1:T(8,128)S(1)} fusion(f32[8,2048]{1,0:T(8,128)} %bitcast.81, f32[8,2048]{1,0:T(8,128)S(1)} %all_gather.3), kind=kOutput, calls=%fused_computation.10 | convolution fusion | flops 1572864 | bytes 131328 | tf_op jit(solution)/shard_map/dot_general | solution.py:63
  49.4 41.8 %all-reduce = (f32[8,8]{0,1:T(8,128)S(1)}, f32[8,8]{0,1:T(8,128)S(1)}) all-reduce(f32[8,8]{0,1:T(8,128)S(1)} %convolution_bitcast_fusion, f32[8,8]{0,1:T(8,128)S(1)} %fusion.83), channel_id=1, replica_groups=mesh['blk'=8,'help'=4] {'blk','help'}, use_global_device_ids=true, to_apply=%region_1.3 | all-reduce | flops 128 | bytes 1024 | tf_op jit(solution)/shard_map/psum | solution.py:71
  91.2 0.7 copy.12
  91.9 0.7 copy.13
  92.5 0.0 reduce-scatter.2.cloned.1.call-done
  (16 shorter events, 0.1 us)
Async XLA Ops:
  7.2 85.4 %reduce-scatter.2.cloned.1.call-start = ((), (), s32[]{:S(2)}) async-start(), calls=%async_computation.1 | async-start | bytes 81920 | tf_op jit(solution)/shard_map/reduce_scatter | solution.py:72
  17.1 13.2 %collective-permute-start = (f32[8,2048]{1,0:T(8,128)S(1)}, f32[8,2048]{1,0:T(8,128)S(1)}, u32[]{:S(2)}, u32[]{:S(2)}) collective-permute-start(f32[8,2048]{1,0:T(8,128)S(1)} %all_gather.3), channel_id=1, source_target_pairs={{0,4},{4,8},{8,12},{12,16},{16,20},{20,24},{24,28},{1,5},{5,9},{9,... | collective-permute-start | bytes 196616 | tf_op jit(solution)/shard_map/ppermute | solution.py:16
  18.3 14.1 %collective-permute-start.2 = (f32[8,2048]{1,0:T(8,128)S(1)}, f32[8,2048]{1,0:T(8,128)S(1)}, u32[]{:S(2)}, u32[]{:S(2)}) collective-permute-start(f32[8,2048]{1,0:T(8,128)S(1)} %all_gather.3), channel_id=1, source_target_pairs={{4,0},{8,4},{12,8},{16,12},{20,16},{24,20},{28,24},{5,1},{9,5},{13... | collective-permute-start | bytes 196616 | tf_op jit(solution)/shard_map/ppermute | solution.py:16
  33.0 7.8 %collective-permute-start.1 = (f32[8,2048]{1,0:T(8,128)S(1)}, f32[8,2048]{1,0:T(8,128)S(1)}, u32[]{:S(2)}, u32[]{:S(2)}) collective-permute-start(f32[8,2048]{1,0:T(8,128)S(1)} %collective-permute-done), channel_id=1, source_target_pairs={{0,4},{4,8},{8,12},{12,16},{16,20},{20,24},{24,28},{1,5},{5,9},{9,... | collective-permute-start | bytes 196616 | tf_op jit(solution)/shard_map/ppermute | solution.py:16
  39.4 4.4 %collective-permute-start.3 = (f32[8,2048]{1,0:T(8,128)S(1)}, f32[8,2048]{1,0:T(8,128)S(1)}, u32[]{:S(2)}, u32[]{:S(2)}) collective-permute-start(f32[8,2048]{1,0:T(8,128)S(1)} %collective-permute-done.2), channel_id=1, source_target_pairs={{4,0},{8,4},{12,8},{16,12},{20,16},{24,20},{28,24},{5,1},{9,5},{13... | collective-permute-start | bytes 196616 | tf_op jit(solution)/shard_map/ppermute | solution.py:16
Sparse Core Ops, SparseCore 0:
  48.5 25.5 reduce-scatter.1
where the time goes:
time: 100 us; the launch traced here: 99.4 us
  blocking collectives  51.7 us (52%)
  between operations  14.4 us (14%)
  matrix products  11.5 us (12%)
  starting transfers between devices  8.77 us (9%)
  local copies, waits for them, and re-layouts  8.77 us (9%)
  other arithmetic  3.34 us (3%)
    psum x1, blocking collectives, local(): lax.psum((early_terms[0], early_terms[1]), ('blk', 'help'))  41.8 us
    all_gather x1, blocking collectives, local(): full_panel = lax.all_gather(vectors, 'help', axis=1, tiled=True)  9.85 us
    ppermute x4, starting transfers between devices, shifted(): lax.ppermute(value, axis, [(source, source + steps) for source in range(i...  8.73 us
    dot_general x5, matrix products, local(): jnp.einsum('ist,stu->isu', pieces, tile_blocks[0, offset_index], precisio...  7.92 us
    convert_element_type x5, other arithmetic, local(): live = (slot_ids < counts[0, offset_index]).astype(jnp.float32)  3.23 us
    gather x5, local copies, waits for them, and re-layouts, local(): pieces = jnp.take(panel_tiles, tile_col[0, offset_index], axis=1)  2.77 us
  transfers between devices with their start and end apart: 5, of which 1 were waited for; matrix products, arithmetic and copies ran while one was open for 19% of the time, Pallas kernels for 0%

commit v1 on v0

--- a/solution.py
+++ b/solution.py
@@ -8,12 +8,73 @@
 BAND = 2
 SLOTS = 3
 NOFF = 5
+GRAM_PAD = 128
 
 
 def shifted(value, axis, steps):
     count = lax.axis_size(axis)
     initial, last = (max(0, -steps), min(count, count - steps))
     return lax.ppermute(value, axis, [(source, source + steps) for source in range(initial, last)])
+
+
+def is_power_of_two(count):
+    return count & (count - 1) == 0
+
+
+def exchanged(value, axis, mask):
+    count = lax.axis_size(axis)
+    return lax.ppermute(value, axis, [(source, source ^ mask) for source in range(count)])
+
+
+def gather_help(piece):
+    count = lax.axis_size("help")
+    if not is_power_of_two(count):
+        return lax.all_gather(piece, "help", axis=1, tiled=True)
+    index = lax.axis_index("help")
+    held = piece
+    mask = 1
+    while mask < count:
+        other = exchanged(held, "help", mask)
+        upper = (index // mask) % 2 == 1
+        held = jnp.where(
+            upper, jnp.concatenate([other, held], axis=1), jnp.concatenate([held, other], axis=1)
+        )
+        mask *= 2
+    return held
+
+
+def reduce_help(partial, gram):
+    count = lax.axis_size("help")
+    if not is_power_of_two(count):
+        return (
+            lax.psum_scatter(partial, "help", scatter_dimension=1, tiled=True),
+            lax.psum(gram, "help"),
+        )
+    index = lax.axis_index("help")
+    held = partial
+    mask = count // 2
+    while mask >= 1:
+        half = held.shape[1] // 2
+        lower, upper = held[:, :half], held[:, half:]
+        high = (index // mask) % 2 == 1
+        keep = jnp.where(high, upper, lower)
+        send = jnp.where(high, lower, upper)
+        arrived = exchanged(jnp.concatenate([send, gram], axis=1), "help", mask)
+        held = keep + arrived[:, :half]
+        gram = gram + arrived[:, half:]
+        mask //= 2
+    return held, gram
+
+
+def reduce_blk(gram):
+    count = lax.axis_size("blk")
+    if not is_power_of_two(count):
+        return lax.psum(gram, "blk")
+    mask = 1
+    while mask < count:
+        gram = gram + exchanged(gram, "blk", mask)
+        mask *= 2
+    return gram
 
 
 def neighbour_panels(source):
@@ -35,7 +96,7 @@
     piece_width = vectors.shape[1]
     group_width = piece_width * lax.axis_size("help")
     group_rows = group_width // TILE
-    full_panel = lax.all_gather(vectors, "help", axis=1, tiled=True)
+    full_panel = gather_help(vectors)
     panels = neighbour_panels(full_panel)
     slot_ids = jnp.arange(SLOTS, dtype=jnp.int32)
     row_ids = jnp.arange(group_rows, dtype=jnp.int32)
@@ -58,19 +119,15 @@
     correlation_term = jnp.dot(
         vectors, vectors.T, precision=lax.Precision.HIGHEST, preferred_element_type=jnp.float32
     )
-    own_panel = panels[BAND]
-    early_terms = (
-        jnp.dot(
-            own_panel,
-            flattened.T,
-            precision=lax.Precision.HIGHEST,
-            preferred_element_type=jnp.float32,
-        ),
-        correlation_term,
+    energy_term = jnp.dot(
+        full_panel, flattened.T, precision=lax.Precision.HIGHEST, preferred_element_type=jnp.float32
     )
-    gram_energy, gram_correlation = lax.psum((early_terms[0], early_terms[1]), ("blk", "help"))
-    product = lax.psum_scatter(flattened, "help", scatter_dimension=1, tiled=True)
-    return (product, gram_energy / basis_size, gram_correlation / basis_size)
+    gram = jnp.zeros((VEC, GRAM_PAD), jnp.float32)
+    gram = gram.at[:, :VEC].set(energy_term).at[:, VEC : 2 * VEC].set(correlation_term)
+    product, gram = reduce_help(flattened, gram)
+    gram = reduce_blk(gram)
+    gram = gram / basis_size
+    return (product, gram[:, :VEC], gram[:, VEC : 2 * VEC])
 
 
 def solution(mesh):

time: 100 us -> 62.2 us (0.62)
  blocking collectives: 51.7 us -> 0 us
  between operations: 14.4 us -> 1.05 us
  starting transfers between devices: 8.77 us -> 21.9 us
  waiting for transfers between devices: 0.95 us -> 11.6 us
  other arithmetic: 3.34 us -> 6.88 us
    psum x1 -> x0, blocking collectives: 41.8 us -> none  [local(): lax.psum((early_terms[0], early_terms[1]), ('blk', 'help'))]
    ppermute x0 -> x7, starting transfers between devices: none -> 13.2 us  [exchanged(): lax.ppermute(value, axis, [(source, source ^ mask) for source in range(co...]
    ppermute x0 -> x7, waiting for transfers between devices: none -> 10.7 us  [exchanged(): lax.ppermute(value, axis, [(source, source ^ mask) for source in range(co...]
    all_gather x1 -> x0, blocking collectives: 9.85 us -> none  [local(): full_panel = lax.all_gather(vectors, 'help', axis=1, tiled=True)]
    unnamed x3 -> x1, local copies, waits for them, and re-layouts: 1.97 us -> 0.02 us
    select_n x0 -> x6, other arithmetic: none -> 1.63 us  [the longest x4 1.61 us: gather_help(): jnp.where(upper, jnp.concatenate([other, held], axis=1), jnp.concatenate(...]
    another operation x0 -> x2, other arithmetic: none -> 1.36 us
  transfers between devices with their start and end apart: 5 -> 11, of which waited for: 1 -> 7; matrix products, arithmetic and copies ran while one was open for 19% -> 32% of each run, Pallas kernels for 0% -> 0%
where the time goes in v1:
time: 62.2 us; the launch traced here: 61.3 us
  starting transfers between devices  21.9 us (35%)
  matrix products  12 us (19%)
  waiting for transfers between devices  11.6 us (19%)
  local copies, waits for them, and re-layouts  7.86 us (13%)
  other arithmetic  6.88 us (11%)
  between operations  1.05 us (2%)
    ppermute x7, starting transfers between devices, exchanged(): lax.ppermute(value, axis, [(source, source ^ mask) for source in range(co...  13.2 us
    ppermute x7, waiting for transfers between devices, exchanged(): lax.ppermute(value, axis, [(source, source ^ mask) for source in range(co...  10.7 us
    ppermute x4, starting transfers between devices, shifted(): lax.ppermute(value, axis, [(source, source + steps) for source in range(i...  8.74 us
    dot_general x5, matrix products, local(): jnp.einsum('ist,stu->isu', pieces, tile_blocks[0, offset_index], precisio...  7.92 us
    convert_element_type x5, other arithmetic, local(): live = (slot_ids < counts[0, offset_index]).astype(jnp.float32)  3.16 us
    gather x5, local copies, waits for them, and re-layouts, local(): pieces = jnp.take(panel_tiles, tile_col[0, offset_index], axis=1)  2.8 us
    dot_general x5, matrix products, local(): jnp.einsum('isu,sr->iru', contribution, one_hot, precision=lax.Precision....  1.64 us
    select_n x4, other arithmetic, gather_help(): jnp.where(upper, jnp.concatenate([other, held], axis=1), jnp.concatenate(...  1.61 us
  transfers between devices with their start and end apart: 11, of which 7 were waited for; matrix products, arithmetic and copies ran while one was open for 32% of the time, Pallas kernels for 0%

profile of v1, /device:TPU:0, one launch (start us, length us, event | category | flops | bytes accessed | tf_op | source)
XLA Modules:
  0.0 61.3 jit_solution(4717356933728715346)
XLA Ops:
  0.6 3.0 %collective-permute-start = (f32[8,512]{1,0:T(8,128)}, f32[8,512]{1,0:T(8,128)S(1)}, u32[]{:S(2)}, u32[]{:S(2)}) collective-permute-start(f32[8,512]{1,0:T(8,128)} %param.11), channel_id=1, source_target_pairs={{0,1},{1,0},{2,3},{3,2},{4,5},{5,4},{6,7},{7,6},{8,9},{9,8},{10,11... | collective-permute-start | bytes 49160 | tf_op jit(solution)/shard_map/ppermute | solution.py:26
  3.6 1.3 %slice_reduce_fusion = (s32[3]{0:T(128)S(1)}, s32[3]{0:T(128)S(1)}, s32[3]{0:T(128)S(1)}, s32[3]{0:T(128)S(1)}, s32[3]{0:T(128)S(1)}) fusion(s32[1,5,3]{1,0,2:T(1,128)} %param.14), kind=kLoop, calls=%fused_computation.108 | loop fusion | bytes 120 | tf_op jit(solution)/shard_map/slice | solution.py:106
  5.1 0.7 %compare_reduce_fusion = pred[]{:T(512)} fusion(), kind=kLoop, calls=%fused_computation.101 | loop fusion | flops 7 | bytes 1 | tf_op jit(solution)/shard_map/reduce.3
  5.8 1.5 %fusion.83 = (s32[1,1]{1,0:T(1,128)}, s32[1,1]{1,0:T(1,128)}, s32[1,1]{1,0:T(1,128)}, s32[1,1]{1,0:T(1,128)}, s32[1,1]{1,0:T(1,128)}) fusion(s32[1,5]{1,0:T(1,128)} %param.15), kind=kLoop, calls=%fused_computation.145 | loop fusion | bytes 40 | tf_op jit(solution)/shard_map/slice | solution.py:107
  7.2 0.6 compare_convert_fusion.4
  7.8 1.3 %slice_reduce_fusion.1 = (s32[3]{0:T(128)S(1)}, s32[3]{0:T(128)S(1)}, s32[3]{0:T(128)S(1)}, s32[3]{0:T(128)S(1)}, s32[3]{0:T(128)S(1)}) fusion(s32[1,5,3]{1,0,2:T(1,128)} %param.13), kind=kLoop, calls=%fused_computation.109 | loop fusion | bytes 120 | tf_op jit(solution)/shard_map/slice | solution.py:111
  9.1 0.7 %compare_convert_fusion.3 = f32[3]{0:T(128)S(1)} fusion(s32[]{:T(128)} %bitcast.6), kind=kLoop, calls=%fused_computation.106 | loop fusion | flops 6 | bytes 16 | tf_op jit(solution)/shard_map/convert_element_type | solution.py:107
  9.8 0.7 %compare_convert_fusion.2 = f32[3]{0:T(128)S(1)} fusion(s32[]{:T(128)} %bitcast.12), kind=kLoop, calls=%fused_computation.105 | loop fusion | flops 6 | bytes 16 | tf_op jit(solution)/shard_map/convert_element_type | solution.py:107
  10.5 0.6 %compare_convert_fusion.1 = f32[3]{0:T(128)S(1)} fusion(s32[]{:T(128)} %bitcast.20), kind=kLoop, calls=%fused_computation.104 | loop fusion | flops 6 | bytes 16 | tf_op jit(solution)/shard_map/convert_element_type | solution.py:107
  11.1 1.6 %convolution_select_fusion = f32[8,8]{1,0:T(8,128)S(1)} fusion(f32[8,512]{1,0:T(8,128)} %param.11, pred[]{:T(512)} %compare_reduce_fusion), kind=kOutput, calls=%fused_computation.10 | convolution fusion | flops 393280 | bytes 16641 | tf_op jit(solution)/shard_map/dot_general | solution.py:119
  12.7 0.7 %compare_convert_fusion = f32[3]{0:T(128)S(1)} fusion(s32[]{:T(128)} %bitcast.26), kind=kLoop, calls=%fused_computation.103 | loop fusion | flops 6 | bytes 16 | tf_op jit(solution)/shard_map/convert_element_type | solution.py:107
  13.5 0.6 %compare_reduce_fusion.1 = pred[]{:T(512)} fusion(), kind=kLoop, calls=%fused_computation.102 | loop fusion | flops 5 | bytes 1 | tf_op jit(solution)/shard_map/reduce.2
  14.1 0.8 %maximum_select_fusion.2 = f32[8,1024]{1,0:T(8,128)S(1)} fusion(f32[8,512]{1,0:T(8,128)} %param.11, f32[8,512]{1,0:T(8,128)S(1)} %collective-permute-done, pred[]{:T(512)S(6)} %eq.88), kind=kLoop, calls=%fused_computation.31 | loop fusion | flops 24576 | bytes 65537 | tf_op jit(solution)/shard_map/jit(_where)/select_n | solution.py:39
  14.9 1.5 %collective-permute-start.1 = (f32[8,1024]{1,0:T(8,128)S(1)}, f32[8,1024]{1,0:T(8,128)S(1)}, u32[]{:S(2)}, u32[]{:S(2)}) collective-permute-start(f32[8,1024]{1,0:T(8,128)S(1)} %maximum_select_fusion.2), channel_id=1, source_target_pairs={{0,2},{1,3},{2,0},{3,1},{4,6},{5,7},{6,4},{7,5},{8,10},{9,11},{10,... | collective-permute-start | bytes 98312 | tf_op jit(solution)/shard_map/ppermute | solution.py:26
  16.4 0.8 %maximum_select_fusion.3 = f32[8,4,256]{2,0,1:T(8,128)S(1)} fusion(f32[8,2,256]{2,0,1:T(8,128)} %bitcast.83, f32[8,2,256]{2,0,1:T(8,128)S(1)} %bitcast.85, pred[]{:T(512)S(6)} %eq.88), kind=kLoop, calls=%fused_computation.32 | loop fusion | flops 24576 | bytes 65537 | tf_op jit(solution)/shard_map/jit(_where)/select_n | solution.py:39
  17.2 1.6 %collective-permute-done.1 = f32[8,1024]{1,0:T(8,128)S(1)} collective-permute-done((f32[8,1024]{1,0:T(8,128)S(1)}, f32[8,1024]{1,0:T(8,128)S(1)}, u32[]{:S(2)}, u32[]{:S(2)}) %collective-permute-start.1) | collective-permute-done | bytes 32800 | tf_op jit(solution)/shard_map/ppermute | solution.py:26
  18.8 1.3 %collective-permute-start.2 = (f32[8,2048]{1,0:T(8,128)S(1)}, f32[8,2048]{1,0:T(8,128)S(1)}, u32[]{:S(2)}, u32[]{:S(2)}) collective-permute-start(f32[8,2048]{1,0:T(8,128)S(1)} %maximum_select_fusion), channel_id=1, source_target_pairs={{0,4},{4,8},{8,12},{12,16},{16,20},{20,24},{24,28},{1,5},{5,9},{9,... | collective-permute-start | bytes 196616 | tf_op jit(solution)/shard_map/ppermute | solution.py:17
  20.1 1.3 %collective-permute-start.4 = (f32[8,2048]{1,0:T(8,128)S(1)}, f32[8,2048]{1,0:T(8,128)S(1)}, u32[]{:S(2)}, u32[]{:S(2)}) collective-permute-start(f32[8,2048]{1,0:T(8,128)S(1)} %maximum_select_fusion), channel_id=1, source_target_pairs={{4,0},{8,4},{12,8},{16,12},{20,16},{24,20},{28,24},{5,1},{9,5},{13... | collective-permute-start | bytes 196616 | tf_op jit(solution)/shard_map/ppermute | solution.py:17
  21.4 0.6 gather_fusion.2
  22.0 1.6 %fusion.5 = f32[3,8,256]{2,1,0:T(8,128)S(1)} fusion(f32[1,5,3,256,256]{4,3,2,1,0:T(8,128)} %param.12, f32[3,8,256]{2,1,0:T(8,128)S(1)} %gather_fusion.2, pred[3]{0:T(512)(128)(4,1)S(1)} %compare_and_fusion.2), kind=kOutput, calls=%fused_computation.16 | convolution fusion | flops 18880512 | bytes 835587 | tf_op jit(solution)/shard_map/ist,stu->isu/dot_general | solution.py:108
  23.6 0.6 gather_fusion.1
  24.2 1.6 %fusion.7 = f32[3,8,256]{2,1,0:T(8,128)S(1)} fusion(f32[1,5,3,256,256]{4,3,2,1,0:T(8,128)} %param.12, f32[3,8,256]{2,1,0:T(8,128)S(1)} %gather_fusion.1, pred[3]{0:T(512)(128)(4,1)S(1)} %compare_and_fusion.3), kind=kOutput, calls=%fused_computation.18 | convolution fusion | flops 18880512 | bytes 835587 | tf_op jit(solution)/shard_map/ist,stu->isu/dot_general | solution.py:108
  25.8 0.6 gather_fusion.3
  26.4 4.8 %collective-permute-start.3 = (f32[8,2048]{1,0:T(8,128)S(1)}, f32[8,2048]{1,0:T(8,128)S(1)}, u32[]{:S(2)}, u32[]{:S(2)}) collective-permute-start(f32[8,2048]{1,0:T(8,128)S(1)} %collective-permute-done.2), channel_id=1, source_target_pairs={{0,4},{4,8},{8,12},{12,16},{16,20},{20,24},{24,28},{1,5},{5,9},{9,... | collective-permute-start | bytes 196616 | tf_op jit(solution)/shard_map/ppermute | solution.py:17
  31.2 1.6 %fusion.3 = f32[3,8,256]{2,1,0:T(8,128)S(1)} fusion(f32[1,5,3,256,256]{4,3,2,1,0:T(8,128)} %param.12, f32[3,8,256]{2,1,0:T(8,128)S(1)} %gather_fusion.3, pred[3]{0:T(512)(128)(4,1)S(1)} %compare_and_fusion.1), kind=kOutput, calls=%fused_computation.14 | convolution fusion | flops 18880512 | bytes 835587 | tf_op jit(solution)/shard_map/ist,stu->isu/dot_general | solution.py:108
  32.8 1.3 %collective-permute-start.5 = (f32[8,2048]{1,0:T(8,128)S(1)}, f32[8,2048]{1,0:T(8,128)S(1)}, u32[]{:S(2)}, u32[]{:S(2)}) collective-permute-start(f32[8,2048]{1,0:T(8,128)S(1)} %collective-permute-done.4), channel_id=1, source_target_pairs={{4,0},{8,4},{12,8},{16,12},{20,16},{24,20},{28,24},{5,1},{9,5},{13... | collective-permute-start | bytes 196616 | tf_op jit(solution)/shard_map/ppermute | solution.py:17
  34.1 0.6 gather_fusion
  34.7 1.6 %fusion.9 = f32[3,8,256]{2,1,0:T(8,128)S(1)} fusion(f32[1,5,3,256,256]{4,3,2,1,0:T(8,128)} %param.12, f32[3,8,256]{2,1,0:T(8,128)S(1)} %gather_fusion, pred[3]{0:T(512)(128)(4,1)S(1)} %compare_and_fusion.4), kind=kOutput, calls=%fused_computation.20 | convolution fusion | flops 18880512 | bytes 835587 | tf_op jit(solution)/shard_map/ist,stu->isu/dot_general | solution.py:108
  36.3 0.9 %collective-permute-done.5 = f32[8,2048]{1,0:T(8,128)S(1)} collective-permute-done((f32[8,2048]{1,0:T(8,128)S(1)}, f32[8,2048]{1,0:T(8,128)S(1)}, u32[]{:S(2)}, u32[]{:S(2)}) %collective-permute-start.5) | collective-permute-done | bytes 65568 | tf_op jit(solution)/shard_map/ppermute | solution.py:17
  37.2 0.5 gather_fusion.4
  37.8 1.6 %fusion.1 = f32[3,8,256]{2,1,0:T(8,128)S(1)} fusion(f32[1,5,3,256,256]{4,3,2,1,0:T(8,128)} %param.12, f32[3,8,256]{2,1,0:T(8,128)S(1)} %gather_fusion.4, pred[3]{0:T(512)(128)(4,1)S(1)} %compare_and_fusion), kind=kOutput, calls=%fused_computation.12 | convolution fusion | flops 18880512 | bytes 835587 | tf_op jit(solution)/shard_map/ist,stu->isu/dot_general | solution.py:108
  39.4 0.4 fusion.20
  39.7 0.3 convolution_add_fusion.3
  40.4 0.3 convolution_add_fusion.1
  40.7 0.3 fusion
  41.1 0.9 %convolution_select_fusion.1 = f32[8,8]{1,0:T(8,128)S(1)} fusion(f32[8,2048]{1,0:T(8,128)S(1)} %maximum_select_fusion, f32[8,2048]{1,0:T(8,128)S(1)} %bitcast.81, pred[]{:T(512)} %compare_reduce_fusion.1), kind=kOutput, calls=%fused_computation.11 | convolution fusion | flops 1572928 | bytes 131329 | tf_op jit(solution)/shard_map/dot_general | solution.py:122
  42.3 1.6 %collective-permute-start.6 = (f32[8,1152]{1,0:T(8,128)S(1)}, f32[8,1152]{1,0:T(8,128)S(1)}, u32[]{:S(2)}, u32[]{:S(2)}) collective-permute-start(f32[8,1152]{1,0:T(8,128)S(1)} %pad_maximum_fusion), channel_id=1, source_target_pairs={{0,2},{1,3},{2,0},{3,1},{4,6},{5,7},{6,4},{7,5},{8,10},{9,11},{10,... | collective-permute-start | bytes 110600 | tf_op jit(solution)/shard_map/ppermute | solution.py:26
  43.9 2.4 %collective-permute-done.6 = f32[8,1152]{1,0:T(8,128)S(1)} collective-permute-done((f32[8,1152]{1,0:T(8,128)S(1)}, f32[8,1152]{1,0:T(8,128)S(1)}, u32[]{:S(2)}, u32[]{:S(2)}) %collective-permute-start.6) | collective-permute-done | bytes 36896 | tf_op jit(solution)/shard_map/ppermute | solution.py:26
  46.3 0.6 collective-permute-start.7
  46.9 3.2 %collective-permute-done.7 = f32[8,640]{1,0:T(8,128)S(1)} collective-permute-done((f32[8,640]{1,0:T(8,128)S(1)}, f32[8,640]{1,0:T(8,128)S(1)}, u32[]{:S(2)}, u32[]{:S(2)}) %collective-permute-start.7) | collective-permute-done | bytes 20512 | tf_op jit(solution)/shard_map/ppermute | solution.py:26
  50.2 0.6 %collective-permute-start.8 = (f32[8,128]{1,0:T(8,128)S(1)}, f32[8,128]{1,0:T(8,128)S(1)}, u32[]{:S(2)}, u32[]{:S(2)}) collective-permute-start(f32[8,128]{1,0:T(8,128)S(1)} %slice_add_fusion.2), channel_id=1, source_target_pairs={{0,4},{4,0},{8,12},{12,8},{16,20},{20,16},{24,28},{28,24},{1,5},{5... | collective-permute-start | bytes 12296 | tf_op jit(solution)/shard_map/ppermute | solution.py:26
  50.8 0.8 %collective-permute-done.8 = f32[8,128]{1,0:T(8,128)S(1)} collective-permute-done((f32[8,128]{1,0:T(8,128)S(1)}, f32[8,128]{1,0:T(8,128)S(1)}, u32[]{:S(2)}, u32[]{:S(2)}) %collective-permute-start.8) | collective-permute-done | bytes 4128 | tf_op jit(solution)/shard_map/ppermute | solution.py:26
  51.7 2.8 %collective-permute-start.9 = (f32[8,128]{1,0:T(8,128)S(1)}, f32[8,128]{1,0:T(8,128)S(1)}, u32[]{:S(2)}, u32[]{:S(2)}) collective-permute-start(f32[8,128]{1,0:T(8,128)S(1)} %add.70), channel_id=1, source_target_pairs={{0,8},{4,12},{8,0},{12,4},{16,24},{20,28},{24,16},{28,20},{1,9},{5... | collective-permute-start | bytes 12296 | tf_op jit(solution)/shard_map/ppermute | solution.py:26
  54.5 1.6 %collective-permute-done.9 = f32[8,128]{1,0:T(8,128)S(1)} collective-permute-done((f32[8,128]{1,0:T(8,128)S(1)}, f32[8,128]{1,0:T(8,128)S(1)}, u32[]{:S(2)}, u32[]{:S(2)}) %collective-permute-start.9) | collective-permute-done | bytes 4128 | tf_op jit(solution)/shard_map/ppermute | solution.py:26
  56.0 3.0 %collective-permute-start.10 = (f32[8,128]{1,0:T(8,128)S(1)}, f32[8,128]{1,0:T(8,128)S(1)}, u32[]{:S(2)}, u32[]{:S(2)}) collective-permute-start(f32[8,128]{1,0:T(8,128)S(1)} %add.71), channel_id=1, source_target_pairs={{0,16},{4,20},{8,24},{12,28},{16,0},{20,4},{24,8},{28,12},{1,17},{... | collective-permute-start | bytes 12296 | tf_op jit(solution)/shard_map/ppermute | solution.py:26
  59.1 0.6 slice_add_fusion.1
  59.7 1.0 %collective-permute-done.10 = f32[8,128]{1,0:T(8,128)S(1)} collective-permute-done((f32[8,128]{1,0:T(8,128)S(1)}, f32[8,128]{1,0:T(8,128)S(1)}, u32[]{:S(2)}, u32[]{:S(2)}) %collective-permute-start.10) | collective-permute-done | bytes 4128 | tf_op jit(solution)/shard_map/ppermute | solution.py:26
  60.7 0.7 %fusion.82 = (f32[8,8]{1,0:T(8,128)}, f32[8,8]{1,0:T(8,128)}) fusion(f32[8,128]{1,0:T(8,128)S(1)} %add_multiply_fusion), kind=kLoop, calls=%fused_computation.144 | loop fusion | bytes 1024 | tf_op jit(solution)/shard_map/slice | solution.py:130
  (35 shorter events, 0.8 us)
Async XLA Ops:
  0.6 13.5 %collective-permute-start = (f32[8,512]{1,0:T(8,128)}, f32[8,512]{1,0:T(8,128)S(1)}, u32[]{:S(2)}, u32[]{:S(2)}) collective-permute-start(f32[8,512]{1,0:T(8,128)} %param.11), channel_id=1, source_target_pairs={{0,1},{1,0},{2,3},{3,2},{4,5},{5,4},{6,7},{7,6},{8,9},{9,8},{10,11... | collective-permute-start | bytes 49160 | tf_op jit(solution)/shard_map/ppermute | solution.py:26
  14.9 3.9 %collective-permute-start.1 = (f32[8,1024]{1,0:T(8,128)S(1)}, f32[8,1024]{1,0:T(8,128)S(1)}, u32[]{:S(2)}, u32[]{:S(2)}) collective-permute-start(f32[8,1024]{1,0:T(8,128)S(1)} %maximum_select_fusion.2), channel_id=1, source_target_pairs={{0,2},{1,3},{2,0},{3,1},{4,6},{5,7},{6,4},{7,5},{8,10},{9,11},{10,... | collective-permute-start | bytes 98312 | tf_op jit(solution)/shard_map/ppermute | solution.py:26
  18.8 4.8 %collective-permute-start.2 = (f32[8,2048]{1,0:T(8,128)S(1)}, f32[8,2048]{1,0:T(8,128)S(1)}, u32[]{:S(2)}, u32[]{:S(2)}) collective-permute-start(f32[8,2048]{1,0:T(8,128)S(1)} %maximum_select_fusion), channel_id=1, source_target_pairs={{0,4},{4,8},{8,12},{12,16},{16,20},{20,24},{24,28},{1,5},{5,9},{9,... | collective-permute-start | bytes 196616 | tf_op jit(solution)/shard_map/ppermute | solution.py:17
  20.1 5.7 %collective-permute-start.4 = (f32[8,2048]{1,0:T(8,128)S(1)}, f32[8,2048]{1,0:T(8,128)S(1)}, u32[]{:S(2)}, u32[]{:S(2)}) collective-permute-start(f32[8,2048]{1,0:T(8,128)S(1)} %maximum_select_fusion), channel_id=1, source_target_pairs={{4,0},{8,4},{12,8},{16,12},{20,16},{24,20},{28,24},{5,1},{9,5},{13... | collective-permute-start | bytes 196616 | tf_op jit(solution)/shard_map/ppermute | solution.py:17
  26.4 7.8 %collective-permute-start.3 = (f32[8,2048]{1,0:T(8,128)S(1)}, f32[8,2048]{1,0:T(8,128)S(1)}, u32[]{:S(2)}, u32[]{:S(2)}) collective-permute-start(f32[8,2048]{1,0:T(8,128)S(1)} %collective-permute-done.2), channel_id=1, source_target_pairs={{0,4},{4,8},{8,12},{12,16},{16,20},{20,24},{24,28},{1,5},{5,9},{9,... | collective-permute-start | bytes 196616 | tf_op jit(solution)/shard_map/ppermute | solution.py:17
  32.8 4.4 %collective-permute-start.5 = (f32[8,2048]{1,0:T(8,128)S(1)}, f32[8,2048]{1,0:T(8,128)S(1)}, u32[]{:S(2)}, u32[]{:S(2)}) collective-permute-start(f32[8,2048]{1,0:T(8,128)S(1)} %collective-permute-done.4), channel_id=1, source_target_pairs={{4,0},{8,4},{12,8},{16,12},{20,16},{24,20},{28,24},{5,1},{9,5},{13... | collective-permute-start | bytes 196616 | tf_op jit(solution)/shard_map/ppermute | solution.py:17
  42.3 4.0 %collective-permute-start.6 = (f32[8,1152]{1,0:T(8,128)S(1)}, f32[8,1152]{1,0:T(8,128)S(1)}, u32[]{:S(2)}, u32[]{:S(2)}) collective-permute-start(f32[8,1152]{1,0:T(8,128)S(1)} %pad_maximum_fusion), channel_id=1, source_target_pairs={{0,2},{1,3},{2,0},{3,1},{4,6},{5,7},{6,4},{7,5},{8,10},{9,11},{10,... | collective-permute-start | bytes 110600 | tf_op jit(solution)/shard_map/ppermute | solution.py:26
  46.3 3.8 %collective-permute-start.7 = (f32[8,640]{1,0:T(8,128)S(1)}, f32[8,640]{1,0:T(8,128)S(1)}, u32[]{:S(2)}, u32[]{:S(2)}) collective-permute-start(f32[8,640]{1,0:T(8,128)S(1)} %pad_maximum_fusion.1), channel_id=1, source_target_pairs={{0,1},{1,0},{2,3},{3,2},{4,5},{5,4},{6,7},{7,6},{8,9},{9,8},{10,11... | collective-permute-start | bytes 61448 | tf_op jit(solution)/shard_map/ppermute | solution.py:26
  50.2 1.5 %collective-permute-start.8 = (f32[8,128]{1,0:T(8,128)S(1)}, f32[8,128]{1,0:T(8,128)S(1)}, u32[]{:S(2)}, u32[]{:S(2)}) collective-permute-start(f32[8,128]{1,0:T(8,128)S(1)} %slice_add_fusion.2), channel_id=1, source_target_pairs={{0,4},{4,0},{8,12},{12,8},{16,20},{20,16},{24,28},{28,24},{1,5},{5... | collective-permute-start | bytes 12296 | tf_op jit(solution)/shard_map/ppermute | solution.py:26
  51.7 4.4 %collective-permute-start.9 = (f32[8,128]{1,0:T(8,128)S(1)}, f32[8,128]{1,0:T(8,128)S(1)}, u32[]{:S(2)}, u32[]{:S(2)}) collective-permute-start(f32[8,128]{1,0:T(8,128)S(1)} %add.70), channel_id=1, source_target_pairs={{0,8},{4,12},{8,0},{12,4},{16,24},{20,28},{24,16},{28,20},{1,9},{5... | collective-permute-start | bytes 12296 | tf_op jit(solution)/shard_map/ppermute | solution.py:26
  56.0 4.6 %collective-permute-start.10 = (f32[8,128]{1,0:T(8,128)S(1)}, f32[8,128]{1,0:T(8,128)S(1)}, u32[]{:S(2)}, u32[]{:S(2)}) collective-permute-start(f32[8,128]{1,0:T(8,128)S(1)} %add.71), channel_id=1, source_target_pairs={{0,16},{4,20},{8,24},{12,28},{16,0},{20,4},{24,8},{28,12},{1,17},{... | collective-permute-start | bytes 12296 | tf_op jit(solution)/shard_map/ppermute | solution.py:26

commit v2 on v1

--- a/solution.py
+++ b/solution.py
@@ -98,22 +98,19 @@
     group_rows = group_width // TILE
     full_panel = gather_help(vectors)
     panels = neighbour_panels(full_panel)
-    slot_ids = jnp.arange(SLOTS, dtype=jnp.int32)
+    stacked = jnp.stack(panels).reshape(NOFF, VEC, group_rows, TILE).transpose(0, 2, 1, 3)
+    offset_ids = jnp.arange(NOFF, dtype=jnp.int32)[:, None]
+    pieces = stacked[offset_ids, tile_col[0]]
+    contribution = jnp.einsum(
+        "osit,ostu->osiu", pieces, tile_blocks[0], precision=lax.Precision.HIGHEST
+    )
+    slot_ids = jnp.arange(SLOTS, dtype=jnp.int32)[None, :]
     row_ids = jnp.arange(group_rows, dtype=jnp.int32)
-    partial_value = jnp.zeros((VEC, group_rows, TILE), jnp.float32)
-    for offset_index in range(NOFF):
-        panel_tiles = panels[offset_index].reshape(VEC, group_rows, TILE)
-        pieces = jnp.take(panel_tiles, tile_col[0, offset_index], axis=1)
-        live = (slot_ids < counts[0, offset_index]).astype(jnp.float32)
-        contribution = jnp.einsum(
-            "ist,stu->isu", pieces, tile_blocks[0, offset_index], precision=lax.Precision.HIGHEST
-        )
-        one_hot = (tile_row[0, offset_index][:, None] == row_ids[None, :]).astype(
-            jnp.float32
-        ) * live[:, None]
-        partial_value = partial_value + jnp.einsum(
-            "isu,sr->iru", contribution, one_hot, precision=lax.Precision.HIGHEST
-        )
+    live = (slot_ids < counts[0][:, None]).astype(jnp.float32)
+    one_hot = (tile_row[0][:, :, None] == row_ids).astype(jnp.float32) * live[:, :, None]
+    partial_value = jnp.einsum(
+        "osiu,osr->iru", contribution, one_hot, precision=lax.Precision.HIGHEST
+    )
     flattened = partial_value.reshape(VEC, group_width)
     basis_size = float(groups * group_width)
     correlation_term = jnp.dot(

time: 62.2 us -> 51.4 us (0.83)
  local copies, waits for them, and re-layouts: 7.86 us -> 2.53 us
  matrix products: 12 us -> 7.08 us
  other arithmetic: 6.88 us -> 4.1 us
  starting transfers between devices: 21.9 us -> 23.5 us
  waiting for transfers between devices: 11.6 us -> 12.7 us
    dot_general x10 -> x2, matrix products: 9.55 us -> 4.66 us  [the longest x1 4.04 us: local(): jnp.einsum('osit,ostu->osiu', pieces, tile_blocks[0], precision=lax.Preci...]
    slice x3 -> x0, local copies, waits for them, and re-layouts: 4.05 us -> none  [the longest x1 1.46 us: local(): live = (slot_ids < counts[0, offset_index]).astype(jnp.float32)]
    convert_element_type x5 -> x1, other arithmetic: 3.16 us -> 0.66 us  [local(): live = (slot_ids < counts[0][:, None]).astype(jnp.float32)]
    gather x5 -> x1, local copies, waits for them, and re-layouts: 2.8 us -> 0.63 us  [local(): pieces = stacked[offset_ids, tile_col[0]]]
    ppermute x4, waiting for transfers between devices: 0.94 us -> 3.02 us  [shifted(): lax.ppermute(value, axis, [(source, source + steps) for source in range(i...]
    ppermute x7, starting transfers between devices: 13.2 us -> 14.3 us  [exchanged(): lax.ppermute(value, axis, [(source, source ^ mask) for source in range(co...]
    ppermute x7, waiting for transfers between devices: 10.7 us -> 9.73 us  [exchanged(): lax.ppermute(value, axis, [(source, source ^ mask) for source in range(co...]
    select_n x4 -> x2, other arithmetic: 1.61 us -> 0.81 us  [gather_help(): jnp.where(upper, jnp.concatenate([other, held], axis=1), jnp.concatenate(...]
  transfers between devices with their start and end apart: 11 -> 11, of which waited for: 7 -> 8; matrix products, arithmetic and copies ran while one was open for 32% -> 11% of each run, Pallas kernels for 0% -> 0%
where the time goes in v2:
time: 51.4 us; the launch traced here: 50.8 us
  starting transfers between devices  23.5 us (46%)
  waiting for transfers between devices  12.7 us (25%)
  matrix products  7.08 us (14%)
  other arithmetic  4.1 us (8%)
  local copies, waits for them, and re-layouts  2.53 us (5%)
  between operations  0.78 us (2%)
    ppermute x7, starting transfers between devices, exchanged(): lax.ppermute(value, axis, [(source, source ^ mask) for source in range(co...  14.3 us
    ppermute x7, waiting for transfers between devices, exchanged(): lax.ppermute(value, axis, [(source, source ^ mask) for source in range(co...  9.73 us
    ppermute x4, starting transfers between devices, shifted(): lax.ppermute(value, axis, [(source, source + steps) for source in range(i...  9.2 us
    dot_general x1, matrix products, local(): jnp.einsum('osit,ostu->osiu', pieces, tile_blocks[0], precision=lax.Preci...  4.04 us
    ppermute x4, waiting for transfers between devices, shifted(): lax.ppermute(value, axis, [(source, source + steps) for source in range(i...  3.02 us
    dot_general x1, matrix products, local(): jnp.dot(vectors, vectors.T, precision=lax.Precision.HIGHEST, preferred_el...  1.57 us
    another operation x2, other arithmetic  1.28 us
  transfers between devices with their start and end apart: 11, of which 8 were waited for; matrix products, arithmetic and copies ran while one was open for 11% of the time, Pallas kernels for 0%

profile of v2, /device:TPU:0, one launch (start us, length us, event | category | flops | bytes accessed | tf_op | source)
XLA Modules:
  0.0 50.8 jit_solution(14641943051880057983)
XLA Ops:
  0.6 3.0 %collective-permute-start = (f32[8,512]{1,0:T(8,128)}, f32[8,512]{1,0:T(8,128)S(1)}, u32[]{:S(2)}, u32[]{:S(2)}) collective-permute-start(f32[8,512]{1,0:T(8,128)} %param.9), channel_id=1, source_target_pairs={{0,1},{1,0},{2,3},{3,2},{4,5},{5,4},{6,7},{7,6},{8,9},{9,8},{10,11... | collective-permute-start | bytes 49160 | tf_op jit(solution)/shard_map/ppermute | solution.py:26
  3.6 0.6 %compare_reduce_fusion = pred[]{:T(512)} fusion(), kind=kLoop, calls=%fused_computation.34 | loop fusion | flops 7 | bytes 1 | tf_op jit(solution)/shard_map/reduce.3
  4.3 1.3 %collective-permute-done = f32[8,512]{1,0:T(8,128)S(1)} collective-permute-done((f32[8,512]{1,0:T(8,128)}, f32[8,512]{1,0:T(8,128)S(1)}, u32[]{:S(2)}, u32[]{:S(2)}) %collective-permute-start) | collective-permute-done | bytes 16416 | tf_op jit(solution)/shard_map/ppermute | solution.py:26
  5.6 0.8 %maximum_select_fusion.2 = f32[8,1024]{1,0:T(8,128)S(1)} fusion(f32[8,512]{1,0:T(8,128)} %param.9, f32[8,512]{1,0:T(8,128)S(1)} %collective-permute-done, pred[]{:T(512)S(6)} %eq.28), kind=kLoop, calls=%fused_computation.12 | loop fusion | flops 24576 | bytes 65537 | tf_op jit(solution)/shard_map/jit(_where)/select_n | solution.py:39
  6.4 2.0 %collective-permute-start.1 = (f32[8,1024]{1,0:T(8,128)S(1)}, f32[8,1024]{1,0:T(8,128)S(1)}, u32[]{:S(2)}, u32[]{:S(2)}) collective-permute-start(f32[8,1024]{1,0:T(8,128)S(1)} %maximum_select_fusion.2), channel_id=1, source_target_pairs={{0,2},{1,3},{2,0},{3,1},{4,6},{5,7},{6,4},{7,5},{8,10},{9,11},{10,... | collective-permute-start | bytes 98312 | tf_op jit(solution)/shard_map/ppermute | solution.py:26
  8.4 1.6 %convolution_select_fusion = f32[8,8]{1,0:T(8,128)S(1)} fusion(f32[8,512]{1,0:T(8,128)} %param.9, pred[]{:T(512)} %compare_reduce_fusion), kind=kOutput, calls=%fused_computation.4 | convolution fusion | flops 393280 | bytes 16641 | tf_op jit(solution)/shard_map/dot_general | solution.py:116
  10.0 0.3 collective-permute-done.1
  10.3 1.3 %collective-permute-start.2 = (f32[8,2048]{1,0:T(8,128)S(1)}, f32[8,2048]{1,0:T(8,128)S(1)}, u32[]{:S(2)}, u32[]{:S(2)}) collective-permute-start(f32[8,2048]{1,0:T(8,128)S(1)} %maximum_select_fusion), channel_id=1, source_target_pairs={{0,4},{4,8},{8,12},{12,16},{16,20},{20,24},{24,28},{1,5},{5,9},{9,... | collective-permute-start | bytes 196616 | tf_op jit(solution)/shard_map/ppermute | solution.py:17
  11.6 0.7 %fusion.12 = s32[5,3,1]{0,2,1:T(1,128)S(1)} fusion(s32[1,5,3]{1,0,2:T(1,128)} %param.12), kind=kLoop, calls=%fused_computation.38 | loop fusion | flops 120 | bytes 120 | tf_op jit(solution)/shard_map/concatenate | solution.py:103
  12.3 1.3 %collective-permute-start.4 = (f32[8,2048]{1,0:T(8,128)S(1)}, f32[8,2048]{1,0:T(8,128)S(1)}, u32[]{:S(2)}, u32[]{:S(2)}) collective-permute-start(f32[8,2048]{1,0:T(8,128)S(1)} %maximum_select_fusion), channel_id=1, source_target_pairs={{4,0},{8,4},{12,8},{16,12},{20,16},{24,20},{28,24},{5,1},{9,5},{13... | collective-permute-start | bytes 196616 | tf_op jit(solution)/shard_map/ppermute | solution.py:17
  13.6 0.0 collective-permute-done.2
  13.6 5.3 %collective-permute-start.3 = (f32[8,2048]{1,0:T(8,128)S(1)}, f32[8,2048]{1,0:T(8,128)S(1)}, u32[]{:S(2)}, u32[]{:S(2)}) collective-permute-start(f32[8,2048]{1,0:T(8,128)S(1)} %collective-permute-done.2), channel_id=1, source_target_pairs={{0,4},{4,8},{8,12},{12,16},{16,20},{20,24},{24,28},{1,5},{5,9},{9,... | collective-permute-start | bytes 196616 | tf_op jit(solution)/shard_map/ppermute | solution.py:17
  19.0 0.7 %fusion.9 = f32[5,3]{0,1:T(4,128)S(1)} fusion(s32[5]{0:T(128)} %bitcast.46), kind=kLoop, calls=%fused_computation.33 | loop fusion | flops 30 | bytes 80 | tf_op jit(solution)/shard_map/convert_element_type | solution.py:109
  19.6 0.1 copy.9
  19.7 0.1 reshape.197
  19.8 0.7 %copy.17 = s32[1,5,3]{1,2,0:T(4,128)S(1)} copy(s32[1,5,3]{1,0,2:T(1,128)} %param.11) | data formatting | bytes 120
  20.5 0.6 %compare_reduce_fusion.1 = pred[]{:T(512)} fusion(), kind=kLoop, calls=%fused_computation.35 | loop fusion | flops 5 | bytes 1 | tf_op jit(solution)/shard_map/reduce.2
  21.1 0.0 collective-permute-done.4
  21.1 1.3 %collective-permute-start.5 = (f32[8,2048]{1,0:T(8,128)S(1)}, f32[8,2048]{1,0:T(8,128)S(1)}, u32[]{:S(2)}, u32[]{:S(2)}) collective-permute-start(f32[8,2048]{1,0:T(8,128)S(1)} %collective-permute-done.4), channel_id=1, source_target_pairs={{4,0},{8,4},{12,8},{16,12},{20,16},{24,20},{28,24},{5,1},{9,5},{13... | collective-permute-start | bytes 196616 | tf_op jit(solution)/shard_map/ppermute | solution.py:17
  22.4 0.0 collective-permute-done.3
  22.5 3.0 %collective-permute-done.5 = f32[8,2048]{1,0:T(8,128)S(1)} collective-permute-done((f32[8,2048]{1,0:T(8,128)S(1)}, f32[8,2048]{1,0:T(8,128)S(1)}, u32[]{:S(2)}, u32[]{:S(2)}) %collective-permute-start.5) | collective-permute-done | bytes 65568 | tf_op jit(solution)/shard_map/ppermute | solution.py:17
  25.5 0.6 %gather_fusion = f32[15,8,256]{2,1,0:T(8,128)S(1)} fusion(f32[5,8,8,256]{3,2,1,0:T(8,128)S(1)} %bitcast.40, s32[15]{0:T(128)S(1)} %reshape.197), kind=kCustom, calls=%fused_computation | custom fusion | bytes 245880 | tf_op jit(solution)/shard_map/gather | solution.py:103
  26.1 4.0 %fusion = f32[5,3,8,256]{3,2,1,0:T(8,128)S(1)} fusion(f32[5,3,8,256]{3,2,1,0:T(8,128)S(1)} %bitcast.37, f32[1,5,3,256,256]{4,3,2,1,0:T(8,128)} %param.10), kind=kOutput, calls=%fused_computation.1 | convolution fusion | flops 94371840 | bytes 4177920 | tf_op jit(solution)/shard_map/osit,ostu->osiu/dot_general | solution.py:104
  30.2 0.6 %convolution_bitcast_fusion = f32[1,8,8,256]{3,2,1,0:T(8,128)S(1)} fusion(f32[5,3,8,256]{3,2,1,0:T(8,128)S(1)} %fusion, f32[5,3]{0,1:T(4,128)S(1)} %fusion.9, s32[5,3]{0,1:T(4,128)S(1)} %bitcast.45), kind=kOutput, calls=%fused_computation.3 | convolution fusion | flops 2949360 | bytes 188536 | tf_op jit(solution)/shard_map/osiu,osr->iru/dot_general | solution.py:111
  30.8 0.9 %convolution_select_fusion.1 = f32[8,8]{1,0:T(8,128)S(1)} fusion(f32[8,2048]{1,0:T(8,128)S(1)} %maximum_select_fusion, f32[8,2048]{1,0:T(8,128)S(1)} %bitcast.35, pred[]{:T(512)} %compare_reduce_fusion.1), kind=kOutput, calls=%fused_computation.5 | convolution fusion | flops 1572928 | bytes 131329 | tf_op jit(solution)/shard_map/dot_general | solution.py:119
  31.7 0.3 scatter.9
  32.0 1.6 %collective-permute-start.6 = (f32[8,1152]{1,0:T(8,128)S(1)}, f32[8,1152]{1,0:T(8,128)S(1)}, u32[]{:S(2)}, u32[]{:S(2)}) collective-permute-start(f32[8,1152]{1,0:T(8,128)S(1)} %pad_maximum_fusion), channel_id=1, source_target_pairs={{0,2},{1,3},{2,0},{3,1},{4,6},{5,7},{6,4},{7,5},{8,10},{9,11},{10,... | collective-permute-start | bytes 110600 | tf_op jit(solution)/shard_map/ppermute | solution.py:26
  33.6 2.4 %collective-permute-done.6 = f32[8,1152]{1,0:T(8,128)S(1)} collective-permute-done((f32[8,1152]{1,0:T(8,128)S(1)}, f32[8,1152]{1,0:T(8,128)S(1)}, u32[]{:S(2)}, u32[]{:S(2)}) %collective-permute-start.6) | collective-permute-done | bytes 36896 | tf_op jit(solution)/shard_map/ppermute | solution.py:26
  36.1 1.6 %collective-permute-start.7 = (f32[8,640]{1,0:T(8,128)S(1)}, f32[8,640]{1,0:T(8,128)S(1)}, u32[]{:S(2)}, u32[]{:S(2)}) collective-permute-start(f32[8,640]{1,0:T(8,128)S(1)} %pad_maximum_fusion.1), channel_id=1, source_target_pairs={{0,1},{1,0},{2,3},{3,2},{4,5},{5,4},{6,7},{7,6},{8,9},{9,8},{10,11... | collective-permute-start | bytes 61448 | tf_op jit(solution)/shard_map/ppermute | solution.py:26
  37.7 2.3 %collective-permute-done.7 = f32[8,640]{1,0:T(8,128)S(1)} collective-permute-done((f32[8,640]{1,0:T(8,128)S(1)}, f32[8,640]{1,0:T(8,128)S(1)}, u32[]{:S(2)}, u32[]{:S(2)}) %collective-permute-start.7) | collective-permute-done | bytes 20512 | tf_op jit(solution)/shard_map/ppermute | solution.py:26
  40.0 0.6 %collective-permute-start.8 = (f32[8,128]{1,0:T(8,128)S(1)}, f32[8,128]{1,0:T(8,128)S(1)}, u32[]{:S(2)}, u32[]{:S(2)}) collective-permute-start(f32[8,128]{1,0:T(8,128)S(1)} %slice_add_fusion.2), channel_id=1, source_target_pairs={{0,4},{4,0},{8,12},{12,8},{16,20},{20,16},{24,28},{28,24},{1,5},{5... | collective-permute-start | bytes 12296 | tf_op jit(solution)/shard_map/ppermute | solution.py:26
  40.6 0.8 %collective-permute-done.8 = f32[8,128]{1,0:T(8,128)S(1)} collective-permute-done((f32[8,128]{1,0:T(8,128)S(1)}, f32[8,128]{1,0:T(8,128)S(1)}, u32[]{:S(2)}, u32[]{:S(2)}) %collective-permute-start.8) | collective-permute-done | bytes 4128 | tf_op jit(solution)/shard_map/ppermute | solution.py:26
  41.4 2.5 %collective-permute-start.9 = (f32[8,128]{1,0:T(8,128)S(1)}, f32[8,128]{1,0:T(8,128)S(1)}, u32[]{:S(2)}, u32[]{:S(2)}) collective-permute-start(f32[8,128]{1,0:T(8,128)S(1)} %add.56), channel_id=1, source_target_pairs={{0,8},{4,12},{8,0},{12,4},{16,24},{20,28},{24,16},{28,20},{1,9},{5... | collective-permute-start | bytes 12296 | tf_op jit(solution)/shard_map/ppermute | solution.py:26
  43.9 1.6 %collective-permute-done.9 = f32[8,128]{1,0:T(8,128)S(1)} collective-permute-done((f32[8,128]{1,0:T(8,128)S(1)}, f32[8,128]{1,0:T(8,128)S(1)}, u32[]{:S(2)}, u32[]{:S(2)}) %collective-permute-start.9) | collective-permute-done | bytes 4128 | tf_op jit(solution)/shard_map/ppermute | solution.py:26
  45.5 3.0 %collective-permute-start.10 = (f32[8,128]{1,0:T(8,128)S(1)}, f32[8,128]{1,0:T(8,128)S(1)}, u32[]{:S(2)}, u32[]{:S(2)}) collective-permute-start(f32[8,128]{1,0:T(8,128)S(1)} %add.57), channel_id=1, source_target_pairs={{0,16},{4,20},{8,24},{12,28},{16,0},{20,4},{24,8},{28,12},{1,17},{... | collective-permute-start | bytes 12296 | tf_op jit(solution)/shard_map/ppermute | solution.py:26
  48.5 0.6 %slice_add_fusion.1 = f32[8,512]{1,0:T(8,128)} fusion(f32[8,640]{1,0:T(8,128)S(1)} %collective-permute-done.7, f32[8,1024]{1,0:T(8,128)S(1)} %slice_add_fusion, pred[]{:T(512)S(6)} %eq.28), kind=kLoop, calls=%fused_computation.15 | loop fusion | flops 8192 | bytes 65537 | tf_op jit(solution)/shard_map/add | solution.py:63
  49.1 1.0 %collective-permute-done.10 = f32[8,128]{1,0:T(8,128)S(1)} collective-permute-done((f32[8,128]{1,0:T(8,128)S(1)}, f32[8,128]{1,0:T(8,128)S(1)}, u32[]{:S(2)}, u32[]{:S(2)}) %collective-permute-start.10) | collective-permute-done | bytes 4128 | tf_op jit(solution)/shard_map/ppermute | solution.py:26
  50.1 0.7 %fusion.14 = (f32[8,8]{1,0:T(8,128)}, f32[8,8]{1,0:T(8,128)}) fusion(f32[8,128]{1,0:T(8,128)S(1)} %add_multiply_fusion), kind=kLoop, calls=%fused_computation.41 | loop fusion | bytes 1024 | tf_op jit(solution)/shard_map/slice | solution.py:127
  (18 shorter events, 0.1 us)
Async XLA Ops:
  0.6 4.9 %collective-permute-start = (f32[8,512]{1,0:T(8,128)}, f32[8,512]{1,0:T(8,128)S(1)}, u32[]{:S(2)}, u32[]{:S(2)}) collective-permute-start(f32[8,512]{1,0:T(8,128)} %param.9), channel_id=1, source_target_pairs={{0,1},{1,0},{2,3},{3,2},{4,5},{5,4},{6,7},{7,6},{8,9},{9,8},{10,11... | collective-permute-start | bytes 49160 | tf_op jit(solution)/shard_map/ppermute | solution.py:26
  6.4 3.9 %collective-permute-start.1 = (f32[8,1024]{1,0:T(8,128)S(1)}, f32[8,1024]{1,0:T(8,128)S(1)}, u32[]{:S(2)}, u32[]{:S(2)}) collective-permute-start(f32[8,1024]{1,0:T(8,128)S(1)} %maximum_select_fusion.2), channel_id=1, source_target_pairs={{0,2},{1,3},{2,0},{3,1},{4,6},{5,7},{6,4},{7,5},{8,10},{9,11},{10,... | collective-permute-start | bytes 98312 | tf_op jit(solution)/shard_map/ppermute | solution.py:26
  10.3 3.3 %collective-permute-start.2 = (f32[8,2048]{1,0:T(8,128)S(1)}, f32[8,2048]{1,0:T(8,128)S(1)}, u32[]{:S(2)}, u32[]{:S(2)}) collective-permute-start(f32[8,2048]{1,0:T(8,128)S(1)} %maximum_select_fusion), channel_id=1, source_target_pairs={{0,4},{4,8},{8,12},{12,16},{16,20},{20,24},{24,28},{1,5},{5,9},{9,... | collective-permute-start | bytes 196616 | tf_op jit(solution)/shard_map/ppermute | solution.py:17
  12.3 8.8 %collective-permute-start.4 = (f32[8,2048]{1,0:T(8,128)S(1)}, f32[8,2048]{1,0:T(8,128)S(1)}, u32[]{:S(2)}, u32[]{:S(2)}) collective-permute-start(f32[8,2048]{1,0:T(8,128)S(1)} %maximum_select_fusion), channel_id=1, source_target_pairs={{4,0},{8,4},{12,8},{16,12},{20,16},{24,20},{28,24},{5,1},{9,5},{13... | collective-permute-start | bytes 196616 | tf_op jit(solution)/shard_map/ppermute | solution.py:17
  13.6 8.8 %collective-permute-start.3 = (f32[8,2048]{1,0:T(8,128)S(1)}, f32[8,2048]{1,0:T(8,128)S(1)}, u32[]{:S(2)}, u32[]{:S(2)}) collective-permute-start(f32[8,2048]{1,0:T(8,128)S(1)} %collective-permute-done.2), channel_id=1, source_target_pairs={{0,4},{4,8},{8,12},{12,16},{16,20},{20,24},{24,28},{1,5},{5,9},{9,... | collective-permute-start | bytes 196616 | tf_op jit(solution)/shard_map/ppermute | solution.py:17
  21.1 4.4 %collective-permute-start.5 = (f32[8,2048]{1,0:T(8,128)S(1)}, f32[8,2048]{1,0:T(8,128)S(1)}, u32[]{:S(2)}, u32[]{:S(2)}) collective-permute-start(f32[8,2048]{1,0:T(8,128)S(1)} %collective-permute-done.4), channel_id=1, source_target_pairs={{4,0},{8,4},{12,8},{16,12},{20,16},{24,20},{28,24},{5,1},{9,5},{13... | collective-permute-start | bytes 196616 | tf_op jit(solution)/shard_map/ppermute | solution.py:17
  32.0 4.0 %collective-permute-start.6 = (f32[8,1152]{1,0:T(8,128)S(1)}, f32[8,1152]{1,0:T(8,128)S(1)}, u32[]{:S(2)}, u32[]{:S(2)}) collective-permute-start(f32[8,1152]{1,0:T(8,128)S(1)} %pad_maximum_fusion), channel_id=1, source_target_pairs={{0,2},{1,3},{2,0},{3,1},{4,6},{5,7},{6,4},{7,5},{8,10},{9,11},{10,... | collective-permute-start | bytes 110600 | tf_op jit(solution)/shard_map/ppermute | solution.py:26
  36.1 3.8 %collective-permute-start.7 = (f32[8,640]{1,0:T(8,128)S(1)}, f32[8,640]{1,0:T(8,128)S(1)}, u32[]{:S(2)}, u32[]{:S(2)}) collective-permute-start(f32[8,640]{1,0:T(8,128)S(1)} %pad_maximum_fusion.1), channel_id=1, source_target_pairs={{0,1},{1,0},{2,3},{3,2},{4,5},{5,4},{6,7},{7,6},{8,9},{9,8},{10,11... | collective-permute-start | bytes 61448 | tf_op jit(solution)/shard_map/ppermute | solution.py:26
  40.0 1.5 %collective-permute-start.8 = (f32[8,128]{1,0:T(8,128)S(1)}, f32[8,128]{1,0:T(8,128)S(1)}, u32[]{:S(2)}, u32[]{:S(2)}) collective-permute-start(f32[8,128]{1,0:T(8,128)S(1)} %slice_add_fusion.2), channel_id=1, source_target_pairs={{0,4},{4,0},{8,12},{12,8},{16,20},{20,16},{24,28},{28,24},{1,5},{5... | collective-permute-start | bytes 12296 | tf_op jit(solution)/shard_map/ppermute | solution.py:26
  41.4 4.1 %collective-permute-start.9 = (f32[8,128]{1,0:T(8,128)S(1)}, f32[8,128]{1,0:T(8,128)S(1)}, u32[]{:S(2)}, u32[]{:S(2)}) collective-permute-start(f32[8,128]{1,0:T(8,128)S(1)} %add.56), channel_id=1, source_target_pairs={{0,8},{4,12},{8,0},{12,4},{16,24},{20,28},{24,16},{28,20},{1,9},{5... | collective-permute-start | bytes 12296 | tf_op jit(solution)/shard_map/ppermute | solution.py:26
  45.5 4.6 %collective-permute-start.10 = (f32[8,128]{1,0:T(8,128)S(1)}, f32[8,128]{1,0:T(8,128)S(1)}, u32[]{:S(2)}, u32[]{:S(2)}) collective-permute-start(f32[8,128]{1,0:T(8,128)S(1)} %add.57), channel_id=1, source_target_pairs={{0,16},{4,20},{8,24},{12,28},{16,0},{20,4},{24,8},{28,12},{1,17},{... | collective-permute-start | bytes 12296 | tf_op jit(solution)/shard_map/ppermute | solution.py:26

commit v3 on v2

--- a/solution.py
+++ b/solution.py
@@ -26,19 +26,21 @@
     return lax.ppermute(value, axis, [(source, source ^ mask) for source in range(count)])
 
 
+def help_order():
+    count = lax.axis_size("help")
+    if not is_power_of_two(count):
+        return jnp.int32(0)
+    return lax.axis_index("help").astype(jnp.int32)
+
+
 def gather_help(piece):
     count = lax.axis_size("help")
     if not is_power_of_two(count):
         return lax.all_gather(piece, "help", axis=1, tiled=True)
-    index = lax.axis_index("help")
     held = piece
     mask = 1
     while mask < count:
-        other = exchanged(held, "help", mask)
-        upper = (index // mask) % 2 == 1
-        held = jnp.where(
-            upper, jnp.concatenate([other, held], axis=1), jnp.concatenate([held, other], axis=1)
-        )
+        held = jnp.concatenate([held, exchanged(held, "help", mask)], axis=1)
         mask *= 2
     return held
 
@@ -50,17 +52,12 @@
             lax.psum_scatter(partial, "help", scatter_dimension=1, tiled=True),
             lax.psum(gram, "help"),
         )
-    index = lax.axis_index("help")
     held = partial
     mask = count // 2
     while mask >= 1:
         half = held.shape[1] // 2
-        lower, upper = held[:, :half], held[:, half:]
-        high = (index // mask) % 2 == 1
-        keep = jnp.where(high, upper, lower)
-        send = jnp.where(high, lower, upper)
-        arrived = exchanged(jnp.concatenate([send, gram], axis=1), "help", mask)
-        held = keep + arrived[:, :half]
+        arrived = exchanged(jnp.concatenate([held[:, half:], gram], axis=1), "help", mask)
+        held = held[:, :half] + arrived[:, :half]
         gram = gram + arrived[:, half:]
         mask //= 2
     return held, gram
@@ -98,19 +95,31 @@
     group_rows = group_width // TILE
     full_panel = gather_help(vectors)
     panels = neighbour_panels(full_panel)
-    stacked = jnp.stack(panels).reshape(NOFF, VEC, group_rows, TILE).transpose(0, 2, 1, 3)
-    offset_ids = jnp.arange(NOFF, dtype=jnp.int32)[:, None]
-    pieces = stacked[offset_ids, tile_col[0]]
-    contribution = jnp.einsum(
-        "osit,ostu->osiu", pieces, tile_blocks[0], precision=lax.Precision.HIGHEST
-    )
+    tiles_per_piece = piece_width // TILE
+    order = help_order()
+
+    def placed(tile_index):
+        return ((tile_index // tiles_per_piece) ^ order) * tiles_per_piece + tile_index % tiles_per_piece
+
+    column_place = placed(tile_col[0])
+    row_place = placed(tile_row[0])
     slot_ids = jnp.arange(SLOTS, dtype=jnp.int32)[None, :]
     row_ids = jnp.arange(group_rows, dtype=jnp.int32)
     live = (slot_ids < counts[0][:, None]).astype(jnp.float32)
-    one_hot = (tile_row[0][:, :, None] == row_ids).astype(jnp.float32) * live[:, :, None]
-    partial_value = jnp.einsum(
-        "osiu,osr->iru", contribution, one_hot, precision=lax.Precision.HIGHEST
-    )
+    one_hot = (row_place[:, :, None] == row_ids).astype(jnp.float32) * live[:, :, None]
+    partial_value = None
+    for batch in ((BAND,), (BAND - 1, BAND + 1), (0, NOFF - 1)):
+        chosen = jnp.array(batch, dtype=jnp.int32)
+        stacked = jnp.stack([panels[o] for o in batch]).reshape(len(batch), VEC, group_rows, TILE)
+        stacked = stacked.transpose(0, 2, 1, 3)
+        pieces = stacked[jnp.arange(len(batch))[:, None], column_place[chosen]]
+        contribution = jnp.einsum(
+            "osit,ostu->osiu", pieces, tile_blocks[0, chosen], precision=lax.Precision.HIGHEST
+        )
+        batch_value = jnp.einsum(
+            "osiu,osr->iru", contribution, one_hot[chosen], precision=lax.Precision.HIGHEST
+        )
+        partial_value = batch_value if partial_value is None else partial_value + batch_value
     flattened = partial_value.reshape(VEC, group_width)
     basis_size = float(groups * group_width)
     correlation_term = jnp.dot(
@@ -119,8 +128,9 @@
     energy_term = jnp.dot(
         full_panel, flattened.T, precision=lax.Precision.HIGHEST, preferred_element_type=jnp.float32
     )
-    gram = jnp.zeros((VEC, GRAM_PAD), jnp.float32)
-    gram = gram.at[:, :VEC].set(energy_term).at[:, VEC : 2 * VEC].set(correlation_term)
+    gram = jnp.concatenate(
+        [energy_term, correlation_term, jnp.zeros((VEC, GRAM_PAD - 2 * VEC), jnp.float32)], axis=1
+    )
     product, gram = reduce_help(flattened, gram)
     gram = reduce_blk(gram)
     gram = gram / basis_size

time: 51.4 us -> 60.2 us (1.17)
  local copies, waits for them, and re-layouts: 2.53 us -> 14.7 us
  other arithmetic: 4.1 us -> 2.26 us
  matrix products: 7.08 us -> 5.9 us
    gather x1 -> x9, local copies, waits for them, and re-layouts: 0.63 us -> 10.9 us  [the longest x2 5.65 us: local(): tile_blocks[0, chosen]]
    ppermute x4, waiting for transfers between devices: 3.02 us -> 0.61 us  [shifted(): lax.ppermute(value, axis, [(source, source + steps) for source in range(i...]
    ppermute x7, waiting for transfers between devices: 9.73 us -> 11.9 us  [exchanged(): lax.ppermute(value, axis, [(source, source ^ mask) for source in range(co...]
    squeeze x0 -> x2, local copies, waits for them, and re-layouts: none -> 1.53 us  [the longest x1 0.77 us: local(): row_place = placed(tile_row[0])]
    another operation x2 -> x0, other arithmetic: 1.28 us -> none
    select_n x4 -> x2, other arithmetic: 0.82 us -> 0.01 us  [the longest x1 0.01 us: local(): pieces = stacked[jnp.arange(len(batch))[:, None], column_place[chosen]]]
    gather x0 -> x1, other arithmetic: none -> 0.66 us  [local(): one_hot[chosen]]
    dot_general x1, matrix products: 1.57 us -> 0.91 us  [local(): jnp.dot(vectors, vectors.T, precision=lax.Precision.HIGHEST, preferred_el...]
  transfers between devices with their start and end apart: 11 -> 11, of which waited for: 8 -> 7; matrix products, arithmetic and copies ran while one was open for 11% -> 29% of each run, Pallas kernels for 0% -> 0%
where the time goes in v3:
time: 60.2 us; the launch traced here: 59.6 us
  starting transfers between devices  23.4 us (39%)
  local copies, waits for them, and re-layouts  14.7 us (24%)
  waiting for transfers between devices  12.5 us (21%)
  matrix products  5.9 us (10%)
  other arithmetic  2.26 us (4%)
  between operations  0.91 us (2%)
    ppermute x7, starting transfers between devices, exchanged(): lax.ppermute(value, axis, [(source, source ^ mask) for source in range(co...  14 us
    ppermute x7, waiting for transfers between devices, exchanged(): lax.ppermute(value, axis, [(source, source ^ mask) for source in range(co...  11.9 us
    ppermute x4, starting transfers between devices, shifted(): lax.ppermute(value, axis, [(source, source + steps) for source in range(i...  9.33 us
    gather x2, local copies, waits for them, and re-layouts, local(): tile_blocks[0, chosen]  5.65 us
    dot_general x3, matrix products, local(): jnp.einsum('osit,ostu->osiu', pieces, tile_blocks[0, chosen], precision=l...  3.31 us
    gather x5, local copies, waits for them, and re-layouts, local(): pieces = stacked[jnp.arange(len(batch))[:, None], column_place[chosen]]  2.95 us
    gather x2, local copies, waits for them, and re-layouts, local(): one_hot[chosen]  2.31 us
    dot_general x3, matrix products, local(): jnp.einsum('osiu,osr->iru', contribution, one_hot[chosen], precision=lax....  1.47 us
  transfers between devices with their start and end apart: 11, of which 7 were waited for; matrix products, arithmetic and copies ran while one was open for 29% of the time, Pallas kernels for 0%

profile of v3, /device:TPU:0, one launch (start us, length us, event | category | flops | bytes accessed | tf_op | source)
XLA Modules:
  0.0 59.6 jit_solution(10094813878209551330)
XLA Ops:
  0.6 3.0 %collective-permute-start = (f32[8,512]{1,0:T(8,128)}, f32[8,512]{1,0:T(8,128)S(1)}, u32[]{:S(2)}, u32[]{:S(2)}) collective-permute-start(f32[8,512]{1,0:T(8,128)} %param.8), channel_id=1, source_target_pairs={{0,1},{1,0},{2,3},{3,2},{4,5},{5,4},{6,7},{7,6},{8,9},{9,8},{10,11... | collective-permute-start | bytes 49160 | tf_op jit(solution)/shard_map/ppermute | solution.py:26
  3.6 0.9 %fusion.38 = f32[8,8]{1,0:T(8,128)S(1)} fusion(f32[8,512]{1,0:T(8,128)} %param.8), kind=kOutput, calls=%fused_computation.89 | convolution fusion | flops 393216 | bytes 16640 | tf_op jit(solution)/shard_map/dot_general | solution.py:125
  4.5 0.7 %constant_dynamic-update-slice_fusion.2 = f32[8,2048]{1,0:T(8,128)S(1)} fusion(f32[8,512]{1,0:T(8,128)} %param.8), kind=kLoop, calls=%fused_computation.30 | loop fusion | bytes 32768
  5.3 0.8 %copy.24 = s32[1,5,3]{2,1,0:T(8,128)S(1)} copy(s32[1,5,3]{1,0,2:T(1,128)} %param.10) | data formatting | bytes 120 | tf_op jit(solution)/shard_map/squeeze | solution.py:105
  6.1 0.8 %copy.25 = s32[1,5,3]{2,1,0:T(8,128)S(1)} copy(s32[1,5,3]{1,0,2:T(1,128)} %param.11) | data formatting | bytes 120 | tf_op jit(solution)/shard_map/squeeze | solution.py:104
  6.9 0.7 %fusion.24 = f32[5,3]{1,0:T(8,128)S(1)} fusion(s32[5]{0:T(128)} %bitcast.110), kind=kLoop, calls=%fused_computation.66 | loop fusion | flops 30 | bytes 80 | tf_op jit(solution)/shard_map/convert_element_type | solution.py:108
  7.6 0.7 %pad_clamp_fusion = (s32[1024]{0:T(1024)S(1)}, s32[1024]{0:T(1024)S(1)}) fusion(s32[2]{0:T(128)S(1)} %compare_select_fusion.2, s32[2]{0:T(128)} %constant.220), kind=kLoop, calls=%fused_computation.49 | loop fusion | flops 2048 | bytes 8208 | tf_op jit(solution)/shard_map/gather | solution.py:120
  8.3 0.6 gather_fusion.6
  8.8 0.6 gather_fusion.2
  9.4 0.1 fusion.8
  9.5 1.2 %gather_fusion.1 = f32[2,3,8]{2,1,0:T(4,128)} fusion(f32[5,3,8]{2,1,0:T(4,128)S(1)} %fusion.8, s32[1024]{0:T(1024)S(1)} %get-tuple-element.41), kind=kCustom, calls=%fused_computation.1 | custom fusion | bytes 392 | tf_op jit(solution)/shard_map/gather | solution.py:120
  10.7 1.2 %gather_fusion.5 = f32[2,3,8]{2,1,0:T(4,128)} fusion(f32[5,3,8]{2,1,0:T(4,128)S(1)} %fusion.8, s32[1024]{0:T(1024)S(1)} %get-tuple-element.40), kind=kCustom, calls=%fused_computation.5 | custom fusion | bytes 392 | tf_op jit(solution)/shard_map/gather | solution.py:120
  11.8 0.6 reshape.264
  12.4 0.1 reshape.292
  12.5 2.9 %gather_fusion.4 = f32[2,3,256,256]{3,2,1,0:T(8,128)S(1)} fusion(f32[1,5,3,256,256]{4,3,2,1,0:T(8,128)} %param.9, s32[2]{0:T(128)} %constant.220), kind=kCustom, calls=%fused_computation.4 | custom fusion | bytes 3145744 | tf_op jit(solution)/shard_map/gather | solution.py:117
  15.4 2.8 %gather_fusion.8 = f32[2,3,256,256]{3,2,1,0:T(8,128)S(1)} fusion(f32[1,5,3,256,256]{4,3,2,1,0:T(8,128)} %param.9, s32[2]{0:T(128)S(1)} %clamp_shift-left_fusion.1), kind=kCustom, calls=%fused_computation.8 | custom fusion | bytes 3145744 | tf_op jit(solution)/shard_map/gather | solution.py:117
  18.2 1.6 %collective-permute-start.1 = (f32[8,1024]{1,0:T(8,128)S(1)}, f32[8,1024]{1,0:T(8,128)S(1)}, u32[]{:S(2)}, u32[]{:S(2)}) collective-permute-start(f32[8,1024]{1,0:T(8,128)S(1)} %pad_maximum_fusion), channel_id=1, source_target_pairs={{0,2},{1,3},{2,0},{3,1},{4,6},{5,7},{6,4},{7,5},{8,10},{9,11},{10,... | collective-permute-start | bytes 98312 | tf_op jit(solution)/shard_map/ppermute | solution.py:26
  19.8 2.4 %collective-permute-done.1 = f32[8,1024]{1,0:T(8,128)S(1)} collective-permute-done((f32[8,1024]{1,0:T(8,128)S(1)}, f32[8,1024]{1,0:T(8,128)S(1)}, u32[]{:S(2)}, u32[]{:S(2)}) %collective-permute-start.1) | collective-permute-done | bytes 32800 | tf_op jit(solution)/shard_map/ppermute | solution.py:26
  22.2 1.3 %collective-permute-start.3 = (f32[8,2048]{1,0:T(8,128)S(1)}, f32[8,2048]{1,0:T(8,128)S(1)}, u32[]{:S(2)}, u32[]{:S(2)}) collective-permute-start(f32[8,2048]{1,0:T(8,128)S(1)} %constant_dynamic-update-slice_fusion), channel_id=1, source_target_pairs={{4,0},{8,4},{12,8},{16,12},{20,16},{24,20},{28,24},{5,1},{9,5},{13... | collective-permute-start | bytes 196616 | tf_op jit(solution)/shard_map/ppermute | solution.py:17
  23.4 3.0 %collective-permute-start.2 = (f32[8,2048]{1,0:T(8,128)S(1)}, f32[8,2048]{1,0:T(8,128)S(1)}, u32[]{:S(2)}, u32[]{:S(2)}) collective-permute-start(f32[8,2048]{1,0:T(8,128)S(1)} %constant_dynamic-update-slice_fusion), channel_id=1, source_target_pairs={{0,4},{4,8},{8,12},{12,16},{16,20},{20,24},{24,28},{1,5},{5,9},{9,... | collective-permute-start | bytes 196616 | tf_op jit(solution)/shard_map/ppermute | solution.py:17
  26.5 0.6 gather_fusion
  27.0 1.6 %fusion.2 = f32[3,8,256]{2,1,0:T(8,128)S(1)} fusion(f32[3,8,256]{2,1,0:T(8,128)S(1)} %gather_fusion, f32[1,5,3,256,256]{4,3,2,1,0:T(8,128)} %param.9), kind=kOutput, calls=%fused_computation.14 | convolution fusion | flops 18874368 | bytes 835584 | tf_op jit(solution)/shard_map/osit,ostu->osiu/dot_general | solution.py:116
  28.7 0.7 %gather_fusion.3 = f32[6,8,256]{2,1,0:T(8,128)S(1)} fusion(f32[2,8,8,256]{3,2,1,0:T(8,128)S(1)} %maximum_bitcast_fusion, s32[6]{0:T(128)} %reshape.264), kind=kCustom, calls=%fused_computation.3 | custom fusion | bytes 98352 | tf_op jit(solution)/shard_map/gather | solution.py:115
  29.4 0.9 %fusion.35 = f32[2,3,8,256]{3,2,1,0:T(8,128)S(1)} fusion(f32[2,3,8,256]{3,2,1,0:T(8,128)S(1)} %bitcast.103, f32[2,3,256,256]{3,2,1,0:T(8,128)S(1)} %gather_fusion.4), kind=kOutput, calls=%fused_computation.86 | convolution fusion | flops 37748736 | bytes 1671168 | tf_op jit(solution)/shard_map/osit,ostu->osiu/dot_general | solution.py:116
  30.3 1.3 %collective-permute-start.5 = (f32[8,2048]{1,0:T(8,128)S(1)}, f32[8,2048]{1,0:T(8,128)S(1)}, u32[]{:S(2)}, u32[]{:S(2)}) collective-permute-start(f32[8,2048]{1,0:T(8,128)S(1)} %collective-permute-done.3), channel_id=1, source_target_pairs={{4,0},{8,4},{12,8},{16,12},{20,16},{24,20},{28,24},{5,1},{9,5},{13... | collective-permute-start | bytes 196616 | tf_op jit(solution)/shard_map/ppermute | solution.py:17
  31.6 3.7 %collective-permute-start.4 = (f32[8,2048]{1,0:T(8,128)S(1)}, f32[8,2048]{1,0:T(8,128)S(1)}, u32[]{:S(2)}, u32[]{:S(2)}) collective-permute-start(f32[8,2048]{1,0:T(8,128)S(1)} %collective-permute-done.2), channel_id=1, source_target_pairs={{0,4},{4,8},{8,12},{12,16},{16,20},{20,24},{24,28},{1,5},{5,9},{9,... | collective-permute-start | bytes 196616 | tf_op jit(solution)/shard_map/ppermute | solution.py:17
  35.3 0.3 convolution_bitcast_fusion.1
  35.6 0.6 collective-permute-done.4
  36.2 0.6 gather_fusion.7
  36.8 0.9 %fusion.36 = f32[2,3,8,256]{3,2,1,0:T(8,128)S(1)} fusion(f32[2,3,8,256]{3,2,1,0:T(8,128)S(1)} %bitcast.104, f32[2,3,256,256]{3,2,1,0:T(8,128)S(1)} %gather_fusion.8), kind=kOutput, calls=%fused_computation.87 | convolution fusion | flops 37748736 | bytes 1671168 | tf_op jit(solution)/shard_map/osit,ostu->osiu/dot_general | solution.py:116
  37.7 0.3 convolution_bitcast_fusion
  37.9 0.9 %fusion.1 = f32[1,8,8,256]{3,2,1,0:T(8,128)S(1)} fusion(f32[8,8,256]{2,0,1:T(8,128)S(1)} %convolution_bitcast_fusion, f32[8,8,256]{2,0,1:T(8,128)S(1)} %convolution_bitcast_fusion.1, f32[3,8,256]{2,1,0:T(8,128)S(1)} %fusion.2, f32[5,3,8]{2,1,0:T(4,128)} %copy-done.1), kind=kOutput, calls=%fused_computation.13 | convolution fusion | flops 622592 | bytes 223232 | tf_op jit(solution)/shard_map/osiu,osr->iru/dot_general | solution.py:119
  38.9 0.2 fusion.37
  39.1 0.1 broadcast_in_dim.17
  39.2 0.1 concatenate.45
  39.3 1.5 %collective-permute-start.6 = (f32[8,1152]{1,0:T(8,128)S(1)}, f32[8,1152]{1,0:T(8,128)S(1)}, u32[]{:S(2)}, u32[]{:S(2)}) collective-permute-start(f32[8,1152]{1,0:T(8,128)S(1)} %concatenate.45), channel_id=1, source_target_pairs={{0,2},{1,3},{2,0},{3,1},{4,6},{5,7},{6,4},{7,5},{8,10},{9,11},{10,... | collective-permute-start | bytes 110600 | tf_op jit(solution)/shard_map/ppermute | solution.py:26
  40.8 2.4 %collective-permute-done.6 = f32[8,1152]{1,0:T(8,128)S(1)} collective-permute-done((f32[8,1152]{1,0:T(8,128)S(1)}, f32[8,1152]{1,0:T(8,128)S(1)}, u32[]{:S(2)}, u32[]{:S(2)}) %collective-permute-start.6) | collective-permute-done | bytes 36896 | tf_op jit(solution)/shard_map/ppermute | solution.py:26
  43.2 0.1 slice_add_fusion.3
  43.3 0.5 collective-permute-start.7
  43.9 3.4 %collective-permute-done.7 = f32[8,640]{1,0:T(8,128)S(1)} collective-permute-done((f32[8,640]{1,0:T(8,128)S(1)}, f32[8,640]{1,0:T(8,128)S(1)}, u32[]{:S(2)}, u32[]{:S(2)}) %collective-permute-start.7) | collective-permute-done | bytes 20512 | tf_op jit(solution)/shard_map/ppermute | solution.py:26
  47.3 0.1 collective-permute-start.8
  47.4 1.1 %collective-permute-done.8 = f32[8,128]{1,0:T(8,128)S(1)} collective-permute-done((f32[8,128]{1,0:T(8,128)S(1)}, f32[8,128]{1,0:T(8,128)S(1)}, u32[]{:S(2)}, u32[]{:S(2)}) %collective-permute-start.8) | collective-permute-done | bytes 4128 | tf_op jit(solution)/shard_map/ppermute | solution.py:26
  48.5 4.2 %collective-permute-start.9 = (f32[8,128]{1,0:T(8,128)S(1)}, f32[8,128]{1,0:T(8,128)S(1)}, u32[]{:S(2)}, u32[]{:S(2)}) collective-permute-start(f32[8,128]{1,0:T(8,128)S(1)} %add.133), channel_id=1, source_target_pairs={{0,8},{4,12},{8,0},{12,4},{16,24},{20,28},{24,16},{28,20},{1,9},{5... | collective-permute-start | bytes 12296 | tf_op jit(solution)/shard_map/ppermute | solution.py:26
  52.7 1.6 %collective-permute-done.9 = f32[8,128]{1,0:T(8,128)S(1)} collective-permute-done((f32[8,128]{1,0:T(8,128)S(1)}, f32[8,128]{1,0:T(8,128)S(1)}, u32[]{:S(2)}, u32[]{:S(2)}) %collective-permute-start.9) | collective-permute-done | bytes 4128 | tf_op jit(solution)/shard_map/ppermute | solution.py:26
  54.3 3.0 %collective-permute-start.10 = (f32[8,128]{1,0:T(8,128)S(1)}, f32[8,128]{1,0:T(8,128)S(1)}, u32[]{:S(2)}, u32[]{:S(2)}) collective-permute-start(f32[8,128]{1,0:T(8,128)S(1)} %add.134), channel_id=1, source_target_pairs={{0,16},{4,20},{8,24},{12,28},{16,0},{20,4},{24,8},{28,12},{1,17},{... | collective-permute-start | bytes 12296 | tf_op jit(solution)/shard_map/ppermute | solution.py:26
  57.3 0.6 %slice_add_fusion.1 = f32[8,512]{1,0:T(8,128)} fusion(f32[8,640]{1,0:T(8,128)S(1)} %collective-permute-done.7, f32[8,1024]{1,0:T(8,128)S(1)} %slice_add_fusion), kind=kLoop, calls=%fused_computation.25 | loop fusion | flops 4096 | bytes 49152 | tf_op jit(solution)/shard_map/add | solution.py:60
  57.9 1.0 %collective-permute-done.10 = f32[8,128]{1,0:T(8,128)S(1)} collective-permute-done((f32[8,128]{1,0:T(8,128)S(1)}, f32[8,128]{1,0:T(8,128)S(1)}, u32[]{:S(2)}, u32[]{:S(2)}) %collective-permute-start.10) | collective-permute-done | bytes 4128 | tf_op jit(solution)/shard_map/ppermute | solution.py:26
  58.9 0.7 %fusion.34 = (f32[8,8]{1,0:T(8,128)}, f32[8,8]{1,0:T(8,128)}) fusion(f32[8,128]{1,0:T(8,128)S(1)} %add_multiply_fusion), kind=kLoop, calls=%fused_computation.85 | loop fusion | bytes 1024 | tf_op jit(solution)/shard_map/slice | solution.py:137
  (34 shorter events, 0.2 us)
Async XLA Ops:
  0.6 17.5 %collective-permute-start = (f32[8,512]{1,0:T(8,128)}, f32[8,512]{1,0:T(8,128)S(1)}, u32[]{:S(2)}, u32[]{:S(2)}) collective-permute-start(f32[8,512]{1,0:T(8,128)} %param.8), channel_id=1, source_target_pairs={{0,1},{1,0},{2,3},{3,2},{4,5},{5,4},{6,7},{7,6},{8,9},{9,8},{10,11... | collective-permute-start | bytes 49160 | tf_op jit(solution)/shard_map/ppermute | solution.py:26
  9.5 5.9 %copy-start.1 = (f32[5,3,8]{2,1,0:T(4,128)}, f32[5,3,8]{2,1,0:T(4,128)S(1)}, u32[]{:S(2)}) copy-start(f32[5,3,8]{2,1,0:T(4,128)S(1)} %fusion.8) | copy-start | bytes 1444
  15.4 2.8 %copy-start = (f32[8,512]{1,0:T(8,128)S(1)}, f32[8,512]{1,0:T(8,128)}, u32[]{:S(2)}) copy-start(f32[8,512]{1,0:T(8,128)} %param.8) | copy-start | bytes 49156
  18.2 4.0 %collective-permute-start.1 = (f32[8,1024]{1,0:T(8,128)S(1)}, f32[8,1024]{1,0:T(8,128)S(1)}, u32[]{:S(2)}, u32[]{:S(2)}) collective-permute-start(f32[8,1024]{1,0:T(8,128)S(1)} %pad_maximum_fusion), channel_id=1, source_target_pairs={{0,2},{1,3},{2,0},{3,1},{4,6},{5,7},{6,4},{7,5},{8,10},{9,11},{10,... | collective-permute-start | bytes 98312 | tf_op jit(solution)/shard_map/ppermute | solution.py:26
  22.2 6.5 %collective-permute-start.3 = (f32[8,2048]{1,0:T(8,128)S(1)}, f32[8,2048]{1,0:T(8,128)S(1)}, u32[]{:S(2)}, u32[]{:S(2)}) collective-permute-start(f32[8,2048]{1,0:T(8,128)S(1)} %constant_dynamic-update-slice_fusion), channel_id=1, source_target_pairs={{4,0},{8,4},{12,8},{16,12},{20,16},{24,20},{28,24},{5,1},{9,5},{13... | collective-permute-start | bytes 196616 | tf_op jit(solution)/shard_map/ppermute | solution.py:17
  23.4 5.2 %collective-permute-start.2 = (f32[8,2048]{1,0:T(8,128)S(1)}, f32[8,2048]{1,0:T(8,128)S(1)}, u32[]{:S(2)}, u32[]{:S(2)}) collective-permute-start(f32[8,2048]{1,0:T(8,128)S(1)} %constant_dynamic-update-slice_fusion), channel_id=1, source_target_pairs={{0,4},{4,8},{8,12},{12,16},{16,20},{20,24},{24,28},{1,5},{5,9},{9,... | collective-permute-start | bytes 196616 | tf_op jit(solution)/shard_map/ppermute | solution.py:17
  29.4 5.9 %copy-start.3 = (f32[2,3,8]{2,1,0:T(4,128)S(1)}, f32[2,3,8]{2,1,0:T(4,128)}, u32[]{:S(2)}) copy-start(f32[2,3,8]{2,1,0:T(4,128)} %gather_fusion.1) | copy-start | bytes 580
  29.4 8.2 %copy-start.2 = (f32[2,3,8]{2,1,0:T(4,128)S(1)}, f32[2,3,8]{2,1,0:T(4,128)}, u32[]{:S(2)}) copy-start(f32[2,3,8]{2,1,0:T(4,128)} %gather_fusion.5) | copy-start | bytes 580
  30.3 5.3 %collective-permute-start.5 = (f32[8,2048]{1,0:T(8,128)S(1)}, f32[8,2048]{1,0:T(8,128)S(1)}, u32[]{:S(2)}, u32[]{:S(2)}) collective-permute-start(f32[8,2048]{1,0:T(8,128)S(1)} %collective-permute-done.3), channel_id=1, source_target_pairs={{4,0},{8,4},{12,8},{16,12},{20,16},{24,20},{28,24},{5,1},{9,5},{13... | collective-permute-start | bytes 196616 | tf_op jit(solution)/shard_map/ppermute | solution.py:17
  31.6 4.6 %collective-permute-start.4 = (f32[8,2048]{1,0:T(8,128)S(1)}, f32[8,2048]{1,0:T(8,128)S(1)}, u32[]{:S(2)}, u32[]{:S(2)}) collective-permute-start(f32[8,2048]{1,0:T(8,128)S(1)} %collective-permute-done.2), channel_id=1, source_target_pairs={{0,4},{4,8},{8,12},{12,16},{16,20},{20,24},{24,28},{1,5},{5,9},{9,... | collective-permute-start | bytes 196616 | tf_op jit(solution)/shard_map/ppermute | solution.py:17
  39.3 4.0 %collective-permute-start.6 = (f32[8,1152]{1,0:T(8,128)S(1)}, f32[8,1152]{1,0:T(8,128)S(1)}, u32[]{:S(2)}, u32[]{:S(2)}) collective-permute-start(f32[8,1152]{1,0:T(8,128)S(1)} %concatenate.45), channel_id=1, source_target_pairs={{0,2},{1,3},{2,0},{3,1},{4,6},{5,7},{6,4},{7,5},{8,10},{9,11},{10,... | collective-permute-start | bytes 110600 | tf_op jit(solution)/shard_map/ppermute | solution.py:26
  43.3 4.0 %collective-permute-start.7 = (f32[8,640]{1,0:T(8,128)S(1)}, f32[8,640]{1,0:T(8,128)S(1)}, u32[]{:S(2)}, u32[]{:S(2)}) collective-permute-start(f32[8,640]{1,0:T(8,128)S(1)} %pad_maximum_fusion.1), channel_id=1, source_target_pairs={{0,1},{1,0},{2,3},{3,2},{4,5},{5,4},{6,7},{7,6},{8,9},{9,8},{10,11... | collective-permute-start | bytes 61448 | tf_op jit(solution)/shard_map/ppermute | solution.py:26
  47.3 1.2 %collective-permute-start.8 = (f32[8,128]{1,0:T(8,128)S(1)}, f32[8,128]{1,0:T(8,128)S(1)}, u32[]{:S(2)}, u32[]{:S(2)}) collective-permute-start(f32[8,128]{1,0:T(8,128)S(1)} %slice_add_fusion.2), channel_id=1, source_target_pairs={{0,4},{4,0},{8,12},{12,8},{16,20},{20,16},{24,28},{28,24},{1,5},{5... | collective-permute-start | bytes 12296 | tf_op jit(solution)/shard_map/ppermute | solution.py:26
  48.5 5.8 %collective-permute-start.9 = (f32[8,128]{1,0:T(8,128)S(1)}, f32[8,128]{1,0:T(8,128)S(1)}, u32[]{:S(2)}, u32[]{:S(2)}) collective-permute-start(f32[8,128]{1,0:T(8,128)S(1)} %add.133), channel_id=1, source_target_pairs={{0,8},{4,12},{8,0},{12,4},{16,24},{20,28},{24,16},{28,20},{1,9},{5... | collective-permute-start | bytes 12296 | tf_op jit(solution)/shard_map/ppermute | solution.py:26
  54.3 4.6 %collective-permute-start.10 = (f32[8,128]{1,0:T(8,128)S(1)}, f32[8,128]{1,0:T(8,128)S(1)}, u32[]{:S(2)}, u32[]{:S(2)}) collective-permute-start(f32[8,128]{1,0:T(8,128)S(1)} %add.134), channel_id=1, source_target_pairs={{0,16},{4,20},{8,24},{12,28},{16,0},{20,4},{24,8},{28,12},{1,17},{... | collective-permute-start | bytes 12296 | tf_op jit(solution)/shard_map/ppermute | solution.py:26

commit v4 on v3

--- a/solution.py
+++ b/solution.py
@@ -108,16 +108,22 @@
     live = (slot_ids < counts[0][:, None]).astype(jnp.float32)
     one_hot = (row_place[:, :, None] == row_ids).astype(jnp.float32) * live[:, :, None]
     partial_value = None
-    for batch in ((BAND,), (BAND - 1, BAND + 1), (0, NOFF - 1)):
-        chosen = jnp.array(batch, dtype=jnp.int32)
+    for first, last, step in ((BAND - 1, BAND + 2, 1), (0, NOFF, NOFF - 1)):
+        batch = list(range(first, last, step))
         stacked = jnp.stack([panels[o] for o in batch]).reshape(len(batch), VEC, group_rows, TILE)
         stacked = stacked.transpose(0, 2, 1, 3)
-        pieces = stacked[jnp.arange(len(batch))[:, None], column_place[chosen]]
+        pieces = stacked[jnp.arange(len(batch))[:, None], column_place[first:last:step]]
         contribution = jnp.einsum(
-            "osit,ostu->osiu", pieces, tile_blocks[0, chosen], precision=lax.Precision.HIGHEST
+            "osit,ostu->osiu",
+            pieces,
+            tile_blocks[0, first:last:step],
+            precision=lax.Precision.HIGHEST,
         )
         batch_value = jnp.einsum(
-            "osiu,osr->iru", contribution, one_hot[chosen], precision=lax.Precision.HIGHEST
+            "osiu,osr->iru",
+            contribution,
+            one_hot[first:last:step],
+            precision=lax.Precision.HIGHEST,
         )
         partial_value = batch_value if partial_value is None else partial_value + batch_value
     flattened = partial_value.reshape(VEC, group_width)

time: 60.2 us -> 49.8 us (0.83)
  local copies, waits for them, and re-layouts: 14.7 us -> 3.27 us
  matrix products: 5.9 us -> 6.83 us
  other arithmetic: 2.26 us -> 3.08 us
    gather x9 -> x2, local copies, waits for them, and re-layouts: 10.9 us -> 1.17 us  [local(): stacked[jnp.arange(len(batch))[:, None], column_place[first:last:step]]]
    squeeze x2 -> x0, local copies, waits for them, and re-layouts: 1.53 us -> none  [the longest x1 0.77 us: local(): row_place = placed(tile_row[0])]
    ppermute x7, starting transfers between devices: 14 us -> 13.1 us  [exchanged(): lax.ppermute(value, axis, [(source, source ^ mask) for source in range(co...]
    dot_general x6 -> x4, matrix products: 4.78 us -> 5.7 us  [the longest x2 5.12 us: local(): jnp.einsum('osit,ostu->osiu', pieces, tile_blocks[0, first:last:step], pr...]
    concatenate x1, other arithmetic: 0.01 us -> 0.72 us  [gather_help(): held = jnp.concatenate([held, exchanged(held, 'help', mask)], axis=1)]
    add x1, other arithmetic: 0.02 us -> 0.71 us  [placed(): (tile_index // tiles_per_piece ^ order) * tiles_per_piece]
    gather x1 -> x0, other arithmetic: 0.66 us -> none  [local(): one_hot[chosen]]
  transfers between devices with their start and end apart: 11 -> 11, of which waited for: 7 -> 7; matrix products, arithmetic and copies ran while one was open for 29% -> 15% of each run, Pallas kernels for 0% -> 0%
where the time goes in v4:
time: 49.8 us; the launch traced here: 49.2 us
  starting transfers between devices  22.9 us (46%)
  waiting for transfers between devices  12.4 us (25%)
  matrix products  6.83 us (14%)
  local copies, waits for them, and re-layouts  3.27 us (7%)
  other arithmetic  3.08 us (6%)
  between operations  0.76 us (2%)
    ppermute x7, starting transfers between devices, exchanged(): lax.ppermute(value, axis, [(source, source ^ mask) for source in range(co...  13.1 us
    ppermute x7, waiting for transfers between devices, exchanged(): lax.ppermute(value, axis, [(source, source ^ mask) for source in range(co...  11.7 us
    ppermute x4, starting transfers between devices, shifted(): lax.ppermute(value, axis, [(source, source + steps) for source in range(i...  9.77 us
    dot_general x2, matrix products, local(): jnp.einsum('osit,ostu->osiu', pieces, tile_blocks[0, first:last:step], pr...  5.12 us
    gather x2, local copies, waits for them, and re-layouts, local(): stacked[jnp.arange(len(batch))[:, None], column_place[first:last:step]]  1.17 us
  transfers between devices with their start and end apart: 11, of which 7 were waited for; matrix products, arithmetic and copies ran while one was open for 15% of the time, Pallas kernels for 0%

profile of v4, /device:TPU:0, one launch (start us, length us, event | category | flops | bytes accessed | tf_op | source)
XLA Modules:
  0.0 49.2 jit_solution(6480020949382609652)
XLA Ops:
  0.6 3.0 %collective-permute-start = (f32[8,512]{1,0:T(8,128)}, f32[8,512]{1,0:T(8,128)S(1)}, u32[]{:S(2)}, u32[]{:S(2)}) collective-permute-start(f32[8,512]{1,0:T(8,128)} %param.5), channel_id=1, source_target_pairs={{0,1},{1,0},{2,3},{3,2},{4,5},{5,4},{6,7},{7,6},{8,9},{9,8},{10,11... | collective-permute-start | bytes 49160 | tf_op jit(solution)/shard_map/ppermute | solution.py:26
  3.6 0.7 %fusion.16 = (s32[5,3]{0,1:T(4,128)S(1)}, s32[5,3]{0,1:T(4,128)S(1)}) fusion(s32[1,5,3]{1,0,2:T(1,128)} %param.7, s32[]{:T(128)S(6)} %axis_index.12, s32[1,5,3]{1,0,2:T(1,128)} %param.8), kind=kLoop, calls=%fused_computation.47 | loop fusion | flops 660 | bytes 244 | tf_op jit(solution)/shard_map/add | solution.py:102
  4.3 0.1 slice.52
  4.4 0.1 fusion.21
  4.5 0.9 %fusion.32 = f32[8,8]{1,0:T(8,128)S(1)} fusion(f32[8,512]{1,0:T(8,128)} %param.5), kind=kOutput, calls=%fused_computation.69 | convolution fusion | flops 393216 | bytes 16640 | tf_op jit(solution)/shard_map/dot_general | solution.py:131
  5.5 0.7 %fusion.13 = f32[5,3]{1,0:T(8,128)S(1)} fusion(s32[5]{0:T(128)} %bitcast.94), kind=kLoop, calls=%fused_computation.34 | loop fusion | flops 30 | bytes 80 | tf_op jit(solution)/shard_map/convert_element_type | solution.py:108
  6.2 0.1 copy.11
  6.3 0.1 copy.12
  6.4 0.1 fusion.10
  6.5 0.7 %constant_dynamic-update-slice_fusion.2 = f32[8,2048]{1,0:T(8,128)S(1)} fusion(f32[8,512]{1,0:T(8,128)} %param.5), kind=kLoop, calls=%fused_computation.24 | loop fusion | bytes 32768
  7.2 0.1 copy.13
  7.3 0.0 collective-permute-done
  7.3 0.7 %pad_maximum_fusion = f32[8,1024]{1,0:T(8,128)S(1)} fusion(f32[8,512]{1,0:T(8,128)S(1)} %collective-permute-done, f32[8,512]{1,0:T(8,128)} %param.5), kind=kLoop, calls=%fused_computation.17 | loop fusion | flops 8192 | bytes 65536 | tf_op jit(solution)/shard_map/concatenate | solution.py:43
  8.0 1.5 %collective-permute-start.1 = (f32[8,1024]{1,0:T(8,128)S(1)}, f32[8,1024]{1,0:T(8,128)S(1)}, u32[]{:S(2)}, u32[]{:S(2)}) collective-permute-start(f32[8,1024]{1,0:T(8,128)S(1)} %pad_maximum_fusion), channel_id=1, source_target_pairs={{0,2},{1,3},{2,0},{3,1},{4,6},{5,7},{6,4},{7,5},{8,10},{9,11},{10,... | collective-permute-start | bytes 98312 | tf_op jit(solution)/shard_map/ppermute | solution.py:26
  9.5 2.4 %collective-permute-done.1 = f32[8,1024]{1,0:T(8,128)S(1)} collective-permute-done((f32[8,1024]{1,0:T(8,128)S(1)}, f32[8,1024]{1,0:T(8,128)S(1)}, u32[]{:S(2)}, u32[]{:S(2)}) %collective-permute-start.1) | collective-permute-done | bytes 32800 | tf_op jit(solution)/shard_map/ppermute | solution.py:26
  11.9 1.3 %collective-permute-start.3 = (f32[8,2048]{1,0:T(8,128)S(1)}, f32[8,2048]{1,0:T(8,128)S(1)}, u32[]{:S(2)}, u32[]{:S(2)}) collective-permute-start(f32[8,2048]{1,0:T(8,128)S(1)} %constant_dynamic-update-slice_fusion), channel_id=1, source_target_pairs={{4,0},{8,4},{12,8},{16,12},{20,16},{24,20},{28,24},{5,1},{9,5},{13... | collective-permute-start | bytes 196616 | tf_op jit(solution)/shard_map/ppermute | solution.py:17
  13.2 3.0 %collective-permute-start.2 = (f32[8,2048]{1,0:T(8,128)S(1)}, f32[8,2048]{1,0:T(8,128)S(1)}, u32[]{:S(2)}, u32[]{:S(2)}) collective-permute-start(f32[8,2048]{1,0:T(8,128)S(1)} %constant_dynamic-update-slice_fusion), channel_id=1, source_target_pairs={{0,4},{4,8},{8,12},{12,16},{16,20},{20,24},{24,28},{1,5},{5,9},{9,... | collective-permute-start | bytes 196616 | tf_op jit(solution)/shard_map/ppermute | solution.py:17
  16.3 0.1 reshape.108
  16.4 0.1 reshape.102
  16.4 0.0 collective-permute-done.3
  16.4 0.7 %collective-permute-done.2 = f32[8,2048]{1,0:T(8,128)S(1)} collective-permute-done((f32[8,2048]{1,0:T(8,128)S(1)}, f32[8,2048]{1,0:T(8,128)S(1)}, u32[]{:S(2)}, u32[]{:S(2)}) %collective-permute-start.2) | collective-permute-done | bytes 65568 | tf_op jit(solution)/shard_map/ppermute | solution.py:17
  17.2 0.6 %gather_fusion = f32[9,8,256]{2,1,0:T(8,128)S(1)} fusion(f32[3,8,8,256]{3,2,1,0:T(8,128)S(1)} %maximum_bitcast_fusion, s32[9]{0:T(128)S(1)} %reshape.102), kind=kCustom, calls=%fused_computation | custom fusion | bytes 147528 | tf_op jit(solution)/shard_map/gather | solution.py:115
  17.8 1.3 %collective-permute-start.5 = (f32[8,2048]{1,0:T(8,128)S(1)}, f32[8,2048]{1,0:T(8,128)S(1)}, u32[]{:S(2)}, u32[]{:S(2)}) collective-permute-start(f32[8,2048]{1,0:T(8,128)S(1)} %collective-permute-done.3), channel_id=1, source_target_pairs={{4,0},{8,4},{12,8},{16,12},{20,16},{24,20},{28,24},{5,1},{9,5},{13... | collective-permute-start | bytes 196616 | tf_op jit(solution)/shard_map/ppermute | solution.py:17
  19.1 4.2 %collective-permute-start.4 = (f32[8,2048]{1,0:T(8,128)S(1)}, f32[8,2048]{1,0:T(8,128)S(1)}, u32[]{:S(2)}, u32[]{:S(2)}) collective-permute-start(f32[8,2048]{1,0:T(8,128)S(1)} %collective-permute-done.2), channel_id=1, source_target_pairs={{0,4},{4,8},{8,12},{12,16},{16,20},{20,24},{24,28},{1,5},{5,9},{9,... | collective-permute-start | bytes 196616 | tf_op jit(solution)/shard_map/ppermute | solution.py:17
  23.2 2.9 %fusion = f32[3,3,8,256]{3,2,1,0:T(8,128)S(1)} fusion(f32[3,3,8,256]{3,2,1,0:T(8,128)S(1)} %bitcast.88, f32[1,5,3,256,256]{4,3,2,1,0:T(8,128)} %param.6), kind=kOutput, calls=%fused_computation.2 | convolution fusion | flops 56623104 | bytes 2506752 | tf_op jit(solution)/shard_map/osit,ostu->osiu/dot_general | solution.py:116
  26.1 0.0 collective-permute-done.5
  26.1 0.0 collective-permute-done.4
  26.1 0.6 %gather_fusion.1 = f32[6,8,256]{2,1,0:T(8,128)S(1)} fusion(f32[2,8,8,256]{3,2,1,0:T(8,128)S(1)} %maximum_bitcast_fusion.1, s32[6]{0:T(128)S(1)} %reshape.108), kind=kCustom, calls=%fused_computation.1 | custom fusion | bytes 98352 | tf_op jit(solution)/shard_map/gather | solution.py:115
  26.7 2.3 %fusion.3 = f32[2,3,8,256]{3,2,1,0:T(8,128)S(1)} fusion(f32[2,3,8,256]{3,2,1,0:T(8,128)S(1)} %bitcast.89, f32[1,5,3,256,256]{4,3,2,1,0:T(8,128)} %param.6), kind=kOutput, calls=%fused_computation.5 | convolution fusion | flops 37748736 | bytes 1671168 | tf_op jit(solution)/shard_map/osit,ostu->osiu/dot_general | solution.py:116
  29.0 0.3 convolution_bitcast_fusion
  29.2 0.3 fusion.7
  29.6 0.2 fusion.31
  29.8 0.1 concatenate.29
  29.9 1.5 %collective-permute-start.6 = (f32[8,1152]{1,0:T(8,128)S(1)}, f32[8,1152]{1,0:T(8,128)S(1)}, u32[]{:S(2)}, u32[]{:S(2)}) collective-permute-start(f32[8,1152]{1,0:T(8,128)S(1)} %concatenate.29), channel_id=1, source_target_pairs={{0,2},{1,3},{2,0},{3,1},{4,6},{5,7},{6,4},{7,5},{8,10},{9,11},{10,... | collective-permute-start | bytes 110600 | tf_op jit(solution)/shard_map/ppermute | solution.py:26
  31.5 2.4 %collective-permute-done.6 = f32[8,1152]{1,0:T(8,128)S(1)} collective-permute-done((f32[8,1152]{1,0:T(8,128)S(1)}, f32[8,1152]{1,0:T(8,128)S(1)}, u32[]{:S(2)}, u32[]{:S(2)}) %collective-permute-start.6) | collective-permute-done | bytes 36896 | tf_op jit(solution)/shard_map/ppermute | solution.py:26
  33.9 0.1 slice_add_fusion.3
  34.0 0.5 %collective-permute-start.7 = (f32[8,640]{1,0:T(8,128)S(1)}, f32[8,640]{1,0:T(8,128)S(1)}, u32[]{:S(2)}, u32[]{:S(2)}) collective-permute-start(f32[8,640]{1,0:T(8,128)S(1)} %pad_maximum_fusion.1), channel_id=1, source_target_pairs={{0,1},{1,0},{2,3},{3,2},{4,5},{5,4},{6,7},{7,6},{8,9},{9,8},{10,11... | collective-permute-start | bytes 61448 | tf_op jit(solution)/shard_map/ppermute | solution.py:26
  34.6 3.2 %collective-permute-done.7 = f32[8,640]{1,0:T(8,128)S(1)} collective-permute-done((f32[8,640]{1,0:T(8,128)S(1)}, f32[8,640]{1,0:T(8,128)S(1)}, u32[]{:S(2)}, u32[]{:S(2)}) %collective-permute-start.7) | collective-permute-done | bytes 20512 | tf_op jit(solution)/shard_map/ppermute | solution.py:26
  37.8 0.1 collective-permute-start.8
  37.9 1.1 %collective-permute-done.8 = f32[8,128]{1,0:T(8,128)S(1)} collective-permute-done((f32[8,128]{1,0:T(8,128)S(1)}, f32[8,128]{1,0:T(8,128)S(1)}, u32[]{:S(2)}, u32[]{:S(2)}) %collective-permute-start.8) | collective-permute-done | bytes 4128 | tf_op jit(solution)/shard_map/ppermute | solution.py:26
  39.0 3.4 %collective-permute-start.9 = (f32[8,128]{1,0:T(8,128)S(1)}, f32[8,128]{1,0:T(8,128)S(1)}, u32[]{:S(2)}, u32[]{:S(2)}) collective-permute-start(f32[8,128]{1,0:T(8,128)S(1)} %add.77), channel_id=1, source_target_pairs={{0,8},{4,12},{8,0},{12,4},{16,24},{20,28},{24,16},{28,20},{1,9},{5... | collective-permute-start | bytes 12296 | tf_op jit(solution)/shard_map/ppermute | solution.py:26
  42.3 1.6 %collective-permute-done.9 = f32[8,128]{1,0:T(8,128)S(1)} collective-permute-done((f32[8,128]{1,0:T(8,128)S(1)}, f32[8,128]{1,0:T(8,128)S(1)}, u32[]{:S(2)}, u32[]{:S(2)}) %collective-permute-start.9) | collective-permute-done | bytes 4128 | tf_op jit(solution)/shard_map/ppermute | solution.py:26
  43.9 3.0 %collective-permute-start.10 = (f32[8,128]{1,0:T(8,128)S(1)}, f32[8,128]{1,0:T(8,128)S(1)}, u32[]{:S(2)}, u32[]{:S(2)}) collective-permute-start(f32[8,128]{1,0:T(8,128)S(1)} %add.78), channel_id=1, source_target_pairs={{0,16},{4,20},{8,24},{12,28},{16,0},{20,4},{24,8},{28,12},{1,17},{... | collective-permute-start | bytes 12296 | tf_op jit(solution)/shard_map/ppermute | solution.py:26
  47.0 0.6 %slice_add_fusion.1 = f32[8,512]{1,0:T(8,128)} fusion(f32[8,640]{1,0:T(8,128)S(1)} %collective-permute-done.7, f32[8,1024]{1,0:T(8,128)S(1)} %slice_add_fusion), kind=kLoop, calls=%fused_computation.19 | loop fusion | flops 4096 | bytes 49152 | tf_op jit(solution)/shard_map/add | solution.py:60
  47.6 1.0 %collective-permute-done.10 = f32[8,128]{1,0:T(8,128)S(1)} collective-permute-done((f32[8,128]{1,0:T(8,128)S(1)}, f32[8,128]{1,0:T(8,128)S(1)}, u32[]{:S(2)}, u32[]{:S(2)}) %collective-permute-start.10) | collective-permute-done | bytes 4128 | tf_op jit(solution)/shard_map/ppermute | solution.py:26
  48.6 0.7 %fusion.30 = (f32[8,8]{1,0:T(8,128)}, f32[8,8]{1,0:T(8,128)}) fusion(f32[8,128]{1,0:T(8,128)S(1)} %add_multiply_fusion), kind=kLoop, calls=%fused_computation.67 | loop fusion | bytes 1024 | tf_op jit(solution)/shard_map/slice | solution.py:143
  (17 shorter events, 0.1 us)
Async XLA Ops:
  0.6 6.7 %collective-permute-start = (f32[8,512]{1,0:T(8,128)}, f32[8,512]{1,0:T(8,128)S(1)}, u32[]{:S(2)}, u32[]{:S(2)}) collective-permute-start(f32[8,512]{1,0:T(8,128)} %param.5), channel_id=1, source_target_pairs={{0,1},{1,0},{2,3},{3,2},{4,5},{5,4},{6,7},{7,6},{8,9},{9,8},{10,11... | collective-permute-start | bytes 49160 | tf_op jit(solution)/shard_map/ppermute | solution.py:26
  8.0 3.9 %collective-permute-start.1 = (f32[8,1024]{1,0:T(8,128)S(1)}, f32[8,1024]{1,0:T(8,128)S(1)}, u32[]{:S(2)}, u32[]{:S(2)}) collective-permute-start(f32[8,1024]{1,0:T(8,128)S(1)} %pad_maximum_fusion), channel_id=1, source_target_pairs={{0,2},{1,3},{2,0},{3,1},{4,6},{5,7},{6,4},{7,5},{8,10},{9,11},{10,... | collective-permute-start | bytes 98312 | tf_op jit(solution)/shard_map/ppermute | solution.py:26
  11.9 4.5 %collective-permute-start.3 = (f32[8,2048]{1,0:T(8,128)S(1)}, f32[8,2048]{1,0:T(8,128)S(1)}, u32[]{:S(2)}, u32[]{:S(2)}) collective-permute-start(f32[8,2048]{1,0:T(8,128)S(1)} %constant_dynamic-update-slice_fusion), channel_id=1, source_target_pairs={{4,0},{8,4},{12,8},{16,12},{20,16},{24,20},{28,24},{5,1},{9,5},{13... | collective-permute-start | bytes 196616 | tf_op jit(solution)/shard_map/ppermute | solution.py:17
  13.2 3.9 %collective-permute-start.2 = (f32[8,2048]{1,0:T(8,128)S(1)}, f32[8,2048]{1,0:T(8,128)S(1)}, u32[]{:S(2)}, u32[]{:S(2)}) collective-permute-start(f32[8,2048]{1,0:T(8,128)S(1)} %constant_dynamic-update-slice_fusion), channel_id=1, source_target_pairs={{0,4},{4,8},{8,12},{12,16},{16,20},{20,24},{24,28},{1,5},{5,9},{9,... | collective-permute-start | bytes 196616 | tf_op jit(solution)/shard_map/ppermute | solution.py:17
  17.8 8.3 %collective-permute-start.5 = (f32[8,2048]{1,0:T(8,128)S(1)}, f32[8,2048]{1,0:T(8,128)S(1)}, u32[]{:S(2)}, u32[]{:S(2)}) collective-permute-start(f32[8,2048]{1,0:T(8,128)S(1)} %collective-permute-done.3), channel_id=1, source_target_pairs={{4,0},{8,4},{12,8},{16,12},{20,16},{24,20},{28,24},{5,1},{9,5},{13... | collective-permute-start | bytes 196616 | tf_op jit(solution)/shard_map/ppermute | solution.py:17
  19.1 7.0 %collective-permute-start.4 = (f32[8,2048]{1,0:T(8,128)S(1)}, f32[8,2048]{1,0:T(8,128)S(1)}, u32[]{:S(2)}, u32[]{:S(2)}) collective-permute-start(f32[8,2048]{1,0:T(8,128)S(1)} %collective-permute-done.2), channel_id=1, source_target_pairs={{0,4},{4,8},{8,12},{12,16},{16,20},{20,24},{24,28},{1,5},{5,9},{9,... | collective-permute-start | bytes 196616 | tf_op jit(solution)/shard_map/ppermute | solution.py:17
  29.9 4.0 %collective-permute-start.6 = (f32[8,1152]{1,0:T(8,128)S(1)}, f32[8,1152]{1,0:T(8,128)S(1)}, u32[]{:S(2)}, u32[]{:S(2)}) collective-permute-start(f32[8,1152]{1,0:T(8,128)S(1)} %concatenate.29), channel_id=1, source_target_pairs={{0,2},{1,3},{2,0},{3,1},{4,6},{5,7},{6,4},{7,5},{8,10},{9,11},{10,... | collective-permute-start | bytes 110600 | tf_op jit(solution)/shard_map/ppermute | solution.py:26
  34.0 3.8 %collective-permute-start.7 = (f32[8,640]{1,0:T(8,128)S(1)}, f32[8,640]{1,0:T(8,128)S(1)}, u32[]{:S(2)}, u32[]{:S(2)}) collective-permute-start(f32[8,640]{1,0:T(8,128)S(1)} %pad_maximum_fusion.1), channel_id=1, source_target_pairs={{0,1},{1,0},{2,3},{3,2},{4,5},{5,4},{6,7},{7,6},{8,9},{9,8},{10,11... | collective-permute-start | bytes 61448 | tf_op jit(solution)/shard_map/ppermute | solution.py:26
  37.8 1.2 %collective-permute-start.8 = (f32[8,128]{1,0:T(8,128)S(1)}, f32[8,128]{1,0:T(8,128)S(1)}, u32[]{:S(2)}, u32[]{:S(2)}) collective-permute-start(f32[8,128]{1,0:T(8,128)S(1)} %slice_add_fusion.2), channel_id=1, source_target_pairs={{0,4},{4,0},{8,12},{12,8},{16,20},{20,16},{24,28},{28,24},{1,5},{5... | collective-permute-start | bytes 12296 | tf_op jit(solution)/shard_map/ppermute | solution.py:26
  39.0 4.9 %collective-permute-start.9 = (f32[8,128]{1,0:T(8,128)S(1)}, f32[8,128]{1,0:T(8,128)S(1)}, u32[]{:S(2)}, u32[]{:S(2)}) collective-permute-start(f32[8,128]{1,0:T(8,128)S(1)} %add.77), channel_id=1, source_target_pairs={{0,8},{4,12},{8,0},{12,4},{16,24},{20,28},{24,16},{28,20},{1,9},{5... | collective-permute-start | bytes 12296 | tf_op jit(solution)/shard_map/ppermute | solution.py:26
  43.9 4.6 %collective-permute-start.10 = (f32[8,128]{1,0:T(8,128)S(1)}, f32[8,128]{1,0:T(8,128)S(1)}, u32[]{:S(2)}, u32[]{:S(2)}) collective-permute-start(f32[8,128]{1,0:T(8,128)S(1)} %add.78), channel_id=1, source_target_pairs={{0,16},{4,20},{8,24},{12,28},{16,0},{20,4},{24,8},{28,12},{1,17},{... | collective-permute-start | bytes 12296 | tf_op jit(solution)/shard_map/ppermute | solution.py:26

commit v5 on v4

--- a/solution.py
+++ b/solution.py
@@ -117,7 +117,7 @@
             "osit,ostu->osiu",
             pieces,
             tile_blocks[0, first:last:step],
-            precision=lax.Precision.HIGHEST,
+            precision=lax.Precision.HIGH,
         )
         batch_value = jnp.einsum(
             "osiu,osr->iru",

time: 49.8 us -> 49.2 us (0.988)
  matrix products: 6.83 us -> 5.94 us
    dot_general x2, matrix products: 5.12 us -> 4.24 us  [local(): jnp.einsum('osit,ostu->osiu', pieces, tile_blocks[0, first:last:step], pr...]
  transfers between devices with their start and end apart: 11 -> 11, of which waited for: 7 -> 7; matrix products, arithmetic and copies ran while one was open for 15% -> 14% of each run, Pallas kernels for 0% -> 0%
where the time goes in v5:
time: 49.2 us; the launch traced here: 48.6 us
  starting transfers between devices  23.1 us (47%)
  waiting for transfers between devices  12.4 us (25%)
  matrix products  5.94 us (12%)
  local copies, waits for them, and re-layouts  3.27 us (7%)
  other arithmetic  3.08 us (6%)
  between operations  0.77 us (2%)
    ppermute x7, starting transfers between devices, exchanged(): lax.ppermute(value, axis, [(source, source ^ mask) for source in range(co...  13.3 us
    ppermute x7, waiting for transfers between devices, exchanged(): lax.ppermute(value, axis, [(source, source ^ mask) for source in range(co...  11.7 us
    ppermute x4, starting transfers between devices, shifted(): lax.ppermute(value, axis, [(source, source + steps) for source in range(i...  9.77 us
    dot_general x2, matrix products, local(): jnp.einsum('osit,ostu->osiu', pieces, tile_blocks[0, first:last:step], pr...  4.24 us
    gather x2, local copies, waits for them, and re-layouts, local(): stacked[jnp.arange(len(batch))[:, None], column_place[first:last:step]]  1.17 us
  transfers between devices with their start and end apart: 11, of which 7 were waited for; matrix products, arithmetic and copies ran while one was open for 14% of the time, Pallas kernels for 0%

profile of v5, /device:TPU:0, one launch (start us, length us, event | category | flops | bytes accessed | tf_op | source)
XLA Modules:
  0.0 48.6 jit_solution(2058156257353277706)
XLA Ops:
  0.6 3.0 %collective-permute-start = (f32[8,512]{1,0:T(8,128)}, f32[8,512]{1,0:T(8,128)S(1)}, u32[]{:S(2)}, u32[]{:S(2)}) collective-permute-start(f32[8,512]{1,0:T(8,128)} %param.5), channel_id=1, source_target_pairs={{0,1},{1,0},{2,3},{3,2},{4,5},{5,4},{6,7},{7,6},{8,9},{9,8},{10,11... | collective-permute-start | bytes 49160 | tf_op jit(solution)/shard_map/ppermute | solution.py:26
  3.6 0.7 %fusion.16 = (s32[5,3]{0,1:T(4,128)S(1)}, s32[5,3]{0,1:T(4,128)S(1)}) fusion(s32[1,5,3]{1,0,2:T(1,128)} %param.7, s32[]{:T(128)S(6)} %axis_index.12, s32[1,5,3]{1,0,2:T(1,128)} %param.8), kind=kLoop, calls=%fused_computation.47 | loop fusion | flops 660 | bytes 244 | tf_op jit(solution)/shard_map/add | solution.py:102
  4.3 0.1 slice.52
  4.4 0.1 fusion.21
  4.5 0.9 %fusion.32 = f32[8,8]{1,0:T(8,128)S(1)} fusion(f32[8,512]{1,0:T(8,128)} %param.5), kind=kOutput, calls=%fused_computation.69 | convolution fusion | flops 393216 | bytes 16640 | tf_op jit(solution)/shard_map/dot_general | solution.py:131
  5.5 0.7 %fusion.13 = f32[5,3]{1,0:T(8,128)S(1)} fusion(s32[5]{0:T(128)} %bitcast.94), kind=kLoop, calls=%fused_computation.34 | loop fusion | flops 30 | bytes 80 | tf_op jit(solution)/shard_map/convert_element_type | solution.py:108
  6.2 0.1 copy.11
  6.3 0.1 copy.12
  6.4 0.1 fusion.10
  6.5 0.7 %constant_dynamic-update-slice_fusion.2 = f32[8,2048]{1,0:T(8,128)S(1)} fusion(f32[8,512]{1,0:T(8,128)} %param.5), kind=kLoop, calls=%fused_computation.24 | loop fusion | bytes 32768
  7.2 0.1 copy.13
  7.3 0.0 collective-permute-done
  7.3 0.7 %pad_maximum_fusion = f32[8,1024]{1,0:T(8,128)S(1)} fusion(f32[8,512]{1,0:T(8,128)S(1)} %collective-permute-done, f32[8,512]{1,0:T(8,128)} %param.5), kind=kLoop, calls=%fused_computation.17 | loop fusion | flops 8192 | bytes 65536 | tf_op jit(solution)/shard_map/concatenate | solution.py:43
  8.0 1.5 %collective-permute-start.1 = (f32[8,1024]{1,0:T(8,128)S(1)}, f32[8,1024]{1,0:T(8,128)S(1)}, u32[]{:S(2)}, u32[]{:S(2)}) collective-permute-start(f32[8,1024]{1,0:T(8,128)S(1)} %pad_maximum_fusion), channel_id=1, source_target_pairs={{0,2},{1,3},{2,0},{3,1},{4,6},{5,7},{6,4},{7,5},{8,10},{9,11},{10,... | collective-permute-start | bytes 98312 | tf_op jit(solution)/shard_map/ppermute | solution.py:26
  9.5 2.4 %collective-permute-done.1 = f32[8,1024]{1,0:T(8,128)S(1)} collective-permute-done((f32[8,1024]{1,0:T(8,128)S(1)}, f32[8,1024]{1,0:T(8,128)S(1)}, u32[]{:S(2)}, u32[]{:S(2)}) %collective-permute-start.1) | collective-permute-done | bytes 32800 | tf_op jit(solution)/shard_map/ppermute | solution.py:26
  11.9 1.3 %collective-permute-start.3 = (f32[8,2048]{1,0:T(8,128)S(1)}, f32[8,2048]{1,0:T(8,128)S(1)}, u32[]{:S(2)}, u32[]{:S(2)}) collective-permute-start(f32[8,2048]{1,0:T(8,128)S(1)} %constant_dynamic-update-slice_fusion), channel_id=1, source_target_pairs={{4,0},{8,4},{12,8},{16,12},{20,16},{24,20},{28,24},{5,1},{9,5},{13... | collective-permute-start | bytes 196616 | tf_op jit(solution)/shard_map/ppermute | solution.py:17
  13.2 3.0 %collective-permute-start.2 = (f32[8,2048]{1,0:T(8,128)S(1)}, f32[8,2048]{1,0:T(8,128)S(1)}, u32[]{:S(2)}, u32[]{:S(2)}) collective-permute-start(f32[8,2048]{1,0:T(8,128)S(1)} %constant_dynamic-update-slice_fusion), channel_id=1, source_target_pairs={{0,4},{4,8},{8,12},{12,16},{16,20},{20,24},{24,28},{1,5},{5,9},{9,... | collective-permute-start | bytes 196616 | tf_op jit(solution)/shard_map/ppermute | solution.py:17
  16.3 0.1 reshape.108
  16.4 0.1 reshape.102
  16.4 0.0 collective-permute-done.3
  16.4 0.7 %collective-permute-done.2 = f32[8,2048]{1,0:T(8,128)S(1)} collective-permute-done((f32[8,2048]{1,0:T(8,128)S(1)}, f32[8,2048]{1,0:T(8,128)S(1)}, u32[]{:S(2)}, u32[]{:S(2)}) %collective-permute-start.2) | collective-permute-done | bytes 65568 | tf_op jit(solution)/shard_map/ppermute | solution.py:17
  17.2 0.6 %gather_fusion = f32[9,8,256]{2,1,0:T(8,128)S(1)} fusion(f32[3,8,8,256]{3,2,1,0:T(8,128)S(1)} %maximum_bitcast_fusion, s32[9]{0:T(128)S(1)} %reshape.102), kind=kCustom, calls=%fused_computation | custom fusion | bytes 147528 | tf_op jit(solution)/shard_map/gather | solution.py:115
  17.8 1.3 %collective-permute-start.5 = (f32[8,2048]{1,0:T(8,128)S(1)}, f32[8,2048]{1,0:T(8,128)S(1)}, u32[]{:S(2)}, u32[]{:S(2)}) collective-permute-start(f32[8,2048]{1,0:T(8,128)S(1)} %collective-permute-done.3), channel_id=1, source_target_pairs={{4,0},{8,4},{12,8},{16,12},{20,16},{24,20},{28,24},{5,1},{9,5},{13... | collective-permute-start | bytes 196616 | tf_op jit(solution)/shard_map/ppermute | solution.py:17
  19.1 4.2 %collective-permute-start.4 = (f32[8,2048]{1,0:T(8,128)S(1)}, f32[8,2048]{1,0:T(8,128)S(1)}, u32[]{:S(2)}, u32[]{:S(2)}) collective-permute-start(f32[8,2048]{1,0:T(8,128)S(1)} %collective-permute-done.2), channel_id=1, source_target_pairs={{0,4},{4,8},{8,12},{12,16},{16,20},{20,24},{24,28},{1,5},{5,9},{9,... | collective-permute-start | bytes 196616 | tf_op jit(solution)/shard_map/ppermute | solution.py:17
  23.2 2.3 %fusion = f32[3,3,8,256]{3,2,1,0:T(8,128)S(1)} fusion(f32[3,3,8,256]{3,2,1,0:T(8,128)S(1)} %bitcast.88, f32[1,5,3,256,256]{4,3,2,1,0:T(8,128)} %param.6), kind=kOutput, calls=%fused_computation.2 | convolution fusion | flops 28311552 | bytes 2506752 | tf_op jit(solution)/shard_map/osit,ostu->osiu/dot_general | solution.py:116
  25.6 0.0 collective-permute-done.5
  25.6 0.0 collective-permute-done.4
  25.6 0.6 %gather_fusion.1 = f32[6,8,256]{2,1,0:T(8,128)S(1)} fusion(f32[2,8,8,256]{3,2,1,0:T(8,128)S(1)} %maximum_bitcast_fusion.1, s32[6]{0:T(128)S(1)} %reshape.108), kind=kCustom, calls=%fused_computation.1 | custom fusion | bytes 98352 | tf_op jit(solution)/shard_map/gather | solution.py:115
  26.2 1.9 %fusion.3 = f32[2,3,8,256]{3,2,1,0:T(8,128)S(1)} fusion(f32[2,3,8,256]{3,2,1,0:T(8,128)S(1)} %bitcast.89, f32[1,5,3,256,256]{4,3,2,1,0:T(8,128)} %param.6), kind=kOutput, calls=%fused_computation.5 | convolution fusion | flops 18874368 | bytes 1671168 | tf_op jit(solution)/shard_map/osit,ostu->osiu/dot_general | solution.py:116
  28.1 0.3 convolution_bitcast_fusion
  28.4 0.3 fusion.7
  28.7 0.2 fusion.31
  28.9 0.1 concatenate.29
  29.1 1.5 %collective-permute-start.6 = (f32[8,1152]{1,0:T(8,128)S(1)}, f32[8,1152]{1,0:T(8,128)S(1)}, u32[]{:S(2)}, u32[]{:S(2)}) collective-permute-start(f32[8,1152]{1,0:T(8,128)S(1)} %concatenate.29), channel_id=1, source_target_pairs={{0,2},{1,3},{2,0},{3,1},{4,6},{5,7},{6,4},{7,5},{8,10},{9,11},{10,... | collective-permute-start | bytes 110600 | tf_op jit(solution)/shard_map/ppermute | solution.py:26
  30.6 2.4 %collective-permute-done.6 = f32[8,1152]{1,0:T(8,128)S(1)} collective-permute-done((f32[8,1152]{1,0:T(8,128)S(1)}, f32[8,1152]{1,0:T(8,128)S(1)}, u32[]{:S(2)}, u32[]{:S(2)}) %collective-permute-start.6) | collective-permute-done | bytes 36896 | tf_op jit(solution)/shard_map/ppermute | solution.py:26
  33.0 0.1 slice_add_fusion.3
  33.1 0.5 %collective-permute-start.7 = (f32[8,640]{1,0:T(8,128)S(1)}, f32[8,640]{1,0:T(8,128)S(1)}, u32[]{:S(2)}, u32[]{:S(2)}) collective-permute-start(f32[8,640]{1,0:T(8,128)S(1)} %pad_maximum_fusion.1), channel_id=1, source_target_pairs={{0,1},{1,0},{2,3},{3,2},{4,5},{5,4},{6,7},{7,6},{8,9},{9,8},{10,11... | collective-permute-start | bytes 61448 | tf_op jit(solution)/shard_map/ppermute | solution.py:26
  33.7 3.2 %collective-permute-done.7 = f32[8,640]{1,0:T(8,128)S(1)} collective-permute-done((f32[8,640]{1,0:T(8,128)S(1)}, f32[8,640]{1,0:T(8,128)S(1)}, u32[]{:S(2)}, u32[]{:S(2)}) %collective-permute-start.7) | collective-permute-done | bytes 20512 | tf_op jit(solution)/shard_map/ppermute | solution.py:26
  36.9 0.1 collective-permute-start.8
  37.0 1.1 %collective-permute-done.8 = f32[8,128]{1,0:T(8,128)S(1)} collective-permute-done((f32[8,128]{1,0:T(8,128)S(1)}, f32[8,128]{1,0:T(8,128)S(1)}, u32[]{:S(2)}, u32[]{:S(2)}) %collective-permute-start.8) | collective-permute-done | bytes 4128 | tf_op jit(solution)/shard_map/ppermute | solution.py:26
  38.1 3.6 %collective-permute-start.9 = (f32[8,128]{1,0:T(8,128)S(1)}, f32[8,128]{1,0:T(8,128)S(1)}, u32[]{:S(2)}, u32[]{:S(2)}) collective-permute-start(f32[8,128]{1,0:T(8,128)S(1)} %add.77), channel_id=1, source_target_pairs={{0,8},{4,12},{8,0},{12,4},{16,24},{20,28},{24,16},{28,20},{1,9},{5... | collective-permute-start | bytes 12296 | tf_op jit(solution)/shard_map/ppermute | solution.py:26
  41.7 1.6 %collective-permute-done.9 = f32[8,128]{1,0:T(8,128)S(1)} collective-permute-done((f32[8,128]{1,0:T(8,128)S(1)}, f32[8,128]{1,0:T(8,128)S(1)}, u32[]{:S(2)}, u32[]{:S(2)}) %collective-permute-start.9) | collective-permute-done | bytes 4128 | tf_op jit(solution)/shard_map/ppermute | solution.py:26
  43.3 3.0 %collective-permute-start.10 = (f32[8,128]{1,0:T(8,128)S(1)}, f32[8,128]{1,0:T(8,128)S(1)}, u32[]{:S(2)}, u32[]{:S(2)}) collective-permute-start(f32[8,128]{1,0:T(8,128)S(1)} %add.78), channel_id=1, source_target_pairs={{0,16},{4,20},{8,24},{12,28},{16,0},{20,4},{24,8},{28,12},{1,17},{... | collective-permute-start | bytes 12296 | tf_op jit(solution)/shard_map/ppermute | solution.py:26
  46.3 0.6 %slice_add_fusion.1 = f32[8,512]{1,0:T(8,128)} fusion(f32[8,640]{1,0:T(8,128)S(1)} %collective-permute-done.7, f32[8,1024]{1,0:T(8,128)S(1)} %slice_add_fusion), kind=kLoop, calls=%fused_computation.19 | loop fusion | flops 4096 | bytes 49152 | tf_op jit(solution)/shard_map/add | solution.py:60
  46.9 1.0 %collective-permute-done.10 = f32[8,128]{1,0:T(8,128)S(1)} collective-permute-done((f32[8,128]{1,0:T(8,128)S(1)}, f32[8,128]{1,0:T(8,128)S(1)}, u32[]{:S(2)}, u32[]{:S(2)}) %collective-permute-start.10) | collective-permute-done | bytes 4128 | tf_op jit(solution)/shard_map/ppermute | solution.py:26
  47.9 0.7 %fusion.30 = (f32[8,8]{1,0:T(8,128)}, f32[8,8]{1,0:T(8,128)}) fusion(f32[8,128]{1,0:T(8,128)S(1)} %add_multiply_fusion), kind=kLoop, calls=%fused_computation.67 | loop fusion | bytes 1024 | tf_op jit(solution)/shard_map/slice | solution.py:143
  (17 shorter events, 0.1 us)
Async XLA Ops:
  0.6 6.7 %collective-permute-start = (f32[8,512]{1,0:T(8,128)}, f32[8,512]{1,0:T(8,128)S(1)}, u32[]{:S(2)}, u32[]{:S(2)}) collective-permute-start(f32[8,512]{1,0:T(8,128)} %param.5), channel_id=1, source_target_pairs={{0,1},{1,0},{2,3},{3,2},{4,5},{5,4},{6,7},{7,6},{8,9},{9,8},{10,11... | collective-permute-start | bytes 49160 | tf_op jit(solution)/shard_map/ppermute | solution.py:26
  8.0 3.9 %collective-permute-start.1 = (f32[8,1024]{1,0:T(8,128)S(1)}, f32[8,1024]{1,0:T(8,128)S(1)}, u32[]{:S(2)}, u32[]{:S(2)}) collective-permute-start(f32[8,1024]{1,0:T(8,128)S(1)} %pad_maximum_fusion), channel_id=1, source_target_pairs={{0,2},{1,3},{2,0},{3,1},{4,6},{5,7},{6,4},{7,5},{8,10},{9,11},{10,... | collective-permute-start | bytes 98312 | tf_op jit(solution)/shard_map/ppermute | solution.py:26
  11.9 4.5 %collective-permute-start.3 = (f32[8,2048]{1,0:T(8,128)S(1)}, f32[8,2048]{1,0:T(8,128)S(1)}, u32[]{:S(2)}, u32[]{:S(2)}) collective-permute-start(f32[8,2048]{1,0:T(8,128)S(1)} %constant_dynamic-update-slice_fusion), channel_id=1, source_target_pairs={{4,0},{8,4},{12,8},{16,12},{20,16},{24,20},{28,24},{5,1},{9,5},{13... | collective-permute-start | bytes 196616 | tf_op jit(solution)/shard_map/ppermute | solution.py:17
  13.2 3.9 %collective-permute-start.2 = (f32[8,2048]{1,0:T(8,128)S(1)}, f32[8,2048]{1,0:T(8,128)S(1)}, u32[]{:S(2)}, u32[]{:S(2)}) collective-permute-start(f32[8,2048]{1,0:T(8,128)S(1)} %constant_dynamic-update-slice_fusion), channel_id=1, source_target_pairs={{0,4},{4,8},{8,12},{12,16},{16,20},{20,24},{24,28},{1,5},{5,9},{9,... | collective-permute-start | bytes 196616 | tf_op jit(solution)/shard_map/ppermute | solution.py:17
  17.8 7.8 %collective-permute-start.5 = (f32[8,2048]{1,0:T(8,128)S(1)}, f32[8,2048]{1,0:T(8,128)S(1)}, u32[]{:S(2)}, u32[]{:S(2)}) collective-permute-start(f32[8,2048]{1,0:T(8,128)S(1)} %collective-permute-done.3), channel_id=1, source_target_pairs={{4,0},{8,4},{12,8},{16,12},{20,16},{24,20},{28,24},{5,1},{9,5},{13... | collective-permute-start | bytes 196616 | tf_op jit(solution)/shard_map/ppermute | solution.py:17
  19.1 6.5 %collective-permute-start.4 = (f32[8,2048]{1,0:T(8,128)S(1)}, f32[8,2048]{1,0:T(8,128)S(1)}, u32[]{:S(2)}, u32[]{:S(2)}) collective-permute-start(f32[8,2048]{1,0:T(8,128)S(1)} %collective-permute-done.2), channel_id=1, source_target_pairs={{0,4},{4,8},{8,12},{12,16},{16,20},{20,24},{24,28},{1,5},{5,9},{9,... | collective-permute-start | bytes 196616 | tf_op jit(solution)/shard_map/ppermute | solution.py:17
  29.1 4.0 %collective-permute-start.6 = (f32[8,1152]{1,0:T(8,128)S(1)}, f32[8,1152]{1,0:T(8,128)S(1)}, u32[]{:S(2)}, u32[]{:S(2)}) collective-permute-start(f32[8,1152]{1,0:T(8,128)S(1)} %concatenate.29), channel_id=1, source_target_pairs={{0,2},{1,3},{2,0},{3,1},{4,6},{5,7},{6,4},{7,5},{8,10},{9,11},{10,... | collective-permute-start | bytes 110600 | tf_op jit(solution)/shard_map/ppermute | solution.py:26
  33.1 3.8 %collective-permute-start.7 = (f32[8,640]{1,0:T(8,128)S(1)}, f32[8,640]{1,0:T(8,128)S(1)}, u32[]{:S(2)}, u32[]{:S(2)}) collective-permute-start(f32[8,640]{1,0:T(8,128)S(1)} %pad_maximum_fusion.1), channel_id=1, source_target_pairs={{0,1},{1,0},{2,3},{3,2},{4,5},{5,4},{6,7},{7,6},{8,9},{9,8},{10,11... | collective-permute-start | bytes 61448 | tf_op jit(solution)/shard_map/ppermute | solution.py:26
  36.9 1.2 %collective-permute-start.8 = (f32[8,128]{1,0:T(8,128)S(1)}, f32[8,128]{1,0:T(8,128)S(1)}, u32[]{:S(2)}, u32[]{:S(2)}) collective-permute-start(f32[8,128]{1,0:T(8,128)S(1)} %slice_add_fusion.2), channel_id=1, source_target_pairs={{0,4},{4,0},{8,12},{12,8},{16,20},{20,16},{24,28},{28,24},{1,5},{5... | collective-permute-start | bytes 12296 | tf_op jit(solution)/shard_map/ppermute | solution.py:26
  38.1 5.2 %collective-permute-start.9 = (f32[8,128]{1,0:T(8,128)S(1)}, f32[8,128]{1,0:T(8,128)S(1)}, u32[]{:S(2)}, u32[]{:S(2)}) collective-permute-start(f32[8,128]{1,0:T(8,128)S(1)} %add.77), channel_id=1, source_target_pairs={{0,8},{4,12},{8,0},{12,4},{16,24},{20,28},{24,16},{28,20},{1,9},{5... | collective-permute-start | bytes 12296 | tf_op jit(solution)/shard_map/ppermute | solution.py:26
  43.3 4.6 %collective-permute-start.10 = (f32[8,128]{1,0:T(8,128)S(1)}, f32[8,128]{1,0:T(8,128)S(1)}, u32[]{:S(2)}, u32[]{:S(2)}) collective-permute-start(f32[8,128]{1,0:T(8,128)S(1)} %add.78), channel_id=1, source_target_pairs={{0,16},{4,20},{8,24},{12,28},{16,0},{20,4},{24,8},{28,12},{1,17},{... | collective-permute-start | bytes 12296 | tf_op jit(solution)/shard_map/ppermute | solution.py:26

commit v6 on v3

--- a/solution.py
+++ b/solution.py
@@ -74,18 +74,17 @@
     return gram
 
 
+def cyclic(value, axis, steps):
+    count = lax.axis_size(axis)
+    return lax.ppermute(value, axis, [(source, (source + steps) % count) for source in range(count)])
+
+
 def neighbour_panels(source):
-    lowers = []
-    uppers = []
-    current = source
-    for hop_index in range(BAND):
-        current = shifted(current, "blk", 1)
-        lowers.append(current)
-    current = source
-    for hop_index in range(BAND):
-        current = shifted(current, "blk", -1)
-        uppers.append(current)
-    return lowers[::-1] + [source] + uppers
+    width = source.shape[1]
+    below = cyclic(source, "blk", 1)
+    above = cyclic(jnp.concatenate([below, source], axis=1), "blk", -2)
+    further = cyclic(below, "blk", 1)
+    return [further, below, source, above[:, :width], above[:, width:]]
 
 
 def local(vectors, tile_blocks, tile_row, tile_col, counts):
@@ -105,19 +104,24 @@
     row_place = placed(tile_row[0])
     slot_ids = jnp.arange(SLOTS, dtype=jnp.int32)[None, :]
     row_ids = jnp.arange(group_rows, dtype=jnp.int32)
-    live = (slot_ids < counts[0][:, None]).astype(jnp.float32)
+    column_blocks = lax.axis_index("blk") + jnp.arange(NOFF, dtype=jnp.int32) - BAND
+    in_band = (column_blocks >= 0) & (column_blocks < groups)
+    live = ((slot_ids < counts[0][:, None]) & in_band[:, None]).astype(jnp.float32)
     one_hot = (row_place[:, :, None] == row_ids).astype(jnp.float32) * live[:, :, None]
     partial_value = None
-    for batch in ((BAND,), (BAND - 1, BAND + 1), (0, NOFF - 1)):
-        chosen = jnp.array(batch, dtype=jnp.int32)
+    for batch in ((BAND - 1, BAND), (0, BAND + 1, BAND + 2)):
+
+        def taken(array):
+            return jnp.concatenate([array[o : o + 1] for o in batch])
+
         stacked = jnp.stack([panels[o] for o in batch]).reshape(len(batch), VEC, group_rows, TILE)
         stacked = stacked.transpose(0, 2, 1, 3)
-        pieces = stacked[jnp.arange(len(batch))[:, None], column_place[chosen]]
+        pieces = stacked[jnp.arange(len(batch))[:, None], taken(column_place)]
         contribution = jnp.einsum(
-            "osit,ostu->osiu", pieces, tile_blocks[0, chosen], precision=lax.Precision.HIGHEST
+            "osit,ostu->osiu", pieces, taken(tile_blocks[0]), precision=lax.Precision.HIGH
         )
         batch_value = jnp.einsum(
-            "osiu,osr->iru", contribution, one_hot[chosen], precision=lax.Precision.HIGHEST
+            "osiu,osr->iru", contribution, taken(one_hot), precision=lax.Precision.HIGHEST
         )
         partial_value = batch_value if partial_value is None else partial_value + batch_value
     flattened = partial_value.reshape(VEC, group_width)

time: 60.2 us -> 49.9 us (0.83)
  starting transfers between devices: 23.4 us -> 9.61 us
  waiting for transfers between devices: 12.5 us -> 25.2 us
  local copies, waits for them, and re-layouts: 14.7 us -> 7.6 us
  matrix products: 5.9 us -> 4 us
    gather x9 -> x2, local copies, waits for them, and re-layouts: 10.9 us -> 1.17 us  [local(): pieces = stacked[jnp.arange(len(batch))[:, None], taken(column_place)]]
    ppermute x4 -> x3, waiting for transfers between devices: 0.61 us -> 9.49 us  [cyclic(): lax.ppermute(value, axis, [(source, (source + steps) % count) for source...]
    ppermute x4 -> x3, starting transfers between devices: 9.33 us -> 1.86 us  [cyclic(): lax.ppermute(value, axis, [(source, (source + steps) % count) for source...]
    ppermute x7, starting transfers between devices: 14 us -> 7.75 us  [exchanged(): lax.ppermute(value, axis, [(source, source ^ mask) for source in range(co...]
    slice x0 -> x6, local copies, waits for them, and re-layouts: none -> 4.48 us  [the longest x5 3.6 us: taken(): return jnp.concatenate([array[o:o + 1] for o in batch])]
    ppermute x7, waiting for transfers between devices: 11.9 us -> 15.7 us  [exchanged(): lax.ppermute(value, axis, [(source, source ^ mask) for source in range(co...]
    dot_general x6 -> x4, matrix products: 4.78 us -> 2.88 us  [the longest x2 2.29 us: local(): jnp.einsum('osit,ostu->osiu', pieces, taken(tile_blocks[0]), precision=la...]
    squeeze x2 -> x0, local copies, waits for them, and re-layouts: 1.53 us -> none  [the longest x1 0.77 us: local(): row_place = placed(tile_row[0])]
  transfers between devices with their start and end apart: 11 -> 10, of which waited for: 7 -> 9; matrix products, arithmetic and copies ran while one was open for 29% -> 18% of each run, Pallas kernels for 0% -> 0%
where the time goes in v6:
time: 49.9 us; the launch traced here: 49.5 us
  waiting for transfers between devices  25.2 us (51%)
  starting transfers between devices  9.61 us (19%)
  local copies, waits for them, and re-layouts  7.6 us (15%)
  matrix products  4 us (8%)
  other arithmetic  2.36 us (5%)
  between operations  0.75 us (2%)
    ppermute x7, waiting for transfers between devices, exchanged(): lax.ppermute(value, axis, [(source, source ^ mask) for source in range(co...  15.7 us
    ppermute x3, waiting for transfers between devices, cyclic(): lax.ppermute(value, axis, [(source, (source + steps) % count) for source...  9.49 us
    ppermute x7, starting transfers between devices, exchanged(): lax.ppermute(value, axis, [(source, source ^ mask) for source in range(co...  7.75 us
    slice x5, local copies, waits for them, and re-layouts, taken(): return jnp.concatenate([array[o:o + 1] for o in batch])  3.6 us
    dot_general x2, matrix products, local(): jnp.einsum('osit,ostu->osiu', pieces, taken(tile_blocks[0]), precision=la...  2.29 us
    ppermute x3, starting transfers between devices, cyclic(): lax.ppermute(value, axis, [(source, (source + steps) % count) for source...  1.86 us
    gather x2, local copies, waits for them, and re-layouts, local(): pieces = stacked[jnp.arange(len(batch))[:, None], taken(column_place)]  1.17 us
  transfers between devices with their start and end apart: 10, of which 9 were waited for; matrix products, arithmetic and copies ran while one was open for 18% of the time, Pallas kernels for 0%

profile of v6, /device:TPU:0, one launch (start us, length us, event | category | flops | bytes accessed | tf_op | source)
XLA Modules:
  0.0 49.5 jit_solution(9882336979339296419)
XLA Ops:
  0.6 3.0 %collective-permute-start = (f32[8,512]{1,0:T(8,128)}, f32[8,512]{1,0:T(8,128)S(1)}, u32[]{:S(2)}, u32[]{:S(2)}) collective-permute-start(f32[8,512]{1,0:T(8,128)} %param.5), channel_id=1, source_target_pairs={{0,1},{1,0},{2,3},{3,2},{4,5},{5,4},{6,7},{7,6},{8,9},{9,8},{10,11... | collective-permute-start | bytes 49160 | tf_op jit(solution)/shard_map/ppermute | solution.py:26
  3.6 0.9 %fusion.42 = f32[8,8]{1,0:T(8,128)S(1)} fusion(f32[8,512]{1,0:T(8,128)} %param.5), kind=kOutput, calls=%fused_computation.87 | convolution fusion | flops 393216 | bytes 16640 | tf_op jit(solution)/shard_map/dot_general | solution.py:129
  4.5 0.7 %constant_dynamic-update-slice_fusion.2 = f32[8,2048]{1,0:T(8,128)S(1)} fusion(f32[8,512]{1,0:T(8,128)} %param.5), kind=kLoop, calls=%fused_computation.34 | loop fusion | bytes 32768
  5.3 0.7 %fusion.21 = (s32[5,3]{0,1:T(4,128)S(1)}, s32[5,3]{0,1:T(4,128)S(1)}) fusion(s32[1,5,3]{1,0,2:T(1,128)} %param.7, s32[]{:T(128)S(6)} %axis_index.22, s32[1,5,3]{1,0,2:T(1,128)} %param.8), kind=kLoop, calls=%fused_computation.59 | loop fusion | flops 660 | bytes 244 | tf_op jit(solution)/shard_map/add | solution.py:101
  6.0 0.1 copy.12
  6.1 0.1 fusion.26
  6.2 0.1 copy.13
  6.3 3.4 %slice_bitcast_fusion.4 = (f32[1,3,256,256]{3,2,1,0:T(8,128)S(1)}, f32[1,3,256,256]{3,2,1,0:T(8,128)S(1)}, f32[1,3,256,256]{3,2,1,0:T(8,128)S(1)}, f32[1,3,256,256]{3,2,1,0:T(8,128)S(1)}, f32[1,3,256,256]{3,2,1,0:T(8,128)}) fusion(f32[1,5,3,256,256]{4,3,2,1,0:T(8,128)} %param.6), kind=kLoop, calls=%fused_computation.20 | loop fusion | bytes 7864320 | tf_op jit(solution)/shard_map/slice | solution.py:115
  9.7 0.0 copy-done.1
  9.7 0.1 fusion.18
  9.8 0.1 fusion.14
  9.8 0.1 slice_reduce_fusion
  10.0 0.1 reshape.213
  10.1 0.1 copy.14
  10.1 0.0 collective-permute-done
  10.2 1.6 %collective-permute-start.1 = (f32[8,1024]{1,0:T(8,128)S(1)}, f32[8,1024]{1,0:T(8,128)S(1)}, u32[]{:S(2)}, u32[]{:S(2)}) collective-permute-start(f32[8,1024]{1,0:T(8,128)S(1)} %pad_maximum_fusion.1), channel_id=1, source_target_pairs={{0,2},{1,3},{2,0},{3,1},{4,6},{5,7},{6,4},{7,5},{8,10},{9,11},{10,... | collective-permute-start | bytes 98312 | tf_op jit(solution)/shard_map/ppermute | solution.py:26
  11.7 2.4 %collective-permute-done.1 = f32[8,1024]{1,0:T(8,128)S(1)} collective-permute-done((f32[8,1024]{1,0:T(8,128)S(1)}, f32[8,1024]{1,0:T(8,128)S(1)}, u32[]{:S(2)}, u32[]{:S(2)}) %collective-permute-start.1) | collective-permute-done | bytes 32800 | tf_op jit(solution)/shard_map/ppermute | solution.py:26
  14.1 0.0 collective-permute-start.2
  14.2 0.1 reshape.219
  14.2 5.4 %collective-permute-done.2 = f32[8,2048]{1,0:T(8,128)S(1)} collective-permute-done((f32[8,2048]{1,0:T(8,128)S(1)}, f32[8,2048]{1,0:T(8,128)S(1)}, u32[]{:S(2)}, u32[]{:S(2)}) %collective-permute-start.2) | collective-permute-done | bytes 65568 | tf_op jit(solution)/shard_map/ppermute | solution.py:79
  19.6 0.7 %pad_maximum_fusion = f32[8,4096]{1,0:T(8,128)} fusion(f32[8,1024]{1,0:T(8,128)S(1)} %collective-permute-done.1, f32[8,512]{1,0:T(8,128)S(1)} %collective-permute-done, f32[8,512]{1,0:T(8,128)S(1)} %copy-done, f32[8,2048]{1,0:T(8,128)S(1)} %collective-permute-done.2), kind=kLoop, calls=%fused_computation.23 | loop fusion | flops 98304 | bytes 262144 | tf_op jit(solution)/shard_map/concatenate | solution.py:85
  20.3 1.8 %collective-permute-start.4 = (f32[8,4096]{1,0:T(8,128)}, f32[8,4096]{1,0:T(8,128)}, u32[]{:S(2)}, u32[]{:S(2)}) collective-permute-start(f32[8,4096]{1,0:T(8,128)} %pad_maximum_fusion), channel_id=1, source_target_pairs={{0,24},{4,28},{8,0},{12,4},{16,8},{20,12},{24,16},{28,20},{1,25},{... | collective-permute-start | bytes 393224 | tf_op jit(solution)/shard_map/ppermute | solution.py:79
  22.1 0.6 %gather_fusion = f32[6,8,256]{2,1,0:T(8,128)S(1)} fusion(f32[2,8,8,256]{3,2,1,0:T(8,128)S(1)} %maximum_bitcast_fusion.1, s32[6]{0:T(128)S(1)} %reshape.213), kind=kCustom, calls=%fused_computation | custom fusion | bytes 98352 | tf_op jit(solution)/shard_map/gather | solution.py:119
  22.7 0.1 collective-permute-start.3
  22.8 0.5 fusion.6
  23.2 2.4 %collective-permute-done.4 = f32[8,4096]{1,0:T(8,128)} collective-permute-done((f32[8,4096]{1,0:T(8,128)}, f32[8,4096]{1,0:T(8,128)}, u32[]{:S(2)}, u32[]{:S(2)}) %collective-permute-start.4) | collective-permute-done | bytes 131104 | tf_op jit(solution)/shard_map/ppermute | solution.py:79
  25.6 0.9 %fusion.39 = (f32[8,2048]{1,0:T(8,128)S(1)}, f32[8,2048]{1,0:T(8,128)S(1)}) fusion(f32[8,4096]{1,0:T(8,128)} %collective-permute-done.4), kind=kLoop, calls=%fused_computation.84 | loop fusion | bytes 262144 | tf_op jit(solution)/shard_map/slice | solution.py:87
  26.5 1.8 %collective-permute-done.3 = f32[8,2048]{1,0:T(8,128)S(1)} collective-permute-done((f32[8,2048]{1,0:T(8,128)S(1)}, f32[8,2048]{1,0:T(8,128)S(1)}, u32[]{:S(2)}, u32[]{:S(2)}) %collective-permute-start.3) | collective-permute-done | bytes 65568 | tf_op jit(solution)/shard_map/ppermute | solution.py:79
  28.3 0.6 %gather_fusion.1 = f32[9,8,256]{2,1,0:T(8,128)S(1)} fusion(f32[3,8,8,256]{3,2,1,0:T(8,128)S(1)} %maximum_bitcast_fusion, s32[9]{0:T(128)S(1)} %reshape.219), kind=kCustom, calls=%fused_computation.1 | custom fusion | bytes 147528 | tf_op jit(solution)/shard_map/gather | solution.py:119
  28.9 1.8 %fusion = f32[3,3,8,256]{3,2,1,0:T(8,128)S(1)} fusion(f32[3,3,8,256]{3,2,1,0:T(8,128)S(1)} %bitcast.98, f32[1,3,256,256]{3,2,1,0:T(8,128)S(1)} %get-tuple-element.6, f32[1,3,256,256]{3,2,1,0:T(8,128)} %get-tuple-element.7, f32[1,3,256,256]{3,2,1,0:T(8,128)S(1)} %get-tuple-element.4), kind=kOutput, calls=%fused_computation.2 | convolution fusion | flops 29491200 | bytes 2506752 | tf_op jit(solution)/shard_map/osit,ostu->osiu/dot_general | solution.py:120
  30.7 0.3 convolution_bitcast_fusion
  31.0 0.3 fusion.11
  31.3 0.2 fusion.41
  31.5 0.1 broadcast_in_dim.11
  31.6 0.1 concatenate.85
  31.6 1.5 %collective-permute-start.5 = (f32[8,1152]{1,0:T(8,128)S(1)}, f32[8,1152]{1,0:T(8,128)S(1)}, u32[]{:S(2)}, u32[]{:S(2)}) collective-permute-start(f32[8,1152]{1,0:T(8,128)S(1)} %concatenate.85), channel_id=1, source_target_pairs={{0,2},{1,3},{2,0},{3,1},{4,6},{5,7},{6,4},{7,5},{8,10},{9,11},{10,... | collective-permute-start | bytes 110600 | tf_op jit(solution)/shard_map/ppermute | solution.py:26
  33.2 2.4 %collective-permute-done.5 = f32[8,1152]{1,0:T(8,128)S(1)} collective-permute-done((f32[8,1152]{1,0:T(8,128)S(1)}, f32[8,1152]{1,0:T(8,128)S(1)}, u32[]{:S(2)}, u32[]{:S(2)}) %collective-permute-start.5) | collective-permute-done | bytes 36896 | tf_op jit(solution)/shard_map/ppermute | solution.py:26
  35.6 0.1 slice_add_fusion.3
  35.7 0.5 %collective-permute-start.6 = (f32[8,640]{1,0:T(8,128)S(1)}, f32[8,640]{1,0:T(8,128)S(1)}, u32[]{:S(2)}, u32[]{:S(2)}) collective-permute-start(f32[8,640]{1,0:T(8,128)S(1)} %pad_maximum_fusion.2), channel_id=1, source_target_pairs={{0,1},{1,0},{2,3},{3,2},{4,5},{5,4},{6,7},{7,6},{8,9},{9,8},{10,11... | collective-permute-start | bytes 61448 | tf_op jit(solution)/shard_map/ppermute | solution.py:26
  36.3 3.2 %collective-permute-done.6 = f32[8,640]{1,0:T(8,128)S(1)} collective-permute-done((f32[8,640]{1,0:T(8,128)S(1)}, f32[8,640]{1,0:T(8,128)S(1)}, u32[]{:S(2)}, u32[]{:S(2)}) %collective-permute-start.6) | collective-permute-done | bytes 20512 | tf_op jit(solution)/shard_map/ppermute | solution.py:26
  39.5 0.0 collective-permute-start.7
  39.5 1.2 %collective-permute-done.7 = f32[8,128]{1,0:T(8,128)S(1)} collective-permute-done((f32[8,128]{1,0:T(8,128)S(1)}, f32[8,128]{1,0:T(8,128)S(1)}, u32[]{:S(2)}, u32[]{:S(2)}) %collective-permute-start.7) | collective-permute-done | bytes 4128 | tf_op jit(solution)/shard_map/ppermute | solution.py:26
  40.7 0.0 collective-permute-start.8
  40.7 3.6 %collective-permute-done.8 = f32[8,128]{1,0:T(8,128)S(1)} collective-permute-done((f32[8,128]{1,0:T(8,128)S(1)}, f32[8,128]{1,0:T(8,128)S(1)}, u32[]{:S(2)}, u32[]{:S(2)}) %collective-permute-start.8) | collective-permute-done | bytes 4128 | tf_op jit(solution)/shard_map/ppermute | solution.py:26
  44.3 1.1 %collective-permute-start.9 = (f32[8,128]{1,0:T(8,128)S(1)}, f32[8,128]{1,0:T(8,128)S(1)}, u32[]{:S(2)}, u32[]{:S(2)}) collective-permute-start(f32[8,128]{1,0:T(8,128)S(1)} %add.102), channel_id=1, source_target_pairs={{0,16},{4,20},{8,24},{12,28},{16,0},{20,4},{24,8},{28,12},{1,17},{... | collective-permute-start | bytes 12296 | tf_op jit(solution)/shard_map/ppermute | solution.py:26
  45.4 0.6 %slice_add_fusion.1 = f32[8,512]{1,0:T(8,128)} fusion(f32[8,640]{1,0:T(8,128)S(1)} %collective-permute-done.6, f32[8,1024]{1,0:T(8,128)S(1)} %slice_add_fusion), kind=kLoop, calls=%fused_computation.29 | loop fusion | flops 4096 | bytes 49152 | tf_op jit(solution)/shard_map/add | solution.py:60
  46.0 2.8 %collective-permute-done.9 = f32[8,128]{1,0:T(8,128)S(1)} collective-permute-done((f32[8,128]{1,0:T(8,128)S(1)}, f32[8,128]{1,0:T(8,128)S(1)}, u32[]{:S(2)}, u32[]{:S(2)}) %collective-permute-start.9) | collective-permute-done | bytes 4128 | tf_op jit(solution)/shard_map/ppermute | solution.py:26
  48.8 0.7 %fusion.40 = (f32[8,8]{1,0:T(8,128)}, f32[8,8]{1,0:T(8,128)}) fusion(f32[8,128]{1,0:T(8,128)S(1)} %add_multiply_fusion), kind=kLoop, calls=%fused_computation.85 | loop fusion | bytes 1024 | tf_op jit(solution)/shard_map/slice | solution.py:141
  (22 shorter events, 0.1 us)
Async XLA Ops:
  0.6 9.5 %collective-permute-start = (f32[8,512]{1,0:T(8,128)}, f32[8,512]{1,0:T(8,128)S(1)}, u32[]{:S(2)}, u32[]{:S(2)}) collective-permute-start(f32[8,512]{1,0:T(8,128)} %param.5), channel_id=1, source_target_pairs={{0,1},{1,0},{2,3},{3,2},{4,5},{5,4},{6,7},{7,6},{8,9},{9,8},{10,11... | collective-permute-start | bytes 49160 | tf_op jit(solution)/shard_map/ppermute | solution.py:26
  6.3 3.4 %copy-start.1 = (s32[1,5]{1,0:T(1,128)S(1)}, s32[1,5]{1,0:T(1,128)}, u32[]{:S(2)}) copy-start(s32[1,5]{1,0:T(1,128)} %param.9) | copy-start | bytes 64
  6.3 3.9 %copy-start = (f32[8,512]{1,0:T(8,128)S(1)}, f32[8,512]{1,0:T(8,128)}, u32[]{:S(2)}) copy-start(f32[8,512]{1,0:T(8,128)} %param.5) | copy-start | bytes 49156
  10.2 4.0 %collective-permute-start.1 = (f32[8,1024]{1,0:T(8,128)S(1)}, f32[8,1024]{1,0:T(8,128)S(1)}, u32[]{:S(2)}, u32[]{:S(2)}) collective-permute-start(f32[8,1024]{1,0:T(8,128)S(1)} %pad_maximum_fusion.1), channel_id=1, source_target_pairs={{0,2},{1,3},{2,0},{3,1},{4,6},{5,7},{6,4},{7,5},{8,10},{9,11},{10,... | collective-permute-start | bytes 98312 | tf_op jit(solution)/shard_map/ppermute | solution.py:26
  14.1 5.5 %collective-permute-start.2 = (f32[8,2048]{1,0:T(8,128)S(1)}, f32[8,2048]{1,0:T(8,128)S(1)}, u32[]{:S(2)}, u32[]{:S(2)}) collective-permute-start(f32[8,2048]{1,0:T(8,128)S(1)} %constant_dynamic-update-slice_fusion), channel_id=1, source_target_pairs={{0,4},{4,8},{8,12},{12,16},{16,20},{20,24},{24,28},{28,0},{1,5},{5... | collective-permute-start | bytes 196616 | tf_op jit(solution)/shard_map/ppermute | solution.py:79
  20.3 5.3 %collective-permute-start.4 = (f32[8,4096]{1,0:T(8,128)}, f32[8,4096]{1,0:T(8,128)}, u32[]{:S(2)}, u32[]{:S(2)}) collective-permute-start(f32[8,4096]{1,0:T(8,128)} %pad_maximum_fusion), channel_id=1, source_target_pairs={{0,24},{4,28},{8,0},{12,4},{16,8},{20,12},{24,16},{28,20},{1,25},{... | collective-permute-start | bytes 393224 | tf_op jit(solution)/shard_map/ppermute | solution.py:79
  22.7 5.5 %collective-permute-start.3 = (f32[8,2048]{1,0:T(8,128)S(1)}, f32[8,2048]{1,0:T(8,128)S(1)}, u32[]{:S(2)}, u32[]{:S(2)}) collective-permute-start(f32[8,2048]{1,0:T(8,128)S(1)} %collective-permute-done.2), channel_id=1, source_target_pairs={{0,4},{4,8},{8,12},{12,16},{16,20},{20,24},{24,28},{28,0},{1,5},{5... | collective-permute-start | bytes 196616 | tf_op jit(solution)/shard_map/ppermute | solution.py:79
  31.6 4.0 %collective-permute-start.5 = (f32[8,1152]{1,0:T(8,128)S(1)}, f32[8,1152]{1,0:T(8,128)S(1)}, u32[]{:S(2)}, u32[]{:S(2)}) collective-permute-start(f32[8,1152]{1,0:T(8,128)S(1)} %concatenate.85), channel_id=1, source_target_pairs={{0,2},{1,3},{2,0},{3,1},{4,6},{5,7},{6,4},{7,5},{8,10},{9,11},{10,... | collective-permute-start | bytes 110600 | tf_op jit(solution)/shard_map/ppermute | solution.py:26
  35.7 3.8 %collective-permute-start.6 = (f32[8,640]{1,0:T(8,128)S(1)}, f32[8,640]{1,0:T(8,128)S(1)}, u32[]{:S(2)}, u32[]{:S(2)}) collective-permute-start(f32[8,640]{1,0:T(8,128)S(1)} %pad_maximum_fusion.2), channel_id=1, source_target_pairs={{0,1},{1,0},{2,3},{3,2},{4,5},{5,4},{6,7},{7,6},{8,9},{9,8},{10,11... | collective-permute-start | bytes 61448 | tf_op jit(solution)/shard_map/ppermute | solution.py:26
  39.5 1.2 %collective-permute-start.7 = (f32[8,128]{1,0:T(8,128)S(1)}, f32[8,128]{1,0:T(8,128)S(1)}, u32[]{:S(2)}, u32[]{:S(2)}) collective-permute-start(f32[8,128]{1,0:T(8,128)S(1)} %slice_add_fusion.2), channel_id=1, source_target_pairs={{0,4},{4,0},{8,12},{12,8},{16,20},{20,16},{24,28},{28,24},{1,5},{5... | collective-permute-start | bytes 12296 | tf_op jit(solution)/shard_map/ppermute | solution.py:26
  40.7 3.6 %collective-permute-start.8 = (f32[8,128]{1,0:T(8,128)S(1)}, f32[8,128]{1,0:T(8,128)S(1)}, u32[]{:S(2)}, u32[]{:S(2)}) collective-permute-start(f32[8,128]{1,0:T(8,128)S(1)} %add.101), channel_id=1, source_target_pairs={{0,8},{4,12},{8,0},{12,4},{16,24},{20,28},{24,16},{28,20},{1,9},{5... | collective-permute-start | bytes 12296 | tf_op jit(solution)/shard_map/ppermute | solution.py:26
  44.3 4.5 %collective-permute-start.9 = (f32[8,128]{1,0:T(8,128)S(1)}, f32[8,128]{1,0:T(8,128)S(1)}, u32[]{:S(2)}, u32[]{:S(2)}) collective-permute-start(f32[8,128]{1,0:T(8,128)S(1)} %add.102), channel_id=1, source_target_pairs={{0,16},{4,20},{8,24},{12,28},{16,0},{20,4},{24,8},{28,12},{1,17},{... | collective-permute-start | bytes 12296 | tf_op jit(solution)/shard_map/ppermute | solution.py:26

commit v7 on v6

--- a/solution.py
+++ b/solution.py
@@ -109,10 +109,10 @@
     live = ((slot_ids < counts[0][:, None]) & in_band[:, None]).astype(jnp.float32)
     one_hot = (row_place[:, :, None] == row_ids).astype(jnp.float32) * live[:, :, None]
     partial_value = None
-    for batch in ((BAND - 1, BAND), (0, BAND + 1, BAND + 2)):
+    for batch in ((BAND - 1, BAND), (BAND + 1, BAND + 2), (0,)):
 
         def taken(array):
-            return jnp.concatenate([array[o : o + 1] for o in batch])
+            return array[batch[0] : batch[-1] + 1]
 
         stacked = jnp.stack([panels[o] for o in batch]).reshape(len(batch), VEC, group_rows, TILE)
         stacked = stacked.transpose(0, 2, 1, 3)

time: 49.9 us -> 50.4 us (1.010)
  local copies, waits for them, and re-layouts: 7.6 us -> 3.78 us
  matrix products: 4 us -> 7.16 us
  other arithmetic: 2.36 us -> 3.93 us
  starting transfers between devices: 9.61 us -> 8.52 us
    slice x5 -> x0, local copies, waits for them, and re-layouts: 3.6 us -> none  [taken(): return jnp.concatenate([array[o:o + 1] for o in batch])]
    dot_general x2 -> x3, matrix products: 2.29 us -> 5.24 us  [local(): jnp.einsum('osit,ostu->osiu', pieces, taken(tile_blocks[0]), precision=la...]
    ppermute x7, starting transfers between devices: 7.75 us -> 6.6 us  [exchanged(): lax.ppermute(value, axis, [(source, source ^ mask) for source in range(co...]
    ppermute x7, waiting for transfers between devices: 15.7 us -> 16.7 us  [exchanged(): lax.ppermute(value, axis, [(source, source ^ mask) for source in range(co...]
    slice x1, local copies, waits for them, and re-layouts: 0.88 us -> 0.02 us  [neighbour_panels(): return [further, below, source, above[:, :width], above[:, width:]]]
    concatenate x1, other arithmetic: 0.01 us -> 0.72 us  [gather_help(): held = jnp.concatenate([held, exchanged(held, 'help', mask)], axis=1)]
    convert_element_type x1, other arithmetic: 0.07 us -> 0.74 us  [local(): ((slot_ids < counts[0][:, None]) & in_band[:, None]).astype(jnp.float32)]
    ppermute x3, waiting for transfers between devices: 9.49 us -> 8.89 us  [cyclic(): lax.ppermute(value, axis, [(source, (source + steps) % count) for source...]
  transfers between devices with their start and end apart: 10 -> 10, of which waited for: 9 -> 8; matrix products, arithmetic and copies ran while one was open for 18% -> 18% of each run, Pallas kernels for 0% -> 0%
where the time goes in v7:
time: 50.4 us; the launch traced here: 49.8 us
  waiting for transfers between devices  25.6 us (51%)
  starting transfers between devices  8.52 us (17%)
  matrix products  7.16 us (14%)
  other arithmetic  3.93 us (8%)
  local copies, waits for them, and re-layouts  3.78 us (8%)
  between operations  0.77 us (2%)
    ppermute x7, waiting for transfers between devices, exchanged(): lax.ppermute(value, axis, [(source, source ^ mask) for source in range(co...  16.7 us
    ppermute x3, waiting for transfers between devices, cyclic(): lax.ppermute(value, axis, [(source, (source + steps) % count) for source...  8.89 us
    ppermute x7, starting transfers between devices, exchanged(): lax.ppermute(value, axis, [(source, source ^ mask) for source in range(co...  6.6 us
    dot_general x3, matrix products, local(): jnp.einsum('osit,ostu->osiu', pieces, taken(tile_blocks[0]), precision=la...  5.24 us
    ppermute x3, starting transfers between devices, cyclic(): lax.ppermute(value, axis, [(source, (source + steps) % count) for source...  1.92 us
    gather x3, local copies, waits for them, and re-layouts, local(): pieces = stacked[jnp.arange(len(batch))[:, None], taken(column_place)]  1.71 us
  transfers between devices with their start and end apart: 10, of which 8 were waited for; matrix products, arithmetic and copies ran while one was open for 18% of the time, Pallas kernels for 0%

profile of v7, /device:TPU:0, one launch (start us, length us, event | category | flops | bytes accessed | tf_op | source)
XLA Modules:
  0.0 49.8 jit_solution(4140312894742023909)
XLA Ops:
  0.6 3.0 %collective-permute-start = (f32[8,512]{1,0:T(8,128)}, f32[8,512]{1,0:T(8,128)S(1)}, u32[]{:S(2)}, u32[]{:S(2)}) collective-permute-start(f32[8,512]{1,0:T(8,128)} %param.5), channel_id=1, source_target_pairs={{0,1},{1,0},{2,3},{3,2},{4,5},{5,4},{6,7},{7,6},{8,9},{9,8},{10,11... | collective-permute-start | bytes 49160 | tf_op jit(solution)/shard_map/ppermute | solution.py:26
  3.6 0.8 %constant_dynamic-update-slice_fusion.2 = f32[8,2048]{1,0:T(8,128)S(1)} fusion(f32[8,512]{1,0:T(8,128)} %param.5), kind=kLoop, calls=%fused_computation.31 | loop fusion | bytes 32768
  4.4 0.7 %fusion.19 = (s32[5,3]{0,1:T(4,128)S(1)}, s32[5,3]{0,1:T(4,128)S(1)}) fusion(s32[1,5,3]{1,0,2:T(1,128)} %param.7, s32[]{:T(128)S(6)} %axis_index.22, s32[1,5,3]{1,0,2:T(1,128)} %param.8), kind=kLoop, calls=%fused_computation.55 | loop fusion | flops 660 | bytes 244 | tf_op jit(solution)/shard_map/add | solution.py:101
  5.1 0.1 fusion.24
  5.2 0.1 fusion.27
  5.3 0.9 %fusion.37 = f32[8,8]{1,0:T(8,128)S(1)} fusion(f32[8,512]{1,0:T(8,128)} %param.5), kind=kOutput, calls=%fused_computation.84 | convolution fusion | flops 393216 | bytes 16640 | tf_op jit(solution)/shard_map/dot_general | solution.py:129
  6.2 0.1 copy.13
  6.3 0.1 copy.11
  6.4 0.1 copy.12
  6.5 0.7 %fusion.16 = f32[5,3]{1,0:T(8,128)S(1)} fusion(s32[5]{0:T(128)} %bitcast.107, pred[5]{0:T(512)(128)(4,1)S(1)} %compare_and_fusion), kind=kLoop, calls=%fused_computation.42 | loop fusion | flops 45 | bytes 85 | tf_op jit(solution)/shard_map/convert_element_type | solution.py:109
  7.3 0.1 fusion.14
  7.4 0.0 collective-permute-done
  7.4 0.7 %pad_maximum_fusion.1 = f32[8,1024]{1,0:T(8,128)S(1)} fusion(f32[8,512]{1,0:T(8,128)S(1)} %collective-permute-done, f32[8,512]{1,0:T(8,128)} %param.5), kind=kLoop, calls=%fused_computation.23 | loop fusion | flops 8192 | bytes 65536 | tf_op jit(solution)/shard_map/concatenate | solution.py:43
  8.1 1.5 %collective-permute-start.1 = (f32[8,1024]{1,0:T(8,128)S(1)}, f32[8,1024]{1,0:T(8,128)S(1)}, u32[]{:S(2)}, u32[]{:S(2)}) collective-permute-start(f32[8,1024]{1,0:T(8,128)S(1)} %pad_maximum_fusion.1), channel_id=1, source_target_pairs={{0,2},{1,3},{2,0},{3,1},{4,6},{5,7},{6,4},{7,5},{8,10},{9,11},{10,... | collective-permute-start | bytes 98312 | tf_op jit(solution)/shard_map/ppermute | solution.py:26
  9.6 2.4 %collective-permute-done.1 = f32[8,1024]{1,0:T(8,128)S(1)} collective-permute-done((f32[8,1024]{1,0:T(8,128)S(1)}, f32[8,1024]{1,0:T(8,128)S(1)}, u32[]{:S(2)}, u32[]{:S(2)}) %collective-permute-start.1) | collective-permute-done | bytes 32800 | tf_op jit(solution)/shard_map/ppermute | solution.py:26
  12.0 0.0 collective-permute-start.2
  12.0 0.1 reshape.146
  12.1 0.1 reshape.140
  12.2 5.3 %collective-permute-done.2 = f32[8,2048]{1,0:T(8,128)S(1)} collective-permute-done((f32[8,2048]{1,0:T(8,128)S(1)}, f32[8,2048]{1,0:T(8,128)S(1)}, u32[]{:S(2)}, u32[]{:S(2)}) %collective-permute-start.2) | collective-permute-done | bytes 65568 | tf_op jit(solution)/shard_map/ppermute | solution.py:79
  17.5 0.7 %pad_maximum_fusion = f32[8,4096]{1,0:T(8,128)S(1)} fusion(f32[8,1024]{1,0:T(8,128)S(1)} %collective-permute-done.1, f32[8,512]{1,0:T(8,128)S(1)} %collective-permute-done, f32[8,512]{1,0:T(8,128)} %param.5, f32[8,2048]{1,0:T(8,128)S(1)} %collective-permute-done.2), kind=kLoop, calls=%fused_computation.18 | loop fusion | flops 98304 | bytes 262144 | tf_op jit(solution)/shard_map/concatenate | solution.py:85
  18.2 1.9 %collective-permute-start.3 = (f32[8,4096]{1,0:T(8,128)S(1)}, f32[8,4096]{1,0:T(8,128)S(1)}, u32[]{:S(2)}, u32[]{:S(2)}) collective-permute-start(f32[8,4096]{1,0:T(8,128)S(1)} %pad_maximum_fusion), channel_id=1, source_target_pairs={{0,24},{4,28},{8,0},{12,4},{16,8},{20,12},{24,16},{28,20},{1,25},{... | collective-permute-start | bytes 393224 | tf_op jit(solution)/shard_map/ppermute | solution.py:79
  20.1 0.6 %gather_fusion = f32[6,8,256]{2,1,0:T(8,128)S(1)} fusion(f32[2,8,8,256]{3,2,1,0:T(8,128)S(1)} %maximum_bitcast_fusion, s32[6]{0:T(128)S(1)} %reshape.140), kind=kCustom, calls=%fused_computation | custom fusion | bytes 98352 | tf_op jit(solution)/shard_map/gather | solution.py:119
  20.7 0.1 collective-permute-start.4
  20.8 1.9 %fusion.2 = f32[2,3,8,256]{3,2,1,0:T(8,128)S(1)} fusion(f32[2,3,8,256]{3,2,1,0:T(8,128)S(1)} %bitcast.104, f32[1,5,3,256,256]{4,3,2,1,0:T(8,128)} %param.6), kind=kOutput, calls=%fused_computation.5 | convolution fusion | flops 18874368 | bytes 1671168 | tf_op jit(solution)/shard_map/osit,ostu->osiu/dot_general | solution.py:120
  22.7 3.6 %collective-permute-done.4 = f32[8,2048]{1,0:T(8,128)S(1)} collective-permute-done((f32[8,2048]{1,0:T(8,128)S(1)}, f32[8,2048]{1,0:T(8,128)S(1)}, u32[]{:S(2)}, u32[]{:S(2)}) %collective-permute-start.4) | collective-permute-done | bytes 65568 | tf_op jit(solution)/shard_map/ppermute | solution.py:79
  26.2 0.6 %gather_fusion.2 = f32[3,8,256]{2,1,0:T(8,128)S(1)} fusion(f32[1,8,8,256]{3,2,1,0:T(8,128)S(1)} %bitcast.106, s32[3]{0:T(128)S(1)} %or_bitcast_fusion), kind=kCustom, calls=%fused_computation.2 | custom fusion | bytes 49176 | tf_op jit(solution)/shard_map/gather | solution.py:119
  26.8 1.4 %fusion.8 = f32[3,8,256]{2,1,0:T(8,128)S(1)} fusion(f32[3,8,256]{2,1,0:T(8,128)S(1)} %gather_fusion.2, f32[1,5,3,256,256]{4,3,2,1,0:T(8,128)} %param.6), kind=kOutput, calls=%fused_computation.14 | convolution fusion | flops 9437184 | bytes 835584 | tf_op jit(solution)/shard_map/osit,ostu->osiu/dot_general | solution.py:120
  28.3 0.6 %gather_fusion.1 = f32[6,8,256]{2,1,0:T(8,128)S(1)} fusion(f32[2,8,8,256]{3,2,1,0:T(8,128)S(1)} %maximum_bitcast_fusion.1, s32[6]{0:T(128)S(1)} %reshape.146), kind=kCustom, calls=%fused_computation.1 | custom fusion | bytes 98352 | tf_op jit(solution)/shard_map/gather | solution.py:119
  28.9 1.9 %fusion = f32[2,3,8,256]{3,2,1,0:T(8,128)S(1)} fusion(f32[2,3,8,256]{3,2,1,0:T(8,128)S(1)} %bitcast.105, f32[1,5,3,256,256]{4,3,2,1,0:T(8,128)} %param.6), kind=kOutput, calls=%fused_computation.3 | convolution fusion | flops 18874368 | bytes 1671168 | tf_op jit(solution)/shard_map/osit,ostu->osiu/dot_general | solution.py:120
  30.8 0.3 convolution_bitcast_fusion
  31.0 0.3 fusion.7
  31.3 0.3 fusion.6
  31.6 0.2 fusion.36
  31.8 0.1 broadcast_in_dim.34
  31.9 0.1 concatenate.38
  32.0 1.5 %collective-permute-start.5 = (f32[8,1152]{1,0:T(8,128)S(1)}, f32[8,1152]{1,0:T(8,128)S(1)}, u32[]{:S(2)}, u32[]{:S(2)}) collective-permute-start(f32[8,1152]{1,0:T(8,128)S(1)} %concatenate.38), channel_id=1, source_target_pairs={{0,2},{1,3},{2,0},{3,1},{4,6},{5,7},{6,4},{7,5},{8,10},{9,11},{10,... | collective-permute-start | bytes 110600 | tf_op jit(solution)/shard_map/ppermute | solution.py:26
  33.5 2.4 %collective-permute-done.5 = f32[8,1152]{1,0:T(8,128)S(1)} collective-permute-done((f32[8,1152]{1,0:T(8,128)S(1)}, f32[8,1152]{1,0:T(8,128)S(1)}, u32[]{:S(2)}, u32[]{:S(2)}) %collective-permute-start.5) | collective-permute-done | bytes 36896 | tf_op jit(solution)/shard_map/ppermute | solution.py:26
  35.9 0.1 slice_add_fusion.3
  36.0 0.5 %collective-permute-start.6 = (f32[8,640]{1,0:T(8,128)S(1)}, f32[8,640]{1,0:T(8,128)S(1)}, u32[]{:S(2)}, u32[]{:S(2)}) collective-permute-start(f32[8,640]{1,0:T(8,128)S(1)} %pad_maximum_fusion.2), channel_id=1, source_target_pairs={{0,1},{1,0},{2,3},{3,2},{4,5},{5,4},{6,7},{7,6},{8,9},{9,8},{10,11... | collective-permute-start | bytes 61448 | tf_op jit(solution)/shard_map/ppermute | solution.py:26
  36.6 3.2 %collective-permute-done.6 = f32[8,640]{1,0:T(8,128)S(1)} collective-permute-done((f32[8,640]{1,0:T(8,128)S(1)}, f32[8,640]{1,0:T(8,128)S(1)}, u32[]{:S(2)}, u32[]{:S(2)}) %collective-permute-start.6) | collective-permute-done | bytes 20512 | tf_op jit(solution)/shard_map/ppermute | solution.py:26
  39.8 0.0 collective-permute-start.7
  39.8 1.2 %collective-permute-done.7 = f32[8,128]{1,0:T(8,128)S(1)} collective-permute-done((f32[8,128]{1,0:T(8,128)S(1)}, f32[8,128]{1,0:T(8,128)S(1)}, u32[]{:S(2)}, u32[]{:S(2)}) %collective-permute-start.7) | collective-permute-done | bytes 4128 | tf_op jit(solution)/shard_map/ppermute | solution.py:26
  41.0 0.0 collective-permute-start.8
  41.0 3.6 %collective-permute-done.8 = f32[8,128]{1,0:T(8,128)S(1)} collective-permute-done((f32[8,128]{1,0:T(8,128)S(1)}, f32[8,128]{1,0:T(8,128)S(1)}, u32[]{:S(2)}, u32[]{:S(2)}) %collective-permute-start.8) | collective-permute-done | bytes 4128 | tf_op jit(solution)/shard_map/ppermute | solution.py:26
  44.6 0.0 collective-permute-start.9
  44.6 0.6 %slice_add_fusion.1 = f32[8,512]{1,0:T(8,128)} fusion(f32[8,640]{1,0:T(8,128)S(1)} %collective-permute-done.6, f32[8,1024]{1,0:T(8,128)S(1)} %slice_add_fusion), kind=kLoop, calls=%fused_computation.26 | loop fusion | flops 4096 | bytes 49152 | tf_op jit(solution)/shard_map/add | solution.py:60
  45.2 3.9 %collective-permute-done.9 = f32[8,128]{1,0:T(8,128)S(1)} collective-permute-done((f32[8,128]{1,0:T(8,128)S(1)}, f32[8,128]{1,0:T(8,128)S(1)}, u32[]{:S(2)}, u32[]{:S(2)}) %collective-permute-start.9) | collective-permute-done | bytes 4128 | tf_op jit(solution)/shard_map/ppermute | solution.py:26
  49.1 0.7 %fusion.35 = (f32[8,8]{1,0:T(8,128)}, f32[8,8]{1,0:T(8,128)}) fusion(f32[8,128]{1,0:T(8,128)S(1)} %add_multiply_fusion), kind=kLoop, calls=%fused_computation.82 | loop fusion | bytes 1024 | tf_op jit(solution)/shard_map/slice | solution.py:141
  (20 shorter events, 0.1 us)
Async XLA Ops:
  0.6 6.7 %collective-permute-start = (f32[8,512]{1,0:T(8,128)}, f32[8,512]{1,0:T(8,128)S(1)}, u32[]{:S(2)}, u32[]{:S(2)}) collective-permute-start(f32[8,512]{1,0:T(8,128)} %param.5), channel_id=1, source_target_pairs={{0,1},{1,0},{2,3},{3,2},{4,5},{5,4},{6,7},{7,6},{8,9},{9,8},{10,11... | collective-permute-start | bytes 49160 | tf_op jit(solution)/shard_map/ppermute | solution.py:26
  8.1 3.9 %collective-permute-start.1 = (f32[8,1024]{1,0:T(8,128)S(1)}, f32[8,1024]{1,0:T(8,128)S(1)}, u32[]{:S(2)}, u32[]{:S(2)}) collective-permute-start(f32[8,1024]{1,0:T(8,128)S(1)} %pad_maximum_fusion.1), channel_id=1, source_target_pairs={{0,2},{1,3},{2,0},{3,1},{4,6},{5,7},{6,4},{7,5},{8,10},{9,11},{10,... | collective-permute-start | bytes 98312 | tf_op jit(solution)/shard_map/ppermute | solution.py:26
  12.0 5.5 %collective-permute-start.2 = (f32[8,2048]{1,0:T(8,128)S(1)}, f32[8,2048]{1,0:T(8,128)S(1)}, u32[]{:S(2)}, u32[]{:S(2)}) collective-permute-start(f32[8,2048]{1,0:T(8,128)S(1)} %constant_dynamic-update-slice_fusion), channel_id=1, source_target_pairs={{0,4},{4,8},{8,12},{12,16},{16,20},{20,24},{24,28},{28,0},{1,5},{5... | collective-permute-start | bytes 196616 | tf_op jit(solution)/shard_map/ppermute | solution.py:79
  18.2 10.0 %collective-permute-start.3 = (f32[8,4096]{1,0:T(8,128)S(1)}, f32[8,4096]{1,0:T(8,128)S(1)}, u32[]{:S(2)}, u32[]{:S(2)}) collective-permute-start(f32[8,4096]{1,0:T(8,128)S(1)} %pad_maximum_fusion), channel_id=1, source_target_pairs={{0,24},{4,28},{8,0},{12,4},{16,8},{20,12},{24,16},{28,20},{1,25},{... | collective-permute-start | bytes 393224 | tf_op jit(solution)/shard_map/ppermute | solution.py:79
  20.7 5.5 %collective-permute-start.4 = (f32[8,2048]{1,0:T(8,128)S(1)}, f32[8,2048]{1,0:T(8,128)S(1)}, u32[]{:S(2)}, u32[]{:S(2)}) collective-permute-start(f32[8,2048]{1,0:T(8,128)S(1)} %collective-permute-done.2), channel_id=1, source_target_pairs={{0,4},{4,8},{8,12},{12,16},{16,20},{20,24},{24,28},{28,0},{1,5},{5... | collective-permute-start | bytes 196616 | tf_op jit(solution)/shard_map/ppermute | solution.py:79
  32.0 4.0 %collective-permute-start.5 = (f32[8,1152]{1,0:T(8,128)S(1)}, f32[8,1152]{1,0:T(8,128)S(1)}, u32[]{:S(2)}, u32[]{:S(2)}) collective-permute-start(f32[8,1152]{1,0:T(8,128)S(1)} %concatenate.38), channel_id=1, source_target_pairs={{0,2},{1,3},{2,0},{3,1},{4,6},{5,7},{6,4},{7,5},{8,10},{9,11},{10,... | collective-permute-start | bytes 110600 | tf_op jit(solution)/shard_map/ppermute | solution.py:26
  36.0 3.8 %collective-permute-start.6 = (f32[8,640]{1,0:T(8,128)S(1)}, f32[8,640]{1,0:T(8,128)S(1)}, u32[]{:S(2)}, u32[]{:S(2)}) collective-permute-start(f32[8,640]{1,0:T(8,128)S(1)} %pad_maximum_fusion.2), channel_id=1, source_target_pairs={{0,1},{1,0},{2,3},{3,2},{4,5},{5,4},{6,7},{7,6},{8,9},{9,8},{10,11... | collective-permute-start | bytes 61448 | tf_op jit(solution)/shard_map/ppermute | solution.py:26
  39.8 1.2 %collective-permute-start.7 = (f32[8,128]{1,0:T(8,128)S(1)}, f32[8,128]{1,0:T(8,128)S(1)}, u32[]{:S(2)}, u32[]{:S(2)}) collective-permute-start(f32[8,128]{1,0:T(8,128)S(1)} %slice_add_fusion.2), channel_id=1, source_target_pairs={{0,4},{4,0},{8,12},{12,8},{16,20},{20,16},{24,28},{28,24},{1,5},{5... | collective-permute-start | bytes 12296 | tf_op jit(solution)/shard_map/ppermute | solution.py:26
  41.0 3.6 %collective-permute-start.8 = (f32[8,128]{1,0:T(8,128)S(1)}, f32[8,128]{1,0:T(8,128)S(1)}, u32[]{:S(2)}, u32[]{:S(2)}) collective-permute-start(f32[8,128]{1,0:T(8,128)S(1)} %add.105), channel_id=1, source_target_pairs={{0,8},{4,12},{8,0},{12,4},{16,24},{20,28},{24,16},{28,20},{1,9},{5... | collective-permute-start | bytes 12296 | tf_op jit(solution)/shard_map/ppermute | solution.py:26
  44.6 4.5 %collective-permute-start.9 = (f32[8,128]{1,0:T(8,128)S(1)}, f32[8,128]{1,0:T(8,128)S(1)}, u32[]{:S(2)}, u32[]{:S(2)}) collective-permute-start(f32[8,128]{1,0:T(8,128)S(1)} %add.106), channel_id=1, source_target_pairs={{0,16},{4,20},{8,24},{12,28},{16,0},{20,4},{24,8},{28,12},{1,17},{... | collective-permute-start | bytes 12296 | tf_op jit(solution)/shard_map/ppermute | solution.py:26

commit v8 on v3

--- a/solution.py
+++ b/solution.py
@@ -88,38 +88,54 @@
     return lowers[::-1] + [source] + uppers
 
 
+def paired_panels(vectors):
+    local_pair = jnp.concatenate([vectors, exchanged(vectors, "blk", 1)], axis=1)
+    gathered = gather_help(local_pair)
+    lower = shifted(gathered, "blk", 2)
+    upper = shifted(gathered, "blk", -2)
+    return gathered, [lower, gathered, upper]
+
+
 def local(vectors, tile_blocks, tile_row, tile_col, counts):
     groups = lax.axis_size("blk")
     piece_width = vectors.shape[1]
     group_width = piece_width * lax.axis_size("help")
     group_rows = group_width // TILE
-    full_panel = gather_help(vectors)
-    panels = neighbour_panels(full_panel)
+    paired = groups % 2 == 0 and is_power_of_two(lax.axis_size("help"))
     tiles_per_piece = piece_width // TILE
     order = help_order()
 
     def placed(tile_index):
         return ((tile_index // tiles_per_piece) ^ order) * tiles_per_piece + tile_index % tiles_per_piece
 
-    column_place = placed(tile_col[0])
-    row_place = placed(tile_row[0])
     slot_ids = jnp.arange(SLOTS, dtype=jnp.int32)[None, :]
     row_ids = jnp.arange(group_rows, dtype=jnp.int32)
     live = (slot_ids < counts[0][:, None]).astype(jnp.float32)
+    offset_ids = jnp.arange(NOFF, dtype=jnp.int32)
+    if paired:
+        gathered, pairs = paired_panels(vectors)
+        helpers = lax.axis_size("help")
+        halves = [pair.reshape(VEC, helpers, 2, piece_width) for pair in pairs]
+        full_panel = halves[1][:, :, 0].reshape(VEC, group_width)
+        stacked = jnp.stack([half[:, :, side] for half in halves for side in range(2)])
+        stacked = stacked.reshape(2 * len(pairs), VEC, group_rows, TILE)
+        core = lax.axis_index("blk") % 2
+        panel_ids = offset_ids + 2 * core * (offset_ids % 2)
+    else:
+        full_panel = gather_help(vectors)
+        stacked = jnp.stack(neighbour_panels(full_panel)).reshape(NOFF, VEC, group_rows, TILE)
+        panel_ids = offset_ids
+    stacked = stacked.transpose(0, 2, 1, 3)
+    column_place = placed(tile_col[0])
+    row_place = placed(tile_row[0])
     one_hot = (row_place[:, :, None] == row_ids).astype(jnp.float32) * live[:, :, None]
-    partial_value = None
-    for batch in ((BAND,), (BAND - 1, BAND + 1), (0, NOFF - 1)):
-        chosen = jnp.array(batch, dtype=jnp.int32)
-        stacked = jnp.stack([panels[o] for o in batch]).reshape(len(batch), VEC, group_rows, TILE)
-        stacked = stacked.transpose(0, 2, 1, 3)
-        pieces = stacked[jnp.arange(len(batch))[:, None], column_place[chosen]]
-        contribution = jnp.einsum(
-            "osit,ostu->osiu", pieces, tile_blocks[0, chosen], precision=lax.Precision.HIGHEST
-        )
-        batch_value = jnp.einsum(
-            "osiu,osr->iru", contribution, one_hot[chosen], precision=lax.Precision.HIGHEST
-        )
-        partial_value = batch_value if partial_value is None else partial_value + batch_value
+    pieces = stacked[panel_ids[:, None], column_place]
+    contribution = jnp.einsum(
+        "osit,ostu->osiu", pieces, tile_blocks[0], precision=lax.Precision.HIGH
+    )
+    partial_value = jnp.einsum(
+        "osiu,osr->iru", contribution, one_hot, precision=lax.Precision.HIGHEST
+    )
     flattened = partial_value.reshape(VEC, group_width)
     basis_size = float(groups * group_width)
     correlation_term = jnp.dot(

time: 60.2 us -> 49.5 us (0.82)
  local copies, waits for them, and re-layouts: 14.7 us -> 2.45 us
  waiting for transfers between devices: 12.5 us -> 19.1 us
  starting transfers between devices: 23.4 us -> 17.3 us
  other arithmetic: 2.26 us -> 4.24 us
  matrix products: 5.9 us -> 4.93 us
    gather x9 -> x1, local copies, waits for them, and re-layouts: 10.9 us -> 0.63 us  [local(): pieces = stacked[panel_ids[:, None], column_place]]
    ppermute x4 -> x2, waiting for transfers between devices: 0.61 us -> 5.52 us  [shifted(): lax.ppermute(value, axis, [(source, source + steps) for source in range(i...]
    ppermute x4 -> x2, starting transfers between devices: 9.33 us -> 5.16 us  [shifted(): lax.ppermute(value, axis, [(source, source + steps) for source in range(i...]
    ppermute x7 -> x8, starting transfers between devices: 14 us -> 12.1 us  [exchanged(): lax.ppermute(value, axis, [(source, source ^ mask) for source in range(co...]
    ppermute x7 -> x8, waiting for transfers between devices: 11.9 us -> 13.6 us  [exchanged(): lax.ppermute(value, axis, [(source, source ^ mask) for source in range(co...]
    squeeze x2 -> x0, local copies, waits for them, and re-layouts: 1.53 us -> none  [the longest x1 0.77 us: local(): row_place = placed(tile_row[0])]
    concatenate x4 -> x3, other arithmetic: 0.03 us -> 1.45 us  [the longest x2 0.73 us: local(): pieces = stacked[panel_ids[:, None], column_place]]
    dot_general x6 -> x2, matrix products: 4.78 us -> 3.8 us  [the longest x1 3.18 us: local(): jnp.einsum('osit,ostu->osiu', pieces, tile_blocks[0], precision=lax.Preci...]
  transfers between devices with their start and end apart: 11 -> 10, of which waited for: 7 -> 9; matrix products, arithmetic and copies ran while one was open for 29% -> 9% of each run, Pallas kernels for 0% -> 0%
where the time goes in v8:
time: 49.5 us; the launch traced here: 48.8 us
  waiting for transfers between devices  19.1 us (39%)
  starting transfers between devices  17.3 us (35%)
  matrix products  4.93 us (10%)
  other arithmetic  4.24 us (9%)
  local copies, waits for them, and re-layouts  2.45 us (5%)
  between operations  0.76 us (2%)
    ppermute x8, waiting for transfers between devices, exchanged(): lax.ppermute(value, axis, [(source, source ^ mask) for source in range(co...  13.6 us
    ppermute x8, starting transfers between devices, exchanged(): lax.ppermute(value, axis, [(source, source ^ mask) for source in range(co...  12.1 us
    ppermute x2, waiting for transfers between devices, shifted(): lax.ppermute(value, axis, [(source, source + steps) for source in range(i...  5.52 us
    ppermute x2, starting transfers between devices, shifted(): lax.ppermute(value, axis, [(source, source + steps) for source in range(i...  5.16 us
    dot_general x1, matrix products, local(): jnp.einsum('osit,ostu->osiu', pieces, tile_blocks[0], precision=lax.Preci...  3.18 us
  transfers between devices with their start and end apart: 10, of which 9 were waited for; matrix products, arithmetic and copies ran while one was open for 9% of the time, Pallas kernels for 0%

profile of v8, /device:TPU:0, one launch (start us, length us, event | category | flops | bytes accessed | tf_op | source)
XLA Modules:
  0.0 48.8 jit_solution(6614543429150864662)
XLA Ops:
  0.6 0.5 %collective-permute-start = (f32[8,512]{1,0:T(8,128)}, f32[8,512]{1,0:T(8,128)S(1)}, u32[]{:S(2)}, u32[]{:S(2)}) collective-permute-start(f32[8,512]{1,0:T(8,128)} %param.5), channel_id=1, source_target_pairs={{0,4},{4,0},{8,12},{12,8},{16,20},{20,16},{24,28},{28,24},{1,5},{5... | collective-permute-start | bytes 49160 | tf_op jit(solution)/shard_map/ppermute | solution.py:26
  1.1 0.9 %fusion.29 = f32[8,8]{1,0:T(8,128)S(1)} fusion(f32[8,512]{1,0:T(8,128)} %param.5), kind=kOutput, calls=%fused_computation.67 | convolution fusion | flops 393216 | bytes 16640 | tf_op jit(solution)/shard_map/dot_general | solution.py:141
  2.1 0.7 %fusion.12 = f32[5,3]{0,1:T(4,128)S(1)} fusion(s32[5]{0:T(128)} %bitcast.79), kind=kLoop, calls=%fused_computation.48 | loop fusion | flops 30 | bytes 80 | tf_op jit(solution)/shard_map/convert_element_type | solution.py:113
  2.8 0.7 %fusion.10 = s32[5,3]{0,1:T(4,128)S(1)} fusion(s32[1,5,3]{1,0,2:T(1,128)} %param.7, s32[]{:T(128)S(6)} %axis_index.22), kind=kLoop, calls=%fused_computation.43 | loop fusion | flops 330 | bytes 124 | tf_op jit(solution)/shard_map/add | solution.py:109
  3.5 0.7 %fusion.18 = s32[5,3,1]{0,2,1:T(1,128)S(1)} fusion(s32[1,5,3]{1,0,2:T(1,128)} %param.8, s32[5]{0:T(128)S(1)} %fusion.22, s32[]{:T(128)S(6)} %axis_index.22), kind=kLoop, calls=%fused_computation.55 | loop fusion | flops 420 | bytes 144 | tf_op jit(solution)/shard_map/concatenate | solution.py:132
  4.2 0.7 %constant_dynamic-update-slice_fusion.3 = f32[8,4096]{1,0:T(8,128)S(1)} fusion(f32[8,512]{1,0:T(8,128)} %param.5), kind=kLoop, calls=%fused_computation.11 | loop fusion | bytes 32768
  4.9 0.1 copy.21
  5.0 0.1 reshape.245
  5.1 0.0 collective-permute-done
  5.1 0.7 %pad_maximum_fusion.1 = f32[8,1024]{1,0:T(8,128)S(1)} fusion(f32[8,512]{1,0:T(8,128)S(1)} %collective-permute-done, f32[8,512]{1,0:T(8,128)} %param.5), kind=kLoop, calls=%fused_computation.7 | loop fusion | flops 8192 | bytes 65536 | tf_op jit(solution)/shard_map/concatenate | solution.py:92
  5.8 2.5 %collective-permute-start.1 = (f32[8,1024]{1,0:T(8,128)S(1)}, f32[8,1024]{1,0:T(8,128)S(1)}, u32[]{:S(2)}, u32[]{:S(2)}) collective-permute-start(f32[8,1024]{1,0:T(8,128)S(1)} %pad_maximum_fusion.1), channel_id=1, source_target_pairs={{0,1},{1,0},{2,3},{3,2},{4,5},{5,4},{6,7},{7,6},{8,9},{9,8},{10,11... | collective-permute-start | bytes 98312 | tf_op jit(solution)/shard_map/ppermute | solution.py:26
  8.3 2.0 %collective-permute-done.1 = f32[8,1024]{1,0:T(8,128)S(1)} collective-permute-done((f32[8,1024]{1,0:T(8,128)S(1)}, f32[8,1024]{1,0:T(8,128)S(1)}, u32[]{:S(2)}, u32[]{:S(2)}) %collective-permute-start.1) | collective-permute-done | bytes 32800 | tf_op jit(solution)/shard_map/ppermute | solution.py:26
  10.3 0.7 %pad_maximum_fusion = f32[8,2048]{1,0:T(8,128)S(1)} fusion(f32[8,1024]{1,0:T(8,128)S(1)} %collective-permute-done.1, f32[8,512]{1,0:T(8,128)S(1)} %collective-permute-done, f32[8,512]{1,0:T(8,128)} %param.5), kind=kLoop, calls=%fused_computation.5 | loop fusion | flops 32768 | bytes 131072 | tf_op jit(solution)/shard_map/concatenate | solution.py:43
  11.1 1.9 %collective-permute-start.2 = (f32[8,2048]{1,0:T(8,128)S(1)}, f32[8,2048]{1,0:T(8,128)S(1)}, u32[]{:S(2)}, u32[]{:S(2)}) collective-permute-start(f32[8,2048]{1,0:T(8,128)S(1)} %pad_maximum_fusion), channel_id=1, source_target_pairs={{0,2},{1,3},{2,0},{3,1},{4,6},{5,7},{6,4},{7,5},{8,10},{9,11},{10,... | collective-permute-start | bytes 196616 | tf_op jit(solution)/shard_map/ppermute | solution.py:26
  13.0 2.4 %collective-permute-done.2 = f32[8,2048]{1,0:T(8,128)S(1)} collective-permute-done((f32[8,2048]{1,0:T(8,128)S(1)}, f32[8,2048]{1,0:T(8,128)S(1)}, u32[]{:S(2)}, u32[]{:S(2)}) %collective-permute-start.2) | collective-permute-done | bytes 65568 | tf_op jit(solution)/shard_map/ppermute | solution.py:26
  15.3 3.9 %collective-permute-start.3 = (f32[8,4096]{1,0:T(8,128)S(1)}, f32[8,4096]{1,0:T(8,128)S(1)}, u32[]{:S(2)}, u32[]{:S(2)}) collective-permute-start(f32[8,4096]{1,0:T(8,128)S(1)} %constant_dynamic-update-slice_fusion), channel_id=1, source_target_pairs={{0,8},{4,12},{8,16},{12,20},{16,24},{20,28},{1,9},{5,13},{9,17},{1... | collective-permute-start | bytes 393224 | tf_op jit(solution)/shard_map/ppermute | solution.py:17
  19.2 1.3 %collective-permute-start.4 = (f32[8,4096]{1,0:T(8,128)S(1)}, f32[8,4096]{1,0:T(8,128)S(1)}, u32[]{:S(2)}, u32[]{:S(2)}) collective-permute-start(f32[8,4096]{1,0:T(8,128)S(1)} %constant_dynamic-update-slice_fusion), channel_id=1, source_target_pairs={{8,0},{12,4},{16,8},{20,12},{24,16},{28,20},{9,1},{13,5},{17,9},{2... | collective-permute-start | bytes 393224 | tf_op jit(solution)/shard_map/ppermute | solution.py:17
  20.5 1.2 %collective-permute-done.3 = f32[8,4096]{1,0:T(8,128)S(1)} collective-permute-done((f32[8,4096]{1,0:T(8,128)S(1)}, f32[8,4096]{1,0:T(8,128)S(1)}, u32[]{:S(2)}, u32[]{:S(2)}) %collective-permute-start.3) | collective-permute-done | bytes 131104 | tf_op jit(solution)/shard_map/ppermute | solution.py:17
  21.7 4.3 %collective-permute-done.4 = f32[8,4096]{1,0:T(8,128)S(1)} collective-permute-done((f32[8,4096]{1,0:T(8,128)S(1)}, f32[8,4096]{1,0:T(8,128)S(1)}, u32[]{:S(2)}, u32[]{:S(2)}) %collective-permute-start.4) | collective-permute-done | bytes 131104 | tf_op jit(solution)/shard_map/ppermute | solution.py:17
  26.1 0.6 %gather_fusion = f32[15,8,256]{2,1,0:T(8,128)S(1)} fusion(f32[6,8,8,256]{3,2,1,0:T(8,128)S(1)} %bitcast.78, s32[15]{0:T(128)S(1)} %reshape.245), kind=kCustom, calls=%fused_computation | custom fusion | bytes 245880 | tf_op jit(solution)/shard_map/gather | solution.py:132
  26.8 3.2 %fusion = f32[5,3,8,256]{3,2,1,0:T(8,128)S(1)} fusion(f32[5,3,8,256]{3,2,1,0:T(8,128)S(1)} %bitcast.69, f32[1,5,3,256,256]{4,3,2,1,0:T(8,128)} %param.6), kind=kOutput, calls=%fused_computation.1 | convolution fusion | flops 47185920 | bytes 4177920 | tf_op jit(solution)/shard_map/osit,ostu->osiu/dot_general | solution.py:133
  30.0 0.6 %convolution_bitcast_fusion = f32[1,8,8,256]{3,2,1,0:T(8,128)S(1)} fusion(f32[5,3,8,256]{3,2,1,0:T(8,128)S(1)} %fusion, f32[5,3]{0,1:T(4,128)S(1)} %fusion.12, s32[5,3]{0,1:T(4,128)S(1)} %fusion.10), kind=kOutput, calls=%fused_computation.3 | convolution fusion | flops 2949360 | bytes 188536 | tf_op jit(solution)/shard_map/osiu,osr->iru/dot_general | solution.py:136
  30.6 0.2 fusion.28
  30.9 0.1 concatenate.29
  31.0 1.5 %collective-permute-start.5 = (f32[8,1152]{1,0:T(8,128)S(1)}, f32[8,1152]{1,0:T(8,128)S(1)}, u32[]{:S(2)}, u32[]{:S(2)}) collective-permute-start(f32[8,1152]{1,0:T(8,128)S(1)} %concatenate.29), channel_id=1, source_target_pairs={{0,2},{1,3},{2,0},{3,1},{4,6},{5,7},{6,4},{7,5},{8,10},{9,11},{10,... | collective-permute-start | bytes 110600 | tf_op jit(solution)/shard_map/ppermute | solution.py:26
  32.5 2.4 %collective-permute-done.5 = f32[8,1152]{1,0:T(8,128)S(1)} collective-permute-done((f32[8,1152]{1,0:T(8,128)S(1)}, f32[8,1152]{1,0:T(8,128)S(1)}, u32[]{:S(2)}, u32[]{:S(2)}) %collective-permute-start.5) | collective-permute-done | bytes 36896 | tf_op jit(solution)/shard_map/ppermute | solution.py:26
  35.0 0.1 slice_add_fusion.3
  35.0 1.5 %collective-permute-start.6 = (f32[8,640]{1,0:T(8,128)S(1)}, f32[8,640]{1,0:T(8,128)S(1)}, u32[]{:S(2)}, u32[]{:S(2)}) collective-permute-start(f32[8,640]{1,0:T(8,128)S(1)} %pad_maximum_fusion.2), channel_id=1, source_target_pairs={{0,1},{1,0},{2,3},{3,2},{4,5},{5,4},{6,7},{7,6},{8,9},{9,8},{10,11... | collective-permute-start | bytes 61448 | tf_op jit(solution)/shard_map/ppermute | solution.py:26
  36.5 2.3 %collective-permute-done.6 = f32[8,640]{1,0:T(8,128)S(1)} collective-permute-done((f32[8,640]{1,0:T(8,128)S(1)}, f32[8,640]{1,0:T(8,128)S(1)}, u32[]{:S(2)}, u32[]{:S(2)}) %collective-permute-start.6) | collective-permute-done | bytes 20512 | tf_op jit(solution)/shard_map/ppermute | solution.py:26
  38.8 0.0 collective-permute-start.7
  38.8 1.2 %collective-permute-done.7 = f32[8,128]{1,0:T(8,128)S(1)} collective-permute-done((f32[8,128]{1,0:T(8,128)S(1)}, f32[8,128]{1,0:T(8,128)S(1)}, u32[]{:S(2)}, u32[]{:S(2)}) %collective-permute-start.7) | collective-permute-done | bytes 4128 | tf_op jit(solution)/shard_map/ppermute | solution.py:26
  40.0 1.6 %collective-permute-start.8 = (f32[8,128]{1,0:T(8,128)S(1)}, f32[8,128]{1,0:T(8,128)S(1)}, u32[]{:S(2)}, u32[]{:S(2)}) collective-permute-start(f32[8,128]{1,0:T(8,128)S(1)} %add.124), channel_id=1, source_target_pairs={{0,8},{4,12},{8,0},{12,4},{16,24},{20,28},{24,16},{28,20},{1,9},{5... | collective-permute-start | bytes 12296 | tf_op jit(solution)/shard_map/ppermute | solution.py:26
  41.6 2.0 %collective-permute-done.8 = f32[8,128]{1,0:T(8,128)S(1)} collective-permute-done((f32[8,128]{1,0:T(8,128)S(1)}, f32[8,128]{1,0:T(8,128)S(1)}, u32[]{:S(2)}, u32[]{:S(2)}) %collective-permute-start.8) | collective-permute-done | bytes 4128 | tf_op jit(solution)/shard_map/ppermute | solution.py:26
  43.6 2.6 %collective-permute-start.9 = (f32[8,128]{1,0:T(8,128)S(1)}, f32[8,128]{1,0:T(8,128)S(1)}, u32[]{:S(2)}, u32[]{:S(2)}) collective-permute-start(f32[8,128]{1,0:T(8,128)S(1)} %add.125), channel_id=1, source_target_pairs={{0,16},{4,20},{8,24},{12,28},{16,0},{20,4},{24,8},{28,12},{1,17},{... | collective-permute-start | bytes 12296 | tf_op jit(solution)/shard_map/ppermute | solution.py:26
  46.2 0.6 %slice_add_fusion.1 = f32[8,512]{1,0:T(8,128)} fusion(f32[8,640]{1,0:T(8,128)S(1)} %collective-permute-done.6, f32[8,1024]{1,0:T(8,128)S(1)} %slice_add_fusion), kind=kLoop, calls=%fused_computation.19 | loop fusion | flops 4096 | bytes 49152 | tf_op jit(solution)/shard_map/add | solution.py:60
  46.8 1.3 %collective-permute-done.9 = f32[8,128]{1,0:T(8,128)S(1)} collective-permute-done((f32[8,128]{1,0:T(8,128)S(1)}, f32[8,128]{1,0:T(8,128)S(1)}, u32[]{:S(2)}, u32[]{:S(2)}) %collective-permute-start.9) | collective-permute-done | bytes 4128 | tf_op jit(solution)/shard_map/ppermute | solution.py:26
  48.1 0.7 %fusion.27 = (f32[8,8]{1,0:T(8,128)}, f32[8,8]{1,0:T(8,128)}) fusion(f32[8,128]{1,0:T(8,128)S(1)} %add_multiply_fusion), kind=kLoop, calls=%fused_computation.65 | loop fusion | bytes 1024 | tf_op jit(solution)/shard_map/slice | solution.py:153
  (23 shorter events, 0.2 us)
Async XLA Ops:
  0.6 4.4 %collective-permute-start = (f32[8,512]{1,0:T(8,128)}, f32[8,512]{1,0:T(8,128)S(1)}, u32[]{:S(2)}, u32[]{:S(2)}) collective-permute-start(f32[8,512]{1,0:T(8,128)} %param.5), channel_id=1, source_target_pairs={{0,4},{4,0},{8,12},{12,8},{16,20},{20,16},{24,28},{28,24},{1,5},{5... | collective-permute-start | bytes 49160 | tf_op jit(solution)/shard_map/ppermute | solution.py:26
  5.8 4.5 %collective-permute-start.1 = (f32[8,1024]{1,0:T(8,128)S(1)}, f32[8,1024]{1,0:T(8,128)S(1)}, u32[]{:S(2)}, u32[]{:S(2)}) collective-permute-start(f32[8,1024]{1,0:T(8,128)S(1)} %pad_maximum_fusion.1), channel_id=1, source_target_pairs={{0,1},{1,0},{2,3},{3,2},{4,5},{5,4},{6,7},{7,6},{8,9},{9,8},{10,11... | collective-permute-start | bytes 98312 | tf_op jit(solution)/shard_map/ppermute | solution.py:26
  11.1 4.3 %collective-permute-start.2 = (f32[8,2048]{1,0:T(8,128)S(1)}, f32[8,2048]{1,0:T(8,128)S(1)}, u32[]{:S(2)}, u32[]{:S(2)}) collective-permute-start(f32[8,2048]{1,0:T(8,128)S(1)} %pad_maximum_fusion), channel_id=1, source_target_pairs={{0,2},{1,3},{2,0},{3,1},{4,6},{5,7},{6,4},{7,5},{8,10},{9,11},{10,... | collective-permute-start | bytes 196616 | tf_op jit(solution)/shard_map/ppermute | solution.py:26
  15.3 6.4 %collective-permute-start.3 = (f32[8,4096]{1,0:T(8,128)S(1)}, f32[8,4096]{1,0:T(8,128)S(1)}, u32[]{:S(2)}, u32[]{:S(2)}) collective-permute-start(f32[8,4096]{1,0:T(8,128)S(1)} %constant_dynamic-update-slice_fusion), channel_id=1, source_target_pairs={{0,8},{4,12},{8,16},{12,20},{16,24},{20,28},{1,9},{5,13},{9,17},{1... | collective-permute-start | bytes 393224 | tf_op jit(solution)/shard_map/ppermute | solution.py:17
  19.2 6.9 %collective-permute-start.4 = (f32[8,4096]{1,0:T(8,128)S(1)}, f32[8,4096]{1,0:T(8,128)S(1)}, u32[]{:S(2)}, u32[]{:S(2)}) collective-permute-start(f32[8,4096]{1,0:T(8,128)S(1)} %constant_dynamic-update-slice_fusion), channel_id=1, source_target_pairs={{8,0},{12,4},{16,8},{20,12},{24,16},{28,20},{9,1},{13,5},{17,9},{2... | collective-permute-start | bytes 393224 | tf_op jit(solution)/shard_map/ppermute | solution.py:17
  31.0 4.0 %collective-permute-start.5 = (f32[8,1152]{1,0:T(8,128)S(1)}, f32[8,1152]{1,0:T(8,128)S(1)}, u32[]{:S(2)}, u32[]{:S(2)}) collective-permute-start(f32[8,1152]{1,0:T(8,128)S(1)} %concatenate.29), channel_id=1, source_target_pairs={{0,2},{1,3},{2,0},{3,1},{4,6},{5,7},{6,4},{7,5},{8,10},{9,11},{10,... | collective-permute-start | bytes 110600 | tf_op jit(solution)/shard_map/ppermute | solution.py:26
  35.0 3.8 %collective-permute-start.6 = (f32[8,640]{1,0:T(8,128)S(1)}, f32[8,640]{1,0:T(8,128)S(1)}, u32[]{:S(2)}, u32[]{:S(2)}) collective-permute-start(f32[8,640]{1,0:T(8,128)S(1)} %pad_maximum_fusion.2), channel_id=1, source_target_pairs={{0,1},{1,0},{2,3},{3,2},{4,5},{5,4},{6,7},{7,6},{8,9},{9,8},{10,11... | collective-permute-start | bytes 61448 | tf_op jit(solution)/shard_map/ppermute | solution.py:26
  38.8 1.2 %collective-permute-start.7 = (f32[8,128]{1,0:T(8,128)S(1)}, f32[8,128]{1,0:T(8,128)S(1)}, u32[]{:S(2)}, u32[]{:S(2)}) collective-permute-start(f32[8,128]{1,0:T(8,128)S(1)} %slice_add_fusion.2), channel_id=1, source_target_pairs={{0,4},{4,0},{8,12},{12,8},{16,20},{20,16},{24,28},{28,24},{1,5},{5... | collective-permute-start | bytes 12296 | tf_op jit(solution)/shard_map/ppermute | solution.py:26
  40.0 3.6 %collective-permute-start.8 = (f32[8,128]{1,0:T(8,128)S(1)}, f32[8,128]{1,0:T(8,128)S(1)}, u32[]{:S(2)}, u32[]{:S(2)}) collective-permute-start(f32[8,128]{1,0:T(8,128)S(1)} %add.124), channel_id=1, source_target_pairs={{0,8},{4,12},{8,0},{12,4},{16,24},{20,28},{24,16},{28,20},{1,9},{5... | collective-permute-start | bytes 12296 | tf_op jit(solution)/shard_map/ppermute | solution.py:26
  43.6 4.5 %collective-permute-start.9 = (f32[8,128]{1,0:T(8,128)S(1)}, f32[8,128]{1,0:T(8,128)S(1)}, u32[]{:S(2)}, u32[]{:S(2)}) collective-permute-start(f32[8,128]{1,0:T(8,128)S(1)} %add.125), channel_id=1, source_target_pairs={{0,16},{4,20},{8,24},{12,28},{16,0},{20,4},{24,8},{28,12},{1,17},{... | collective-permute-start | bytes 12296 | tf_op jit(solution)/shard_map/ppermute | solution.py:26

commit v9 on v8

--- a/solution.py
+++ b/solution.py
@@ -108,12 +108,16 @@
     def placed(tile_index):
         return ((tile_index // tiles_per_piece) ^ order) * tiles_per_piece + tile_index % tiles_per_piece
 
+    if paired:
+        gathered, pairs = paired_panels(vectors)
+        tile_row, tile_col, counts, vectors, _ = lax.optimization_barrier(
+            (tile_row, tile_col, counts, vectors, gathered)
+        )
     slot_ids = jnp.arange(SLOTS, dtype=jnp.int32)[None, :]
     row_ids = jnp.arange(group_rows, dtype=jnp.int32)
     live = (slot_ids < counts[0][:, None]).astype(jnp.float32)
     offset_ids = jnp.arange(NOFF, dtype=jnp.int32)
     if paired:
-        gathered, pairs = paired_panels(vectors)
         helpers = lax.axis_size("help")
         halves = [pair.reshape(VEC, helpers, 2, piece_width) for pair in pairs]
         full_panel = halves[1][:, :, 0].reshape(VEC, group_width)

time: 49.5 us -> 46.9 us (0.947)
  waiting for transfers between devices: 19.1 us -> 16 us
  starting transfers between devices: 17.3 us -> 17.9 us
    ppermute x2, waiting for transfers between devices: 5.52 us -> 2.33 us  [shifted(): lax.ppermute(value, axis, [(source, source + steps) for source in range(i...]
  transfers between devices with their start and end apart: 10 -> 10, of which waited for: 9 -> 9; matrix products, arithmetic and copies ran while one was open for 9% -> 10% of each run, Pallas kernels for 0% -> 0%
where the time goes in v9:
time: 46.9 us; the launch traced here: 46.3 us
  starting transfers between devices  17.9 us (38%)
  waiting for transfers between devices  16 us (34%)
  matrix products  4.93 us (11%)
  other arithmetic  4.25 us (9%)
  local copies, waits for them, and re-layouts  2.45 us (5%)
  between operations  0.75 us (2%)
    ppermute x8, waiting for transfers between devices, exchanged(): lax.ppermute(value, axis, [(source, source ^ mask) for source in range(co...  13.7 us
    ppermute x8, starting transfers between devices, exchanged(): lax.ppermute(value, axis, [(source, source ^ mask) for source in range(co...  12.6 us
    ppermute x2, starting transfers between devices, shifted(): lax.ppermute(value, axis, [(source, source + steps) for source in range(i...  5.27 us
    dot_general x1, matrix products, local(): jnp.einsum('osit,ostu->osiu', pieces, tile_blocks[0], precision=lax.Preci...  3.18 us
    ppermute x2, waiting for transfers between devices, shifted(): lax.ppermute(value, axis, [(source, source + steps) for source in range(i...  2.33 us
  transfers between devices with their start and end apart: 10, of which 9 were waited for; matrix products, arithmetic and copies ran while one was open for 10% of the time, Pallas kernels for 0%

profile of v9, /device:TPU:0, one launch (start us, length us, event | category | flops | bytes accessed | tf_op | source)
XLA Modules:
  0.0 46.3 jit_solution(11341808595904455715)
XLA Ops:
  0.6 0.5 %collective-permute-start = (f32[8,512]{1,0:T(8,128)}, f32[8,512]{1,0:T(8,128)S(1)}, u32[]{:S(2)}, u32[]{:S(2)}) collective-permute-start(f32[8,512]{1,0:T(8,128)} %param.5), channel_id=1, source_target_pairs={{0,4},{4,0},{8,12},{12,8},{16,20},{20,16},{24,28},{28,24},{1,5},{5... | collective-permute-start | bytes 49160 | tf_op jit(solution)/shard_map/ppermute | solution.py:26
  1.1 0.7 %constant_dynamic-update-slice_fusion.3 = f32[8,4096]{1,0:T(8,128)S(1)} fusion(f32[8,512]{1,0:T(8,128)} %param.5), kind=kLoop, calls=%fused_computation.11 | loop fusion | bytes 32768
  1.9 0.3 collective-permute-done
  2.2 0.7 %pad_maximum_fusion.1 = f32[8,1024]{1,0:T(8,128)S(1)} fusion(f32[8,512]{1,0:T(8,128)S(1)} %collective-permute-done, f32[8,512]{1,0:T(8,128)} %param.5), kind=kLoop, calls=%fused_computation.7 | loop fusion | flops 8192 | bytes 65536 | tf_op jit(solution)/shard_map/concatenate | solution.py:92
  2.9 2.8 %collective-permute-start.1 = (f32[8,1024]{1,0:T(8,128)S(1)}, f32[8,1024]{1,0:T(8,128)S(1)}, u32[]{:S(2)}, u32[]{:S(2)}) collective-permute-start(f32[8,1024]{1,0:T(8,128)S(1)} %pad_maximum_fusion.1), channel_id=1, source_target_pairs={{0,1},{1,0},{2,3},{3,2},{4,5},{5,4},{6,7},{7,6},{8,9},{9,8},{10,11... | collective-permute-start | bytes 98312 | tf_op jit(solution)/shard_map/ppermute | solution.py:26
  5.8 1.9 %collective-permute-done.1 = f32[8,1024]{1,0:T(8,128)S(1)} collective-permute-done((f32[8,1024]{1,0:T(8,128)S(1)}, f32[8,1024]{1,0:T(8,128)S(1)}, u32[]{:S(2)}, u32[]{:S(2)}) %collective-permute-start.1) | collective-permute-done | bytes 32800 | tf_op jit(solution)/shard_map/ppermute | solution.py:26
  7.6 0.7 %pad_maximum_fusion = f32[8,2048]{1,0:T(8,128)S(1)} fusion(f32[8,1024]{1,0:T(8,128)S(1)} %collective-permute-done.1, f32[8,512]{1,0:T(8,128)S(1)} %collective-permute-done, f32[8,512]{1,0:T(8,128)} %param.5), kind=kLoop, calls=%fused_computation.5 | loop fusion | flops 32768 | bytes 131072 | tf_op jit(solution)/shard_map/concatenate | solution.py:43
  8.4 2.1 %collective-permute-start.2 = (f32[8,2048]{1,0:T(8,128)S(1)}, f32[8,2048]{1,0:T(8,128)S(1)}, u32[]{:S(2)}, u32[]{:S(2)}) collective-permute-start(f32[8,2048]{1,0:T(8,128)S(1)} %pad_maximum_fusion), channel_id=1, source_target_pairs={{0,2},{1,3},{2,0},{3,1},{4,6},{5,7},{6,4},{7,5},{8,10},{9,11},{10,... | collective-permute-start | bytes 196616 | tf_op jit(solution)/shard_map/ppermute | solution.py:26
  10.4 2.2 %collective-permute-done.2 = f32[8,2048]{1,0:T(8,128)S(1)} collective-permute-done((f32[8,2048]{1,0:T(8,128)S(1)}, f32[8,2048]{1,0:T(8,128)S(1)}, u32[]{:S(2)}, u32[]{:S(2)}) %collective-permute-start.2) | collective-permute-done | bytes 65568 | tf_op jit(solution)/shard_map/ppermute | solution.py:26
  12.7 4.0 %collective-permute-start.3 = (f32[8,4096]{1,0:T(8,128)S(1)}, f32[8,4096]{1,0:T(8,128)S(1)}, u32[]{:S(2)}, u32[]{:S(2)}) collective-permute-start(f32[8,4096]{1,0:T(8,128)S(1)} %constant_dynamic-update-slice_fusion), channel_id=1, source_target_pairs={{0,8},{4,12},{8,16},{12,20},{16,24},{20,28},{1,9},{5,13},{9,17},{1... | collective-permute-start | bytes 393224 | tf_op jit(solution)/shard_map/ppermute | solution.py:17
  16.7 1.3 %collective-permute-start.4 = (f32[8,4096]{1,0:T(8,128)S(1)}, f32[8,4096]{1,0:T(8,128)S(1)}, u32[]{:S(2)}, u32[]{:S(2)}) collective-permute-start(f32[8,4096]{1,0:T(8,128)S(1)} %constant_dynamic-update-slice_fusion), channel_id=1, source_target_pairs={{8,0},{12,4},{16,8},{20,12},{24,16},{28,20},{9,1},{13,5},{17,9},{2... | collective-permute-start | bytes 393224 | tf_op jit(solution)/shard_map/ppermute | solution.py:17
  18.0 0.7 %fusion.18 = s32[5,3,1]{0,2,1:T(1,128)S(1)} fusion(s32[1,5,3]{1,0,2:T(1,128)} %param.8, s32[5]{0:T(128)S(1)} %fusion.22, s32[]{:T(128)S(6)} %axis_index.22), kind=kLoop, calls=%fused_computation.55 | loop fusion | flops 420 | bytes 144 | tf_op jit(solution)/shard_map/concatenate | solution.py:136
  18.7 0.1 copy.21
  18.8 0.1 reshape.245
  18.9 0.7 %fusion.10 = s32[5,3]{0,1:T(4,128)S(1)} fusion(s32[1,5,3]{1,0,2:T(1,128)} %param.7, s32[]{:T(128)S(6)} %axis_index.22), kind=kLoop, calls=%fused_computation.43 | loop fusion | flops 330 | bytes 124 | tf_op jit(solution)/shard_map/add | solution.py:109
  19.6 0.9 %fusion.29 = f32[8,8]{1,0:T(8,128)S(1)} fusion(f32[8,512]{1,0:T(8,128)} %param.5), kind=kOutput, calls=%fused_computation.67 | convolution fusion | flops 393216 | bytes 16640 | tf_op jit(solution)/shard_map/dot_general | solution.py:145
  20.5 0.7 %fusion.12 = f32[5,3]{0,1:T(4,128)S(1)} fusion(s32[5]{0:T(128)} %bitcast.79), kind=kLoop, calls=%fused_computation.48 | loop fusion | flops 30 | bytes 80 | tf_op jit(solution)/shard_map/convert_element_type | solution.py:118
  21.2 0.0 collective-permute-done.3
  21.2 2.3 %collective-permute-done.4 = f32[8,4096]{1,0:T(8,128)S(1)} collective-permute-done((f32[8,4096]{1,0:T(8,128)S(1)}, f32[8,4096]{1,0:T(8,128)S(1)}, u32[]{:S(2)}, u32[]{:S(2)}) %collective-permute-start.4) | collective-permute-done | bytes 131104 | tf_op jit(solution)/shard_map/ppermute | solution.py:17
  23.6 0.6 %gather_fusion = f32[15,8,256]{2,1,0:T(8,128)S(1)} fusion(f32[6,8,8,256]{3,2,1,0:T(8,128)S(1)} %bitcast.78, s32[15]{0:T(128)S(1)} %reshape.245), kind=kCustom, calls=%fused_computation | custom fusion | bytes 245880 | tf_op jit(solution)/shard_map/gather | solution.py:136
  24.2 3.2 %fusion = f32[5,3,8,256]{3,2,1,0:T(8,128)S(1)} fusion(f32[5,3,8,256]{3,2,1,0:T(8,128)S(1)} %bitcast.69, f32[1,5,3,256,256]{4,3,2,1,0:T(8,128)} %param.6), kind=kOutput, calls=%fused_computation.1 | convolution fusion | flops 47185920 | bytes 4177920 | tf_op jit(solution)/shard_map/osit,ostu->osiu/dot_general | solution.py:137
  27.4 0.6 %convolution_bitcast_fusion = f32[1,8,8,256]{3,2,1,0:T(8,128)S(1)} fusion(f32[5,3,8,256]{3,2,1,0:T(8,128)S(1)} %fusion, f32[5,3]{0,1:T(4,128)S(1)} %fusion.12, s32[5,3]{0,1:T(4,128)S(1)} %fusion.10), kind=kOutput, calls=%fused_computation.3 | convolution fusion | flops 2949360 | bytes 188536 | tf_op jit(solution)/shard_map/osiu,osr->iru/dot_general | solution.py:140
  28.1 0.2 fusion.28
  28.3 0.1 concatenate.29
  28.4 1.5 %collective-permute-start.5 = (f32[8,1152]{1,0:T(8,128)S(1)}, f32[8,1152]{1,0:T(8,128)S(1)}, u32[]{:S(2)}, u32[]{:S(2)}) collective-permute-start(f32[8,1152]{1,0:T(8,128)S(1)} %concatenate.29), channel_id=1, source_target_pairs={{0,2},{1,3},{2,0},{3,1},{4,6},{5,7},{6,4},{7,5},{8,10},{9,11},{10,... | collective-permute-start | bytes 110600 | tf_op jit(solution)/shard_map/ppermute | solution.py:26
  30.0 2.4 %collective-permute-done.5 = f32[8,1152]{1,0:T(8,128)S(1)} collective-permute-done((f32[8,1152]{1,0:T(8,128)S(1)}, f32[8,1152]{1,0:T(8,128)S(1)}, u32[]{:S(2)}, u32[]{:S(2)}) %collective-permute-start.5) | collective-permute-done | bytes 36896 | tf_op jit(solution)/shard_map/ppermute | solution.py:26
  32.4 0.1 slice_add_fusion.3
  32.5 1.5 %collective-permute-start.6 = (f32[8,640]{1,0:T(8,128)S(1)}, f32[8,640]{1,0:T(8,128)S(1)}, u32[]{:S(2)}, u32[]{:S(2)}) collective-permute-start(f32[8,640]{1,0:T(8,128)S(1)} %pad_maximum_fusion.2), channel_id=1, source_target_pairs={{0,1},{1,0},{2,3},{3,2},{4,5},{5,4},{6,7},{7,6},{8,9},{9,8},{10,11... | collective-permute-start | bytes 61448 | tf_op jit(solution)/shard_map/ppermute | solution.py:26
  34.0 2.3 %collective-permute-done.6 = f32[8,640]{1,0:T(8,128)S(1)} collective-permute-done((f32[8,640]{1,0:T(8,128)S(1)}, f32[8,640]{1,0:T(8,128)S(1)}, u32[]{:S(2)}, u32[]{:S(2)}) %collective-permute-start.6) | collective-permute-done | bytes 20512 | tf_op jit(solution)/shard_map/ppermute | solution.py:26
  36.3 0.0 collective-permute-start.7
  36.3 1.2 %collective-permute-done.7 = f32[8,128]{1,0:T(8,128)S(1)} collective-permute-done((f32[8,128]{1,0:T(8,128)S(1)}, f32[8,128]{1,0:T(8,128)S(1)}, u32[]{:S(2)}, u32[]{:S(2)}) %collective-permute-start.7) | collective-permute-done | bytes 4128 | tf_op jit(solution)/shard_map/ppermute | solution.py:26
  37.5 1.6 %collective-permute-start.8 = (f32[8,128]{1,0:T(8,128)S(1)}, f32[8,128]{1,0:T(8,128)S(1)}, u32[]{:S(2)}, u32[]{:S(2)}) collective-permute-start(f32[8,128]{1,0:T(8,128)S(1)} %add.124), channel_id=1, source_target_pairs={{0,8},{4,12},{8,0},{12,4},{16,24},{20,28},{24,16},{28,20},{1,9},{5... | collective-permute-start | bytes 12296 | tf_op jit(solution)/shard_map/ppermute | solution.py:26
  39.0 2.0 %collective-permute-done.8 = f32[8,128]{1,0:T(8,128)S(1)} collective-permute-done((f32[8,128]{1,0:T(8,128)S(1)}, f32[8,128]{1,0:T(8,128)S(1)}, u32[]{:S(2)}, u32[]{:S(2)}) %collective-permute-start.8) | collective-permute-done | bytes 4128 | tf_op jit(solution)/shard_map/ppermute | solution.py:26
  41.1 2.6 %collective-permute-start.9 = (f32[8,128]{1,0:T(8,128)S(1)}, f32[8,128]{1,0:T(8,128)S(1)}, u32[]{:S(2)}, u32[]{:S(2)}) collective-permute-start(f32[8,128]{1,0:T(8,128)S(1)} %add.125), channel_id=1, source_target_pairs={{0,16},{4,20},{8,24},{12,28},{16,0},{20,4},{24,8},{28,12},{1,17},{... | collective-permute-start | bytes 12296 | tf_op jit(solution)/shard_map/ppermute | solution.py:26
  43.7 0.6 %slice_add_fusion.1 = f32[8,512]{1,0:T(8,128)} fusion(f32[8,640]{1,0:T(8,128)S(1)} %collective-permute-done.6, f32[8,1024]{1,0:T(8,128)S(1)} %slice_add_fusion), kind=kLoop, calls=%fused_computation.19 | loop fusion | flops 4096 | bytes 49152 | tf_op jit(solution)/shard_map/add | solution.py:60
  44.3 1.3 %collective-permute-done.9 = f32[8,128]{1,0:T(8,128)S(1)} collective-permute-done((f32[8,128]{1,0:T(8,128)S(1)}, f32[8,128]{1,0:T(8,128)S(1)}, u32[]{:S(2)}, u32[]{:S(2)}) %collective-permute-start.9) | collective-permute-done | bytes 4128 | tf_op jit(solution)/shard_map/ppermute | solution.py:26
  45.6 0.7 %fusion.27 = (f32[8,8]{1,0:T(8,128)}, f32[8,8]{1,0:T(8,128)}) fusion(f32[8,128]{1,0:T(8,128)S(1)} %add_multiply_fusion), kind=kLoop, calls=%fused_computation.65 | loop fusion | bytes 1024 | tf_op jit(solution)/shard_map/slice | solution.py:157
  (23 shorter events, 0.2 us)
Async XLA Ops:
  0.6 1.6 %collective-permute-start = (f32[8,512]{1,0:T(8,128)}, f32[8,512]{1,0:T(8,128)S(1)}, u32[]{:S(2)}, u32[]{:S(2)}) collective-permute-start(f32[8,512]{1,0:T(8,128)} %param.5), channel_id=1, source_target_pairs={{0,4},{4,0},{8,12},{12,8},{16,20},{20,16},{24,28},{28,24},{1,5},{5... | collective-permute-start | bytes 49160 | tf_op jit(solution)/shard_map/ppermute | solution.py:26
  2.9 4.7 %collective-permute-start.1 = (f32[8,1024]{1,0:T(8,128)S(1)}, f32[8,1024]{1,0:T(8,128)S(1)}, u32[]{:S(2)}, u32[]{:S(2)}) collective-permute-start(f32[8,1024]{1,0:T(8,128)S(1)} %pad_maximum_fusion.1), channel_id=1, source_target_pairs={{0,1},{1,0},{2,3},{3,2},{4,5},{5,4},{6,7},{7,6},{8,9},{9,8},{10,11... | collective-permute-start | bytes 98312 | tf_op jit(solution)/shard_map/ppermute | solution.py:26
  8.4 4.3 %collective-permute-start.2 = (f32[8,2048]{1,0:T(8,128)S(1)}, f32[8,2048]{1,0:T(8,128)S(1)}, u32[]{:S(2)}, u32[]{:S(2)}) collective-permute-start(f32[8,2048]{1,0:T(8,128)S(1)} %pad_maximum_fusion), channel_id=1, source_target_pairs={{0,2},{1,3},{2,0},{3,1},{4,6},{5,7},{6,4},{7,5},{8,10},{9,11},{10,... | collective-permute-start | bytes 196616 | tf_op jit(solution)/shard_map/ppermute | solution.py:26
  12.7 8.5 %collective-permute-start.3 = (f32[8,4096]{1,0:T(8,128)S(1)}, f32[8,4096]{1,0:T(8,128)S(1)}, u32[]{:S(2)}, u32[]{:S(2)}) collective-permute-start(f32[8,4096]{1,0:T(8,128)S(1)} %constant_dynamic-update-slice_fusion), channel_id=1, source_target_pairs={{0,8},{4,12},{8,16},{12,20},{16,24},{20,28},{1,9},{5,13},{9,17},{1... | collective-permute-start | bytes 393224 | tf_op jit(solution)/shard_map/ppermute | solution.py:17
  16.7 6.9 %collective-permute-start.4 = (f32[8,4096]{1,0:T(8,128)S(1)}, f32[8,4096]{1,0:T(8,128)S(1)}, u32[]{:S(2)}, u32[]{:S(2)}) collective-permute-start(f32[8,4096]{1,0:T(8,128)S(1)} %constant_dynamic-update-slice_fusion), channel_id=1, source_target_pairs={{8,0},{12,4},{16,8},{20,12},{24,16},{28,20},{9,1},{13,5},{17,9},{2... | collective-permute-start | bytes 393224 | tf_op jit(solution)/shard_map/ppermute | solution.py:17
  28.4 4.0 %collective-permute-start.5 = (f32[8,1152]{1,0:T(8,128)S(1)}, f32[8,1152]{1,0:T(8,128)S(1)}, u32[]{:S(2)}, u32[]{:S(2)}) collective-permute-start(f32[8,1152]{1,0:T(8,128)S(1)} %concatenate.29), channel_id=1, source_target_pairs={{0,2},{1,3},{2,0},{3,1},{4,6},{5,7},{6,4},{7,5},{8,10},{9,11},{10,... | collective-permute-start | bytes 110600 | tf_op jit(solution)/shard_map/ppermute | solution.py:26
  32.5 3.8 %collective-permute-start.6 = (f32[8,640]{1,0:T(8,128)S(1)}, f32[8,640]{1,0:T(8,128)S(1)}, u32[]{:S(2)}, u32[]{:S(2)}) collective-permute-start(f32[8,640]{1,0:T(8,128)S(1)} %pad_maximum_fusion.2), channel_id=1, source_target_pairs={{0,1},{1,0},{2,3},{3,2},{4,5},{5,4},{6,7},{7,6},{8,9},{9,8},{10,11... | collective-permute-start | bytes 61448 | tf_op jit(solution)/shard_map/ppermute | solution.py:26
  36.3 1.2 %collective-permute-start.7 = (f32[8,128]{1,0:T(8,128)S(1)}, f32[8,128]{1,0:T(8,128)S(1)}, u32[]{:S(2)}, u32[]{:S(2)}) collective-permute-start(f32[8,128]{1,0:T(8,128)S(1)} %slice_add_fusion.2), channel_id=1, source_target_pairs={{0,4},{4,0},{8,12},{12,8},{16,20},{20,16},{24,28},{28,24},{1,5},{5... | collective-permute-start | bytes 12296 | tf_op jit(solution)/shard_map/ppermute | solution.py:26
  37.5 3.6 %collective-permute-start.8 = (f32[8,128]{1,0:T(8,128)S(1)}, f32[8,128]{1,0:T(8,128)S(1)}, u32[]{:S(2)}, u32[]{:S(2)}) collective-permute-start(f32[8,128]{1,0:T(8,128)S(1)} %add.124), channel_id=1, source_target_pairs={{0,8},{4,12},{8,0},{12,4},{16,24},{20,28},{24,16},{28,20},{1,9},{5... | collective-permute-start | bytes 12296 | tf_op jit(solution)/shard_map/ppermute | solution.py:26
  41.1 4.5 %collective-permute-start.9 = (f32[8,128]{1,0:T(8,128)S(1)}, f32[8,128]{1,0:T(8,128)S(1)}, u32[]{:S(2)}, u32[]{:S(2)}) collective-permute-start(f32[8,128]{1,0:T(8,128)S(1)} %add.125), channel_id=1, source_target_pairs={{0,16},{4,20},{8,24},{12,28},{16,0},{20,4},{24,8},{28,12},{1,17},{... | collective-permute-start | bytes 12296 | tf_op jit(solution)/shard_map/ppermute | solution.py:26

commit v10 on v5

--- a/solution.py
+++ b/solution.py
@@ -93,39 +93,58 @@
     piece_width = vectors.shape[1]
     group_width = piece_width * lax.axis_size("help")
     group_rows = group_width // TILE
-    full_panel = gather_help(vectors)
-    panels = neighbour_panels(full_panel)
+    paired = groups % 2 == 0 and is_power_of_two(lax.axis_size("help"))
     tiles_per_piece = piece_width // TILE
     order = help_order()
 
     def placed(tile_index):
         return ((tile_index // tiles_per_piece) ^ order) * tiles_per_piece + tile_index % tiles_per_piece
 
-    column_place = placed(tile_col[0])
-    row_place = placed(tile_row[0])
+    core = lax.axis_index("blk") % 2
+    if paired:
+        full_panel = gather_help(vectors)
+        lower = shifted(full_panel, "blk", BAND)
+        upper = shifted(full_panel, "blk", -BAND)
+        trio = [lower, full_panel, upper]
+        partner = exchanged(jnp.concatenate(trio, axis=1), "blk", 1)
+        partner = [partner[:, k * group_width : (k + 1) * group_width] for k in range(3)]
+        tile_row, tile_col, counts, vectors, _ = lax.optimization_barrier(
+            (tile_row, tile_col, counts, vectors, full_panel)
+        )
+    else:
+        full_panel = gather_help(vectors)
+        trio = neighbour_panels(full_panel)
     slot_ids = jnp.arange(SLOTS, dtype=jnp.int32)[None, :]
     row_ids = jnp.arange(group_rows, dtype=jnp.int32)
     live = (slot_ids < counts[0][:, None]).astype(jnp.float32)
+    column_place = placed(tile_col[0])
+    row_place = placed(tile_row[0])
     one_hot = (row_place[:, :, None] == row_ids).astype(jnp.float32) * live[:, :, None]
-    partial_value = None
-    for first, last, step in ((BAND - 1, BAND + 2, 1), (0, NOFF, NOFF - 1)):
-        batch = list(range(first, last, step))
-        stacked = jnp.stack([panels[o] for o in batch]).reshape(len(batch), VEC, group_rows, TILE)
+
+    def batch_product(sources, panel_ids, first, last, step):
+        stacked = jnp.stack(sources).reshape(len(sources), VEC, group_rows, TILE)
         stacked = stacked.transpose(0, 2, 1, 3)
-        pieces = stacked[jnp.arange(len(batch))[:, None], column_place[first:last:step]]
+        pieces = stacked[panel_ids[:, None], column_place[first:last:step]]
         contribution = jnp.einsum(
             "osit,ostu->osiu",
             pieces,
             tile_blocks[0, first:last:step],
             precision=lax.Precision.HIGH,
         )
-        batch_value = jnp.einsum(
+        return jnp.einsum(
             "osiu,osr->iru",
             contribution,
             one_hot[first:last:step],
             precision=lax.Precision.HIGHEST,
         )
-        partial_value = batch_value if partial_value is None else partial_value + batch_value
+
+    if paired:
+        partial_value = batch_product(trio, jnp.arange(3, dtype=jnp.int32), 0, NOFF, BAND)
+        partial_value = partial_value + batch_product(
+            partner, jnp.arange(2, dtype=jnp.int32) + core, 1, NOFF - 1, BAND
+        )
+    else:
+        partial_value = batch_product(trio, jnp.arange(NOFF, dtype=jnp.int32), 0, NOFF, 1)
     flattened = partial_value.reshape(VEC, group_width)
     basis_size = float(groups * group_width)
     correlation_term = jnp.dot(

time: 49.2 us -> 45.4 us (0.923)
  starting transfers between devices: 23.1 us -> 18 us
  local copies, waits for them, and re-layouts: 3.27 us -> 4.18 us
    ppermute x4 -> x2, starting transfers between devices: 9.77 us -> 5.27 us  [shifted(): lax.ppermute(value, axis, [(source, source + steps) for source in range(i...]
    unnamed x3 -> x7, local copies, waits for them, and re-layouts: 0.75 us -> 1.52 us
    ppermute x7 -> x8, starting transfers between devices: 13.3 us -> 12.7 us  [exchanged(): lax.ppermute(value, axis, [(source, source ^ mask) for source in range(co...]
    ppermute x7 -> x8, waiting for transfers between devices: 11.7 us -> 11.8 us  [exchanged(): lax.ppermute(value, axis, [(source, source ^ mask) for source in range(co...]
  transfers between devices with their start and end apart: 11 -> 10, of which waited for: 7 -> 8; matrix products, arithmetic and copies ran while one was open for 14% -> 18% of each run, Pallas kernels for 0% -> 0%
where the time goes in v10:
time: 45.4 us; the launch traced here: 44.7 us
  starting transfers between devices  18 us (40%)
  waiting for transfers between devices  12.7 us (28%)
  matrix products  5.95 us (13%)
  local copies, waits for them, and re-layouts  4.18 us (9%)
  other arithmetic  3.09 us (7%)
  between operations  0.76 us (2%)
    ppermute x8, starting transfers between devices, exchanged(): lax.ppermute(value, axis, [(source, source ^ mask) for source in range(co...  12.7 us
    ppermute x8, waiting for transfers between devices, exchanged(): lax.ppermute(value, axis, [(source, source ^ mask) for source in range(co...  11.8 us
    ppermute x2, starting transfers between devices, shifted(): lax.ppermute(value, axis, [(source, source + steps) for source in range(i...  5.27 us
    dot_general x2, matrix products, batch_product(): jnp.einsum('osit,ostu->osiu', pieces, tile_blocks[0, first:last:step], pr...  4.24 us
    unnamed x7, local copies, waits for them, and re-layouts  1.52 us
    gather x2, local copies, waits for them, and re-layouts, batch_product(): pieces = stacked[panel_ids[:, None], column_place[first:last:step]]  1.17 us
    dot_general x1, matrix products, local(): jnp.dot(vectors, vectors.T, precision=lax.Precision.HIGHEST, preferred_el...  0.92 us
    ppermute x2, waiting for transfers between devices, shifted(): lax.ppermute(value, axis, [(source, source + steps) for source in range(i...  0.92 us
  transfers between devices with their start and end apart: 10, of which 8 were waited for; matrix products, arithmetic and copies ran while one was open for 18% of the time, Pallas kernels for 0%

profile of v10, /device:TPU:0, one launch (start us, length us, event | category | flops | bytes accessed | tf_op | source)
XLA Modules:
  0.0 44.7 jit_solution(8402346604309354357)
XLA Ops:
  0.6 3.0 %collective-permute-start = (f32[8,512]{1,0:T(8,128)}, f32[8,512]{1,0:T(8,128)S(1)}, u32[]{:S(2)}, u32[]{:S(2)}) collective-permute-start(f32[8,512]{1,0:T(8,128)} %param.5), channel_id=1, source_target_pairs={{0,1},{1,0},{2,3},{3,2},{4,5},{5,4},{6,7},{7,6},{8,9},{9,8},{10,11... | collective-permute-start | bytes 49160 | tf_op jit(solution)/shard_map/ppermute | solution.py:26
  3.6 0.8 %constant_dynamic-update-slice_fusion.2 = f32[8,2048]{1,0:T(8,128)S(1)} fusion(f32[8,512]{1,0:T(8,128)} %param.5), kind=kLoop, calls=%fused_computation.21 | loop fusion | bytes 32768
  4.4 1.2 %collective-permute-done = f32[8,512]{1,0:T(8,128)S(1)} collective-permute-done((f32[8,512]{1,0:T(8,128)}, f32[8,512]{1,0:T(8,128)S(1)}, u32[]{:S(2)}, u32[]{:S(2)}) %collective-permute-start) | collective-permute-done | bytes 16416 | tf_op jit(solution)/shard_map/ppermute | solution.py:26
  5.6 0.7 %pad_maximum_fusion = f32[8,1024]{1,0:T(8,128)S(1)} fusion(f32[8,512]{1,0:T(8,128)S(1)} %collective-permute-done, f32[8,512]{1,0:T(8,128)} %param.5), kind=kLoop, calls=%fused_computation.17 | loop fusion | flops 8192 | bytes 65536 | tf_op jit(solution)/shard_map/concatenate | solution.py:43
  6.3 2.0 %collective-permute-start.1 = (f32[8,1024]{1,0:T(8,128)S(1)}, f32[8,1024]{1,0:T(8,128)S(1)}, u32[]{:S(2)}, u32[]{:S(2)}) collective-permute-start(f32[8,1024]{1,0:T(8,128)S(1)} %pad_maximum_fusion), channel_id=1, source_target_pairs={{0,2},{1,3},{2,0},{3,1},{4,6},{5,7},{6,4},{7,5},{8,10},{9,11},{10,... | collective-permute-start | bytes 98312 | tf_op jit(solution)/shard_map/ppermute | solution.py:26
  8.3 1.9 %collective-permute-done.1 = f32[8,1024]{1,0:T(8,128)S(1)} collective-permute-done((f32[8,1024]{1,0:T(8,128)S(1)}, f32[8,1024]{1,0:T(8,128)S(1)}, u32[]{:S(2)}, u32[]{:S(2)}) %collective-permute-start.1) | collective-permute-done | bytes 32800 | tf_op jit(solution)/shard_map/ppermute | solution.py:26
  10.2 4.0 %collective-permute-start.2 = (f32[8,2048]{1,0:T(8,128)S(1)}, f32[8,2048]{1,0:T(8,128)S(1)}, u32[]{:S(2)}, u32[]{:S(2)}) collective-permute-start(f32[8,2048]{1,0:T(8,128)S(1)} %constant_dynamic-update-slice_fusion), channel_id=1, source_target_pairs={{0,8},{4,12},{8,16},{12,20},{16,24},{20,28},{1,9},{5,13},{9,17},{1... | collective-permute-start | bytes 196616 | tf_op jit(solution)/shard_map/ppermute | solution.py:17
  14.2 1.3 %collective-permute-start.3 = (f32[8,2048]{1,0:T(8,128)S(1)}, f32[8,2048]{1,0:T(8,128)S(1)}, u32[]{:S(2)}, u32[]{:S(2)}) collective-permute-start(f32[8,2048]{1,0:T(8,128)S(1)} %constant_dynamic-update-slice_fusion), channel_id=1, source_target_pairs={{8,0},{12,4},{16,8},{20,12},{24,16},{28,20},{9,1},{13,5},{17,9},{2... | collective-permute-start | bytes 196616 | tf_op jit(solution)/shard_map/ppermute | solution.py:17
  15.5 0.7 %fusion.18 = (s32[5,3]{0,1:T(4,128)S(1)}, s32[5,3]{0,1:T(4,128)S(1)}) fusion(s32[1,5,3]{1,0,2:T(1,128)} %param.7, s32[]{:T(128)S(6)} %axis_index.22, s32[1,5,3]{1,0,2:T(1,128)} %param.8), kind=kLoop, calls=%fused_computation.54 | loop fusion | flops 660 | bytes 244 | tf_op jit(solution)/shard_map/add | solution.py:101
  16.2 0.1 slice.64
  16.3 0.1 slice.58
  16.4 0.1 copy.13
  16.5 0.7 %fusion.15 = f32[5,3]{1,0:T(8,128)S(1)} fusion(s32[5]{0:T(128)} %bitcast.96), kind=kLoop, calls=%fused_computation.40 | loop fusion | flops 30 | bytes 80 | tf_op jit(solution)/shard_map/convert_element_type | solution.py:119
  17.3 0.1 copy.11
  17.4 0.1 copy.12
  17.5 0.9 %fusion.37 = f32[8,8]{1,0:T(8,128)S(1)} fusion(f32[8,512]{1,0:T(8,128)} %param.5), kind=kOutput, calls=%fused_computation.79 | convolution fusion | flops 393216 | bytes 16640 | tf_op jit(solution)/shard_map/dot_general | solution.py:150
  18.4 0.1 fusion.10
  18.5 0.1 bitcast_or_fusion.1
  18.5 0.1 reshape.121
  18.6 0.1 reshape.115
  18.7 0.0 collective-permute-done.2
  18.7 0.7 %constant_dynamic-update-slice_fusion.6 = f32[8,6144]{1,0:T(8,128)S(1)} fusion(f32[8,6144]{1,0:T(8,128)S(1)} %constant_dynamic-update-slice_fusion.7, f32[8,512]{1,0:T(8,128)} %param.5), kind=kLoop, calls=%fused_computation.25 | loop fusion | bytes 32768
  19.5 0.9 %collective-permute-done.3 = f32[8,2048]{1,0:T(8,128)S(1)} collective-permute-done((f32[8,2048]{1,0:T(8,128)S(1)}, f32[8,2048]{1,0:T(8,128)S(1)}, u32[]{:S(2)}, u32[]{:S(2)}) %collective-permute-start.3) | collective-permute-done | bytes 65568 | tf_op jit(solution)/shard_map/ppermute | solution.py:17
  20.4 0.0 collective-permute-start.4
  20.4 0.6 %gather_fusion = f32[9,8,256]{2,1,0:T(8,128)S(1)} fusion(f32[3,8,8,256]{3,2,1,0:T(8,128)S(1)} %maximum_bitcast_fusion, s32[9]{0:T(128)S(1)} %reshape.115), kind=kCustom, calls=%fused_computation | custom fusion | bytes 147528 | tf_op jit(solution)/shard_map/gather | solution.py:127
  21.0 2.3 %fusion = f32[3,3,8,256]{3,2,1,0:T(8,128)S(1)} fusion(f32[3,3,8,256]{3,2,1,0:T(8,128)S(1)} %bitcast.89, f32[1,5,3,256,256]{4,3,2,1,0:T(8,128)} %param.6), kind=kOutput, calls=%fused_computation.2 | convolution fusion | flops 28311552 | bytes 2506752 | tf_op jit(solution)/shard_map/osit,ostu->osiu/dot_general | solution.py:128
  23.4 0.0 collective-permute-done.4
  23.4 0.6 %gather_fusion.1 = f32[6,8,256]{2,1,0:T(8,128)S(1)} fusion(f32[3,8,8,256]{3,2,1,0:T(8,128)S(1)} %maximum_bitcast_fusion.1, s32[6]{0:T(128)S(1)} %reshape.121), kind=kCustom, calls=%fused_computation.1 | custom fusion | bytes 98352 | tf_op jit(solution)/shard_map/gather | solution.py:127
  24.0 1.9 %fusion.3 = f32[2,3,8,256]{3,2,1,0:T(8,128)S(1)} fusion(f32[2,3,8,256]{3,2,1,0:T(8,128)S(1)} %bitcast.95, f32[1,5,3,256,256]{4,3,2,1,0:T(8,128)} %param.6), kind=kOutput, calls=%fused_computation.5 | convolution fusion | flops 18874368 | bytes 1671168 | tf_op jit(solution)/shard_map/osit,ostu->osiu/dot_general | solution.py:128
  25.9 0.3 convolution_bitcast_fusion
  26.2 0.3 fusion.7
  26.5 0.2 fusion.36
  26.7 0.1 concatenate.34
  26.9 1.5 %collective-permute-start.5 = (f32[8,1152]{1,0:T(8,128)S(1)}, f32[8,1152]{1,0:T(8,128)S(1)}, u32[]{:S(2)}, u32[]{:S(2)}) collective-permute-start(f32[8,1152]{1,0:T(8,128)S(1)} %concatenate.34), channel_id=1, source_target_pairs={{0,2},{1,3},{2,0},{3,1},{4,6},{5,7},{6,4},{7,5},{8,10},{9,11},{10,... | collective-permute-start | bytes 110600 | tf_op jit(solution)/shard_map/ppermute | solution.py:26
  28.4 2.4 %collective-permute-done.5 = f32[8,1152]{1,0:T(8,128)S(1)} collective-permute-done((f32[8,1152]{1,0:T(8,128)S(1)}, f32[8,1152]{1,0:T(8,128)S(1)}, u32[]{:S(2)}, u32[]{:S(2)}) %collective-permute-start.5) | collective-permute-done | bytes 36896 | tf_op jit(solution)/shard_map/ppermute | solution.py:26
  30.9 0.1 slice_add_fusion.3
  30.9 1.5 %collective-permute-start.6 = (f32[8,640]{1,0:T(8,128)S(1)}, f32[8,640]{1,0:T(8,128)S(1)}, u32[]{:S(2)}, u32[]{:S(2)}) collective-permute-start(f32[8,640]{1,0:T(8,128)S(1)} %pad_maximum_fusion.1), channel_id=1, source_target_pairs={{0,1},{1,0},{2,3},{3,2},{4,5},{5,4},{6,7},{7,6},{8,9},{9,8},{10,11... | collective-permute-start | bytes 61448 | tf_op jit(solution)/shard_map/ppermute | solution.py:26
  32.4 2.3 %collective-permute-done.6 = f32[8,640]{1,0:T(8,128)S(1)} collective-permute-done((f32[8,640]{1,0:T(8,128)S(1)}, f32[8,640]{1,0:T(8,128)S(1)}, u32[]{:S(2)}, u32[]{:S(2)}) %collective-permute-start.6) | collective-permute-done | bytes 20512 | tf_op jit(solution)/shard_map/ppermute | solution.py:26
  34.7 0.0 collective-permute-start.7
  34.7 1.2 %collective-permute-done.7 = f32[8,128]{1,0:T(8,128)S(1)} collective-permute-done((f32[8,128]{1,0:T(8,128)S(1)}, f32[8,128]{1,0:T(8,128)S(1)}, u32[]{:S(2)}, u32[]{:S(2)}) %collective-permute-start.7) | collective-permute-done | bytes 4128 | tf_op jit(solution)/shard_map/ppermute | solution.py:26
  35.9 1.8 %collective-permute-start.8 = (f32[8,128]{1,0:T(8,128)S(1)}, f32[8,128]{1,0:T(8,128)S(1)}, u32[]{:S(2)}, u32[]{:S(2)}) collective-permute-start(f32[8,128]{1,0:T(8,128)S(1)} %add.102), channel_id=1, source_target_pairs={{0,8},{4,12},{8,0},{12,4},{16,24},{20,28},{24,16},{28,20},{1,9},{5... | collective-permute-start | bytes 12296 | tf_op jit(solution)/shard_map/ppermute | solution.py:26
  37.7 1.8 %collective-permute-done.8 = f32[8,128]{1,0:T(8,128)S(1)} collective-permute-done((f32[8,128]{1,0:T(8,128)S(1)}, f32[8,128]{1,0:T(8,128)S(1)}, u32[]{:S(2)}, u32[]{:S(2)}) %collective-permute-start.8) | collective-permute-done | bytes 4128 | tf_op jit(solution)/shard_map/ppermute | solution.py:26
  39.5 2.8 %collective-permute-start.9 = (f32[8,128]{1,0:T(8,128)S(1)}, f32[8,128]{1,0:T(8,128)S(1)}, u32[]{:S(2)}, u32[]{:S(2)}) collective-permute-start(f32[8,128]{1,0:T(8,128)S(1)} %add.103), channel_id=1, source_target_pairs={{0,16},{4,20},{8,24},{12,28},{16,0},{20,4},{24,8},{28,12},{1,17},{... | collective-permute-start | bytes 12296 | tf_op jit(solution)/shard_map/ppermute | solution.py:26
  42.3 0.6 %slice_add_fusion.1 = f32[8,512]{1,0:T(8,128)} fusion(f32[8,640]{1,0:T(8,128)S(1)} %collective-permute-done.6, f32[8,1024]{1,0:T(8,128)S(1)} %slice_add_fusion), kind=kLoop, calls=%fused_computation.27 | loop fusion | flops 4096 | bytes 49152 | tf_op jit(solution)/shard_map/add | solution.py:60
  43.0 1.1 %collective-permute-done.9 = f32[8,128]{1,0:T(8,128)S(1)} collective-permute-done((f32[8,128]{1,0:T(8,128)S(1)}, f32[8,128]{1,0:T(8,128)S(1)}, u32[]{:S(2)}, u32[]{:S(2)}) %collective-permute-start.9) | collective-permute-done | bytes 4128 | tf_op jit(solution)/shard_map/ppermute | solution.py:26
  44.0 0.7 %fusion.35 = (f32[8,8]{1,0:T(8,128)}, f32[8,8]{1,0:T(8,128)}) fusion(f32[8,128]{1,0:T(8,128)S(1)} %add_multiply_fusion), kind=kLoop, calls=%fused_computation.77 | loop fusion | bytes 1024 | tf_op jit(solution)/shard_map/slice | solution.py:162
  (23 shorter events, 0.2 us)
Async XLA Ops:
  0.6 4.9 %collective-permute-start = (f32[8,512]{1,0:T(8,128)}, f32[8,512]{1,0:T(8,128)S(1)}, u32[]{:S(2)}, u32[]{:S(2)}) collective-permute-start(f32[8,512]{1,0:T(8,128)} %param.5), channel_id=1, source_target_pairs={{0,1},{1,0},{2,3},{3,2},{4,5},{5,4},{6,7},{7,6},{8,9},{9,8},{10,11... | collective-permute-start | bytes 49160 | tf_op jit(solution)/shard_map/ppermute | solution.py:26
  6.3 3.9 %collective-permute-start.1 = (f32[8,1024]{1,0:T(8,128)S(1)}, f32[8,1024]{1,0:T(8,128)S(1)}, u32[]{:S(2)}, u32[]{:S(2)}) collective-permute-start(f32[8,1024]{1,0:T(8,128)S(1)} %pad_maximum_fusion), channel_id=1, source_target_pairs={{0,2},{1,3},{2,0},{3,1},{4,6},{5,7},{6,4},{7,5},{8,10},{9,11},{10,... | collective-permute-start | bytes 98312 | tf_op jit(solution)/shard_map/ppermute | solution.py:26
  10.2 8.5 %collective-permute-start.2 = (f32[8,2048]{1,0:T(8,128)S(1)}, f32[8,2048]{1,0:T(8,128)S(1)}, u32[]{:S(2)}, u32[]{:S(2)}) collective-permute-start(f32[8,2048]{1,0:T(8,128)S(1)} %constant_dynamic-update-slice_fusion), channel_id=1, source_target_pairs={{0,8},{4,12},{8,16},{12,20},{16,24},{20,28},{1,9},{5,13},{9,17},{1... | collective-permute-start | bytes 196616 | tf_op jit(solution)/shard_map/ppermute | solution.py:17
  14.2 6.2 %collective-permute-start.3 = (f32[8,2048]{1,0:T(8,128)S(1)}, f32[8,2048]{1,0:T(8,128)S(1)}, u32[]{:S(2)}, u32[]{:S(2)}) collective-permute-start(f32[8,2048]{1,0:T(8,128)S(1)} %constant_dynamic-update-slice_fusion), channel_id=1, source_target_pairs={{8,0},{12,4},{16,8},{20,12},{24,16},{28,20},{9,1},{13,5},{17,9},{2... | collective-permute-start | bytes 196616 | tf_op jit(solution)/shard_map/ppermute | solution.py:17
  20.4 3.0 %collective-permute-start.4 = (f32[8,6144]{1,0:T(8,128)S(1)}, f32[8,6144]{1,0:T(8,128)S(1)}, u32[]{:S(2)}, u32[]{:S(2)}) collective-permute-start(f32[8,6144]{1,0:T(8,128)S(1)} %constant_dynamic-update-slice_fusion.3), channel_id=1, source_target_pairs={{0,4},{4,0},{8,12},{12,8},{16,20},{20,16},{24,28},{28,24},{1,5},{5... | collective-permute-start | bytes 589832 | tf_op jit(solution)/shard_map/ppermute | solution.py:26
  26.9 4.0 %collective-permute-start.5 = (f32[8,1152]{1,0:T(8,128)S(1)}, f32[8,1152]{1,0:T(8,128)S(1)}, u32[]{:S(2)}, u32[]{:S(2)}) collective-permute-start(f32[8,1152]{1,0:T(8,128)S(1)} %concatenate.34), channel_id=1, source_target_pairs={{0,2},{1,3},{2,0},{3,1},{4,6},{5,7},{6,4},{7,5},{8,10},{9,11},{10,... | collective-permute-start | bytes 110600 | tf_op jit(solution)/shard_map/ppermute | solution.py:26
  30.9 3.8 %collective-permute-start.6 = (f32[8,640]{1,0:T(8,128)S(1)}, f32[8,640]{1,0:T(8,128)S(1)}, u32[]{:S(2)}, u32[]{:S(2)}) collective-permute-start(f32[8,640]{1,0:T(8,128)S(1)} %pad_maximum_fusion.1), channel_id=1, source_target_pairs={{0,1},{1,0},{2,3},{3,2},{4,5},{5,4},{6,7},{7,6},{8,9},{9,8},{10,11... | collective-permute-start | bytes 61448 | tf_op jit(solution)/shard_map/ppermute | solution.py:26
  34.7 1.2 %collective-permute-start.7 = (f32[8,128]{1,0:T(8,128)S(1)}, f32[8,128]{1,0:T(8,128)S(1)}, u32[]{:S(2)}, u32[]{:S(2)}) collective-permute-start(f32[8,128]{1,0:T(8,128)S(1)} %slice_add_fusion.2), channel_id=1, source_target_pairs={{0,4},{4,0},{8,12},{12,8},{16,20},{20,16},{24,28},{28,24},{1,5},{5... | collective-permute-start | bytes 12296 | tf_op jit(solution)/shard_map/ppermute | solution.py:26
  35.9 3.6 %collective-permute-start.8 = (f32[8,128]{1,0:T(8,128)S(1)}, f32[8,128]{1,0:T(8,128)S(1)}, u32[]{:S(2)}, u32[]{:S(2)}) collective-permute-start(f32[8,128]{1,0:T(8,128)S(1)} %add.102), channel_id=1, source_target_pairs={{0,8},{4,12},{8,0},{12,4},{16,24},{20,28},{24,16},{28,20},{1,9},{5... | collective-permute-start | bytes 12296 | tf_op jit(solution)/shard_map/ppermute | solution.py:26
  39.5 4.5 %collective-permute-start.9 = (f32[8,128]{1,0:T(8,128)S(1)}, f32[8,128]{1,0:T(8,128)S(1)}, u32[]{:S(2)}, u32[]{:S(2)}) collective-permute-start(f32[8,128]{1,0:T(8,128)S(1)} %add.103), channel_id=1, source_target_pairs={{0,16},{4,20},{8,24},{12,28},{16,0},{20,4},{24,8},{28,12},{1,17},{... | collective-permute-start | bytes 12296 | tf_op jit(solution)/shard_map/ppermute | solution.py:26

commit v11 on v10

--- a/solution.py
+++ b/solution.py
@@ -139,7 +139,10 @@
         )
 
     if paired:
-        partial_value = batch_product(trio, jnp.arange(3, dtype=jnp.int32), 0, NOFF, BAND)
+        partial_value = batch_product(trio[1:2], jnp.arange(1, dtype=jnp.int32), BAND, BAND + 1, 1)
+        partial_value = partial_value + batch_product(
+            [trio[0], trio[2]], jnp.arange(2, dtype=jnp.int32), 0, NOFF, NOFF - 1
+        )
         partial_value = partial_value + batch_product(
             partner, jnp.arange(2, dtype=jnp.int32) + core, 1, NOFF - 1, BAND
         )

time: 45.4 us -> 47.2 us (1.040)
  matrix products: 5.95 us -> 7.17 us
  waiting for transfers between devices: 12.7 us -> 11.5 us
  starting transfers between devices: 18 us -> 19.1 us
  local copies, waits for them, and re-layouts: 4.18 us -> 4.73 us
    ppermute x8, starting transfers between devices: 12.7 us -> 13.8 us  [exchanged(): lax.ppermute(value, axis, [(source, source ^ mask) for source in range(co...]
    dot_general x2 -> x3, matrix products: 4.24 us -> 5.25 us  [batch_product(): jnp.einsum('osit,ostu->osiu', pieces, tile_blocks[0, first:last:step], pr...]
    ppermute x2, waiting for transfers between devices: 0.92 us -> 0.01 us  [shifted(): lax.ppermute(value, axis, [(source, source + steps) for source in range(i...]
    gather x2 -> x3, local copies, waits for them, and re-layouts: 1.17 us -> 1.74 us  [batch_product(): pieces = stacked[panel_ids[:, None], column_place[first:last:step]]]
  transfers between devices with their start and end apart: 10 -> 10, of which waited for: 8 -> 7; matrix products, arithmetic and copies ran while one was open for 18% -> 22% of each run, Pallas kernels for 0% -> 0%
where the time goes in v11:
time: 47.2 us; the launch traced here: 46.6 us
  starting transfers between devices  19.1 us (40%)
  waiting for transfers between devices  11.5 us (24%)
  matrix products  7.17 us (15%)
  local copies, waits for them, and re-layouts  4.73 us (10%)
  other arithmetic  3.26 us (7%)
  between operations  0.8 us (2%)
    ppermute x8, starting transfers between devices, exchanged(): lax.ppermute(value, axis, [(source, source ^ mask) for source in range(co...  13.8 us
    ppermute x8, waiting for transfers between devices, exchanged(): lax.ppermute(value, axis, [(source, source ^ mask) for source in range(co...  11.5 us
    ppermute x2, starting transfers between devices, shifted(): lax.ppermute(value, axis, [(source, source + steps) for source in range(i...  5.27 us
    dot_general x3, matrix products, batch_product(): jnp.einsum('osit,ostu->osiu', pieces, tile_blocks[0, first:last:step], pr...  5.25 us
    gather x3, local copies, waits for them, and re-layouts, batch_product(): pieces = stacked[panel_ids[:, None], column_place[first:last:step]]  1.74 us
    unnamed x7, local copies, waits for them, and re-layouts  1.51 us
  transfers between devices with their start and end apart: 10, of which 7 were waited for; matrix products, arithmetic and copies ran while one was open for 22% of the time, Pallas kernels for 0%

profile of v11, /device:TPU:0, one launch (start us, length us, event | category | flops | bytes accessed | tf_op | source)
XLA Modules:
  0.0 46.6 jit_solution(17608835224403463505)
XLA Ops:
  0.6 3.0 %collective-permute-start = (f32[8,512]{1,0:T(8,128)}, f32[8,512]{1,0:T(8,128)S(1)}, u32[]{:S(2)}, u32[]{:S(2)}) collective-permute-start(f32[8,512]{1,0:T(8,128)} %param.5), channel_id=1, source_target_pairs={{0,1},{1,0},{2,3},{3,2},{4,5},{5,4},{6,7},{7,6},{8,9},{9,8},{10,11... | collective-permute-start | bytes 49160 | tf_op jit(solution)/shard_map/ppermute | solution.py:26
  3.6 0.8 %constant_dynamic-update-slice_fusion.2 = f32[8,2048]{1,0:T(8,128)S(1)} fusion(f32[8,512]{1,0:T(8,128)} %param.5), kind=kLoop, calls=%fused_computation.27 | loop fusion | bytes 32768
  4.4 1.2 %collective-permute-done = f32[8,512]{1,0:T(8,128)S(1)} collective-permute-done((f32[8,512]{1,0:T(8,128)}, f32[8,512]{1,0:T(8,128)S(1)}, u32[]{:S(2)}, u32[]{:S(2)}) %collective-permute-start) | collective-permute-done | bytes 16416 | tf_op jit(solution)/shard_map/ppermute | solution.py:26
  5.6 0.7 %pad_maximum_fusion = f32[8,1024]{1,0:T(8,128)S(1)} fusion(f32[8,512]{1,0:T(8,128)S(1)} %collective-permute-done, f32[8,512]{1,0:T(8,128)} %param.5), kind=kLoop, calls=%fused_computation.22 | loop fusion | flops 8192 | bytes 65536 | tf_op jit(solution)/shard_map/concatenate | solution.py:43
  6.3 2.0 %collective-permute-start.1 = (f32[8,1024]{1,0:T(8,128)S(1)}, f32[8,1024]{1,0:T(8,128)S(1)}, u32[]{:S(2)}, u32[]{:S(2)}) collective-permute-start(f32[8,1024]{1,0:T(8,128)S(1)} %pad_maximum_fusion), channel_id=1, source_target_pairs={{0,2},{1,3},{2,0},{3,1},{4,6},{5,7},{6,4},{7,5},{8,10},{9,11},{10,... | collective-permute-start | bytes 98312 | tf_op jit(solution)/shard_map/ppermute | solution.py:26
  8.3 1.9 %collective-permute-done.1 = f32[8,1024]{1,0:T(8,128)S(1)} collective-permute-done((f32[8,1024]{1,0:T(8,128)S(1)}, f32[8,1024]{1,0:T(8,128)S(1)}, u32[]{:S(2)}, u32[]{:S(2)}) %collective-permute-start.1) | collective-permute-done | bytes 32800 | tf_op jit(solution)/shard_map/ppermute | solution.py:26
  10.2 4.0 %collective-permute-start.2 = (f32[8,2048]{1,0:T(8,128)S(1)}, f32[8,2048]{1,0:T(8,128)S(1)}, u32[]{:S(2)}, u32[]{:S(2)}) collective-permute-start(f32[8,2048]{1,0:T(8,128)S(1)} %constant_dynamic-update-slice_fusion), channel_id=1, source_target_pairs={{0,8},{4,12},{8,16},{12,20},{16,24},{20,28},{1,9},{5,13},{9,17},{1... | collective-permute-start | bytes 196616 | tf_op jit(solution)/shard_map/ppermute | solution.py:17
  14.2 1.3 %collective-permute-start.3 = (f32[8,2048]{1,0:T(8,128)S(1)}, f32[8,2048]{1,0:T(8,128)S(1)}, u32[]{:S(2)}, u32[]{:S(2)}) collective-permute-start(f32[8,2048]{1,0:T(8,128)S(1)} %constant_dynamic-update-slice_fusion), channel_id=1, source_target_pairs={{8,0},{12,4},{16,8},{20,12},{24,16},{28,20},{9,1},{13,5},{17,9},{2... | collective-permute-start | bytes 196616 | tf_op jit(solution)/shard_map/ppermute | solution.py:17
  15.5 0.7 %fusion.22 = (s32[5,3]{0,1:T(4,128)S(1)}, s32[5,3]{0,1:T(4,128)S(1)}) fusion(s32[1,5,3]{1,0,2:T(1,128)} %param.7, s32[]{:T(128)S(6)} %axis_index.22, s32[1,5,3]{1,0,2:T(1,128)} %param.8), kind=kLoop, calls=%fused_computation.61 | loop fusion | flops 660 | bytes 244 | tf_op jit(solution)/shard_map/add | solution.py:101
  16.2 0.1 slice.76
  16.3 0.1 slice.70
  16.4 0.2 fusion.26
  16.6 0.1 copy.13
  16.7 0.7 %fusion.19 = f32[5,3]{1,0:T(8,128)S(1)} fusion(s32[5]{0:T(128)} %bitcast.107), kind=kLoop, calls=%fused_computation.47 | loop fusion | flops 30 | bytes 80 | tf_op jit(solution)/shard_map/convert_element_type | solution.py:119
  17.4 0.1 copy.11
  17.5 0.1 copy.12
  17.6 0.9 %fusion.42 = f32[8,8]{1,0:T(8,128)S(1)} fusion(f32[8,512]{1,0:T(8,128)} %param.5), kind=kOutput, calls=%fused_computation.90 | convolution fusion | flops 393216 | bytes 16640 | tf_op jit(solution)/shard_map/dot_general | solution.py:153
  18.6 0.1 bitcast_or_fusion
  18.6 0.1 fusion.14
  18.7 0.6 %gather_fusion = f32[3,8,256]{2,1,0:T(8,128)S(1)} fusion(f32[1,8,8,256]{3,2,1,0:T(8,128)S(1)} %bitcast.106, s32[3]{0:T(128)S(1)} %or_bitcast_fusion), kind=kCustom, calls=%fused_computation | custom fusion | bytes 49176 | tf_op jit(solution)/shard_map/gather | solution.py:127
  19.3 1.4 %fusion.8 = f32[3,8,256]{2,1,0:T(8,128)S(1)} fusion(f32[3,8,256]{2,1,0:T(8,128)S(1)} %gather_fusion, f32[1,5,3,256,256]{4,3,2,1,0:T(8,128)} %param.6), kind=kOutput, calls=%fused_computation.14 | convolution fusion | flops 9437184 | bytes 835584 | tf_op jit(solution)/shard_map/osit,ostu->osiu/dot_general | solution.py:128
  20.7 0.1 reshape.143
  20.8 0.1 reshape.137
  20.9 0.0 collective-permute-done.2
  20.9 0.7 %constant_dynamic-update-slice_fusion.6 = f32[8,6144]{1,0:T(8,128)S(1)} fusion(f32[8,6144]{1,0:T(8,128)S(1)} %constant_dynamic-update-slice_fusion.7, f32[8,512]{1,0:T(8,128)} %param.5), kind=kLoop, calls=%fused_computation.31 | loop fusion | bytes 32768
  21.7 0.0 collective-permute-done.3
  21.7 0.1 collective-permute-start.4
  21.8 0.6 %gather_fusion.1 = f32[6,8,256]{2,1,0:T(8,128)S(1)} fusion(f32[2,8,8,256]{3,2,1,0:T(8,128)S(1)} %maximum_bitcast_fusion.1, s32[6]{0:T(128)S(1)} %reshape.137), kind=kCustom, calls=%fused_computation.1 | custom fusion | bytes 98352 | tf_op jit(solution)/shard_map/gather | solution.py:127
  22.4 1.9 %fusion.2 = f32[2,3,8,256]{3,2,1,0:T(8,128)S(1)} fusion(f32[2,3,8,256]{3,2,1,0:T(8,128)S(1)} %bitcast.104, f32[1,5,3,256,256]{4,3,2,1,0:T(8,128)} %param.6), kind=kOutput, calls=%fused_computation.5 | convolution fusion | flops 18874368 | bytes 1671168 | tf_op jit(solution)/shard_map/osit,ostu->osiu/dot_general | solution.py:128
  24.3 0.3 convolution_bitcast_fusion.1
  24.6 0.6 %gather_fusion.2 = f32[6,8,256]{2,1,0:T(8,128)S(1)} fusion(f32[3,8,8,256]{3,2,1,0:T(8,128)S(1)} %maximum_bitcast_fusion, s32[6]{0:T(128)S(1)} %reshape.143), kind=kCustom, calls=%fused_computation.2 | custom fusion | bytes 98352 | tf_op jit(solution)/shard_map/gather | solution.py:127
  25.2 1.9 %fusion = f32[2,3,8,256]{3,2,1,0:T(8,128)S(1)} fusion(f32[2,3,8,256]{3,2,1,0:T(8,128)S(1)} %bitcast.105, f32[1,5,3,256,256]{4,3,2,1,0:T(8,128)} %param.6), kind=kOutput, calls=%fused_computation.3 | convolution fusion | flops 18874368 | bytes 1671168 | tf_op jit(solution)/shard_map/osit,ostu->osiu/dot_general | solution.py:128
  27.1 0.3 convolution_bitcast_fusion
  27.4 0.3 fusion.7
  27.7 0.2 fusion.41
  27.9 0.1 concatenate.38
  28.0 1.5 %collective-permute-start.5 = (f32[8,1152]{1,0:T(8,128)S(1)}, f32[8,1152]{1,0:T(8,128)S(1)}, u32[]{:S(2)}, u32[]{:S(2)}) collective-permute-start(f32[8,1152]{1,0:T(8,128)S(1)} %concatenate.38), channel_id=1, source_target_pairs={{0,2},{1,3},{2,0},{3,1},{4,6},{5,7},{6,4},{7,5},{8,10},{9,11},{10,... | collective-permute-start | bytes 110600 | tf_op jit(solution)/shard_map/ppermute | solution.py:26
  29.6 2.4 %collective-permute-done.5 = f32[8,1152]{1,0:T(8,128)S(1)} collective-permute-done((f32[8,1152]{1,0:T(8,128)S(1)}, f32[8,1152]{1,0:T(8,128)S(1)}, u32[]{:S(2)}, u32[]{:S(2)}) %collective-permute-start.5) | collective-permute-done | bytes 36896 | tf_op jit(solution)/shard_map/ppermute | solution.py:26
  32.0 0.1 slice_add_fusion.3
  32.1 1.5 %collective-permute-start.6 = (f32[8,640]{1,0:T(8,128)S(1)}, f32[8,640]{1,0:T(8,128)S(1)}, u32[]{:S(2)}, u32[]{:S(2)}) collective-permute-start(f32[8,640]{1,0:T(8,128)S(1)} %pad_maximum_fusion.1), channel_id=1, source_target_pairs={{0,1},{1,0},{2,3},{3,2},{4,5},{5,4},{6,7},{7,6},{8,9},{9,8},{10,11... | collective-permute-start | bytes 61448 | tf_op jit(solution)/shard_map/ppermute | solution.py:26
  33.6 2.3 %collective-permute-done.6 = f32[8,640]{1,0:T(8,128)S(1)} collective-permute-done((f32[8,640]{1,0:T(8,128)S(1)}, f32[8,640]{1,0:T(8,128)S(1)}, u32[]{:S(2)}, u32[]{:S(2)}) %collective-permute-start.6) | collective-permute-done | bytes 20512 | tf_op jit(solution)/shard_map/ppermute | solution.py:26
  35.9 1.2 %collective-permute-done.7 = f32[8,128]{1,0:T(8,128)S(1)} collective-permute-done((f32[8,128]{1,0:T(8,128)S(1)}, f32[8,128]{1,0:T(8,128)S(1)}, u32[]{:S(2)}, u32[]{:S(2)}) %collective-permute-start.7) | collective-permute-done | bytes 4128 | tf_op jit(solution)/shard_map/ppermute | solution.py:26
  37.1 2.6 %collective-permute-start.8 = (f32[8,128]{1,0:T(8,128)S(1)}, f32[8,128]{1,0:T(8,128)S(1)}, u32[]{:S(2)}, u32[]{:S(2)}) collective-permute-start(f32[8,128]{1,0:T(8,128)S(1)} %add.113), channel_id=1, source_target_pairs={{0,8},{4,12},{8,0},{12,4},{16,24},{20,28},{24,16},{28,20},{1,9},{5... | collective-permute-start | bytes 12296 | tf_op jit(solution)/shard_map/ppermute | solution.py:26
  39.7 1.6 %collective-permute-done.8 = f32[8,128]{1,0:T(8,128)S(1)} collective-permute-done((f32[8,128]{1,0:T(8,128)S(1)}, f32[8,128]{1,0:T(8,128)S(1)}, u32[]{:S(2)}, u32[]{:S(2)}) %collective-permute-start.8) | collective-permute-done | bytes 4128 | tf_op jit(solution)/shard_map/ppermute | solution.py:26
  41.3 3.0 %collective-permute-start.9 = (f32[8,128]{1,0:T(8,128)S(1)}, f32[8,128]{1,0:T(8,128)S(1)}, u32[]{:S(2)}, u32[]{:S(2)}) collective-permute-start(f32[8,128]{1,0:T(8,128)S(1)} %add.114), channel_id=1, source_target_pairs={{0,16},{4,20},{8,24},{12,28},{16,0},{20,4},{24,8},{28,12},{1,17},{... | collective-permute-start | bytes 12296 | tf_op jit(solution)/shard_map/ppermute | solution.py:26
  44.3 0.6 %slice_add_fusion.1 = f32[8,512]{1,0:T(8,128)} fusion(f32[8,640]{1,0:T(8,128)S(1)} %collective-permute-done.6, f32[8,1024]{1,0:T(8,128)S(1)} %slice_add_fusion), kind=kLoop, calls=%fused_computation.33 | loop fusion | flops 4096 | bytes 49152 | tf_op jit(solution)/shard_map/add | solution.py:60
  44.9 1.0 %collective-permute-done.9 = f32[8,128]{1,0:T(8,128)S(1)} collective-permute-done((f32[8,128]{1,0:T(8,128)S(1)}, f32[8,128]{1,0:T(8,128)S(1)}, u32[]{:S(2)}, u32[]{:S(2)}) %collective-permute-start.9) | collective-permute-done | bytes 4128 | tf_op jit(solution)/shard_map/ppermute | solution.py:26
  45.9 0.7 %fusion.40 = (f32[8,8]{1,0:T(8,128)}, f32[8,8]{1,0:T(8,128)}) fusion(f32[8,128]{1,0:T(8,128)S(1)} %add_multiply_fusion), kind=kLoop, calls=%fused_computation.88 | loop fusion | bytes 1024 | tf_op jit(solution)/shard_map/slice | solution.py:165
  (27 shorter events, 0.2 us)
Async XLA Ops:
  0.6 4.9 %collective-permute-start = (f32[8,512]{1,0:T(8,128)}, f32[8,512]{1,0:T(8,128)S(1)}, u32[]{:S(2)}, u32[]{:S(2)}) collective-permute-start(f32[8,512]{1,0:T(8,128)} %param.5), channel_id=1, source_target_pairs={{0,1},{1,0},{2,3},{3,2},{4,5},{5,4},{6,7},{7,6},{8,9},{9,8},{10,11... | collective-permute-start | bytes 49160 | tf_op jit(solution)/shard_map/ppermute | solution.py:26
  6.3 3.9 %collective-permute-start.1 = (f32[8,1024]{1,0:T(8,128)S(1)}, f32[8,1024]{1,0:T(8,128)S(1)}, u32[]{:S(2)}, u32[]{:S(2)}) collective-permute-start(f32[8,1024]{1,0:T(8,128)S(1)} %pad_maximum_fusion), channel_id=1, source_target_pairs={{0,2},{1,3},{2,0},{3,1},{4,6},{5,7},{6,4},{7,5},{8,10},{9,11},{10,... | collective-permute-start | bytes 98312 | tf_op jit(solution)/shard_map/ppermute | solution.py:26
  10.2 10.7 %collective-permute-start.2 = (f32[8,2048]{1,0:T(8,128)S(1)}, f32[8,2048]{1,0:T(8,128)S(1)}, u32[]{:S(2)}, u32[]{:S(2)}) collective-permute-start(f32[8,2048]{1,0:T(8,128)S(1)} %constant_dynamic-update-slice_fusion), channel_id=1, source_target_pairs={{0,8},{4,12},{8,16},{12,20},{16,24},{20,28},{1,9},{5,13},{9,17},{1... | collective-permute-start | bytes 196616 | tf_op jit(solution)/shard_map/ppermute | solution.py:17
  14.2 7.5 %collective-permute-start.3 = (f32[8,2048]{1,0:T(8,128)S(1)}, f32[8,2048]{1,0:T(8,128)S(1)}, u32[]{:S(2)}, u32[]{:S(2)}) collective-permute-start(f32[8,2048]{1,0:T(8,128)S(1)} %constant_dynamic-update-slice_fusion), channel_id=1, source_target_pairs={{8,0},{12,4},{16,8},{20,12},{24,16},{28,20},{9,1},{13,5},{17,9},{2... | collective-permute-start | bytes 196616 | tf_op jit(solution)/shard_map/ppermute | solution.py:17
  21.7 2.9 %collective-permute-start.4 = (f32[8,6144]{1,0:T(8,128)S(1)}, f32[8,6144]{1,0:T(8,128)S(1)}, u32[]{:S(2)}, u32[]{:S(2)}) collective-permute-start(f32[8,6144]{1,0:T(8,128)S(1)} %constant_dynamic-update-slice_fusion.3), channel_id=1, source_target_pairs={{0,4},{4,0},{8,12},{12,8},{16,20},{20,16},{24,28},{28,24},{1,5},{5... | collective-permute-start | bytes 589832 | tf_op jit(solution)/shard_map/ppermute | solution.py:26
  28.0 4.0 %collective-permute-start.5 = (f32[8,1152]{1,0:T(8,128)S(1)}, f32[8,1152]{1,0:T(8,128)S(1)}, u32[]{:S(2)}, u32[]{:S(2)}) collective-permute-start(f32[8,1152]{1,0:T(8,128)S(1)} %concatenate.38), channel_id=1, source_target_pairs={{0,2},{1,3},{2,0},{3,1},{4,6},{5,7},{6,4},{7,5},{8,10},{9,11},{10,... | collective-permute-start | bytes 110600 | tf_op jit(solution)/shard_map/ppermute | solution.py:26
  32.1 3.8 %collective-permute-start.6 = (f32[8,640]{1,0:T(8,128)S(1)}, f32[8,640]{1,0:T(8,128)S(1)}, u32[]{:S(2)}, u32[]{:S(2)}) collective-permute-start(f32[8,640]{1,0:T(8,128)S(1)} %pad_maximum_fusion.1), channel_id=1, source_target_pairs={{0,1},{1,0},{2,3},{3,2},{4,5},{5,4},{6,7},{7,6},{8,9},{9,8},{10,11... | collective-permute-start | bytes 61448 | tf_op jit(solution)/shard_map/ppermute | solution.py:26
  35.9 1.2 %collective-permute-start.7 = (f32[8,128]{1,0:T(8,128)S(1)}, f32[8,128]{1,0:T(8,128)S(1)}, u32[]{:S(2)}, u32[]{:S(2)}) collective-permute-start(f32[8,128]{1,0:T(8,128)S(1)} %slice_add_fusion.2), channel_id=1, source_target_pairs={{0,4},{4,0},{8,12},{12,8},{16,20},{20,16},{24,28},{28,24},{1,5},{5... | collective-permute-start | bytes 12296 | tf_op jit(solution)/shard_map/ppermute | solution.py:26
  37.1 4.2 %collective-permute-start.8 = (f32[8,128]{1,0:T(8,128)S(1)}, f32[8,128]{1,0:T(8,128)S(1)}, u32[]{:S(2)}, u32[]{:S(2)}) collective-permute-start(f32[8,128]{1,0:T(8,128)S(1)} %add.113), channel_id=1, source_target_pairs={{0,8},{4,12},{8,0},{12,4},{16,24},{20,28},{24,16},{28,20},{1,9},{5... | collective-permute-start | bytes 12296 | tf_op jit(solution)/shard_map/ppermute | solution.py:26
  41.3 4.6 %collective-permute-start.9 = (f32[8,128]{1,0:T(8,128)S(1)}, f32[8,128]{1,0:T(8,128)S(1)}, u32[]{:S(2)}, u32[]{:S(2)}) collective-permute-start(f32[8,128]{1,0:T(8,128)S(1)} %add.114), channel_id=1, source_target_pairs={{0,16},{4,20},{8,24},{12,28},{16,0},{20,4},{24,8},{28,12},{1,17},{... | collective-permute-start | bytes 12296 | tf_op jit(solution)/shard_map/ppermute | solution.py:26

commit v12 on v11

--- a/solution.py
+++ b/solution.py
@@ -139,12 +139,12 @@
         )
 
     if paired:
-        partial_value = batch_product(trio[1:2], jnp.arange(1, dtype=jnp.int32), BAND, BAND + 1, 1)
-        partial_value = partial_value + batch_product(
+        partial_value = batch_product(
             [trio[0], trio[2]], jnp.arange(2, dtype=jnp.int32), 0, NOFF, NOFF - 1
         )
+        middle_ids = jnp.stack([core, jnp.int32(3), core + 1]).astype(jnp.int32)
         partial_value = partial_value + batch_product(
-            partner, jnp.arange(2, dtype=jnp.int32) + core, 1, NOFF - 1, BAND
+            partner + [trio[1]], middle_ids, BAND - 1, BAND + 2, 1
         )
     else:
         partial_value = batch_product(trio, jnp.arange(NOFF, dtype=jnp.int32), 0, NOFF, 1)

time: 47.2 us -> 45.6 us (0.966)
  matrix products: 7.17 us -> 5.96 us
  starting transfers between devices: 19.1 us -> 20 us
  local copies, waits for them, and re-layouts: 4.73 us -> 4.06 us
  waiting for transfers between devices: 11.5 us -> 10.9 us
    dot_general x3 -> x2, matrix products: 5.25 us -> 4.24 us  [batch_product(): jnp.einsum('osit,ostu->osiu', pieces, tile_blocks[0, first:last:step], pr...]
    ppermute x2, starting transfers between devices: 5.27 us -> 5.9 us  [shifted(): lax.ppermute(value, axis, [(source, source + steps) for source in range(i...]
    ppermute x8, waiting for transfers between devices: 11.5 us -> 10.9 us  [exchanged(): lax.ppermute(value, axis, [(source, source ^ mask) for source in range(co...]
    gather x3 -> x2, local copies, waits for them, and re-layouts: 1.74 us -> 1.17 us  [batch_product(): pieces = stacked[panel_ids[:, None], column_place[first:last:step]]]
  transfers between devices with their start and end apart: 10 -> 10, of which waited for: 7 -> 7; matrix products, arithmetic and copies ran while one was open for 22% -> 15% of each run, Pallas kernels for 0% -> 0%
where the time goes in v12:
time: 45.6 us; the launch traced here: 44.9 us
  starting transfers between devices  20 us (44%)
  waiting for transfers between devices  10.9 us (24%)
  matrix products  5.96 us (13%)
  local copies, waits for them, and re-layouts  4.06 us (9%)
  other arithmetic  3.23 us (7%)
  between operations  0.77 us (2%)
    ppermute x8, starting transfers between devices, exchanged(): lax.ppermute(value, axis, [(source, source ^ mask) for source in range(co...  14.1 us
    ppermute x8, waiting for transfers between devices, exchanged(): lax.ppermute(value, axis, [(source, source ^ mask) for source in range(co...  10.9 us
    ppermute x2, starting transfers between devices, shifted(): lax.ppermute(value, axis, [(source, source + steps) for source in range(i...  5.9 us
    dot_general x2, matrix products, batch_product(): jnp.einsum('osit,ostu->osiu', pieces, tile_blocks[0, first:last:step], pr...  4.24 us
    unnamed x7, local copies, waits for them, and re-layouts  1.51 us
    gather x2, local copies, waits for them, and re-layouts, batch_product(): pieces = stacked[panel_ids[:, None], column_place[first:last:step]]  1.17 us
    dot_general x1, matrix products, local(): jnp.dot(vectors, vectors.T, precision=lax.Precision.HIGHEST, preferred_el...  0.92 us
  transfers between devices with their start and end apart: 10, of which 7 were waited for; matrix products, arithmetic and copies ran while one was open for 15% of the time, Pallas kernels for 0%

profile of v12, /device:TPU:0, one launch (start us, length us, event | category | flops | bytes accessed | tf_op | source)
XLA Modules:
  0.0 44.9 jit_solution(3310381697805846700)
XLA Ops:
  0.6 3.0 %collective-permute-start = (f32[8,512]{1,0:T(8,128)}, f32[8,512]{1,0:T(8,128)S(1)}, u32[]{:S(2)}, u32[]{:S(2)}) collective-permute-start(f32[8,512]{1,0:T(8,128)} %param.5), channel_id=1, source_target_pairs={{0,1},{1,0},{2,3},{3,2},{4,5},{5,4},{6,7},{7,6},{8,9},{9,8},{10,11... | collective-permute-start | bytes 49160 | tf_op jit(solution)/shard_map/ppermute | solution.py:26
  3.6 0.8 %constant_dynamic-update-slice_fusion.2 = f32[8,2048]{1,0:T(8,128)S(1)} fusion(f32[8,512]{1,0:T(8,128)} %param.5), kind=kLoop, calls=%fused_computation.21 | loop fusion | bytes 32768
  4.4 0.1 fusion.31
  4.5 1.1 %collective-permute-done = f32[8,512]{1,0:T(8,128)S(1)} collective-permute-done((f32[8,512]{1,0:T(8,128)}, f32[8,512]{1,0:T(8,128)S(1)}, u32[]{:S(2)}, u32[]{:S(2)}) %collective-permute-start) | collective-permute-done | bytes 16416 | tf_op jit(solution)/shard_map/ppermute | solution.py:26
  5.6 0.7 %pad_maximum_fusion = f32[8,1024]{1,0:T(8,128)S(1)} fusion(f32[8,512]{1,0:T(8,128)S(1)} %collective-permute-done, f32[8,512]{1,0:T(8,128)} %param.5), kind=kLoop, calls=%fused_computation.17 | loop fusion | flops 8192 | bytes 65536 | tf_op jit(solution)/shard_map/concatenate | solution.py:43
  6.3 2.0 %collective-permute-start.1 = (f32[8,1024]{1,0:T(8,128)S(1)}, f32[8,1024]{1,0:T(8,128)S(1)}, u32[]{:S(2)}, u32[]{:S(2)}) collective-permute-start(f32[8,1024]{1,0:T(8,128)S(1)} %pad_maximum_fusion), channel_id=1, source_target_pairs={{0,2},{1,3},{2,0},{3,1},{4,6},{5,7},{6,4},{7,5},{8,10},{9,11},{10,... | collective-permute-start | bytes 98312 | tf_op jit(solution)/shard_map/ppermute | solution.py:26
  8.3 1.9 %collective-permute-done.1 = f32[8,1024]{1,0:T(8,128)S(1)} collective-permute-done((f32[8,1024]{1,0:T(8,128)S(1)}, f32[8,1024]{1,0:T(8,128)S(1)}, u32[]{:S(2)}, u32[]{:S(2)}) %collective-permute-start.1) | collective-permute-done | bytes 32800 | tf_op jit(solution)/shard_map/ppermute | solution.py:26
  10.2 0.7 %fusion.16 = (s32[5,3]{0,1:T(4,128)S(1)}, s32[5,3]{0,1:T(4,128)S(1)}) fusion(s32[1,5,3]{1,0,2:T(1,128)} %param.7, s32[]{:T(128)S(6)} %axis_index.22, s32[1,5,3]{1,0,2:T(1,128)} %param.8), kind=kLoop, calls=%fused_computation.53 | loop fusion | flops 660 | bytes 244 | tf_op jit(solution)/shard_map/add | solution.py:101
  10.9 0.1 fusion.23
  11.0 0.1 slice.58
  11.1 1.3 %collective-permute-start.3 = (f32[8,2048]{1,0:T(8,128)S(1)}, f32[8,2048]{1,0:T(8,128)S(1)}, u32[]{:S(2)}, u32[]{:S(2)}) collective-permute-start(f32[8,2048]{1,0:T(8,128)S(1)} %constant_dynamic-update-slice_fusion), channel_id=1, source_target_pairs={{8,0},{12,4},{16,8},{20,12},{24,16},{28,20},{9,1},{13,5},{17,9},{2... | collective-permute-start | bytes 196616 | tf_op jit(solution)/shard_map/ppermute | solution.py:17
  12.4 4.6 %collective-permute-start.2 = (f32[8,2048]{1,0:T(8,128)S(1)}, f32[8,2048]{1,0:T(8,128)S(1)}, u32[]{:S(2)}, u32[]{:S(2)}) collective-permute-start(f32[8,2048]{1,0:T(8,128)S(1)} %constant_dynamic-update-slice_fusion), channel_id=1, source_target_pairs={{0,8},{4,12},{8,16},{12,20},{16,24},{20,28},{1,9},{5,13},{9,17},{1... | collective-permute-start | bytes 196616 | tf_op jit(solution)/shard_map/ppermute | solution.py:17
  17.0 0.1 copy.11
  17.1 0.1 copy.12
  17.2 0.1 copy.13
  17.3 0.9 %fusion.35 = f32[8,8]{1,0:T(8,128)S(1)} fusion(f32[8,512]{1,0:T(8,128)} %param.5), kind=kOutput, calls=%fused_computation.78 | convolution fusion | flops 393216 | bytes 16640 | tf_op jit(solution)/shard_map/dot_general | solution.py:153
  18.2 0.7 %fusion.13 = f32[5,3]{1,0:T(8,128)S(1)} fusion(s32[5]{0:T(128)} %bitcast.98), kind=kLoop, calls=%fused_computation.39 | loop fusion | flops 30 | bytes 80 | tf_op jit(solution)/shard_map/convert_element_type | solution.py:119
  19.0 0.1 bitcast_or_fusion
  19.1 0.1 fusion.10
  19.1 0.1 reshape.167
  19.2 0.1 reshape.173
  19.3 0.0 collective-permute-done.2
  19.3 0.7 %constant_dynamic-update-slice_fusion.6 = f32[8,6144]{1,0:T(8,128)S(1)} fusion(f32[8,6144]{1,0:T(8,128)S(1)} %constant_dynamic-update-slice_fusion.7, f32[8,512]{1,0:T(8,128)} %param.5), kind=kLoop, calls=%fused_computation.25 | loop fusion | bytes 32768
  20.0 0.0 collective-permute-done.3
  20.1 0.1 collective-permute-start.4
  20.2 0.6 %gather_fusion = f32[6,8,256]{2,1,0:T(8,128)S(1)} fusion(f32[2,8,8,256]{3,2,1,0:T(8,128)S(1)} %maximum_bitcast_fusion.1, s32[6]{0:T(128)S(1)} %reshape.167), kind=kCustom, calls=%fused_computation | custom fusion | bytes 98352 | tf_op jit(solution)/shard_map/gather | solution.py:127
  20.8 1.9 %fusion.3 = f32[2,3,8,256]{3,2,1,0:T(8,128)S(1)} fusion(f32[2,3,8,256]{3,2,1,0:T(8,128)S(1)} %bitcast.97, f32[1,5,3,256,256]{4,3,2,1,0:T(8,128)} %param.6), kind=kOutput, calls=%fused_computation.5 | convolution fusion | flops 18874368 | bytes 1671168 | tf_op jit(solution)/shard_map/osit,ostu->osiu/dot_general | solution.py:128
  22.7 0.0 collective-permute-done.4
  22.7 0.6 %gather_fusion.1 = f32[9,8,256]{2,1,0:T(8,128)S(1)} fusion(f32[4,8,8,256]{3,2,1,0:T(8,128)S(1)} %maximum_bitcast_fusion, s32[9]{0:T(128)S(1)} %reshape.173), kind=kCustom, calls=%fused_computation.1 | custom fusion | bytes 147528 | tf_op jit(solution)/shard_map/gather | solution.py:127
  23.3 2.3 %fusion = f32[3,3,8,256]{3,2,1,0:T(8,128)S(1)} fusion(f32[3,3,8,256]{3,2,1,0:T(8,128)S(1)} %bitcast.91, f32[1,5,3,256,256]{4,3,2,1,0:T(8,128)} %param.6), kind=kOutput, calls=%fused_computation.2 | convolution fusion | flops 28311552 | bytes 2506752 | tf_op jit(solution)/shard_map/osit,ostu->osiu/dot_general | solution.py:128
  25.6 0.3 convolution_bitcast_fusion
  26.0 0.3 fusion.7
  26.3 0.2 fusion.34
  26.5 0.1 broadcast_in_dim.14
  26.6 0.1 concatenate.44
  26.6 2.0 %collective-permute-start.5 = (f32[8,1152]{1,0:T(8,128)S(1)}, f32[8,1152]{1,0:T(8,128)S(1)}, u32[]{:S(2)}, u32[]{:S(2)}) collective-permute-start(f32[8,1152]{1,0:T(8,128)S(1)} %concatenate.44), channel_id=1, source_target_pairs={{0,2},{1,3},{2,0},{3,1},{4,6},{5,7},{6,4},{7,5},{8,10},{9,11},{10,... | collective-permute-start | bytes 110600 | tf_op jit(solution)/shard_map/ppermute | solution.py:26
  28.6 2.1 %collective-permute-done.5 = f32[8,1152]{1,0:T(8,128)S(1)} collective-permute-done((f32[8,1152]{1,0:T(8,128)S(1)}, f32[8,1152]{1,0:T(8,128)S(1)}, u32[]{:S(2)}, u32[]{:S(2)}) %collective-permute-start.5) | collective-permute-done | bytes 36896 | tf_op jit(solution)/shard_map/ppermute | solution.py:26
  30.7 0.1 slice_add_fusion.3
  30.8 1.8 %collective-permute-start.6 = (f32[8,640]{1,0:T(8,128)S(1)}, f32[8,640]{1,0:T(8,128)S(1)}, u32[]{:S(2)}, u32[]{:S(2)}) collective-permute-start(f32[8,640]{1,0:T(8,128)S(1)} %pad_maximum_fusion.1), channel_id=1, source_target_pairs={{0,1},{1,0},{2,3},{3,2},{4,5},{5,4},{6,7},{7,6},{8,9},{9,8},{10,11... | collective-permute-start | bytes 61448 | tf_op jit(solution)/shard_map/ppermute | solution.py:26
  32.6 2.0 %collective-permute-done.6 = f32[8,640]{1,0:T(8,128)S(1)} collective-permute-done((f32[8,640]{1,0:T(8,128)S(1)}, f32[8,640]{1,0:T(8,128)S(1)}, u32[]{:S(2)}, u32[]{:S(2)}) %collective-permute-start.6) | collective-permute-done | bytes 20512 | tf_op jit(solution)/shard_map/ppermute | solution.py:26
  34.6 0.0 collective-permute-start.7
  34.6 1.2 %collective-permute-done.7 = f32[8,128]{1,0:T(8,128)S(1)} collective-permute-done((f32[8,128]{1,0:T(8,128)S(1)}, f32[8,128]{1,0:T(8,128)S(1)}, u32[]{:S(2)}, u32[]{:S(2)}) %collective-permute-start.7) | collective-permute-done | bytes 4128 | tf_op jit(solution)/shard_map/ppermute | solution.py:26
  35.8 2.0 %collective-permute-start.8 = (f32[8,128]{1,0:T(8,128)S(1)}, f32[8,128]{1,0:T(8,128)S(1)}, u32[]{:S(2)}, u32[]{:S(2)}) collective-permute-start(f32[8,128]{1,0:T(8,128)S(1)} %add.94), channel_id=1, source_target_pairs={{0,8},{4,12},{8,0},{12,4},{16,24},{20,28},{24,16},{28,20},{1,9},{5... | collective-permute-start | bytes 12296 | tf_op jit(solution)/shard_map/ppermute | solution.py:26
  37.7 1.7 %collective-permute-done.8 = f32[8,128]{1,0:T(8,128)S(1)} collective-permute-done((f32[8,128]{1,0:T(8,128)S(1)}, f32[8,128]{1,0:T(8,128)S(1)}, u32[]{:S(2)}, u32[]{:S(2)}) %collective-permute-start.8) | collective-permute-done | bytes 4128 | tf_op jit(solution)/shard_map/ppermute | solution.py:26
  39.4 3.3 %collective-permute-start.9 = (f32[8,128]{1,0:T(8,128)S(1)}, f32[8,128]{1,0:T(8,128)S(1)}, u32[]{:S(2)}, u32[]{:S(2)}) collective-permute-start(f32[8,128]{1,0:T(8,128)S(1)} %add.95), channel_id=1, source_target_pairs={{0,16},{4,20},{8,24},{12,28},{16,0},{20,4},{24,8},{28,12},{1,17},{... | collective-permute-start | bytes 12296 | tf_op jit(solution)/shard_map/ppermute | solution.py:26
  42.7 0.6 %slice_add_fusion.1 = f32[8,512]{1,0:T(8,128)} fusion(f32[8,640]{1,0:T(8,128)S(1)} %collective-permute-done.6, f32[8,1024]{1,0:T(8,128)S(1)} %slice_add_fusion), kind=kLoop, calls=%fused_computation.27 | loop fusion | flops 4096 | bytes 49152 | tf_op jit(solution)/shard_map/add | solution.py:60
  43.3 1.0 %collective-permute-done.9 = f32[8,128]{1,0:T(8,128)S(1)} collective-permute-done((f32[8,128]{1,0:T(8,128)S(1)}, f32[8,128]{1,0:T(8,128)S(1)}, u32[]{:S(2)}, u32[]{:S(2)}) %collective-permute-start.9) | collective-permute-done | bytes 4128 | tf_op jit(solution)/shard_map/ppermute | solution.py:26
  44.3 0.7 %fusion.33 = (f32[8,8]{1,0:T(8,128)}, f32[8,8]{1,0:T(8,128)}) fusion(f32[8,128]{1,0:T(8,128)S(1)} %add_multiply_fusion), kind=kLoop, calls=%fused_computation.76 | loop fusion | bytes 1024 | tf_op jit(solution)/shard_map/slice | solution.py:165
  (20 shorter events, 0.1 us)
Async XLA Ops:
  0.6 4.9 %collective-permute-start = (f32[8,512]{1,0:T(8,128)}, f32[8,512]{1,0:T(8,128)S(1)}, u32[]{:S(2)}, u32[]{:S(2)}) collective-permute-start(f32[8,512]{1,0:T(8,128)} %param.5), channel_id=1, source_target_pairs={{0,1},{1,0},{2,3},{3,2},{4,5},{5,4},{6,7},{7,6},{8,9},{9,8},{10,11... | collective-permute-start | bytes 49160 | tf_op jit(solution)/shard_map/ppermute | solution.py:26
  6.3 3.9 %collective-permute-start.1 = (f32[8,1024]{1,0:T(8,128)S(1)}, f32[8,1024]{1,0:T(8,128)S(1)}, u32[]{:S(2)}, u32[]{:S(2)}) collective-permute-start(f32[8,1024]{1,0:T(8,128)S(1)} %pad_maximum_fusion), channel_id=1, source_target_pairs={{0,2},{1,3},{2,0},{3,1},{4,6},{5,7},{6,4},{7,5},{8,10},{9,11},{10,... | collective-permute-start | bytes 98312 | tf_op jit(solution)/shard_map/ppermute | solution.py:26
  11.1 8.9 %collective-permute-start.3 = (f32[8,2048]{1,0:T(8,128)S(1)}, f32[8,2048]{1,0:T(8,128)S(1)}, u32[]{:S(2)}, u32[]{:S(2)}) collective-permute-start(f32[8,2048]{1,0:T(8,128)S(1)} %constant_dynamic-update-slice_fusion), channel_id=1, source_target_pairs={{8,0},{12,4},{16,8},{20,12},{24,16},{28,20},{9,1},{13,5},{17,9},{2... | collective-permute-start | bytes 196616 | tf_op jit(solution)/shard_map/ppermute | solution.py:17
  12.4 6.9 %collective-permute-start.2 = (f32[8,2048]{1,0:T(8,128)S(1)}, f32[8,2048]{1,0:T(8,128)S(1)}, u32[]{:S(2)}, u32[]{:S(2)}) collective-permute-start(f32[8,2048]{1,0:T(8,128)S(1)} %constant_dynamic-update-slice_fusion), channel_id=1, source_target_pairs={{0,8},{4,12},{8,16},{12,20},{16,24},{20,28},{1,9},{5,13},{9,17},{1... | collective-permute-start | bytes 196616 | tf_op jit(solution)/shard_map/ppermute | solution.py:17
  20.1 2.6 %collective-permute-start.4 = (f32[8,6144]{1,0:T(8,128)S(1)}, f32[8,6144]{1,0:T(8,128)S(1)}, u32[]{:S(2)}, u32[]{:S(2)}) collective-permute-start(f32[8,6144]{1,0:T(8,128)S(1)} %constant_dynamic-update-slice_fusion.3), channel_id=1, source_target_pairs={{0,4},{4,0},{8,12},{12,8},{16,20},{20,16},{24,28},{28,24},{1,5},{5... | collective-permute-start | bytes 589832 | tf_op jit(solution)/shard_map/ppermute | solution.py:26
  26.6 4.1 %collective-permute-start.5 = (f32[8,1152]{1,0:T(8,128)S(1)}, f32[8,1152]{1,0:T(8,128)S(1)}, u32[]{:S(2)}, u32[]{:S(2)}) collective-permute-start(f32[8,1152]{1,0:T(8,128)S(1)} %concatenate.44), channel_id=1, source_target_pairs={{0,2},{1,3},{2,0},{3,1},{4,6},{5,7},{6,4},{7,5},{8,10},{9,11},{10,... | collective-permute-start | bytes 110600 | tf_op jit(solution)/shard_map/ppermute | solution.py:26
  30.8 3.8 %collective-permute-start.6 = (f32[8,640]{1,0:T(8,128)S(1)}, f32[8,640]{1,0:T(8,128)S(1)}, u32[]{:S(2)}, u32[]{:S(2)}) collective-permute-start(f32[8,640]{1,0:T(8,128)S(1)} %pad_maximum_fusion.1), channel_id=1, source_target_pairs={{0,1},{1,0},{2,3},{3,2},{4,5},{5,4},{6,7},{7,6},{8,9},{9,8},{10,11... | collective-permute-start | bytes 61448 | tf_op jit(solution)/shard_map/ppermute | solution.py:26
  34.6 1.2 %collective-permute-start.7 = (f32[8,128]{1,0:T(8,128)S(1)}, f32[8,128]{1,0:T(8,128)S(1)}, u32[]{:S(2)}, u32[]{:S(2)}) collective-permute-start(f32[8,128]{1,0:T(8,128)S(1)} %slice_add_fusion.2), channel_id=1, source_target_pairs={{0,4},{4,0},{8,12},{12,8},{16,20},{20,16},{24,28},{28,24},{1,5},{5... | collective-permute-start | bytes 12296 | tf_op jit(solution)/shard_map/ppermute | solution.py:26
  35.8 3.6 %collective-permute-start.8 = (f32[8,128]{1,0:T(8,128)S(1)}, f32[8,128]{1,0:T(8,128)S(1)}, u32[]{:S(2)}, u32[]{:S(2)}) collective-permute-start(f32[8,128]{1,0:T(8,128)S(1)} %add.94), channel_id=1, source_target_pairs={{0,8},{4,12},{8,0},{12,4},{16,24},{20,28},{24,16},{28,20},{1,9},{5... | collective-permute-start | bytes 12296 | tf_op jit(solution)/shard_map/ppermute | solution.py:26
  39.4 4.9 %collective-permute-start.9 = (f32[8,128]{1,0:T(8,128)S(1)}, f32[8,128]{1,0:T(8,128)S(1)}, u32[]{:S(2)}, u32[]{:S(2)}) collective-permute-start(f32[8,128]{1,0:T(8,128)S(1)} %add.95), channel_id=1, source_target_pairs={{0,16},{4,20},{8,24},{12,28},{16,0},{20,4},{24,8},{28,12},{1,17},{... | collective-permute-start | bytes 12296 | tf_op jit(solution)/shard_map/ppermute | solution.py:26

commit v13 on v10

--- a/solution.py
+++ b/solution.py
@@ -102,18 +102,23 @@
 
     core = lax.axis_index("blk") % 2
     if paired:
-        full_panel = gather_help(vectors)
-        lower = shifted(full_panel, "blk", BAND)
-        upper = shifted(full_panel, "blk", -BAND)
-        trio = [lower, full_panel, upper]
-        partner = exchanged(jnp.concatenate(trio, axis=1), "blk", 1)
-        partner = [partner[:, k * group_width : (k + 1) * group_width] for k in range(3)]
+        helpers = lax.axis_size("help")
+        own_pair = gather_help(jnp.concatenate([vectors, exchanged(vectors, "blk", 1)], axis=1))
+        crossing = [(b, b + 2) for b in range(0, groups - 2, 2)]
+        crossing += [(b, b - 2) for b in range(3, groups, 2)]
+        remote = lax.ppermute(own_pair, "blk", crossing)
+        partner_remote = exchanged(remote, "blk", 1)
+        sources = []
+        for pair in (own_pair, remote, partner_remote):
+            halves = pair.reshape(VEC, helpers, 2, piece_width)
+            sources += [halves[:, :, side].reshape(VEC, group_width) for side in range(2)]
+        full_panel = sources[0]
         tile_row, tile_col, counts, vectors, _ = lax.optimization_barrier(
-            (tile_row, tile_col, counts, vectors, full_panel)
+            (tile_row, tile_col, counts, vectors, own_pair)
         )
     else:
         full_panel = gather_help(vectors)
-        trio = neighbour_panels(full_panel)
+        sources = neighbour_panels(full_panel)
     slot_ids = jnp.arange(SLOTS, dtype=jnp.int32)[None, :]
     row_ids = jnp.arange(group_rows, dtype=jnp.int32)
     live = (slot_ids < counts[0][:, None]).astype(jnp.float32)
@@ -139,12 +144,14 @@
         )
 
     if paired:
-        partial_value = batch_product(trio, jnp.arange(3, dtype=jnp.int32), 0, NOFF, BAND)
-        partial_value = partial_value + batch_product(
-            partner, jnp.arange(2, dtype=jnp.int32) + core, 1, NOFF - 1, BAND
+        panel_ids = jnp.where(
+            core == 0,
+            jnp.array([2, 3, 0, 1, 5], dtype=jnp.int32),
+            jnp.array([5, 1, 0, 3, 2], dtype=jnp.int32),
         )
     else:
-        partial_value = batch_product(trio, jnp.arange(NOFF, dtype=jnp.int32), 0, NOFF, 1)
+        panel_ids = jnp.arange(NOFF, dtype=jnp.int32)
+    partial_value = batch_product(sources, panel_ids, 0, NOFF, 1)
     flattened = partial_value.reshape(VEC, group_width)
     basis_size = float(groups * group_width)
     correlation_term = jnp.dot(

time: 45.4 us -> 44.7 us (0.985)
  waiting for transfers between devices: 12.7 us -> 14.6 us
  other arithmetic: 3.09 us -> 4.9 us
  local copies, waits for them, and re-layouts: 4.18 us -> 2.45 us
  starting transfers between devices: 18 us -> 16.4 us
  matrix products: 5.95 us -> 4.93 us
    ppermute x8 -> x9, waiting for transfers between devices: 11.8 us -> 14.6 us  [exchanged(): lax.ppermute(value, axis, [(source, source ^ mask) for source in range(co...]
    ppermute x2 -> x1, starting transfers between devices: 5.27 us -> 3.88 us  [local(): remote = lax.ppermute(own_pair, 'blk', crossing)]
    concatenate x5 -> x2, other arithmetic: 0.1 us -> 1.37 us  [batch_product(): pieces = stacked[panel_ids[:, None], column_place[first:last:step]]]
    dot_general x2 -> x1, matrix products: 4.24 us -> 3.18 us  [batch_product(): jnp.einsum('osit,ostu->osiu', pieces, tile_blocks[0, first:last:step], pr...]
    ppermute x2 -> x1, waiting for transfers between devices: 0.92 us -> 0.01 us  [local(): remote = lax.ppermute(own_pair, 'blk', crossing)]
    unnamed x7 -> x9, local copies, waits for them, and re-layouts: 1.52 us -> 0.79 us
    concatenate x0 -> x1, other arithmetic: none -> 0.72 us  [local(): jnp.concatenate([vectors, exchanged(vectors, 'blk', 1)], axis=1)]
    gather x2 -> x1, local copies, waits for them, and re-layouts: 1.17 us -> 0.63 us  [batch_product(): pieces = stacked[panel_ids[:, None], column_place[first:last:step]]]
  transfers between devices with their start and end apart: 10 -> 10, of which waited for: 8 -> 8; matrix products, arithmetic and copies ran while one was open for 18% -> 12% of each run, Pallas kernels for 0% -> 0%
where the time goes in v13:
time: 44.7 us; the launch traced here: 44 us
  starting transfers between devices  16.4 us (37%)
  waiting for transfers between devices  14.6 us (33%)
  matrix products  4.93 us (11%)
  other arithmetic  4.9 us (11%)
  local copies, waits for them, and re-layouts  2.45 us (5%)
  between operations  0.76 us (2%)
    ppermute x9, waiting for transfers between devices, exchanged(): lax.ppermute(value, axis, [(source, source ^ mask) for source in range(co...  14.6 us
    ppermute x9, starting transfers between devices, exchanged(): lax.ppermute(value, axis, [(source, source ^ mask) for source in range(co...  12.5 us
    ppermute x1, starting transfers between devices, local(): remote = lax.ppermute(own_pair, 'blk', crossing)  3.88 us
    dot_general x1, matrix products, batch_product(): jnp.einsum('osit,ostu->osiu', pieces, tile_blocks[0, first:last:step], pr...  3.18 us
    concatenate x2, other arithmetic, batch_product(): pieces = stacked[panel_ids[:, None], column_place[first:last:step]]  1.37 us
    dot_general x1, matrix products, local(): jnp.dot(vectors, vectors.T, precision=lax.Precision.HIGHEST, preferred_el...  0.92 us
  transfers between devices with their start and end apart: 10, of which 8 were waited for; matrix products, arithmetic and copies ran while one was open for 12% of the time, Pallas kernels for 0%

profile of v13, /device:TPU:0, one launch (start us, length us, event | category | flops | bytes accessed | tf_op | source)
XLA Modules:
  0.0 44.0 jit_solution(3889410194932897461)
XLA Ops:
  0.6 0.5 %collective-permute-start = (f32[8,512]{1,0:T(8,128)}, f32[8,512]{1,0:T(8,128)S(1)}, u32[]{:S(2)}, u32[]{:S(2)}) collective-permute-start(f32[8,512]{1,0:T(8,128)} %param.7), channel_id=1, source_target_pairs={{0,4},{4,0},{8,12},{12,8},{16,20},{20,16},{24,28},{28,24},{1,5},{5... | collective-permute-start | bytes 49160 | tf_op jit(solution)/shard_map/ppermute | solution.py:26
  1.1 0.7 %fusion.20 = s32[5]{0:T(128)S(1)} fusion(s32[5]{0:T(128)} %constant.71.clone, s32[5]{0:T(128)} %constant.72.clone, pred[]{:T(512)S(6)} %eq.24), kind=kLoop, calls=%fused_computation.58 | loop fusion | flops 30 | bytes 61 | tf_op jit(solution)/shard_map/concatenate | solution.py:132
  1.8 0.7 %constant_dynamic-update-slice_fusion.3 = f32[8,4096]{1,0:T(8,128)S(1)} fusion(f32[8,512]{1,0:T(8,128)} %param.7), kind=kLoop, calls=%fused_computation.11 | loop fusion | bytes 32768
  2.5 0.0 collective-permute-done
  2.5 0.7 %pad_maximum_fusion.1 = f32[8,1024]{1,0:T(8,128)S(1)} fusion(f32[8,512]{1,0:T(8,128)S(1)} %collective-permute-done, f32[8,512]{1,0:T(8,128)} %param.7), kind=kLoop, calls=%fused_computation.7 | loop fusion | flops 8192 | bytes 65536 | tf_op jit(solution)/shard_map/concatenate | solution.py:106
  3.3 2.5 %collective-permute-start.1 = (f32[8,1024]{1,0:T(8,128)S(1)}, f32[8,1024]{1,0:T(8,128)S(1)}, u32[]{:S(2)}, u32[]{:S(2)}) collective-permute-start(f32[8,1024]{1,0:T(8,128)S(1)} %pad_maximum_fusion.1), channel_id=1, source_target_pairs={{0,1},{1,0},{2,3},{3,2},{4,5},{5,4},{6,7},{7,6},{8,9},{9,8},{10,11... | collective-permute-start | bytes 98312 | tf_op jit(solution)/shard_map/ppermute | solution.py:26
  5.8 2.0 %collective-permute-done.1 = f32[8,1024]{1,0:T(8,128)S(1)} collective-permute-done((f32[8,1024]{1,0:T(8,128)S(1)}, f32[8,1024]{1,0:T(8,128)S(1)}, u32[]{:S(2)}, u32[]{:S(2)}) %collective-permute-start.1) | collective-permute-done | bytes 32800 | tf_op jit(solution)/shard_map/ppermute | solution.py:26
  7.8 0.7 %pad_maximum_fusion = f32[8,2048]{1,0:T(8,128)S(1)} fusion(f32[8,1024]{1,0:T(8,128)S(1)} %collective-permute-done.1, f32[8,512]{1,0:T(8,128)S(1)} %collective-permute-done, f32[8,512]{1,0:T(8,128)} %param.7), kind=kLoop, calls=%fused_computation.5 | loop fusion | flops 32768 | bytes 131072 | tf_op jit(solution)/shard_map/concatenate | solution.py:43
  8.5 1.9 %collective-permute-start.2 = (f32[8,2048]{1,0:T(8,128)S(1)}, f32[8,2048]{1,0:T(8,128)S(1)}, u32[]{:S(2)}, u32[]{:S(2)}) collective-permute-start(f32[8,2048]{1,0:T(8,128)S(1)} %pad_maximum_fusion), channel_id=1, source_target_pairs={{0,2},{1,3},{2,0},{3,1},{4,6},{5,7},{6,4},{7,5},{8,10},{9,11},{10,... | collective-permute-start | bytes 196616 | tf_op jit(solution)/shard_map/ppermute | solution.py:26
  10.4 2.3 %collective-permute-done.2 = f32[8,2048]{1,0:T(8,128)S(1)} collective-permute-done((f32[8,2048]{1,0:T(8,128)S(1)}, f32[8,2048]{1,0:T(8,128)S(1)}, u32[]{:S(2)}, u32[]{:S(2)}) %collective-permute-start.2) | collective-permute-done | bytes 65568 | tf_op jit(solution)/shard_map/ppermute | solution.py:26
  12.8 3.9 %collective-permute-start.3 = (f32[8,4096]{1,0:T(8,128)S(1)}, f32[8,4096]{1,0:T(8,128)S(1)}, u32[]{:S(2)}, u32[]{:S(2)}) collective-permute-start(f32[8,4096]{1,0:T(8,128)S(1)} %constant_dynamic-update-slice_fusion), channel_id=1, source_target_pairs={{0,8},{8,16},{16,24},{12,4},{20,12},{28,20},{1,9},{9,17},{17,25},{... | collective-permute-start | bytes 393224 | tf_op jit(solution)/shard_map/ppermute | solution.py:109
  16.7 0.7 %fusion.12 = f32[5,3]{0,1:T(4,128)S(1)} fusion(s32[5]{0:T(128)} %bitcast.79), kind=kLoop, calls=%fused_computation.48 | loop fusion | flops 30 | bytes 80 | tf_op jit(solution)/shard_map/convert_element_type | solution.py:124
  17.4 0.9 %fusion.27 = f32[8,8]{1,0:T(8,128)S(1)} fusion(f32[8,512]{1,0:T(8,128)} %param.7), kind=kOutput, calls=%fused_computation.65 | convolution fusion | flops 393216 | bytes 16640 | tf_op jit(solution)/shard_map/dot_general | solution.py:157
  18.3 0.7 %fusion.10 = s32[5,3]{0,1:T(4,128)S(1)} fusion(s32[1,5,3]{1,0,2:T(1,128)} %param.9, s32[]{:T(128)S(6)} %axis_index.22), kind=kLoop, calls=%fused_computation.43 | loop fusion | flops 330 | bytes 124 | tf_op jit(solution)/shard_map/add | solution.py:101
  19.0 0.7 %fusion.18 = s32[5,3,1]{0,2,1:T(1,128)S(1)} fusion(s32[1,5,3]{1,0,2:T(1,128)} %param.10, s32[5]{0:T(128)S(1)} %fusion.20, s32[]{:T(128)S(6)} %axis_index.22), kind=kLoop, calls=%fused_computation.54 | loop fusion | flops 420 | bytes 144 | tf_op jit(solution)/shard_map/concatenate | solution.py:132
  19.7 0.1 copy.23
  19.8 0.1 reshape.229
  19.9 0.0 collective-permute-done.3
  19.9 0.1 collective-permute-start.4
  20.0 1.3 %collective-permute-done.4 = f32[8,4096]{1,0:T(8,128)S(1)} collective-permute-done((f32[8,4096]{1,0:T(8,128)S(1)}, f32[8,4096]{1,0:T(8,128)S(1)}, u32[]{:S(2)}, u32[]{:S(2)}) %collective-permute-start.4) | collective-permute-done | bytes 131104 | tf_op jit(solution)/shard_map/ppermute | solution.py:26
  21.4 0.6 %gather_fusion = f32[15,8,256]{2,1,0:T(8,128)S(1)} fusion(f32[6,8,8,256]{3,2,1,0:T(8,128)S(1)} %bitcast.78, s32[15]{0:T(128)S(1)} %reshape.229), kind=kCustom, calls=%fused_computation | custom fusion | bytes 245880 | tf_op jit(solution)/shard_map/gather | solution.py:132
  22.0 3.2 %fusion = f32[5,3,8,256]{3,2,1,0:T(8,128)S(1)} fusion(f32[5,3,8,256]{3,2,1,0:T(8,128)S(1)} %bitcast.69, f32[1,5,3,256,256]{4,3,2,1,0:T(8,128)} %param.8), kind=kOutput, calls=%fused_computation.1 | convolution fusion | flops 47185920 | bytes 4177920 | tf_op jit(solution)/shard_map/osit,ostu->osiu/dot_general | solution.py:133
  25.2 0.6 %convolution_bitcast_fusion = f32[1,8,8,256]{3,2,1,0:T(8,128)S(1)} fusion(f32[5,3,8,256]{3,2,1,0:T(8,128)S(1)} %fusion, f32[5,3]{0,1:T(4,128)S(1)} %fusion.12, s32[5,3]{0,1:T(4,128)S(1)} %fusion.10), kind=kOutput, calls=%fused_computation.3 | convolution fusion | flops 2949360 | bytes 188536 | tf_op jit(solution)/shard_map/osiu,osr->iru/dot_general | solution.py:139
  25.9 0.2 fusion.26
  26.1 0.1 concatenate.29
  26.2 1.5 %collective-permute-start.5 = (f32[8,1152]{1,0:T(8,128)S(1)}, f32[8,1152]{1,0:T(8,128)S(1)}, u32[]{:S(2)}, u32[]{:S(2)}) collective-permute-start(f32[8,1152]{1,0:T(8,128)S(1)} %concatenate.29), channel_id=1, source_target_pairs={{0,2},{1,3},{2,0},{3,1},{4,6},{5,7},{6,4},{7,5},{8,10},{9,11},{10,... | collective-permute-start | bytes 110600 | tf_op jit(solution)/shard_map/ppermute | solution.py:26
  27.7 2.4 %collective-permute-done.5 = f32[8,1152]{1,0:T(8,128)S(1)} collective-permute-done((f32[8,1152]{1,0:T(8,128)S(1)}, f32[8,1152]{1,0:T(8,128)S(1)}, u32[]{:S(2)}, u32[]{:S(2)}) %collective-permute-start.5) | collective-permute-done | bytes 36896 | tf_op jit(solution)/shard_map/ppermute | solution.py:26
  30.2 0.1 slice_add_fusion.3
  30.3 1.5 %collective-permute-start.6 = (f32[8,640]{1,0:T(8,128)S(1)}, f32[8,640]{1,0:T(8,128)S(1)}, u32[]{:S(2)}, u32[]{:S(2)}) collective-permute-start(f32[8,640]{1,0:T(8,128)S(1)} %pad_maximum_fusion.2), channel_id=1, source_target_pairs={{0,1},{1,0},{2,3},{3,2},{4,5},{5,4},{6,7},{7,6},{8,9},{9,8},{10,11... | collective-permute-start | bytes 61448 | tf_op jit(solution)/shard_map/ppermute | solution.py:26
  31.8 2.3 %collective-permute-done.6 = f32[8,640]{1,0:T(8,128)S(1)} collective-permute-done((f32[8,640]{1,0:T(8,128)S(1)}, f32[8,640]{1,0:T(8,128)S(1)}, u32[]{:S(2)}, u32[]{:S(2)}) %collective-permute-start.6) | collective-permute-done | bytes 20512 | tf_op jit(solution)/shard_map/ppermute | solution.py:26
  34.1 0.0 collective-permute-start.7
  34.1 1.2 %collective-permute-done.7 = f32[8,128]{1,0:T(8,128)S(1)} collective-permute-done((f32[8,128]{1,0:T(8,128)S(1)}, f32[8,128]{1,0:T(8,128)S(1)}, u32[]{:S(2)}, u32[]{:S(2)}) %collective-permute-start.7) | collective-permute-done | bytes 4128 | tf_op jit(solution)/shard_map/ppermute | solution.py:26
  35.3 1.7 %collective-permute-start.8 = (f32[8,128]{1,0:T(8,128)S(1)}, f32[8,128]{1,0:T(8,128)S(1)}, u32[]{:S(2)}, u32[]{:S(2)}) collective-permute-start(f32[8,128]{1,0:T(8,128)S(1)} %add.101), channel_id=1, source_target_pairs={{0,8},{4,12},{8,0},{12,4},{16,24},{20,28},{24,16},{28,20},{1,9},{5... | collective-permute-start | bytes 12296 | tf_op jit(solution)/shard_map/ppermute | solution.py:26
  37.0 1.9 %collective-permute-done.8 = f32[8,128]{1,0:T(8,128)S(1)} collective-permute-done((f32[8,128]{1,0:T(8,128)S(1)}, f32[8,128]{1,0:T(8,128)S(1)}, u32[]{:S(2)}, u32[]{:S(2)}) %collective-permute-start.8) | collective-permute-done | bytes 4128 | tf_op jit(solution)/shard_map/ppermute | solution.py:26
  38.9 2.7 %collective-permute-start.9 = (f32[8,128]{1,0:T(8,128)S(1)}, f32[8,128]{1,0:T(8,128)S(1)}, u32[]{:S(2)}, u32[]{:S(2)}) collective-permute-start(f32[8,128]{1,0:T(8,128)S(1)} %add.102), channel_id=1, source_target_pairs={{0,16},{4,20},{8,24},{12,28},{16,0},{20,4},{24,8},{28,12},{1,17},{... | collective-permute-start | bytes 12296 | tf_op jit(solution)/shard_map/ppermute | solution.py:26
  41.6 0.6 %slice_add_fusion.1 = f32[8,512]{1,0:T(8,128)} fusion(f32[8,640]{1,0:T(8,128)S(1)} %collective-permute-done.6, f32[8,1024]{1,0:T(8,128)S(1)} %slice_add_fusion), kind=kLoop, calls=%fused_computation.19 | loop fusion | flops 4096 | bytes 49152 | tf_op jit(solution)/shard_map/add | solution.py:60
  42.2 1.2 %collective-permute-done.9 = f32[8,128]{1,0:T(8,128)S(1)} collective-permute-done((f32[8,128]{1,0:T(8,128)S(1)}, f32[8,128]{1,0:T(8,128)S(1)}, u32[]{:S(2)}, u32[]{:S(2)}) %collective-permute-start.9) | collective-permute-done | bytes 4128 | tf_op jit(solution)/shard_map/ppermute | solution.py:26
  43.4 0.7 %fusion.25 = (f32[8,8]{1,0:T(8,128)}, f32[8,8]{1,0:T(8,128)}) fusion(f32[8,128]{1,0:T(8,128)S(1)} %add_multiply_fusion), kind=kLoop, calls=%fused_computation.63 | loop fusion | bytes 1024 | tf_op jit(solution)/shard_map/slice | solution.py:169
  (22 shorter events, 0.2 us)
Async XLA Ops:
  0.6 1.9 %collective-permute-start = (f32[8,512]{1,0:T(8,128)}, f32[8,512]{1,0:T(8,128)S(1)}, u32[]{:S(2)}, u32[]{:S(2)}) collective-permute-start(f32[8,512]{1,0:T(8,128)} %param.7), channel_id=1, source_target_pairs={{0,4},{4,0},{8,12},{12,8},{16,20},{20,16},{24,28},{28,24},{1,5},{5... | collective-permute-start | bytes 49160 | tf_op jit(solution)/shard_map/ppermute | solution.py:26
  3.3 4.5 %collective-permute-start.1 = (f32[8,1024]{1,0:T(8,128)S(1)}, f32[8,1024]{1,0:T(8,128)S(1)}, u32[]{:S(2)}, u32[]{:S(2)}) collective-permute-start(f32[8,1024]{1,0:T(8,128)S(1)} %pad_maximum_fusion.1), channel_id=1, source_target_pairs={{0,1},{1,0},{2,3},{3,2},{4,5},{5,4},{6,7},{7,6},{8,9},{9,8},{10,11... | collective-permute-start | bytes 98312 | tf_op jit(solution)/shard_map/ppermute | solution.py:26
  8.5 4.3 %collective-permute-start.2 = (f32[8,2048]{1,0:T(8,128)S(1)}, f32[8,2048]{1,0:T(8,128)S(1)}, u32[]{:S(2)}, u32[]{:S(2)}) collective-permute-start(f32[8,2048]{1,0:T(8,128)S(1)} %pad_maximum_fusion), channel_id=1, source_target_pairs={{0,2},{1,3},{2,0},{3,1},{4,6},{5,7},{6,4},{7,5},{8,10},{9,11},{10,... | collective-permute-start | bytes 196616 | tf_op jit(solution)/shard_map/ppermute | solution.py:26
  12.8 7.1 %collective-permute-start.3 = (f32[8,4096]{1,0:T(8,128)S(1)}, f32[8,4096]{1,0:T(8,128)S(1)}, u32[]{:S(2)}, u32[]{:S(2)}) collective-permute-start(f32[8,4096]{1,0:T(8,128)S(1)} %constant_dynamic-update-slice_fusion), channel_id=1, source_target_pairs={{0,8},{8,16},{16,24},{12,4},{20,12},{28,20},{1,9},{9,17},{17,25},{... | collective-permute-start | bytes 393224 | tf_op jit(solution)/shard_map/ppermute | solution.py:109
  19.9 1.4 %collective-permute-start.4 = (f32[8,4096]{1,0:T(8,128)S(1)}, f32[8,4096]{1,0:T(8,128)S(1)}, u32[]{:S(2)}, u32[]{:S(2)}) collective-permute-start(f32[8,4096]{1,0:T(8,128)S(1)} %collective-permute-done.3), channel_id=1, source_target_pairs={{0,4},{4,0},{8,12},{12,8},{16,20},{20,16},{24,28},{28,24},{1,5},{5... | collective-permute-start | bytes 393224 | tf_op jit(solution)/shard_map/ppermute | solution.py:26
  26.2 4.0 %collective-permute-start.5 = (f32[8,1152]{1,0:T(8,128)S(1)}, f32[8,1152]{1,0:T(8,128)S(1)}, u32[]{:S(2)}, u32[]{:S(2)}) collective-permute-start(f32[8,1152]{1,0:T(8,128)S(1)} %concatenate.29), channel_id=1, source_target_pairs={{0,2},{1,3},{2,0},{3,1},{4,6},{5,7},{6,4},{7,5},{8,10},{9,11},{10,... | collective-permute-start | bytes 110600 | tf_op jit(solution)/shard_map/ppermute | solution.py:26
  30.3 3.8 %collective-permute-start.6 = (f32[8,640]{1,0:T(8,128)S(1)}, f32[8,640]{1,0:T(8,128)S(1)}, u32[]{:S(2)}, u32[]{:S(2)}) collective-permute-start(f32[8,640]{1,0:T(8,128)S(1)} %pad_maximum_fusion.2), channel_id=1, source_target_pairs={{0,1},{1,0},{2,3},{3,2},{4,5},{5,4},{6,7},{7,6},{8,9},{9,8},{10,11... | collective-permute-start | bytes 61448 | tf_op jit(solution)/shard_map/ppermute | solution.py:26
  34.1 1.2 %collective-permute-start.7 = (f32[8,128]{1,0:T(8,128)S(1)}, f32[8,128]{1,0:T(8,128)S(1)}, u32[]{:S(2)}, u32[]{:S(2)}) collective-permute-start(f32[8,128]{1,0:T(8,128)S(1)} %slice_add_fusion.2), channel_id=1, source_target_pairs={{0,4},{4,0},{8,12},{12,8},{16,20},{20,16},{24,28},{28,24},{1,5},{5... | collective-permute-start | bytes 12296 | tf_op jit(solution)/shard_map/ppermute | solution.py:26
  35.3 3.6 %collective-permute-start.8 = (f32[8,128]{1,0:T(8,128)S(1)}, f32[8,128]{1,0:T(8,128)S(1)}, u32[]{:S(2)}, u32[]{:S(2)}) collective-permute-start(f32[8,128]{1,0:T(8,128)S(1)} %add.101), channel_id=1, source_target_pairs={{0,8},{4,12},{8,0},{12,4},{16,24},{20,28},{24,16},{28,20},{1,9},{5... | collective-permute-start | bytes 12296 | tf_op jit(solution)/shard_map/ppermute | solution.py:26
  38.9 4.5 %collective-permute-start.9 = (f32[8,128]{1,0:T(8,128)S(1)}, f32[8,128]{1,0:T(8,128)S(1)}, u32[]{:S(2)}, u32[]{:S(2)}) collective-permute-start(f32[8,128]{1,0:T(8,128)S(1)} %add.102), channel_id=1, source_target_pairs={{0,16},{4,20},{8,24},{12,28},{16,0},{20,4},{24,8},{28,12},{1,17},{... | collective-permute-start | bytes 12296 | tf_op jit(solution)/shard_map/ppermute | solution.py:26

commit v14 on v13

--- a/solution.py
+++ b/solution.py
@@ -103,7 +103,15 @@
     core = lax.axis_index("blk") % 2
     if paired:
         helpers = lax.axis_size("help")
-        own_pair = gather_help(jnp.concatenate([vectors, exchanged(vectors, "blk", 1)], axis=1))
+        own_pair = jnp.concatenate([vectors, exchanged(vectors, "blk", 1)], axis=1)
+        own_pair = jnp.concatenate([own_pair, exchanged(own_pair, "help", 1)], axis=1)
+        tile_row, tile_col, counts, vectors, _ = lax.optimization_barrier(
+            (tile_row, tile_col, counts, vectors, own_pair)
+        )
+        mask = 2
+        while mask < helpers:
+            own_pair = jnp.concatenate([own_pair, exchanged(own_pair, "help", mask)], axis=1)
+            mask *= 2
         crossing = [(b, b + 2) for b in range(0, groups - 2, 2)]
         crossing += [(b, b - 2) for b in range(3, groups, 2)]
         remote = lax.ppermute(own_pair, "blk", crossing)
@@ -113,9 +121,6 @@
             halves = pair.reshape(VEC, helpers, 2, piece_width)
             sources += [halves[:, :, side].reshape(VEC, group_width) for side in range(2)]
         full_panel = sources[0]
-        tile_row, tile_col, counts, vectors, _ = lax.optimization_barrier(
-            (tile_row, tile_col, counts, vectors, own_pair)
-        )
     else:
         full_panel = gather_help(vectors)
         sources = neighbour_panels(full_panel)

time: 44.7 us -> 44.2 us (0.989)
  other arithmetic: 4.9 us -> 4.18 us
    ppermute x1, waiting for transfers between devices: 0.01 us -> 2.45 us  [local(): remote = lax.ppermute(own_pair, 'blk', crossing)]
    ppermute x9, waiting for transfers between devices: 14.6 us -> 12.2 us  [exchanged(): lax.ppermute(value, axis, [(source, source ^ mask) for source in range(co...]
    concatenate x2 -> x1, other arithmetic: 1.44 us -> 0.72 us  [local(): own_pair = jnp.concatenate([vectors, exchanged(vectors, 'blk', 1)], axis=1)]
    ppermute x9, starting transfers between devices: 12.5 us -> 13.1 us  [exchanged(): lax.ppermute(value, axis, [(source, source ^ mask) for source in range(co...]
where the time goes in v14:
time: 44.2 us; the launch traced here: 43.6 us
  starting transfers between devices  16.6 us (38%)
  waiting for transfers between devices  14.7 us (33%)
  matrix products  4.93 us (11%)
  other arithmetic  4.18 us (9%)
  local copies, waits for them, and re-layouts  2.45 us (6%)
  between operations  0.76 us (2%)
    ppermute x9, starting transfers between devices, exchanged(): lax.ppermute(value, axis, [(source, source ^ mask) for source in range(co...  13.1 us
    ppermute x9, waiting for transfers between devices, exchanged(): lax.ppermute(value, axis, [(source, source ^ mask) for source in range(co...  12.2 us
    ppermute x1, starting transfers between devices, local(): remote = lax.ppermute(own_pair, 'blk', crossing)  3.49 us
    dot_general x1, matrix products, batch_product(): jnp.einsum('osit,ostu->osiu', pieces, tile_blocks[0, first:last:step], pr...  3.18 us
    ppermute x1, waiting for transfers between devices, local(): remote = lax.ppermute(own_pair, 'blk', crossing)  2.45 us
    concatenate x2, other arithmetic, batch_product(): pieces = stacked[panel_ids[:, None], column_place[first:last:step]]  1.37 us
    dot_general x1, matrix products, local(): jnp.dot(vectors, vectors.T, precision=lax.Precision.HIGHEST, preferred_el...  0.92 us
  transfers between devices with their start and end apart: 10, of which 8 were waited for; matrix products, arithmetic and copies ran while one was open for 12% of the time, Pallas kernels for 0%

profile of v14, /device:TPU:0, one launch (start us, length us, event | category | flops | bytes accessed | tf_op | source)
XLA Modules:
  0.0 43.6 jit_solution(6313029436630344895)
XLA Ops:
  0.6 0.5 %collective-permute-start = (f32[8,512]{1,0:T(8,128)}, f32[8,512]{1,0:T(8,128)S(1)}, u32[]{:S(2)}, u32[]{:S(2)}) collective-permute-start(f32[8,512]{1,0:T(8,128)} %param.7), channel_id=1, source_target_pairs={{0,4},{4,0},{8,12},{12,8},{16,20},{20,16},{24,28},{28,24},{1,5},{5... | collective-permute-start | bytes 49160 | tf_op jit(solution)/shard_map/ppermute | solution.py:26
  1.1 0.7 %fusion.20 = s32[5]{0:T(128)S(1)} fusion(s32[5]{0:T(128)} %constant.71.clone, s32[5]{0:T(128)} %constant.72.clone, pred[]{:T(512)S(6)} %eq.24), kind=kLoop, calls=%fused_computation.60 | loop fusion | flops 30 | bytes 61 | tf_op jit(solution)/shard_map/concatenate | solution.py:137
  1.8 0.7 %constant_dynamic-update-slice_fusion.2 = (f32[8,2048]{1,0:T(8,128)S(1)}, f32[8,4096]{1,0:T(8,128)S(1)}) fusion(f32[8,512]{1,0:T(8,128)} %param.7), kind=kLoop, calls=%fused_computation.9 | loop fusion | bytes 49152
  2.5 0.0 collective-permute-done
  2.5 0.7 %pad_maximum_fusion = f32[8,1024]{1,0:T(8,128)S(1)} fusion(f32[8,512]{1,0:T(8,128)S(1)} %collective-permute-done, f32[8,512]{1,0:T(8,128)} %param.7), kind=kLoop, calls=%fused_computation.6 | loop fusion | flops 8192 | bytes 65536 | tf_op jit(solution)/shard_map/concatenate | solution.py:106
  3.3 2.5 %collective-permute-start.1 = (f32[8,1024]{1,0:T(8,128)S(1)}, f32[8,1024]{1,0:T(8,128)S(1)}, u32[]{:S(2)}, u32[]{:S(2)}) collective-permute-start(f32[8,1024]{1,0:T(8,128)S(1)} %pad_maximum_fusion), channel_id=1, source_target_pairs={{0,1},{1,0},{2,3},{3,2},{4,5},{5,4},{6,7},{7,6},{8,9},{9,8},{10,11... | collective-permute-start | bytes 98312 | tf_op jit(solution)/shard_map/ppermute | solution.py:26
  5.8 2.0 %collective-permute-done.1 = f32[8,1024]{1,0:T(8,128)S(1)} collective-permute-done((f32[8,1024]{1,0:T(8,128)S(1)}, f32[8,1024]{1,0:T(8,128)S(1)}, u32[]{:S(2)}, u32[]{:S(2)}) %collective-permute-start.1) | collective-permute-done | bytes 32800 | tf_op jit(solution)/shard_map/ppermute | solution.py:26
  7.8 1.9 %collective-permute-start.2 = (f32[8,2048]{1,0:T(8,128)S(1)}, f32[8,2048]{1,0:T(8,128)S(1)}, u32[]{:S(2)}, u32[]{:S(2)}) collective-permute-start(f32[8,2048]{1,0:T(8,128)S(1)} %get-tuple-element.17), channel_id=1, source_target_pairs={{0,2},{1,3},{2,0},{3,1},{4,6},{5,7},{6,4},{7,5},{8,10},{9,11},{10,... | collective-permute-start | bytes 196616 | tf_op jit(solution)/shard_map/ppermute | solution.py:26
  9.7 0.9 %fusion.27 = f32[8,8]{1,0:T(8,128)S(1)} fusion(f32[8,512]{1,0:T(8,128)} %param.7), kind=kOutput, calls=%fused_computation.67 | convolution fusion | flops 393216 | bytes 16640 | tf_op jit(solution)/shard_map/dot_general | solution.py:162
  10.7 0.7 %fusion.10 = s32[5,3]{0,1:T(4,128)S(1)} fusion(s32[1,5,3]{1,0,2:T(1,128)} %param.9, s32[]{:T(128)S(6)} %axis_index.22), kind=kLoop, calls=%fused_computation.45 | loop fusion | flops 330 | bytes 124 | tf_op jit(solution)/shard_map/add | solution.py:101
  11.4 0.7 %fusion.18 = s32[5,3,1]{0,2,1:T(1,128)S(1)} fusion(s32[1,5,3]{1,0,2:T(1,128)} %param.10, s32[5]{0:T(128)S(1)} %fusion.20, s32[]{:T(128)S(6)} %axis_index.22), kind=kLoop, calls=%fused_computation.56 | loop fusion | flops 420 | bytes 144 | tf_op jit(solution)/shard_map/concatenate | solution.py:137
  12.1 0.7 %fusion.12 = f32[5,3]{0,1:T(4,128)S(1)} fusion(s32[5]{0:T(128)} %bitcast.79), kind=kLoop, calls=%fused_computation.50 | loop fusion | flops 30 | bytes 80 | tf_op jit(solution)/shard_map/convert_element_type | solution.py:129
  12.7 0.1 copy.23
  12.8 0.1 reshape.229
  12.9 0.0 collective-permute-done.2
  12.9 3.5 %collective-permute-start.3 = (f32[8,4096]{1,0:T(8,128)S(1)}, f32[8,4096]{1,0:T(8,128)S(1)}, u32[]{:S(2)}, u32[]{:S(2)}) collective-permute-start(f32[8,4096]{1,0:T(8,128)S(1)} %constant_dynamic-update-slice_fusion.3), channel_id=1, source_target_pairs={{0,8},{8,16},{16,24},{12,4},{20,12},{28,20},{1,9},{9,17},{17,25},{... | collective-permute-start | bytes 393224 | tf_op jit(solution)/shard_map/ppermute | solution.py:117
  16.5 2.4 %collective-permute-done.3 = f32[8,4096]{1,0:T(8,128)S(1)} collective-permute-done((f32[8,4096]{1,0:T(8,128)S(1)}, f32[8,4096]{1,0:T(8,128)S(1)}, u32[]{:S(2)}, u32[]{:S(2)}) %collective-permute-start.3) | collective-permute-done | bytes 131104 | tf_op jit(solution)/shard_map/ppermute | solution.py:117
  18.9 0.1 collective-permute-start.4
  19.0 1.3 %collective-permute-done.4 = f32[8,4096]{1,0:T(8,128)S(1)} collective-permute-done((f32[8,4096]{1,0:T(8,128)S(1)}, f32[8,4096]{1,0:T(8,128)S(1)}, u32[]{:S(2)}, u32[]{:S(2)}) %collective-permute-start.4) | collective-permute-done | bytes 131104 | tf_op jit(solution)/shard_map/ppermute | solution.py:26
  20.4 0.6 %gather_fusion = f32[15,8,256]{2,1,0:T(8,128)S(1)} fusion(f32[6,8,8,256]{3,2,1,0:T(8,128)S(1)} %bitcast.78, s32[15]{0:T(128)S(1)} %reshape.229), kind=kCustom, calls=%fused_computation | custom fusion | bytes 245880 | tf_op jit(solution)/shard_map/gather | solution.py:137
  21.0 3.2 %fusion = f32[5,3,8,256]{3,2,1,0:T(8,128)S(1)} fusion(f32[5,3,8,256]{3,2,1,0:T(8,128)S(1)} %bitcast.69, f32[1,5,3,256,256]{4,3,2,1,0:T(8,128)} %param.8), kind=kOutput, calls=%fused_computation.1 | convolution fusion | flops 47185920 | bytes 4177920 | tf_op jit(solution)/shard_map/osit,ostu->osiu/dot_general | solution.py:138
  24.2 0.6 %convolution_bitcast_fusion = f32[1,8,8,256]{3,2,1,0:T(8,128)S(1)} fusion(f32[5,3,8,256]{3,2,1,0:T(8,128)S(1)} %fusion, f32[5,3]{0,1:T(4,128)S(1)} %fusion.12, s32[5,3]{0,1:T(4,128)S(1)} %fusion.10), kind=kOutput, calls=%fused_computation.3 | convolution fusion | flops 2949360 | bytes 188536 | tf_op jit(solution)/shard_map/osiu,osr->iru/dot_general | solution.py:144
  24.9 0.2 fusion.26
  25.1 0.1 concatenate.29
  25.2 1.1 %collective-permute-start.5 = (f32[8,1152]{1,0:T(8,128)S(1)}, f32[8,1152]{1,0:T(8,128)S(1)}, u32[]{:S(2)}, u32[]{:S(2)}) collective-permute-start(f32[8,1152]{1,0:T(8,128)S(1)} %concatenate.29), channel_id=1, source_target_pairs={{0,2},{1,3},{2,0},{3,1},{4,6},{5,7},{6,4},{7,5},{8,10},{9,11},{10,... | collective-permute-start | bytes 110600 | tf_op jit(solution)/shard_map/ppermute | solution.py:26
  26.3 2.9 %collective-permute-done.5 = f32[8,1152]{1,0:T(8,128)S(1)} collective-permute-done((f32[8,1152]{1,0:T(8,128)S(1)}, f32[8,1152]{1,0:T(8,128)S(1)}, u32[]{:S(2)}, u32[]{:S(2)}) %collective-permute-start.5) | collective-permute-done | bytes 36896 | tf_op jit(solution)/shard_map/ppermute | solution.py:26
  29.2 0.1 slice_add_fusion.3
  29.3 1.5 %collective-permute-start.6 = (f32[8,640]{1,0:T(8,128)S(1)}, f32[8,640]{1,0:T(8,128)S(1)}, u32[]{:S(2)}, u32[]{:S(2)}) collective-permute-start(f32[8,640]{1,0:T(8,128)S(1)} %pad_maximum_fusion.1), channel_id=1, source_target_pairs={{0,1},{1,0},{2,3},{3,2},{4,5},{5,4},{6,7},{7,6},{8,9},{9,8},{10,11... | collective-permute-start | bytes 61448 | tf_op jit(solution)/shard_map/ppermute | solution.py:26
  30.8 2.3 %collective-permute-done.6 = f32[8,640]{1,0:T(8,128)S(1)} collective-permute-done((f32[8,640]{1,0:T(8,128)S(1)}, f32[8,640]{1,0:T(8,128)S(1)}, u32[]{:S(2)}, u32[]{:S(2)}) %collective-permute-start.6) | collective-permute-done | bytes 20512 | tf_op jit(solution)/shard_map/ppermute | solution.py:26
  33.1 0.0 collective-permute-start.7
  33.1 1.2 %collective-permute-done.7 = f32[8,128]{1,0:T(8,128)S(1)} collective-permute-done((f32[8,128]{1,0:T(8,128)S(1)}, f32[8,128]{1,0:T(8,128)S(1)}, u32[]{:S(2)}, u32[]{:S(2)}) %collective-permute-start.7) | collective-permute-done | bytes 4128 | tf_op jit(solution)/shard_map/ppermute | solution.py:26
  34.3 2.4 %collective-permute-start.8 = (f32[8,128]{1,0:T(8,128)S(1)}, f32[8,128]{1,0:T(8,128)S(1)}, u32[]{:S(2)}, u32[]{:S(2)}) collective-permute-start(f32[8,128]{1,0:T(8,128)S(1)} %add.101), channel_id=1, source_target_pairs={{0,8},{4,12},{8,0},{12,4},{16,24},{20,28},{24,16},{28,20},{1,9},{5... | collective-permute-start | bytes 12296 | tf_op jit(solution)/shard_map/ppermute | solution.py:26
  36.7 1.6 %collective-permute-done.8 = f32[8,128]{1,0:T(8,128)S(1)} collective-permute-done((f32[8,128]{1,0:T(8,128)S(1)}, f32[8,128]{1,0:T(8,128)S(1)}, u32[]{:S(2)}, u32[]{:S(2)}) %collective-permute-start.8) | collective-permute-done | bytes 4128 | tf_op jit(solution)/shard_map/ppermute | solution.py:26
  38.3 3.0 %collective-permute-start.9 = (f32[8,128]{1,0:T(8,128)S(1)}, f32[8,128]{1,0:T(8,128)S(1)}, u32[]{:S(2)}, u32[]{:S(2)}) collective-permute-start(f32[8,128]{1,0:T(8,128)S(1)} %add.102), channel_id=1, source_target_pairs={{0,16},{4,20},{8,24},{12,28},{16,0},{20,4},{24,8},{28,12},{1,17},{... | collective-permute-start | bytes 12296 | tf_op jit(solution)/shard_map/ppermute | solution.py:26
  41.3 0.6 %slice_add_fusion.1 = f32[8,512]{1,0:T(8,128)} fusion(f32[8,640]{1,0:T(8,128)S(1)} %collective-permute-done.6, f32[8,1024]{1,0:T(8,128)S(1)} %slice_add_fusion), kind=kLoop, calls=%fused_computation.21 | loop fusion | flops 4096 | bytes 49152 | tf_op jit(solution)/shard_map/add | solution.py:60
  41.9 1.0 %collective-permute-done.9 = f32[8,128]{1,0:T(8,128)S(1)} collective-permute-done((f32[8,128]{1,0:T(8,128)S(1)}, f32[8,128]{1,0:T(8,128)S(1)}, u32[]{:S(2)}, u32[]{:S(2)}) %collective-permute-start.9) | collective-permute-done | bytes 4128 | tf_op jit(solution)/shard_map/ppermute | solution.py:26
  42.9 0.7 %fusion.25 = (f32[8,8]{1,0:T(8,128)}, f32[8,8]{1,0:T(8,128)}) fusion(f32[8,128]{1,0:T(8,128)S(1)} %add_multiply_fusion), kind=kLoop, calls=%fused_computation.65 | loop fusion | bytes 1024 | tf_op jit(solution)/shard_map/slice | solution.py:174
  (22 shorter events, 0.2 us)
Async XLA Ops:
  0.6 1.9 %collective-permute-start = (f32[8,512]{1,0:T(8,128)}, f32[8,512]{1,0:T(8,128)S(1)}, u32[]{:S(2)}, u32[]{:S(2)}) collective-permute-start(f32[8,512]{1,0:T(8,128)} %param.7), channel_id=1, source_target_pairs={{0,4},{4,0},{8,12},{12,8},{16,20},{20,16},{24,28},{28,24},{1,5},{5... | collective-permute-start | bytes 49160 | tf_op jit(solution)/shard_map/ppermute | solution.py:26
  3.3 4.5 %collective-permute-start.1 = (f32[8,1024]{1,0:T(8,128)S(1)}, f32[8,1024]{1,0:T(8,128)S(1)}, u32[]{:S(2)}, u32[]{:S(2)}) collective-permute-start(f32[8,1024]{1,0:T(8,128)S(1)} %pad_maximum_fusion), channel_id=1, source_target_pairs={{0,1},{1,0},{2,3},{3,2},{4,5},{5,4},{6,7},{7,6},{8,9},{9,8},{10,11... | collective-permute-start | bytes 98312 | tf_op jit(solution)/shard_map/ppermute | solution.py:26
  7.8 5.1 %collective-permute-start.2 = (f32[8,2048]{1,0:T(8,128)S(1)}, f32[8,2048]{1,0:T(8,128)S(1)}, u32[]{:S(2)}, u32[]{:S(2)}) collective-permute-start(f32[8,2048]{1,0:T(8,128)S(1)} %get-tuple-element.17), channel_id=1, source_target_pairs={{0,2},{1,3},{2,0},{3,1},{4,6},{5,7},{6,4},{7,5},{8,10},{9,11},{10,... | collective-permute-start | bytes 196616 | tf_op jit(solution)/shard_map/ppermute | solution.py:26
  12.9 6.0 %collective-permute-start.3 = (f32[8,4096]{1,0:T(8,128)S(1)}, f32[8,4096]{1,0:T(8,128)S(1)}, u32[]{:S(2)}, u32[]{:S(2)}) collective-permute-start(f32[8,4096]{1,0:T(8,128)S(1)} %constant_dynamic-update-slice_fusion.3), channel_id=1, source_target_pairs={{0,8},{8,16},{16,24},{12,4},{20,12},{28,20},{1,9},{9,17},{17,25},{... | collective-permute-start | bytes 393224 | tf_op jit(solution)/shard_map/ppermute | solution.py:117
  18.9 1.4 %collective-permute-start.4 = (f32[8,4096]{1,0:T(8,128)S(1)}, f32[8,4096]{1,0:T(8,128)S(1)}, u32[]{:S(2)}, u32[]{:S(2)}) collective-permute-start(f32[8,4096]{1,0:T(8,128)S(1)} %collective-permute-done.3), channel_id=1, source_target_pairs={{0,4},{4,0},{8,12},{12,8},{16,20},{20,16},{24,28},{28,24},{1,5},{5... | collective-permute-start | bytes 393224 | tf_op jit(solution)/shard_map/ppermute | solution.py:26
  25.2 4.0 %collective-permute-start.5 = (f32[8,1152]{1,0:T(8,128)S(1)}, f32[8,1152]{1,0:T(8,128)S(1)}, u32[]{:S(2)}, u32[]{:S(2)}) collective-permute-start(f32[8,1152]{1,0:T(8,128)S(1)} %concatenate.29), channel_id=1, source_target_pairs={{0,2},{1,3},{2,0},{3,1},{4,6},{5,7},{6,4},{7,5},{8,10},{9,11},{10,... | collective-permute-start | bytes 110600 | tf_op jit(solution)/shard_map/ppermute | solution.py:26
  29.3 3.8 %collective-permute-start.6 = (f32[8,640]{1,0:T(8,128)S(1)}, f32[8,640]{1,0:T(8,128)S(1)}, u32[]{:S(2)}, u32[]{:S(2)}) collective-permute-start(f32[8,640]{1,0:T(8,128)S(1)} %pad_maximum_fusion.1), channel_id=1, source_target_pairs={{0,1},{1,0},{2,3},{3,2},{4,5},{5,4},{6,7},{7,6},{8,9},{9,8},{10,11... | collective-permute-start | bytes 61448 | tf_op jit(solution)/shard_map/ppermute | solution.py:26
  33.1 1.2 %collective-permute-start.7 = (f32[8,128]{1,0:T(8,128)S(1)}, f32[8,128]{1,0:T(8,128)S(1)}, u32[]{:S(2)}, u32[]{:S(2)}) collective-permute-start(f32[8,128]{1,0:T(8,128)S(1)} %slice_add_fusion.2), channel_id=1, source_target_pairs={{0,4},{4,0},{8,12},{12,8},{16,20},{20,16},{24,28},{28,24},{1,5},{5... | collective-permute-start | bytes 12296 | tf_op jit(solution)/shard_map/ppermute | solution.py:26
  34.3 4.0 %collective-permute-start.8 = (f32[8,128]{1,0:T(8,128)S(1)}, f32[8,128]{1,0:T(8,128)S(1)}, u32[]{:S(2)}, u32[]{:S(2)}) collective-permute-start(f32[8,128]{1,0:T(8,128)S(1)} %add.101), channel_id=1, source_target_pairs={{0,8},{4,12},{8,0},{12,4},{16,24},{20,28},{24,16},{28,20},{1,9},{5... | collective-permute-start | bytes 12296 | tf_op jit(solution)/shard_map/ppermute | solution.py:26
  38.3 4.6 %collective-permute-start.9 = (f32[8,128]{1,0:T(8,128)S(1)}, f32[8,128]{1,0:T(8,128)S(1)}, u32[]{:S(2)}, u32[]{:S(2)}) collective-permute-start(f32[8,128]{1,0:T(8,128)S(1)} %add.102), channel_id=1, source_target_pairs={{0,16},{4,20},{8,24},{12,28},{16,0},{20,4},{24,8},{28,12},{1,17},{... | collective-permute-start | bytes 12296 | tf_op jit(solution)/shard_map/ppermute | solution.py:26

commit v15 on v14

--- a/solution.py
+++ b/solution.py
@@ -104,9 +104,10 @@
     if paired:
         helpers = lax.axis_size("help")
         own_pair = jnp.concatenate([vectors, exchanged(vectors, "blk", 1)], axis=1)
+        vectors, _ = lax.optimization_barrier((vectors, own_pair))
         own_pair = jnp.concatenate([own_pair, exchanged(own_pair, "help", 1)], axis=1)
-        tile_row, tile_col, counts, vectors, _ = lax.optimization_barrier(
-            (tile_row, tile_col, counts, vectors, own_pair)
+        tile_row, tile_col, counts, _ = lax.optimization_barrier(
+            (tile_row, tile_col, counts, own_pair)
         )
         mask = 2
         while mask < helpers:

time: 44.2 us -> 43 us (0.973)
  waiting for transfers between devices: 14.7 us -> 13.4 us
  starting transfers between devices: 16.6 us -> 17.5 us
  other arithmetic: 4.18 us -> 3.44 us
    ppermute x9, waiting for transfers between devices: 12.2 us -> 11 us  [exchanged(): lax.ppermute(value, axis, [(source, source ^ mask) for source in range(co...]
    concatenate x1 -> x0, other arithmetic: 0.72 us -> none  [local(): own_pair = jnp.concatenate([vectors, exchanged(vectors, 'blk', 1)], axis=1)]
    ppermute x9, starting transfers between devices: 13.1 us -> 13.6 us  [exchanged(): lax.ppermute(value, axis, [(source, source ^ mask) for source in range(co...]
  transfers between devices with their start and end apart: 10 -> 10, of which waited for: 8 -> 9; matrix products, arithmetic and copies ran while one was open for 12% -> 12% of each run, Pallas kernels for 0% -> 0%
where the time goes in v15:
time: 43 us; the launch traced here: 42.5 us
  starting transfers between devices  17.5 us (41%)
  waiting for transfers between devices  13.4 us (31%)
  matrix products  4.93 us (11%)
  other arithmetic  3.44 us (8%)
  local copies, waits for them, and re-layouts  2.45 us (6%)
  between operations  0.76 us (2%)
    ppermute x9, starting transfers between devices, exchanged(): lax.ppermute(value, axis, [(source, source ^ mask) for source in range(co...  13.6 us
    ppermute x9, waiting for transfers between devices, exchanged(): lax.ppermute(value, axis, [(source, source ^ mask) for source in range(co...  11 us
    ppermute x1, starting transfers between devices, local(): remote = lax.ppermute(own_pair, 'blk', crossing)  3.87 us
    dot_general x1, matrix products, batch_product(): jnp.einsum('osit,ostu->osiu', pieces, tile_blocks[0, first:last:step], pr...  3.18 us
    ppermute x1, waiting for transfers between devices, local(): remote = lax.ppermute(own_pair, 'blk', crossing)  2.45 us
    concatenate x2, other arithmetic, batch_product(): pieces = stacked[panel_ids[:, None], column_place[first:last:step]]  1.37 us
    dot_general x1, matrix products, local(): jnp.dot(vectors, vectors.T, precision=lax.Precision.HIGHEST, preferred_el...  0.92 us
  transfers between devices with their start and end apart: 10, of which 9 were waited for; matrix products, arithmetic and copies ran while one was open for 12% of the time, Pallas kernels for 0%

profile of v15, /device:TPU:0, one launch (start us, length us, event | category | flops | bytes accessed | tf_op | source)
XLA Modules:
  0.0 42.5 jit_solution(5463000183317270698)
XLA Ops:
  0.6 0.5 %collective-permute-start = (f32[8,512]{1,0:T(8,128)}, f32[8,512]{1,0:T(8,128)S(1)}, u32[]{:S(2)}, u32[]{:S(2)}) collective-permute-start(f32[8,512]{1,0:T(8,128)} %param.7), channel_id=1, source_target_pairs={{0,4},{4,0},{8,12},{12,8},{16,20},{20,16},{24,28},{28,24},{1,5},{5... | collective-permute-start | bytes 49160 | tf_op jit(solution)/shard_map/ppermute | solution.py:26
  1.1 0.7 %fusion.20 = s32[5]{0:T(128)S(1)} fusion(s32[5]{0:T(128)} %constant.71.clone, s32[5]{0:T(128)} %constant.72.clone, pred[]{:T(512)S(6)} %eq.24), kind=kLoop, calls=%fused_computation.61 | loop fusion | flops 30 | bytes 61 | tf_op jit(solution)/shard_map/concatenate | solution.py:138
  1.8 0.7 %constant_dynamic-update-slice_fusion.4 = (f32[8,2048]{1,0:T(8,128)S(1)}, f32[8,1024]{1,0:T(8,128)S(1)}, f32[8,4096]{1,0:T(8,128)S(1)}) fusion(f32[8,512]{1,0:T(8,128)} %param.7), kind=kLoop, calls=%fused_computation.10 | loop fusion | bytes 65536
  2.5 0.0 collective-permute-done
  2.5 2.6 %collective-permute-start.1 = (f32[8,1024]{1,0:T(8,128)S(1)}, f32[8,1024]{1,0:T(8,128)S(1)}, u32[]{:S(2)}, u32[]{:S(2)}) collective-permute-start(f32[8,1024]{1,0:T(8,128)S(1)} %get-tuple-element.21), channel_id=1, source_target_pairs={{0,1},{1,0},{2,3},{3,2},{4,5},{5,4},{6,7},{7,6},{8,9},{9,8},{10,11... | collective-permute-start | bytes 98312 | tf_op jit(solution)/shard_map/ppermute | solution.py:26
  5.1 0.9 %fusion.27 = f32[8,8]{1,0:T(8,128)S(1)} fusion(f32[8,512]{1,0:T(8,128)} %param.7), kind=kOutput, calls=%fused_computation.68 | convolution fusion | flops 393216 | bytes 16640 | tf_op jit(solution)/shard_map/dot_general | solution.py:163
  6.1 1.1 %collective-permute-done.1 = f32[8,1024]{1,0:T(8,128)S(1)} collective-permute-done((f32[8,1024]{1,0:T(8,128)S(1)}, f32[8,1024]{1,0:T(8,128)S(1)}, u32[]{:S(2)}, u32[]{:S(2)}) %collective-permute-start.1) | collective-permute-done | bytes 32800 | tf_op jit(solution)/shard_map/ppermute | solution.py:26
  7.2 1.9 %collective-permute-start.2 = (f32[8,2048]{1,0:T(8,128)S(1)}, f32[8,2048]{1,0:T(8,128)S(1)}, u32[]{:S(2)}, u32[]{:S(2)}) collective-permute-start(f32[8,2048]{1,0:T(8,128)S(1)} %get-tuple-element.17), channel_id=1, source_target_pairs={{0,2},{1,3},{2,0},{3,1},{4,6},{5,7},{6,4},{7,5},{8,10},{9,11},{10,... | collective-permute-start | bytes 196616 | tf_op jit(solution)/shard_map/ppermute | solution.py:26
  9.1 0.7 %fusion.10 = s32[5,3]{0,1:T(4,128)S(1)} fusion(s32[1,5,3]{1,0,2:T(1,128)} %param.9, s32[]{:T(128)S(6)} %axis_index.22), kind=kLoop, calls=%fused_computation.46 | loop fusion | flops 330 | bytes 124 | tf_op jit(solution)/shard_map/add | solution.py:101
  9.8 0.7 %fusion.18 = s32[5,3,1]{0,2,1:T(1,128)S(1)} fusion(s32[1,5,3]{1,0,2:T(1,128)} %param.10, s32[5]{0:T(128)S(1)} %fusion.20, s32[]{:T(128)S(6)} %axis_index.22), kind=kLoop, calls=%fused_computation.57 | loop fusion | flops 420 | bytes 144 | tf_op jit(solution)/shard_map/concatenate | solution.py:138
  10.5 0.7 %fusion.12 = f32[5,3]{0,1:T(4,128)S(1)} fusion(s32[5]{0:T(128)} %bitcast.79), kind=kLoop, calls=%fused_computation.51 | loop fusion | flops 30 | bytes 80 | tf_op jit(solution)/shard_map/convert_element_type | solution.py:130
  11.1 0.1 copy.23
  11.2 0.1 reshape.229
  11.3 0.1 collective-permute-done.2
  11.4 3.9 %collective-permute-start.3 = (f32[8,4096]{1,0:T(8,128)S(1)}, f32[8,4096]{1,0:T(8,128)S(1)}, u32[]{:S(2)}, u32[]{:S(2)}) collective-permute-start(f32[8,4096]{1,0:T(8,128)S(1)} %constant_dynamic-update-slice_fusion.5), channel_id=1, source_target_pairs={{0,8},{8,16},{16,24},{12,4},{20,12},{28,20},{1,9},{9,17},{17,25},{... | collective-permute-start | bytes 393224 | tf_op jit(solution)/shard_map/ppermute | solution.py:118
  15.4 2.4 %collective-permute-done.3 = f32[8,4096]{1,0:T(8,128)S(1)} collective-permute-done((f32[8,4096]{1,0:T(8,128)S(1)}, f32[8,4096]{1,0:T(8,128)S(1)}, u32[]{:S(2)}, u32[]{:S(2)}) %collective-permute-start.3) | collective-permute-done | bytes 131104 | tf_op jit(solution)/shard_map/ppermute | solution.py:118
  17.8 0.1 collective-permute-start.4
  17.9 1.3 %collective-permute-done.4 = f32[8,4096]{1,0:T(8,128)S(1)} collective-permute-done((f32[8,4096]{1,0:T(8,128)S(1)}, f32[8,4096]{1,0:T(8,128)S(1)}, u32[]{:S(2)}, u32[]{:S(2)}) %collective-permute-start.4) | collective-permute-done | bytes 131104 | tf_op jit(solution)/shard_map/ppermute | solution.py:26
  19.3 0.6 %gather_fusion = f32[15,8,256]{2,1,0:T(8,128)S(1)} fusion(f32[6,8,8,256]{3,2,1,0:T(8,128)S(1)} %bitcast.78, s32[15]{0:T(128)S(1)} %reshape.229), kind=kCustom, calls=%fused_computation | custom fusion | bytes 245880 | tf_op jit(solution)/shard_map/gather | solution.py:138
  19.9 3.2 %fusion = f32[5,3,8,256]{3,2,1,0:T(8,128)S(1)} fusion(f32[5,3,8,256]{3,2,1,0:T(8,128)S(1)} %bitcast.69, f32[1,5,3,256,256]{4,3,2,1,0:T(8,128)} %param.8), kind=kOutput, calls=%fused_computation.1 | convolution fusion | flops 47185920 | bytes 4177920 | tf_op jit(solution)/shard_map/osit,ostu->osiu/dot_general | solution.py:139
  23.1 0.6 %convolution_bitcast_fusion = f32[1,8,8,256]{3,2,1,0:T(8,128)S(1)} fusion(f32[5,3,8,256]{3,2,1,0:T(8,128)S(1)} %fusion, f32[5,3]{0,1:T(4,128)S(1)} %fusion.12, s32[5,3]{0,1:T(4,128)S(1)} %fusion.10), kind=kOutput, calls=%fused_computation.3 | convolution fusion | flops 2949360 | bytes 188536 | tf_op jit(solution)/shard_map/osiu,osr->iru/dot_general | solution.py:145
  23.8 0.2 fusion.26
  24.0 0.1 concatenate.29
  24.1 1.5 %collective-permute-start.5 = (f32[8,1152]{1,0:T(8,128)S(1)}, f32[8,1152]{1,0:T(8,128)S(1)}, u32[]{:S(2)}, u32[]{:S(2)}) collective-permute-start(f32[8,1152]{1,0:T(8,128)S(1)} %concatenate.29), channel_id=1, source_target_pairs={{0,2},{1,3},{2,0},{3,1},{4,6},{5,7},{6,4},{7,5},{8,10},{9,11},{10,... | collective-permute-start | bytes 110600 | tf_op jit(solution)/shard_map/ppermute | solution.py:26
  25.6 2.4 %collective-permute-done.5 = f32[8,1152]{1,0:T(8,128)S(1)} collective-permute-done((f32[8,1152]{1,0:T(8,128)S(1)}, f32[8,1152]{1,0:T(8,128)S(1)}, u32[]{:S(2)}, u32[]{:S(2)}) %collective-permute-start.5) | collective-permute-done | bytes 36896 | tf_op jit(solution)/shard_map/ppermute | solution.py:26
  28.1 0.1 slice_add_fusion.3
  28.2 1.5 %collective-permute-start.6 = (f32[8,640]{1,0:T(8,128)S(1)}, f32[8,640]{1,0:T(8,128)S(1)}, u32[]{:S(2)}, u32[]{:S(2)}) collective-permute-start(f32[8,640]{1,0:T(8,128)S(1)} %pad_maximum_fusion), channel_id=1, source_target_pairs={{0,1},{1,0},{2,3},{3,2},{4,5},{5,4},{6,7},{7,6},{8,9},{9,8},{10,11... | collective-permute-start | bytes 61448 | tf_op jit(solution)/shard_map/ppermute | solution.py:26
  29.7 2.3 %collective-permute-done.6 = f32[8,640]{1,0:T(8,128)S(1)} collective-permute-done((f32[8,640]{1,0:T(8,128)S(1)}, f32[8,640]{1,0:T(8,128)S(1)}, u32[]{:S(2)}, u32[]{:S(2)}) %collective-permute-start.6) | collective-permute-done | bytes 20512 | tf_op jit(solution)/shard_map/ppermute | solution.py:26
  32.0 0.0 collective-permute-start.7
  32.0 1.2 %collective-permute-done.7 = f32[8,128]{1,0:T(8,128)S(1)} collective-permute-done((f32[8,128]{1,0:T(8,128)S(1)}, f32[8,128]{1,0:T(8,128)S(1)}, u32[]{:S(2)}, u32[]{:S(2)}) %collective-permute-start.7) | collective-permute-done | bytes 4128 | tf_op jit(solution)/shard_map/ppermute | solution.py:26
  33.2 2.4 %collective-permute-start.8 = (f32[8,128]{1,0:T(8,128)S(1)}, f32[8,128]{1,0:T(8,128)S(1)}, u32[]{:S(2)}, u32[]{:S(2)}) collective-permute-start(f32[8,128]{1,0:T(8,128)S(1)} %add.101), channel_id=1, source_target_pairs={{0,8},{4,12},{8,0},{12,4},{16,24},{20,28},{24,16},{28,20},{1,9},{5... | collective-permute-start | bytes 12296 | tf_op jit(solution)/shard_map/ppermute | solution.py:26
  35.6 1.6 %collective-permute-done.8 = f32[8,128]{1,0:T(8,128)S(1)} collective-permute-done((f32[8,128]{1,0:T(8,128)S(1)}, f32[8,128]{1,0:T(8,128)S(1)}, u32[]{:S(2)}, u32[]{:S(2)}) %collective-permute-start.8) | collective-permute-done | bytes 4128 | tf_op jit(solution)/shard_map/ppermute | solution.py:26
  37.2 3.0 %collective-permute-start.9 = (f32[8,128]{1,0:T(8,128)S(1)}, f32[8,128]{1,0:T(8,128)S(1)}, u32[]{:S(2)}, u32[]{:S(2)}) collective-permute-start(f32[8,128]{1,0:T(8,128)S(1)} %add.102), channel_id=1, source_target_pairs={{0,16},{4,20},{8,24},{12,28},{16,0},{20,4},{24,8},{28,12},{1,17},{... | collective-permute-start | bytes 12296 | tf_op jit(solution)/shard_map/ppermute | solution.py:26
  40.2 0.6 %slice_add_fusion.1 = f32[8,512]{1,0:T(8,128)} fusion(f32[8,640]{1,0:T(8,128)S(1)} %collective-permute-done.6, f32[8,1024]{1,0:T(8,128)S(1)} %slice_add_fusion), kind=kLoop, calls=%fused_computation.22 | loop fusion | flops 4096 | bytes 49152 | tf_op jit(solution)/shard_map/add | solution.py:60
  40.8 1.0 %collective-permute-done.9 = f32[8,128]{1,0:T(8,128)S(1)} collective-permute-done((f32[8,128]{1,0:T(8,128)S(1)}, f32[8,128]{1,0:T(8,128)S(1)}, u32[]{:S(2)}, u32[]{:S(2)}) %collective-permute-start.9) | collective-permute-done | bytes 4128 | tf_op jit(solution)/shard_map/ppermute | solution.py:26
  41.8 0.7 %fusion.25 = (f32[8,8]{1,0:T(8,128)}, f32[8,8]{1,0:T(8,128)}) fusion(f32[8,128]{1,0:T(8,128)S(1)} %add_multiply_fusion), kind=kLoop, calls=%fused_computation.66 | loop fusion | bytes 1024 | tf_op jit(solution)/shard_map/slice | solution.py:175
  (22 shorter events, 0.2 us)
Async XLA Ops:
  0.6 1.9 %collective-permute-start = (f32[8,512]{1,0:T(8,128)}, f32[8,512]{1,0:T(8,128)S(1)}, u32[]{:S(2)}, u32[]{:S(2)}) collective-permute-start(f32[8,512]{1,0:T(8,128)} %param.7), channel_id=1, source_target_pairs={{0,4},{4,0},{8,12},{12,8},{16,20},{20,16},{24,28},{28,24},{1,5},{5... | collective-permute-start | bytes 49160 | tf_op jit(solution)/shard_map/ppermute | solution.py:26
  2.5 4.6 %collective-permute-start.1 = (f32[8,1024]{1,0:T(8,128)S(1)}, f32[8,1024]{1,0:T(8,128)S(1)}, u32[]{:S(2)}, u32[]{:S(2)}) collective-permute-start(f32[8,1024]{1,0:T(8,128)S(1)} %get-tuple-element.21), channel_id=1, source_target_pairs={{0,1},{1,0},{2,3},{3,2},{4,5},{5,4},{6,7},{7,6},{8,9},{9,8},{10,11... | collective-permute-start | bytes 98312 | tf_op jit(solution)/shard_map/ppermute | solution.py:26
  7.2 4.3 %collective-permute-start.2 = (f32[8,2048]{1,0:T(8,128)S(1)}, f32[8,2048]{1,0:T(8,128)S(1)}, u32[]{:S(2)}, u32[]{:S(2)}) collective-permute-start(f32[8,2048]{1,0:T(8,128)S(1)} %get-tuple-element.17), channel_id=1, source_target_pairs={{0,2},{1,3},{2,0},{3,1},{4,6},{5,7},{6,4},{7,5},{8,10},{9,11},{10,... | collective-permute-start | bytes 196616 | tf_op jit(solution)/shard_map/ppermute | solution.py:26
  11.4 6.4 %collective-permute-start.3 = (f32[8,4096]{1,0:T(8,128)S(1)}, f32[8,4096]{1,0:T(8,128)S(1)}, u32[]{:S(2)}, u32[]{:S(2)}) collective-permute-start(f32[8,4096]{1,0:T(8,128)S(1)} %constant_dynamic-update-slice_fusion.5), channel_id=1, source_target_pairs={{0,8},{8,16},{16,24},{12,4},{20,12},{28,20},{1,9},{9,17},{17,25},{... | collective-permute-start | bytes 393224 | tf_op jit(solution)/shard_map/ppermute | solution.py:118
  17.8 1.4 %collective-permute-start.4 = (f32[8,4096]{1,0:T(8,128)S(1)}, f32[8,4096]{1,0:T(8,128)S(1)}, u32[]{:S(2)}, u32[]{:S(2)}) collective-permute-start(f32[8,4096]{1,0:T(8,128)S(1)} %collective-permute-done.3), channel_id=1, source_target_pairs={{0,4},{4,0},{8,12},{12,8},{16,20},{20,16},{24,28},{28,24},{1,5},{5... | collective-permute-start | bytes 393224 | tf_op jit(solution)/shard_map/ppermute | solution.py:26
  24.1 4.0 %collective-permute-start.5 = (f32[8,1152]{1,0:T(8,128)S(1)}, f32[8,1152]{1,0:T(8,128)S(1)}, u32[]{:S(2)}, u32[]{:S(2)}) collective-permute-start(f32[8,1152]{1,0:T(8,128)S(1)} %concatenate.29), channel_id=1, source_target_pairs={{0,2},{1,3},{2,0},{3,1},{4,6},{5,7},{6,4},{7,5},{8,10},{9,11},{10,... | collective-permute-start | bytes 110600 | tf_op jit(solution)/shard_map/ppermute | solution.py:26
  28.2 3.8 %collective-permute-start.6 = (f32[8,640]{1,0:T(8,128)S(1)}, f32[8,640]{1,0:T(8,128)S(1)}, u32[]{:S(2)}, u32[]{:S(2)}) collective-permute-start(f32[8,640]{1,0:T(8,128)S(1)} %pad_maximum_fusion), channel_id=1, source_target_pairs={{0,1},{1,0},{2,3},{3,2},{4,5},{5,4},{6,7},{7,6},{8,9},{9,8},{10,11... | collective-permute-start | bytes 61448 | tf_op jit(solution)/shard_map/ppermute | solution.py:26
  32.0 1.2 %collective-permute-start.7 = (f32[8,128]{1,0:T(8,128)S(1)}, f32[8,128]{1,0:T(8,128)S(1)}, u32[]{:S(2)}, u32[]{:S(2)}) collective-permute-start(f32[8,128]{1,0:T(8,128)S(1)} %slice_add_fusion.2), channel_id=1, source_target_pairs={{0,4},{4,0},{8,12},{12,8},{16,20},{20,16},{24,28},{28,24},{1,5},{5... | collective-permute-start | bytes 12296 | tf_op jit(solution)/shard_map/ppermute | solution.py:26
  33.2 4.0 %collective-permute-start.8 = (f32[8,128]{1,0:T(8,128)S(1)}, f32[8,128]{1,0:T(8,128)S(1)}, u32[]{:S(2)}, u32[]{:S(2)}) collective-permute-start(f32[8,128]{1,0:T(8,128)S(1)} %add.101), channel_id=1, source_target_pairs={{0,8},{4,12},{8,0},{12,4},{16,24},{20,28},{24,16},{28,20},{1,9},{5... | collective-permute-start | bytes 12296 | tf_op jit(solution)/shard_map/ppermute | solution.py:26
  37.2 4.6 %collective-permute-start.9 = (f32[8,128]{1,0:T(8,128)S(1)}, f32[8,128]{1,0:T(8,128)S(1)}, u32[]{:S(2)}, u32[]{:S(2)}) collective-permute-start(f32[8,128]{1,0:T(8,128)S(1)} %add.102), channel_id=1, source_target_pairs={{0,16},{4,20},{8,24},{12,28},{16,0},{20,4},{24,8},{28,12},{1,17},{... | collective-permute-start | bytes 12296 | tf_op jit(solution)/shard_map/ppermute | solution.py:26

commit v16 on v15

--- a/solution.py
+++ b/solution.py
@@ -106,13 +106,12 @@
         own_pair = jnp.concatenate([vectors, exchanged(vectors, "blk", 1)], axis=1)
         vectors, _ = lax.optimization_barrier((vectors, own_pair))
         own_pair = jnp.concatenate([own_pair, exchanged(own_pair, "help", 1)], axis=1)
-        tile_row, tile_col, counts, _ = lax.optimization_barrier(
-            (tile_row, tile_col, counts, own_pair)
-        )
+        tile_col, _ = lax.optimization_barrier((tile_col, own_pair))
         mask = 2
         while mask < helpers:
             own_pair = jnp.concatenate([own_pair, exchanged(own_pair, "help", mask)], axis=1)
             mask *= 2
+        tile_row, counts, _ = lax.optimization_barrier((tile_row, counts, own_pair))
         crossing = [(b, b + 2) for b in range(0, groups - 2, 2)]
         crossing += [(b, b - 2) for b in range(3, groups, 2)]
         remote = lax.ppermute(own_pair, "blk", crossing)

time: 43 us -> 43 us (level)
    ppermute x9, waiting for transfers between devices: 11 us -> 12.3 us  [exchanged(): lax.ppermute(value, axis, [(source, source ^ mask) for source in range(co...]
    ppermute x1, waiting for transfers between devices: 2.45 us -> 1.09 us  [local(): remote = lax.ppermute(own_pair, 'blk', crossing)]
where the time goes in v16:
time: 43 us; the launch traced here: 42.5 us
  starting transfers between devices  17.5 us (41%)
  waiting for transfers between devices  13.4 us (31%)
  matrix products  4.93 us (11%)
  other arithmetic  3.44 us (8%)
  local copies, waits for them, and re-layouts  2.45 us (6%)
  between operations  0.75 us (2%)
    ppermute x9, starting transfers between devices, exchanged(): lax.ppermute(value, axis, [(source, source ^ mask) for source in range(co...  13.6 us
    ppermute x9, waiting for transfers between devices, exchanged(): lax.ppermute(value, axis, [(source, source ^ mask) for source in range(co...  12.3 us
    ppermute x1, starting transfers between devices, local(): remote = lax.ppermute(own_pair, 'blk', crossing)  3.87 us
    dot_general x1, matrix products, batch_product(): jnp.einsum('osit,ostu->osiu', pieces, tile_blocks[0, first:last:step], pr...  3.18 us
    concatenate x2, other arithmetic, batch_product(): pieces = stacked[panel_ids[:, None], column_place[first:last:step]]  1.37 us
    ppermute x1, waiting for transfers between devices, local(): remote = lax.ppermute(own_pair, 'blk', crossing)  1.09 us
    dot_general x1, matrix products, local(): jnp.dot(vectors, vectors.T, precision=lax.Precision.HIGHEST, preferred_el...  0.92 us
  transfers between devices with their start and end apart: 10, of which 9 were waited for; matrix products, arithmetic and copies ran while one was open for 12% of the time, Pallas kernels for 0%

profile of v16, /device:TPU:0, one launch (start us, length us, event | category | flops | bytes accessed | tf_op | source)
XLA Modules:
  0.0 42.5 jit_solution(598611973914933764)
XLA Ops:
  0.6 0.5 %collective-permute-start = (f32[8,512]{1,0:T(8,128)}, f32[8,512]{1,0:T(8,128)S(1)}, u32[]{:S(2)}, u32[]{:S(2)}) collective-permute-start(f32[8,512]{1,0:T(8,128)} %param.7), channel_id=1, source_target_pairs={{0,4},{4,0},{8,12},{12,8},{16,20},{20,16},{24,28},{28,24},{1,5},{5... | collective-permute-start | bytes 49160 | tf_op jit(solution)/shard_map/ppermute | solution.py:26
  1.1 0.7 %fusion.20 = s32[5]{0:T(128)S(1)} fusion(s32[5]{0:T(128)} %constant.71.clone, s32[5]{0:T(128)} %constant.72.clone, pred[]{:T(512)S(6)} %eq.24), kind=kLoop, calls=%fused_computation.61 | loop fusion | flops 30 | bytes 61 | tf_op jit(solution)/shard_map/concatenate | solution.py:137
  1.8 0.7 %constant_dynamic-update-slice_fusion.4 = (f32[8,2048]{1,0:T(8,128)S(1)}, f32[8,1024]{1,0:T(8,128)S(1)}, f32[8,4096]{1,0:T(8,128)S(1)}) fusion(f32[8,512]{1,0:T(8,128)} %param.7), kind=kLoop, calls=%fused_computation.10 | loop fusion | bytes 65536
  2.5 0.0 collective-permute-done
  2.5 2.6 %collective-permute-start.1 = (f32[8,1024]{1,0:T(8,128)S(1)}, f32[8,1024]{1,0:T(8,128)S(1)}, u32[]{:S(2)}, u32[]{:S(2)}) collective-permute-start(f32[8,1024]{1,0:T(8,128)S(1)} %get-tuple-element.21), channel_id=1, source_target_pairs={{0,1},{1,0},{2,3},{3,2},{4,5},{5,4},{6,7},{7,6},{8,9},{9,8},{10,11... | collective-permute-start | bytes 98312 | tf_op jit(solution)/shard_map/ppermute | solution.py:26
  5.1 0.9 %fusion.27 = f32[8,8]{1,0:T(8,128)S(1)} fusion(f32[8,512]{1,0:T(8,128)} %param.7), kind=kOutput, calls=%fused_computation.68 | convolution fusion | flops 393216 | bytes 16640 | tf_op jit(solution)/shard_map/dot_general | solution.py:162
  6.1 1.1 %collective-permute-done.1 = f32[8,1024]{1,0:T(8,128)S(1)} collective-permute-done((f32[8,1024]{1,0:T(8,128)S(1)}, f32[8,1024]{1,0:T(8,128)S(1)}, u32[]{:S(2)}, u32[]{:S(2)}) %collective-permute-start.1) | collective-permute-done | bytes 32800 | tf_op jit(solution)/shard_map/ppermute | solution.py:26
  7.2 1.9 %collective-permute-start.2 = (f32[8,2048]{1,0:T(8,128)S(1)}, f32[8,2048]{1,0:T(8,128)S(1)}, u32[]{:S(2)}, u32[]{:S(2)}) collective-permute-start(f32[8,2048]{1,0:T(8,128)S(1)} %get-tuple-element.17), channel_id=1, source_target_pairs={{0,2},{1,3},{2,0},{3,1},{4,6},{5,7},{6,4},{7,5},{8,10},{9,11},{10,... | collective-permute-start | bytes 196616 | tf_op jit(solution)/shard_map/ppermute | solution.py:26
  9.1 0.7 %fusion.18 = s32[5,3,1]{0,2,1:T(1,128)S(1)} fusion(s32[1,5,3]{1,0,2:T(1,128)} %param.10, s32[5]{0:T(128)S(1)} %fusion.20, s32[]{:T(128)S(6)} %axis_index.22), kind=kLoop, calls=%fused_computation.57 | loop fusion | flops 420 | bytes 144 | tf_op jit(solution)/shard_map/concatenate | solution.py:137
  9.8 0.1 copy.23
  9.9 0.1 reshape.229
  10.0 1.5 %collective-permute-done.2 = f32[8,2048]{1,0:T(8,128)S(1)} collective-permute-done((f32[8,2048]{1,0:T(8,128)S(1)}, f32[8,2048]{1,0:T(8,128)S(1)}, u32[]{:S(2)}, u32[]{:S(2)}) %collective-permute-start.2) | collective-permute-done | bytes 65568 | tf_op jit(solution)/shard_map/ppermute | solution.py:26
  11.4 3.9 %collective-permute-start.3 = (f32[8,4096]{1,0:T(8,128)S(1)}, f32[8,4096]{1,0:T(8,128)S(1)}, u32[]{:S(2)}, u32[]{:S(2)}) collective-permute-start(f32[8,4096]{1,0:T(8,128)S(1)} %constant_dynamic-update-slice_fusion.5), channel_id=1, source_target_pairs={{0,8},{8,16},{16,24},{12,4},{20,12},{28,20},{1,9},{9,17},{17,25},{... | collective-permute-start | bytes 393224 | tf_op jit(solution)/shard_map/ppermute | solution.py:117
  15.3 0.7 %fusion.10 = s32[5,3]{0,1:T(4,128)S(1)} fusion(s32[1,5,3]{1,0,2:T(1,128)} %param.9, s32[]{:T(128)S(6)} %axis_index.22), kind=kLoop, calls=%fused_computation.46 | loop fusion | flops 330 | bytes 124 | tf_op jit(solution)/shard_map/add | solution.py:101
  16.0 0.7 %fusion.12 = f32[5,3]{0,1:T(4,128)S(1)} fusion(s32[5]{0:T(128)} %bitcast.79), kind=kLoop, calls=%fused_computation.51 | loop fusion | flops 30 | bytes 80 | tf_op jit(solution)/shard_map/convert_element_type | solution.py:129
  16.7 1.1 %collective-permute-done.3 = f32[8,4096]{1,0:T(8,128)S(1)} collective-permute-done((f32[8,4096]{1,0:T(8,128)S(1)}, f32[8,4096]{1,0:T(8,128)S(1)}, u32[]{:S(2)}, u32[]{:S(2)}) %collective-permute-start.3) | collective-permute-done | bytes 131104 | tf_op jit(solution)/shard_map/ppermute | solution.py:117
  17.8 0.1 collective-permute-start.4
  17.9 1.3 %collective-permute-done.4 = f32[8,4096]{1,0:T(8,128)S(1)} collective-permute-done((f32[8,4096]{1,0:T(8,128)S(1)}, f32[8,4096]{1,0:T(8,128)S(1)}, u32[]{:S(2)}, u32[]{:S(2)}) %collective-permute-start.4) | collective-permute-done | bytes 131104 | tf_op jit(solution)/shard_map/ppermute | solution.py:26
  19.3 0.6 %gather_fusion = f32[15,8,256]{2,1,0:T(8,128)S(1)} fusion(f32[6,8,8,256]{3,2,1,0:T(8,128)S(1)} %bitcast.78, s32[15]{0:T(128)S(1)} %reshape.229), kind=kCustom, calls=%fused_computation | custom fusion | bytes 245880 | tf_op jit(solution)/shard_map/gather | solution.py:137
  19.9 3.2 %fusion = f32[5,3,8,256]{3,2,1,0:T(8,128)S(1)} fusion(f32[5,3,8,256]{3,2,1,0:T(8,128)S(1)} %bitcast.69, f32[1,5,3,256,256]{4,3,2,1,0:T(8,128)} %param.8), kind=kOutput, calls=%fused_computation.1 | convolution fusion | flops 47185920 | bytes 4177920 | tf_op jit(solution)/shard_map/osit,ostu->osiu/dot_general | solution.py:138
  23.1 0.6 %convolution_bitcast_fusion = f32[1,8,8,256]{3,2,1,0:T(8,128)S(1)} fusion(f32[5,3,8,256]{3,2,1,0:T(8,128)S(1)} %fusion, f32[5,3]{0,1:T(4,128)S(1)} %fusion.12, s32[5,3]{0,1:T(4,128)S(1)} %fusion.10), kind=kOutput, calls=%fused_computation.3 | convolution fusion | flops 2949360 | bytes 188536 | tf_op jit(solution)/shard_map/osiu,osr->iru/dot_general | solution.py:144
  23.8 0.2 fusion.26
  24.0 0.1 concatenate.29
  24.1 1.5 %collective-permute-start.5 = (f32[8,1152]{1,0:T(8,128)S(1)}, f32[8,1152]{1,0:T(8,128)S(1)}, u32[]{:S(2)}, u32[]{:S(2)}) collective-permute-start(f32[8,1152]{1,0:T(8,128)S(1)} %concatenate.29), channel_id=1, source_target_pairs={{0,2},{1,3},{2,0},{3,1},{4,6},{5,7},{6,4},{7,5},{8,10},{9,11},{10,... | collective-permute-start | bytes 110600 | tf_op jit(solution)/shard_map/ppermute | solution.py:26
  25.6 2.4 %collective-permute-done.5 = f32[8,1152]{1,0:T(8,128)S(1)} collective-permute-done((f32[8,1152]{1,0:T(8,128)S(1)}, f32[8,1152]{1,0:T(8,128)S(1)}, u32[]{:S(2)}, u32[]{:S(2)}) %collective-permute-start.5) | collective-permute-done | bytes 36896 | tf_op jit(solution)/shard_map/ppermute | solution.py:26
  28.1 0.1 slice_add_fusion.3
  28.2 1.5 %collective-permute-start.6 = (f32[8,640]{1,0:T(8,128)S(1)}, f32[8,640]{1,0:T(8,128)S(1)}, u32[]{:S(2)}, u32[]{:S(2)}) collective-permute-start(f32[8,640]{1,0:T(8,128)S(1)} %pad_maximum_fusion), channel_id=1, source_target_pairs={{0,1},{1,0},{2,3},{3,2},{4,5},{5,4},{6,7},{7,6},{8,9},{9,8},{10,11... | collective-permute-start | bytes 61448 | tf_op jit(solution)/shard_map/ppermute | solution.py:26
  29.7 2.3 %collective-permute-done.6 = f32[8,640]{1,0:T(8,128)S(1)} collective-permute-done((f32[8,640]{1,0:T(8,128)S(1)}, f32[8,640]{1,0:T(8,128)S(1)}, u32[]{:S(2)}, u32[]{:S(2)}) %collective-permute-start.6) | collective-permute-done | bytes 20512 | tf_op jit(solution)/shard_map/ppermute | solution.py:26
  32.0 0.0 collective-permute-start.7
  32.0 1.2 %collective-permute-done.7 = f32[8,128]{1,0:T(8,128)S(1)} collective-permute-done((f32[8,128]{1,0:T(8,128)S(1)}, f32[8,128]{1,0:T(8,128)S(1)}, u32[]{:S(2)}, u32[]{:S(2)}) %collective-permute-start.7) | collective-permute-done | bytes 4128 | tf_op jit(solution)/shard_map/ppermute | solution.py:26
  33.2 2.4 %collective-permute-start.8 = (f32[8,128]{1,0:T(8,128)S(1)}, f32[8,128]{1,0:T(8,128)S(1)}, u32[]{:S(2)}, u32[]{:S(2)}) collective-permute-start(f32[8,128]{1,0:T(8,128)S(1)} %add.101), channel_id=1, source_target_pairs={{0,8},{4,12},{8,0},{12,4},{16,24},{20,28},{24,16},{28,20},{1,9},{5... | collective-permute-start | bytes 12296 | tf_op jit(solution)/shard_map/ppermute | solution.py:26
  35.6 1.6 %collective-permute-done.8 = f32[8,128]{1,0:T(8,128)S(1)} collective-permute-done((f32[8,128]{1,0:T(8,128)S(1)}, f32[8,128]{1,0:T(8,128)S(1)}, u32[]{:S(2)}, u32[]{:S(2)}) %collective-permute-start.8) | collective-permute-done | bytes 4128 | tf_op jit(solution)/shard_map/ppermute | solution.py:26
  37.2 3.0 %collective-permute-start.9 = (f32[8,128]{1,0:T(8,128)S(1)}, f32[8,128]{1,0:T(8,128)S(1)}, u32[]{:S(2)}, u32[]{:S(2)}) collective-permute-start(f32[8,128]{1,0:T(8,128)S(1)} %add.102), channel_id=1, source_target_pairs={{0,16},{4,20},{8,24},{12,28},{16,0},{20,4},{24,8},{28,12},{1,17},{... | collective-permute-start | bytes 12296 | tf_op jit(solution)/shard_map/ppermute | solution.py:26
  40.2 0.6 %slice_add_fusion.1 = f32[8,512]{1,0:T(8,128)} fusion(f32[8,640]{1,0:T(8,128)S(1)} %collective-permute-done.6, f32[8,1024]{1,0:T(8,128)S(1)} %slice_add_fusion), kind=kLoop, calls=%fused_computation.22 | loop fusion | flops 4096 | bytes 49152 | tf_op jit(solution)/shard_map/add | solution.py:60
  40.8 1.0 %collective-permute-done.9 = f32[8,128]{1,0:T(8,128)S(1)} collective-permute-done((f32[8,128]{1,0:T(8,128)S(1)}, f32[8,128]{1,0:T(8,128)S(1)}, u32[]{:S(2)}, u32[]{:S(2)}) %collective-permute-start.9) | collective-permute-done | bytes 4128 | tf_op jit(solution)/shard_map/ppermute | solution.py:26
  41.8 0.7 %fusion.25 = (f32[8,8]{1,0:T(8,128)}, f32[8,8]{1,0:T(8,128)}) fusion(f32[8,128]{1,0:T(8,128)S(1)} %add_multiply_fusion), kind=kLoop, calls=%fused_computation.66 | loop fusion | bytes 1024 | tf_op jit(solution)/shard_map/slice | solution.py:174
  (22 shorter events, 0.2 us)
Async XLA Ops:
  0.6 1.9 %collective-permute-start = (f32[8,512]{1,0:T(8,128)}, f32[8,512]{1,0:T(8,128)S(1)}, u32[]{:S(2)}, u32[]{:S(2)}) collective-permute-start(f32[8,512]{1,0:T(8,128)} %param.7), channel_id=1, source_target_pairs={{0,4},{4,0},{8,12},{12,8},{16,20},{20,16},{24,28},{28,24},{1,5},{5... | collective-permute-start | bytes 49160 | tf_op jit(solution)/shard_map/ppermute | solution.py:26
  2.5 4.6 %collective-permute-start.1 = (f32[8,1024]{1,0:T(8,128)S(1)}, f32[8,1024]{1,0:T(8,128)S(1)}, u32[]{:S(2)}, u32[]{:S(2)}) collective-permute-start(f32[8,1024]{1,0:T(8,128)S(1)} %get-tuple-element.21), channel_id=1, source_target_pairs={{0,1},{1,0},{2,3},{3,2},{4,5},{5,4},{6,7},{7,6},{8,9},{9,8},{10,11... | collective-permute-start | bytes 98312 | tf_op jit(solution)/shard_map/ppermute | solution.py:26
  7.2 4.3 %collective-permute-start.2 = (f32[8,2048]{1,0:T(8,128)S(1)}, f32[8,2048]{1,0:T(8,128)S(1)}, u32[]{:S(2)}, u32[]{:S(2)}) collective-permute-start(f32[8,2048]{1,0:T(8,128)S(1)} %get-tuple-element.17), channel_id=1, source_target_pairs={{0,2},{1,3},{2,0},{3,1},{4,6},{5,7},{6,4},{7,5},{8,10},{9,11},{10,... | collective-permute-start | bytes 196616 | tf_op jit(solution)/shard_map/ppermute | solution.py:26
  11.4 6.4 %collective-permute-start.3 = (f32[8,4096]{1,0:T(8,128)S(1)}, f32[8,4096]{1,0:T(8,128)S(1)}, u32[]{:S(2)}, u32[]{:S(2)}) collective-permute-start(f32[8,4096]{1,0:T(8,128)S(1)} %constant_dynamic-update-slice_fusion.5), channel_id=1, source_target_pairs={{0,8},{8,16},{16,24},{12,4},{20,12},{28,20},{1,9},{9,17},{17,25},{... | collective-permute-start | bytes 393224 | tf_op jit(solution)/shard_map/ppermute | solution.py:117
  17.8 1.4 %collective-permute-start.4 = (f32[8,4096]{1,0:T(8,128)S(1)}, f32[8,4096]{1,0:T(8,128)S(1)}, u32[]{:S(2)}, u32[]{:S(2)}) collective-permute-start(f32[8,4096]{1,0:T(8,128)S(1)} %collective-permute-done.3), channel_id=1, source_target_pairs={{0,4},{4,0},{8,12},{12,8},{16,20},{20,16},{24,28},{28,24},{1,5},{5... | collective-permute-start | bytes 393224 | tf_op jit(solution)/shard_map/ppermute | solution.py:26
  24.1 4.0 %collective-permute-start.5 = (f32[8,1152]{1,0:T(8,128)S(1)}, f32[8,1152]{1,0:T(8,128)S(1)}, u32[]{:S(2)}, u32[]{:S(2)}) collective-permute-start(f32[8,1152]{1,0:T(8,128)S(1)} %concatenate.29), channel_id=1, source_target_pairs={{0,2},{1,3},{2,0},{3,1},{4,6},{5,7},{6,4},{7,5},{8,10},{9,11},{10,... | collective-permute-start | bytes 110600 | tf_op jit(solution)/shard_map/ppermute | solution.py:26
  28.2 3.8 %collective-permute-start.6 = (f32[8,640]{1,0:T(8,128)S(1)}, f32[8,640]{1,0:T(8,128)S(1)}, u32[]{:S(2)}, u32[]{:S(2)}) collective-permute-start(f32[8,640]{1,0:T(8,128)S(1)} %pad_maximum_fusion), channel_id=1, source_target_pairs={{0,1},{1,0},{2,3},{3,2},{4,5},{5,4},{6,7},{7,6},{8,9},{9,8},{10,11... | collective-permute-start | bytes 61448 | tf_op jit(solution)/shard_map/ppermute | solution.py:26
  32.0 1.2 %collective-permute-start.7 = (f32[8,128]{1,0:T(8,128)S(1)}, f32[8,128]{1,0:T(8,128)S(1)}, u32[]{:S(2)}, u32[]{:S(2)}) collective-permute-start(f32[8,128]{1,0:T(8,128)S(1)} %slice_add_fusion.2), channel_id=1, source_target_pairs={{0,4},{4,0},{8,12},{12,8},{16,20},{20,16},{24,28},{28,24},{1,5},{5... | collective-permute-start | bytes 12296 | tf_op jit(solution)/shard_map/ppermute | solution.py:26
  33.2 4.0 %collective-permute-start.8 = (f32[8,128]{1,0:T(8,128)S(1)}, f32[8,128]{1,0:T(8,128)S(1)}, u32[]{:S(2)}, u32[]{:S(2)}) collective-permute-start(f32[8,128]{1,0:T(8,128)S(1)} %add.101), channel_id=1, source_target_pairs={{0,8},{4,12},{8,0},{12,4},{16,24},{20,28},{24,16},{28,20},{1,9},{5... | collective-permute-start | bytes 12296 | tf_op jit(solution)/shard_map/ppermute | solution.py:26
  37.2 4.6 %collective-permute-start.9 = (f32[8,128]{1,0:T(8,128)S(1)}, f32[8,128]{1,0:T(8,128)S(1)}, u32[]{:S(2)}, u32[]{:S(2)}) collective-permute-start(f32[8,128]{1,0:T(8,128)S(1)} %add.102), channel_id=1, source_target_pairs={{0,16},{4,20},{8,24},{12,28},{16,0},{20,4},{24,8},{28,12},{1,17},{... | collective-permute-start | bytes 12296 | tf_op jit(solution)/shard_map/ppermute | solution.py:26

commit v17 on v15

--- a/solution.py
+++ b/solution.py
@@ -146,7 +146,7 @@
             "osiu,osr->iru",
             contribution,
             one_hot[first:last:step],
-            precision=lax.Precision.HIGHEST,
+            precision=lax.Precision.HIGH,
         )
 
     if paired:
@@ -164,7 +164,7 @@
         vectors, vectors.T, precision=lax.Precision.HIGHEST, preferred_element_type=jnp.float32
     )
     energy_term = jnp.dot(
-        full_panel, flattened.T, precision=lax.Precision.HIGHEST, preferred_element_type=jnp.float32
+        full_panel, flattened.T, precision=lax.Precision.HIGH, preferred_element_type=jnp.float32
     )
     gram = jnp.concatenate(
         [energy_term, correlation_term, jnp.zeros((VEC, GRAM_PAD - 2 * VEC), jnp.float32)], axis=1

time: 43 us -> 42.6 us (level)
  no operation moved by 1% of the time
where the time goes in v17:
time: 42.6 us; the launch traced here: 42.2 us
  starting transfers between devices  17.5 us (41%)
  waiting for transfers between devices  13.4 us (31%)
  matrix products  4.62 us (11%)
  other arithmetic  3.44 us (8%)
  local copies, waits for them, and re-layouts  2.45 us (6%)
  between operations  0.76 us (2%)
    ppermute x9, starting transfers between devices, exchanged(): lax.ppermute(value, axis, [(source, source ^ mask) for source in range(co...  13.6 us
    ppermute x9, waiting for transfers between devices, exchanged(): lax.ppermute(value, axis, [(source, source ^ mask) for source in range(co...  11 us
    ppermute x1, starting transfers between devices, local(): remote = lax.ppermute(own_pair, 'blk', crossing)  3.87 us
    dot_general x1, matrix products, batch_product(): jnp.einsum('osit,ostu->osiu', pieces, tile_blocks[0, first:last:step], pr...  3.18 us
    ppermute x1, waiting for transfers between devices, local(): remote = lax.ppermute(own_pair, 'blk', crossing)  2.45 us
    concatenate x2, other arithmetic, batch_product(): pieces = stacked[panel_ids[:, None], column_place[first:last:step]]  1.37 us
    dot_general x1, matrix products, local(): jnp.dot(vectors, vectors.T, precision=lax.Precision.HIGHEST, preferred_el...  0.92 us
  transfers between devices with their start and end apart: 10, of which 9 were waited for; matrix products, arithmetic and copies ran while one was open for 12% of the time, Pallas kernels for 0%

profile of v17, /device:TPU:0, one launch (start us, length us, event | category | flops | bytes accessed | tf_op | source)
XLA Modules:
  0.0 42.2 jit_solution(676770870975315447)
XLA Ops:
  0.6 0.5 %collective-permute-start = (f32[8,512]{1,0:T(8,128)}, f32[8,512]{1,0:T(8,128)S(1)}, u32[]{:S(2)}, u32[]{:S(2)}) collective-permute-start(f32[8,512]{1,0:T(8,128)} %param.7), channel_id=1, source_target_pairs={{0,4},{4,0},{8,12},{12,8},{16,20},{20,16},{24,28},{28,24},{1,5},{5... | collective-permute-start | bytes 49160 | tf_op jit(solution)/shard_map/ppermute | solution.py:26
  1.1 0.7 %fusion.20 = s32[5]{0:T(128)S(1)} fusion(s32[5]{0:T(128)} %constant.71.clone, s32[5]{0:T(128)} %constant.72.clone, pred[]{:T(512)S(6)} %eq.24), kind=kLoop, calls=%fused_computation.61 | loop fusion | flops 30 | bytes 61 | tf_op jit(solution)/shard_map/concatenate | solution.py:138
  1.8 0.7 %constant_dynamic-update-slice_fusion.4 = (f32[8,2048]{1,0:T(8,128)S(1)}, f32[8,1024]{1,0:T(8,128)S(1)}, f32[8,4096]{1,0:T(8,128)S(1)}) fusion(f32[8,512]{1,0:T(8,128)} %param.7), kind=kLoop, calls=%fused_computation.10 | loop fusion | bytes 65536
  2.5 0.0 collective-permute-done
  2.5 2.6 %collective-permute-start.1 = (f32[8,1024]{1,0:T(8,128)S(1)}, f32[8,1024]{1,0:T(8,128)S(1)}, u32[]{:S(2)}, u32[]{:S(2)}) collective-permute-start(f32[8,1024]{1,0:T(8,128)S(1)} %get-tuple-element.21), channel_id=1, source_target_pairs={{0,1},{1,0},{2,3},{3,2},{4,5},{5,4},{6,7},{7,6},{8,9},{9,8},{10,11... | collective-permute-start | bytes 98312 | tf_op jit(solution)/shard_map/ppermute | solution.py:26
  5.1 0.9 %fusion.27 = f32[8,8]{1,0:T(8,128)S(1)} fusion(f32[8,512]{1,0:T(8,128)} %param.7), kind=kOutput, calls=%fused_computation.68 | convolution fusion | flops 393216 | bytes 16640 | tf_op jit(solution)/shard_map/dot_general | solution.py:163
  6.1 1.1 %collective-permute-done.1 = f32[8,1024]{1,0:T(8,128)S(1)} collective-permute-done((f32[8,1024]{1,0:T(8,128)S(1)}, f32[8,1024]{1,0:T(8,128)S(1)}, u32[]{:S(2)}, u32[]{:S(2)}) %collective-permute-start.1) | collective-permute-done | bytes 32800 | tf_op jit(solution)/shard_map/ppermute | solution.py:26
  7.2 1.9 %collective-permute-start.2 = (f32[8,2048]{1,0:T(8,128)S(1)}, f32[8,2048]{1,0:T(8,128)S(1)}, u32[]{:S(2)}, u32[]{:S(2)}) collective-permute-start(f32[8,2048]{1,0:T(8,128)S(1)} %get-tuple-element.17), channel_id=1, source_target_pairs={{0,2},{1,3},{2,0},{3,1},{4,6},{5,7},{6,4},{7,5},{8,10},{9,11},{10,... | collective-permute-start | bytes 196616 | tf_op jit(solution)/shard_map/ppermute | solution.py:26
  9.1 0.7 %fusion.10 = s32[5,3]{0,1:T(4,128)S(1)} fusion(s32[1,5,3]{1,0,2:T(1,128)} %param.9, s32[]{:T(128)S(6)} %axis_index.22), kind=kLoop, calls=%fused_computation.46 | loop fusion | flops 330 | bytes 124 | tf_op jit(solution)/shard_map/add | solution.py:101
  9.8 0.7 %fusion.18 = s32[5,3,1]{0,2,1:T(1,128)S(1)} fusion(s32[1,5,3]{1,0,2:T(1,128)} %param.10, s32[5]{0:T(128)S(1)} %fusion.20, s32[]{:T(128)S(6)} %axis_index.22), kind=kLoop, calls=%fused_computation.57 | loop fusion | flops 420 | bytes 144 | tf_op jit(solution)/shard_map/concatenate | solution.py:138
  10.5 0.7 %fusion.12 = f32[5,3]{0,1:T(4,128)S(1)} fusion(s32[5]{0:T(128)} %bitcast.79), kind=kLoop, calls=%fused_computation.51 | loop fusion | flops 30 | bytes 80 | tf_op jit(solution)/shard_map/convert_element_type | solution.py:130
  11.1 0.1 copy.23
  11.2 0.1 reshape.229
  11.3 0.1 collective-permute-done.2
  11.4 3.9 %collective-permute-start.3 = (f32[8,4096]{1,0:T(8,128)S(1)}, f32[8,4096]{1,0:T(8,128)S(1)}, u32[]{:S(2)}, u32[]{:S(2)}) collective-permute-start(f32[8,4096]{1,0:T(8,128)S(1)} %constant_dynamic-update-slice_fusion.5), channel_id=1, source_target_pairs={{0,8},{8,16},{16,24},{12,4},{20,12},{28,20},{1,9},{9,17},{17,25},{... | collective-permute-start | bytes 393224 | tf_op jit(solution)/shard_map/ppermute | solution.py:118
  15.4 2.4 %collective-permute-done.3 = f32[8,4096]{1,0:T(8,128)S(1)} collective-permute-done((f32[8,4096]{1,0:T(8,128)S(1)}, f32[8,4096]{1,0:T(8,128)S(1)}, u32[]{:S(2)}, u32[]{:S(2)}) %collective-permute-start.3) | collective-permute-done | bytes 131104 | tf_op jit(solution)/shard_map/ppermute | solution.py:118
  17.8 0.1 collective-permute-start.4
  17.9 1.3 %collective-permute-done.4 = f32[8,4096]{1,0:T(8,128)S(1)} collective-permute-done((f32[8,4096]{1,0:T(8,128)S(1)}, f32[8,4096]{1,0:T(8,128)S(1)}, u32[]{:S(2)}, u32[]{:S(2)}) %collective-permute-start.4) | collective-permute-done | bytes 131104 | tf_op jit(solution)/shard_map/ppermute | solution.py:26
  19.3 0.6 %gather_fusion = f32[15,8,256]{2,1,0:T(8,128)S(1)} fusion(f32[6,8,8,256]{3,2,1,0:T(8,128)S(1)} %bitcast.78, s32[15]{0:T(128)S(1)} %reshape.229), kind=kCustom, calls=%fused_computation | custom fusion | bytes 245880 | tf_op jit(solution)/shard_map/gather | solution.py:138
  19.9 3.2 %fusion = f32[5,3,8,256]{3,2,1,0:T(8,128)S(1)} fusion(f32[5,3,8,256]{3,2,1,0:T(8,128)S(1)} %bitcast.69, f32[1,5,3,256,256]{4,3,2,1,0:T(8,128)} %param.8), kind=kOutput, calls=%fused_computation.1 | convolution fusion | flops 47185920 | bytes 4177920 | tf_op jit(solution)/shard_map/osit,ostu->osiu/dot_general | solution.py:139
  23.1 0.4 convolution_bitcast_fusion
  23.6 0.1 fusion.26
  23.7 0.1 concatenate.29
  23.8 1.5 %collective-permute-start.5 = (f32[8,1152]{1,0:T(8,128)S(1)}, f32[8,1152]{1,0:T(8,128)S(1)}, u32[]{:S(2)}, u32[]{:S(2)}) collective-permute-start(f32[8,1152]{1,0:T(8,128)S(1)} %concatenate.29), channel_id=1, source_target_pairs={{0,2},{1,3},{2,0},{3,1},{4,6},{5,7},{6,4},{7,5},{8,10},{9,11},{10,... | collective-permute-start | bytes 110600 | tf_op jit(solution)/shard_map/ppermute | solution.py:26
  25.3 2.4 %collective-permute-done.5 = f32[8,1152]{1,0:T(8,128)S(1)} collective-permute-done((f32[8,1152]{1,0:T(8,128)S(1)}, f32[8,1152]{1,0:T(8,128)S(1)}, u32[]{:S(2)}, u32[]{:S(2)}) %collective-permute-start.5) | collective-permute-done | bytes 36896 | tf_op jit(solution)/shard_map/ppermute | solution.py:26
  27.8 0.1 slice_add_fusion.3
  27.9 1.5 %collective-permute-start.6 = (f32[8,640]{1,0:T(8,128)S(1)}, f32[8,640]{1,0:T(8,128)S(1)}, u32[]{:S(2)}, u32[]{:S(2)}) collective-permute-start(f32[8,640]{1,0:T(8,128)S(1)} %pad_maximum_fusion), channel_id=1, source_target_pairs={{0,1},{1,0},{2,3},{3,2},{4,5},{5,4},{6,7},{7,6},{8,9},{9,8},{10,11... | collective-permute-start | bytes 61448 | tf_op jit(solution)/shard_map/ppermute | solution.py:26
  29.4 2.3 %collective-permute-done.6 = f32[8,640]{1,0:T(8,128)S(1)} collective-permute-done((f32[8,640]{1,0:T(8,128)S(1)}, f32[8,640]{1,0:T(8,128)S(1)}, u32[]{:S(2)}, u32[]{:S(2)}) %collective-permute-start.6) | collective-permute-done | bytes 20512 | tf_op jit(solution)/shard_map/ppermute | solution.py:26
  31.7 0.0 collective-permute-start.7
  31.7 1.2 %collective-permute-done.7 = f32[8,128]{1,0:T(8,128)S(1)} collective-permute-done((f32[8,128]{1,0:T(8,128)S(1)}, f32[8,128]{1,0:T(8,128)S(1)}, u32[]{:S(2)}, u32[]{:S(2)}) %collective-permute-start.7) | collective-permute-done | bytes 4128 | tf_op jit(solution)/shard_map/ppermute | solution.py:26
  32.8 2.4 %collective-permute-start.8 = (f32[8,128]{1,0:T(8,128)S(1)}, f32[8,128]{1,0:T(8,128)S(1)}, u32[]{:S(2)}, u32[]{:S(2)}) collective-permute-start(f32[8,128]{1,0:T(8,128)S(1)} %add.101), channel_id=1, source_target_pairs={{0,8},{4,12},{8,0},{12,4},{16,24},{20,28},{24,16},{28,20},{1,9},{5... | collective-permute-start | bytes 12296 | tf_op jit(solution)/shard_map/ppermute | solution.py:26
  35.3 1.6 %collective-permute-done.8 = f32[8,128]{1,0:T(8,128)S(1)} collective-permute-done((f32[8,128]{1,0:T(8,128)S(1)}, f32[8,128]{1,0:T(8,128)S(1)}, u32[]{:S(2)}, u32[]{:S(2)}) %collective-permute-start.8) | collective-permute-done | bytes 4128 | tf_op jit(solution)/shard_map/ppermute | solution.py:26
  36.9 3.0 %collective-permute-start.9 = (f32[8,128]{1,0:T(8,128)S(1)}, f32[8,128]{1,0:T(8,128)S(1)}, u32[]{:S(2)}, u32[]{:S(2)}) collective-permute-start(f32[8,128]{1,0:T(8,128)S(1)} %add.102), channel_id=1, source_target_pairs={{0,16},{4,20},{8,24},{12,28},{16,0},{20,4},{24,8},{28,12},{1,17},{... | collective-permute-start | bytes 12296 | tf_op jit(solution)/shard_map/ppermute | solution.py:26
  39.9 0.6 %slice_add_fusion.1 = f32[8,512]{1,0:T(8,128)} fusion(f32[8,640]{1,0:T(8,128)S(1)} %collective-permute-done.6, f32[8,1024]{1,0:T(8,128)S(1)} %slice_add_fusion), kind=kLoop, calls=%fused_computation.22 | loop fusion | flops 4096 | bytes 49152 | tf_op jit(solution)/shard_map/add | solution.py:60
  40.5 1.0 %collective-permute-done.9 = f32[8,128]{1,0:T(8,128)S(1)} collective-permute-done((f32[8,128]{1,0:T(8,128)S(1)}, f32[8,128]{1,0:T(8,128)S(1)}, u32[]{:S(2)}, u32[]{:S(2)}) %collective-permute-start.9) | collective-permute-done | bytes 4128 | tf_op jit(solution)/shard_map/ppermute | solution.py:26
  41.5 0.7 %fusion.25 = (f32[8,8]{1,0:T(8,128)}, f32[8,8]{1,0:T(8,128)}) fusion(f32[8,128]{1,0:T(8,128)S(1)} %add_multiply_fusion), kind=kLoop, calls=%fused_computation.66 | loop fusion | bytes 1024 | tf_op jit(solution)/shard_map/slice | solution.py:175
  (22 shorter events, 0.2 us)
Async XLA Ops:
  0.6 1.9 %collective-permute-start = (f32[8,512]{1,0:T(8,128)}, f32[8,512]{1,0:T(8,128)S(1)}, u32[]{:S(2)}, u32[]{:S(2)}) collective-permute-start(f32[8,512]{1,0:T(8,128)} %param.7), channel_id=1, source_target_pairs={{0,4},{4,0},{8,12},{12,8},{16,20},{20,16},{24,28},{28,24},{1,5},{5... | collective-permute-start | bytes 49160 | tf_op jit(solution)/shard_map/ppermute | solution.py:26
  2.5 4.6 %collective-permute-start.1 = (f32[8,1024]{1,0:T(8,128)S(1)}, f32[8,1024]{1,0:T(8,128)S(1)}, u32[]{:S(2)}, u32[]{:S(2)}) collective-permute-start(f32[8,1024]{1,0:T(8,128)S(1)} %get-tuple-element.21), channel_id=1, source_target_pairs={{0,1},{1,0},{2,3},{3,2},{4,5},{5,4},{6,7},{7,6},{8,9},{9,8},{10,11... | collective-permute-start | bytes 98312 | tf_op jit(solution)/shard_map/ppermute | solution.py:26
  7.2 4.3 %collective-permute-start.2 = (f32[8,2048]{1,0:T(8,128)S(1)}, f32[8,2048]{1,0:T(8,128)S(1)}, u32[]{:S(2)}, u32[]{:S(2)}) collective-permute-start(f32[8,2048]{1,0:T(8,128)S(1)} %get-tuple-element.17), channel_id=1, source_target_pairs={{0,2},{1,3},{2,0},{3,1},{4,6},{5,7},{6,4},{7,5},{8,10},{9,11},{10,... | collective-permute-start | bytes 196616 | tf_op jit(solution)/shard_map/ppermute | solution.py:26
  11.4 6.4 %collective-permute-start.3 = (f32[8,4096]{1,0:T(8,128)S(1)}, f32[8,4096]{1,0:T(8,128)S(1)}, u32[]{:S(2)}, u32[]{:S(2)}) collective-permute-start(f32[8,4096]{1,0:T(8,128)S(1)} %constant_dynamic-update-slice_fusion.5), channel_id=1, source_target_pairs={{0,8},{8,16},{16,24},{12,4},{20,12},{28,20},{1,9},{9,17},{17,25},{... | collective-permute-start | bytes 393224 | tf_op jit(solution)/shard_map/ppermute | solution.py:118
  17.8 1.4 %collective-permute-start.4 = (f32[8,4096]{1,0:T(8,128)S(1)}, f32[8,4096]{1,0:T(8,128)S(1)}, u32[]{:S(2)}, u32[]{:S(2)}) collective-permute-start(f32[8,4096]{1,0:T(8,128)S(1)} %collective-permute-done.3), channel_id=1, source_target_pairs={{0,4},{4,0},{8,12},{12,8},{16,20},{20,16},{24,28},{28,24},{1,5},{5... | collective-permute-start | bytes 393224 | tf_op jit(solution)/shard_map/ppermute | solution.py:26
  23.8 4.0 %collective-permute-start.5 = (f32[8,1152]{1,0:T(8,128)S(1)}, f32[8,1152]{1,0:T(8,128)S(1)}, u32[]{:S(2)}, u32[]{:S(2)}) collective-permute-start(f32[8,1152]{1,0:T(8,128)S(1)} %concatenate.29), channel_id=1, source_target_pairs={{0,2},{1,3},{2,0},{3,1},{4,6},{5,7},{6,4},{7,5},{8,10},{9,11},{10,... | collective-permute-start | bytes 110600 | tf_op jit(solution)/shard_map/ppermute | solution.py:26
  27.9 3.8 %collective-permute-start.6 = (f32[8,640]{1,0:T(8,128)S(1)}, f32[8,640]{1,0:T(8,128)S(1)}, u32[]{:S(2)}, u32[]{:S(2)}) collective-permute-start(f32[8,640]{1,0:T(8,128)S(1)} %pad_maximum_fusion), channel_id=1, source_target_pairs={{0,1},{1,0},{2,3},{3,2},{4,5},{5,4},{6,7},{7,6},{8,9},{9,8},{10,11... | collective-permute-start | bytes 61448 | tf_op jit(solution)/shard_map/ppermute | solution.py:26
  31.7 1.2 %collective-permute-start.7 = (f32[8,128]{1,0:T(8,128)S(1)}, f32[8,128]{1,0:T(8,128)S(1)}, u32[]{:S(2)}, u32[]{:S(2)}) collective-permute-start(f32[8,128]{1,0:T(8,128)S(1)} %slice_add_fusion.2), channel_id=1, source_target_pairs={{0,4},{4,0},{8,12},{12,8},{16,20},{20,16},{24,28},{28,24},{1,5},{5... | collective-permute-start | bytes 12296 | tf_op jit(solution)/shard_map/ppermute | solution.py:26
  32.8 4.0 %collective-permute-start.8 = (f32[8,128]{1,0:T(8,128)S(1)}, f32[8,128]{1,0:T(8,128)S(1)}, u32[]{:S(2)}, u32[]{:S(2)}) collective-permute-start(f32[8,128]{1,0:T(8,128)S(1)} %add.101), channel_id=1, source_target_pairs={{0,8},{4,12},{8,0},{12,4},{16,24},{20,28},{24,16},{28,20},{1,9},{5... | collective-permute-start | bytes 12296 | tf_op jit(solution)/shard_map/ppermute | solution.py:26
  36.9 4.6 %collective-permute-start.9 = (f32[8,128]{1,0:T(8,128)S(1)}, f32[8,128]{1,0:T(8,128)S(1)}, u32[]{:S(2)}, u32[]{:S(2)}) collective-permute-start(f32[8,128]{1,0:T(8,128)S(1)} %add.102), channel_id=1, source_target_pairs={{0,16},{4,20},{8,24},{12,28},{16,0},{20,4},{24,8},{28,12},{1,17},{... | collective-permute-start | bytes 12296 | tf_op jit(solution)/shard_map/ppermute | solution.py:26

commit v18 on v17

--- a/solution.py
+++ b/solution.py
@@ -113,6 +113,7 @@
         while mask < helpers:
             own_pair = jnp.concatenate([own_pair, exchanged(own_pair, "help", mask)], axis=1)
             mask *= 2
+        core, _ = lax.optimization_barrier((core, own_pair))
         crossing = [(b, b + 2) for b in range(0, groups - 2, 2)]
         crossing += [(b, b - 2) for b in range(3, groups, 2)]
         remote = lax.ppermute(own_pair, "blk", crossing)

time: 42.6 us -> 42.6 us (level)
  waiting for transfers between devices: 13.4 us -> 12.8 us
  starting transfers between devices: 17.5 us -> 18 us
    ppermute x1, waiting for transfers between devices: 2.45 us -> 0.9 us  [local(): remote = lax.ppermute(own_pair, 'blk', crossing)]
    ppermute x9, waiting for transfers between devices: 11 us -> 11.9 us  [exchanged(): lax.ppermute(value, axis, [(source, source ^ mask) for source in range(co...]
  transfers between devices with their start and end apart: 10 -> 10, of which waited for: 9 -> 10; matrix products, arithmetic and copies ran while one was open for 12% -> 12% of each run, Pallas kernels for 0% -> 0%
where the time goes in v18:
time: 42.6 us; the launch traced here: 42.1 us
  starting transfers between devices  18 us (42%)
  waiting for transfers between devices  12.8 us (30%)
  matrix products  4.62 us (11%)
  other arithmetic  3.44 us (8%)
  local copies, waits for them, and re-layouts  2.45 us (6%)
  between operations  0.75 us (2%)
    ppermute x9, starting transfers between devices, exchanged(): lax.ppermute(value, axis, [(source, source ^ mask) for source in range(co...  14 us
    ppermute x9, waiting for transfers between devices, exchanged(): lax.ppermute(value, axis, [(source, source ^ mask) for source in range(co...  11.9 us
    ppermute x1, starting transfers between devices, local(): remote = lax.ppermute(own_pair, 'blk', crossing)  3.98 us
    dot_general x1, matrix products, batch_product(): jnp.einsum('osit,ostu->osiu', pieces, tile_blocks[0, first:last:step], pr...  3.18 us
    concatenate x2, other arithmetic, batch_product(): pieces = stacked[panel_ids[:, None], column_place[first:last:step]]  1.38 us
    dot_general x1, matrix products, local(): jnp.dot(vectors, vectors.T, precision=lax.Precision.HIGHEST, preferred_el...  0.92 us
    ppermute x1, waiting for transfers between devices, local(): remote = lax.ppermute(own_pair, 'blk', crossing)  0.9 us
  transfers between devices with their start and end apart: 10, of which 10 were waited for; matrix products, arithmetic and copies ran while one was open for 12% of the time, Pallas kernels for 0%

profile of v18, /device:TPU:0, one launch (start us, length us, event | category | flops | bytes accessed | tf_op | source)
XLA Modules:
  0.0 42.1 jit_solution(11155669646168968099)
XLA Ops:
  0.6 0.5 %collective-permute-start = (f32[8,512]{1,0:T(8,128)}, f32[8,512]{1,0:T(8,128)S(1)}, u32[]{:S(2)}, u32[]{:S(2)}) collective-permute-start(f32[8,512]{1,0:T(8,128)} %param.7), channel_id=1, source_target_pairs={{0,4},{4,0},{8,12},{12,8},{16,20},{20,16},{24,28},{28,24},{1,5},{5... | collective-permute-start | bytes 49160 | tf_op jit(solution)/shard_map/ppermute | solution.py:26
  1.1 0.7 %constant_dynamic-update-slice_fusion.4 = (f32[8,2048]{1,0:T(8,128)S(1)}, f32[8,1024]{1,0:T(8,128)S(1)}, f32[8,4096]{1,0:T(8,128)S(1)}) fusion(f32[8,512]{1,0:T(8,128)} %param.7), kind=kLoop, calls=%fused_computation.10 | loop fusion | bytes 65536
  1.9 0.3 collective-permute-done
  2.2 2.8 %collective-permute-start.1 = (f32[8,1024]{1,0:T(8,128)S(1)}, f32[8,1024]{1,0:T(8,128)S(1)}, u32[]{:S(2)}, u32[]{:S(2)}) collective-permute-start(f32[8,1024]{1,0:T(8,128)S(1)} %get-tuple-element.23), channel_id=1, source_target_pairs={{0,1},{1,0},{2,3},{3,2},{4,5},{5,4},{6,7},{7,6},{8,9},{9,8},{10,11... | collective-permute-start | bytes 98312 | tf_op jit(solution)/shard_map/ppermute | solution.py:26
  5.0 0.9 %fusion.27 = f32[8,8]{1,0:T(8,128)S(1)} fusion(f32[8,512]{1,0:T(8,128)} %param.7), kind=kOutput, calls=%fused_computation.68 | convolution fusion | flops 393216 | bytes 16640 | tf_op jit(solution)/shard_map/dot_general | solution.py:164
  6.0 1.0 %collective-permute-done.1 = f32[8,1024]{1,0:T(8,128)S(1)} collective-permute-done((f32[8,1024]{1,0:T(8,128)S(1)}, f32[8,1024]{1,0:T(8,128)S(1)}, u32[]{:S(2)}, u32[]{:S(2)}) %collective-permute-start.1) | collective-permute-done | bytes 32800 | tf_op jit(solution)/shard_map/ppermute | solution.py:26
  6.9 2.1 %collective-permute-start.2 = (f32[8,2048]{1,0:T(8,128)S(1)}, f32[8,2048]{1,0:T(8,128)S(1)}, u32[]{:S(2)}, u32[]{:S(2)}) collective-permute-start(f32[8,2048]{1,0:T(8,128)S(1)} %get-tuple-element.19), channel_id=1, source_target_pairs={{0,2},{1,3},{2,0},{3,1},{4,6},{5,7},{6,4},{7,5},{8,10},{9,11},{10,... | collective-permute-start | bytes 196616 | tf_op jit(solution)/shard_map/ppermute | solution.py:26
  9.0 0.7 %fusion.10 = s32[5,3]{0,1:T(4,128)S(1)} fusion(s32[1,5,3]{1,0,2:T(1,128)} %param.9, s32[]{:T(128)S(6)} %axis_index.22), kind=kLoop, calls=%fused_computation.46 | loop fusion | flops 330 | bytes 124 | tf_op jit(solution)/shard_map/add | solution.py:101
  9.7 0.7 %fusion.12 = f32[5,3]{0,1:T(4,128)S(1)} fusion(s32[5]{0:T(128)} %bitcast.79), kind=kLoop, calls=%fused_computation.51 | loop fusion | flops 30 | bytes 80 | tf_op jit(solution)/shard_map/convert_element_type | solution.py:131
  10.3 0.9 %collective-permute-done.2 = f32[8,2048]{1,0:T(8,128)S(1)} collective-permute-done((f32[8,2048]{1,0:T(8,128)S(1)}, f32[8,2048]{1,0:T(8,128)S(1)}, u32[]{:S(2)}, u32[]{:S(2)}) %collective-permute-start.2) | collective-permute-done | bytes 65568 | tf_op jit(solution)/shard_map/ppermute | solution.py:26
  11.2 4.0 %collective-permute-start.3 = (f32[8,4096]{1,0:T(8,128)S(1)}, f32[8,4096]{1,0:T(8,128)S(1)}, u32[]{:S(2)}, u32[]{:S(2)}) collective-permute-start(f32[8,4096]{1,0:T(8,128)S(1)} %constant_dynamic-update-slice_fusion.5), channel_id=1, source_target_pairs={{0,8},{8,16},{16,24},{12,4},{20,12},{28,20},{1,9},{9,17},{17,25},{... | collective-permute-start | bytes 393224 | tf_op jit(solution)/shard_map/ppermute | solution.py:119
  15.2 0.7 %fusion.20 = s32[5]{0:T(128)S(1)} fusion(s32[5]{0:T(128)} %constant.71.clone, s32[5]{0:T(128)} %constant.72.clone, pred[]{:T(512)S(6)} %eq.24), kind=kLoop, calls=%fused_computation.61 | loop fusion | flops 30 | bytes 61 | tf_op jit(solution)/shard_map/concatenate | solution.py:139
  15.9 0.7 %fusion.18 = s32[5,3,1]{0,2,1:T(1,128)S(1)} fusion(s32[1,5,3]{1,0,2:T(1,128)} %param.10, s32[5]{0:T(128)S(1)} %fusion.20, s32[]{:T(128)S(6)} %axis_index.22), kind=kLoop, calls=%fused_computation.57 | loop fusion | flops 420 | bytes 144 | tf_op jit(solution)/shard_map/concatenate | solution.py:139
  16.6 0.1 copy.23
  16.7 0.1 reshape.229
  16.8 0.9 %collective-permute-done.3 = f32[8,4096]{1,0:T(8,128)S(1)} collective-permute-done((f32[8,4096]{1,0:T(8,128)S(1)}, f32[8,4096]{1,0:T(8,128)S(1)}, u32[]{:S(2)}, u32[]{:S(2)}) %collective-permute-start.3) | collective-permute-done | bytes 131104 | tf_op jit(solution)/shard_map/ppermute | solution.py:119
  17.7 0.1 collective-permute-start.4
  17.8 1.3 %collective-permute-done.4 = f32[8,4096]{1,0:T(8,128)S(1)} collective-permute-done((f32[8,4096]{1,0:T(8,128)S(1)}, f32[8,4096]{1,0:T(8,128)S(1)}, u32[]{:S(2)}, u32[]{:S(2)}) %collective-permute-start.4) | collective-permute-done | bytes 131104 | tf_op jit(solution)/shard_map/ppermute | solution.py:26
  19.2 0.6 %gather_fusion = f32[15,8,256]{2,1,0:T(8,128)S(1)} fusion(f32[6,8,8,256]{3,2,1,0:T(8,128)S(1)} %bitcast.78, s32[15]{0:T(128)S(1)} %reshape.229), kind=kCustom, calls=%fused_computation | custom fusion | bytes 245880 | tf_op jit(solution)/shard_map/gather | solution.py:139
  19.8 3.2 %fusion = f32[5,3,8,256]{3,2,1,0:T(8,128)S(1)} fusion(f32[5,3,8,256]{3,2,1,0:T(8,128)S(1)} %bitcast.69, f32[1,5,3,256,256]{4,3,2,1,0:T(8,128)} %param.8), kind=kOutput, calls=%fused_computation.1 | convolution fusion | flops 47185920 | bytes 4177920 | tf_op jit(solution)/shard_map/osit,ostu->osiu/dot_general | solution.py:140
  23.0 0.4 convolution_bitcast_fusion
  23.5 0.1 fusion.26
  23.6 0.1 concatenate.29
  23.7 1.5 %collective-permute-start.5 = (f32[8,1152]{1,0:T(8,128)S(1)}, f32[8,1152]{1,0:T(8,128)S(1)}, u32[]{:S(2)}, u32[]{:S(2)}) collective-permute-start(f32[8,1152]{1,0:T(8,128)S(1)} %concatenate.29), channel_id=1, source_target_pairs={{0,2},{1,3},{2,0},{3,1},{4,6},{5,7},{6,4},{7,5},{8,10},{9,11},{10,... | collective-permute-start | bytes 110600 | tf_op jit(solution)/shard_map/ppermute | solution.py:26
  25.2 2.4 %collective-permute-done.5 = f32[8,1152]{1,0:T(8,128)S(1)} collective-permute-done((f32[8,1152]{1,0:T(8,128)S(1)}, f32[8,1152]{1,0:T(8,128)S(1)}, u32[]{:S(2)}, u32[]{:S(2)}) %collective-permute-start.5) | collective-permute-done | bytes 36896 | tf_op jit(solution)/shard_map/ppermute | solution.py:26
  27.7 0.1 slice_add_fusion.3
  27.8 1.5 %collective-permute-start.6 = (f32[8,640]{1,0:T(8,128)S(1)}, f32[8,640]{1,0:T(8,128)S(1)}, u32[]{:S(2)}, u32[]{:S(2)}) collective-permute-start(f32[8,640]{1,0:T(8,128)S(1)} %pad_maximum_fusion), channel_id=1, source_target_pairs={{0,1},{1,0},{2,3},{3,2},{4,5},{5,4},{6,7},{7,6},{8,9},{9,8},{10,11... | collective-permute-start | bytes 61448 | tf_op jit(solution)/shard_map/ppermute | solution.py:26
  29.3 2.3 %collective-permute-done.6 = f32[8,640]{1,0:T(8,128)S(1)} collective-permute-done((f32[8,640]{1,0:T(8,128)S(1)}, f32[8,640]{1,0:T(8,128)S(1)}, u32[]{:S(2)}, u32[]{:S(2)}) %collective-permute-start.6) | collective-permute-done | bytes 20512 | tf_op jit(solution)/shard_map/ppermute | solution.py:26
  31.6 0.0 collective-permute-start.7
  31.6 1.2 %collective-permute-done.7 = f32[8,128]{1,0:T(8,128)S(1)} collective-permute-done((f32[8,128]{1,0:T(8,128)S(1)}, f32[8,128]{1,0:T(8,128)S(1)}, u32[]{:S(2)}, u32[]{:S(2)}) %collective-permute-start.7) | collective-permute-done | bytes 4128 | tf_op jit(solution)/shard_map/ppermute | solution.py:26
  32.7 2.4 %collective-permute-start.8 = (f32[8,128]{1,0:T(8,128)S(1)}, f32[8,128]{1,0:T(8,128)S(1)}, u32[]{:S(2)}, u32[]{:S(2)}) collective-permute-start(f32[8,128]{1,0:T(8,128)S(1)} %add.101), channel_id=1, source_target_pairs={{0,8},{4,12},{8,0},{12,4},{16,24},{20,28},{24,16},{28,20},{1,9},{5... | collective-permute-start | bytes 12296 | tf_op jit(solution)/shard_map/ppermute | solution.py:26
  35.2 1.6 %collective-permute-done.8 = f32[8,128]{1,0:T(8,128)S(1)} collective-permute-done((f32[8,128]{1,0:T(8,128)S(1)}, f32[8,128]{1,0:T(8,128)S(1)}, u32[]{:S(2)}, u32[]{:S(2)}) %collective-permute-start.8) | collective-permute-done | bytes 4128 | tf_op jit(solution)/shard_map/ppermute | solution.py:26
  36.8 3.0 %collective-permute-start.9 = (f32[8,128]{1,0:T(8,128)S(1)}, f32[8,128]{1,0:T(8,128)S(1)}, u32[]{:S(2)}, u32[]{:S(2)}) collective-permute-start(f32[8,128]{1,0:T(8,128)S(1)} %add.102), channel_id=1, source_target_pairs={{0,16},{4,20},{8,24},{12,28},{16,0},{20,4},{24,8},{28,12},{1,17},{... | collective-permute-start | bytes 12296 | tf_op jit(solution)/shard_map/ppermute | solution.py:26
  39.8 0.6 %slice_add_fusion.1 = f32[8,512]{1,0:T(8,128)} fusion(f32[8,640]{1,0:T(8,128)S(1)} %collective-permute-done.6, f32[8,1024]{1,0:T(8,128)S(1)} %slice_add_fusion), kind=kLoop, calls=%fused_computation.22 | loop fusion | flops 4096 | bytes 49152 | tf_op jit(solution)/shard_map/add | solution.py:60
  40.4 1.0 %collective-permute-done.9 = f32[8,128]{1,0:T(8,128)S(1)} collective-permute-done((f32[8,128]{1,0:T(8,128)S(1)}, f32[8,128]{1,0:T(8,128)S(1)}, u32[]{:S(2)}, u32[]{:S(2)}) %collective-permute-start.9) | collective-permute-done | bytes 4128 | tf_op jit(solution)/shard_map/ppermute | solution.py:26
  41.4 0.7 %fusion.25 = (f32[8,8]{1,0:T(8,128)}, f32[8,8]{1,0:T(8,128)}) fusion(f32[8,128]{1,0:T(8,128)S(1)} %add_multiply_fusion), kind=kLoop, calls=%fused_computation.66 | loop fusion | bytes 1024 | tf_op jit(solution)/shard_map/slice | solution.py:176
  (22 shorter events, 0.2 us)
Async XLA Ops:
  0.6 1.6 %collective-permute-start = (f32[8,512]{1,0:T(8,128)}, f32[8,512]{1,0:T(8,128)S(1)}, u32[]{:S(2)}, u32[]{:S(2)}) collective-permute-start(f32[8,512]{1,0:T(8,128)} %param.7), channel_id=1, source_target_pairs={{0,4},{4,0},{8,12},{12,8},{16,20},{20,16},{24,28},{28,24},{1,5},{5... | collective-permute-start | bytes 49160 | tf_op jit(solution)/shard_map/ppermute | solution.py:26
  2.2 4.7 %collective-permute-start.1 = (f32[8,1024]{1,0:T(8,128)S(1)}, f32[8,1024]{1,0:T(8,128)S(1)}, u32[]{:S(2)}, u32[]{:S(2)}) collective-permute-start(f32[8,1024]{1,0:T(8,128)S(1)} %get-tuple-element.23), channel_id=1, source_target_pairs={{0,1},{1,0},{2,3},{3,2},{4,5},{5,4},{6,7},{7,6},{8,9},{9,8},{10,11... | collective-permute-start | bytes 98312 | tf_op jit(solution)/shard_map/ppermute | solution.py:26
  6.9 4.3 %collective-permute-start.2 = (f32[8,2048]{1,0:T(8,128)S(1)}, f32[8,2048]{1,0:T(8,128)S(1)}, u32[]{:S(2)}, u32[]{:S(2)}) collective-permute-start(f32[8,2048]{1,0:T(8,128)S(1)} %get-tuple-element.19), channel_id=1, source_target_pairs={{0,2},{1,3},{2,0},{3,1},{4,6},{5,7},{6,4},{7,5},{8,10},{9,11},{10,... | collective-permute-start | bytes 196616 | tf_op jit(solution)/shard_map/ppermute | solution.py:26
  11.2 6.5 %collective-permute-start.3 = (f32[8,4096]{1,0:T(8,128)S(1)}, f32[8,4096]{1,0:T(8,128)S(1)}, u32[]{:S(2)}, u32[]{:S(2)}) collective-permute-start(f32[8,4096]{1,0:T(8,128)S(1)} %constant_dynamic-update-slice_fusion.5), channel_id=1, source_target_pairs={{0,8},{8,16},{16,24},{12,4},{20,12},{28,20},{1,9},{9,17},{17,25},{... | collective-permute-start | bytes 393224 | tf_op jit(solution)/shard_map/ppermute | solution.py:119
  17.7 1.4 %collective-permute-start.4 = (f32[8,4096]{1,0:T(8,128)S(1)}, f32[8,4096]{1,0:T(8,128)S(1)}, u32[]{:S(2)}, u32[]{:S(2)}) collective-permute-start(f32[8,4096]{1,0:T(8,128)S(1)} %collective-permute-done.3), channel_id=1, source_target_pairs={{0,4},{4,0},{8,12},{12,8},{16,20},{20,16},{24,28},{28,24},{1,5},{5... | collective-permute-start | bytes 393224 | tf_op jit(solution)/shard_map/ppermute | solution.py:26
  23.7 4.0 %collective-permute-start.5 = (f32[8,1152]{1,0:T(8,128)S(1)}, f32[8,1152]{1,0:T(8,128)S(1)}, u32[]{:S(2)}, u32[]{:S(2)}) collective-permute-start(f32[8,1152]{1,0:T(8,128)S(1)} %concatenate.29), channel_id=1, source_target_pairs={{0,2},{1,3},{2,0},{3,1},{4,6},{5,7},{6,4},{7,5},{8,10},{9,11},{10,... | collective-permute-start | bytes 110600 | tf_op jit(solution)/shard_map/ppermute | solution.py:26
  27.8 3.8 %collective-permute-start.6 = (f32[8,640]{1,0:T(8,128)S(1)}, f32[8,640]{1,0:T(8,128)S(1)}, u32[]{:S(2)}, u32[]{:S(2)}) collective-permute-start(f32[8,640]{1,0:T(8,128)S(1)} %pad_maximum_fusion), channel_id=1, source_target_pairs={{0,1},{1,0},{2,3},{3,2},{4,5},{5,4},{6,7},{7,6},{8,9},{9,8},{10,11... | collective-permute-start | bytes 61448 | tf_op jit(solution)/shard_map/ppermute | solution.py:26
  31.6 1.2 %collective-permute-start.7 = (f32[8,128]{1,0:T(8,128)S(1)}, f32[8,128]{1,0:T(8,128)S(1)}, u32[]{:S(2)}, u32[]{:S(2)}) collective-permute-start(f32[8,128]{1,0:T(8,128)S(1)} %slice_add_fusion.2), channel_id=1, source_target_pairs={{0,4},{4,0},{8,12},{12,8},{16,20},{20,16},{24,28},{28,24},{1,5},{5... | collective-permute-start | bytes 12296 | tf_op jit(solution)/shard_map/ppermute | solution.py:26
  32.7 4.0 %collective-permute-start.8 = (f32[8,128]{1,0:T(8,128)S(1)}, f32[8,128]{1,0:T(8,128)S(1)}, u32[]{:S(2)}, u32[]{:S(2)}) collective-permute-start(f32[8,128]{1,0:T(8,128)S(1)} %add.101), channel_id=1, source_target_pairs={{0,8},{4,12},{8,0},{12,4},{16,24},{20,28},{24,16},{28,20},{1,9},{5... | collective-permute-start | bytes 12296 | tf_op jit(solution)/shard_map/ppermute | solution.py:26
  36.8 4.6 %collective-permute-start.9 = (f32[8,128]{1,0:T(8,128)S(1)}, f32[8,128]{1,0:T(8,128)S(1)}, u32[]{:S(2)}, u32[]{:S(2)}) collective-permute-start(f32[8,128]{1,0:T(8,128)S(1)} %add.102), channel_id=1, source_target_pairs={{0,16},{4,20},{8,24},{12,28},{16,0},{20,4},{24,8},{28,12},{1,17},{... | collective-permute-start | bytes 12296 | tf_op jit(solution)/shard_map/ppermute | solution.py:26

commit v19 on v18

--- a/solution.py
+++ b/solution.py
@@ -170,9 +170,13 @@
     gram = jnp.concatenate(
         [energy_term, correlation_term, jnp.zeros((VEC, GRAM_PAD - 2 * VEC), jnp.float32)], axis=1
     )
+    exact_scale = is_power_of_two(groups * group_width)
+    if exact_scale:
+        gram = gram / basis_size
     product, gram = reduce_help(flattened, gram)
     gram = reduce_blk(gram)
-    gram = gram / basis_size
+    if not exact_scale:
+        gram = gram / basis_size
     return (product, gram[:, :VEC], gram[:, VEC : 2 * VEC])
 
 

time: 42.6 us -> 42.6 us (level)
  transfers between devices with their start and end apart: 10 -> 10, of which waited for: 10 -> 10; matrix products, arithmetic and copies ran while one was open for 12% -> 13% of each run, Pallas kernels for 0% -> 0%
where the time goes in v19:
time: 42.6 us; the launch traced here: 42.1 us
  starting transfers between devices  18 us (42%)
  waiting for transfers between devices  12.8 us (30%)
  matrix products  4.62 us (11%)
  other arithmetic  3.58 us (8%)
  local copies, waits for them, and re-layouts  2.4 us (6%)
  between operations  0.75 us (2%)
    ppermute x9, starting transfers between devices, exchanged(): lax.ppermute(value, axis, [(source, source ^ mask) for source in range(co...  14 us
    ppermute x9, waiting for transfers between devices, exchanged(): lax.ppermute(value, axis, [(source, source ^ mask) for source in range(co...  11.9 us
    ppermute x1, starting transfers between devices, local(): remote = lax.ppermute(own_pair, 'blk', crossing)  3.98 us
    dot_general x1, matrix products, batch_product(): jnp.einsum('osit,ostu->osiu', pieces, tile_blocks[0, first:last:step], pr...  3.18 us
    concatenate x2, other arithmetic, batch_product(): pieces = stacked[panel_ids[:, None], column_place[first:last:step]]  1.38 us
    dot_general x1, matrix products, local(): jnp.dot(vectors, vectors.T, precision=lax.Precision.HIGHEST, preferred_el...  0.92 us
    ppermute x1, waiting for transfers between devices, local(): remote = lax.ppermute(own_pair, 'blk', crossing)  0.9 us
  transfers between devices with their start and end apart: 10, of which 10 were waited for; matrix products, arithmetic and copies ran while one was open for 13% of the time, Pallas kernels for 0%

profile of v19, /device:TPU:0, one launch (start us, length us, event | category | flops | bytes accessed | tf_op | source)
XLA Modules:
  0.0 42.1 jit_solution(2289560765016737539)
XLA Ops:
  0.6 0.5 %collective-permute-start = (f32[8,512]{1,0:T(8,128)}, f32[8,512]{1,0:T(8,128)S(1)}, u32[]{:S(2)}, u32[]{:S(2)}) collective-permute-start(f32[8,512]{1,0:T(8,128)} %param.7), channel_id=1, source_target_pairs={{0,4},{4,0},{8,12},{12,8},{16,20},{20,16},{24,28},{28,24},{1,5},{5... | collective-permute-start | bytes 49160 | tf_op jit(solution)/shard_map/ppermute | solution.py:26
  1.1 0.7 %constant_dynamic-update-slice_fusion.4 = (f32[8,2048]{1,0:T(8,128)S(1)}, f32[8,1024]{1,0:T(8,128)S(1)}, f32[8,4096]{1,0:T(8,128)S(1)}) fusion(f32[8,512]{1,0:T(8,128)} %param.7), kind=kLoop, calls=%fused_computation.11 | loop fusion | bytes 65536
  1.9 0.1 pad.6.clone
  1.9 0.2 collective-permute-done
  2.2 2.8 %collective-permute-start.1 = (f32[8,1024]{1,0:T(8,128)S(1)}, f32[8,1024]{1,0:T(8,128)S(1)}, u32[]{:S(2)}, u32[]{:S(2)}) collective-permute-start(f32[8,1024]{1,0:T(8,128)S(1)} %get-tuple-element.23), channel_id=1, source_target_pairs={{0,1},{1,0},{2,3},{3,2},{4,5},{5,4},{6,7},{7,6},{8,9},{9,8},{10,11... | collective-permute-start | bytes 98312 | tf_op jit(solution)/shard_map/ppermute | solution.py:26
  5.0 0.9 %fusion.27 = f32[8,8]{1,0:T(8,128)S(1)} fusion(f32[8,512]{1,0:T(8,128)} %param.7), kind=kOutput, calls=%fused_computation.69 | convolution fusion | flops 393216 | bytes 16640 | tf_op jit(solution)/shard_map/dot_general | solution.py:164
  6.0 1.0 %collective-permute-done.1 = f32[8,1024]{1,0:T(8,128)S(1)} collective-permute-done((f32[8,1024]{1,0:T(8,128)S(1)}, f32[8,1024]{1,0:T(8,128)S(1)}, u32[]{:S(2)}, u32[]{:S(2)}) %collective-permute-start.1) | collective-permute-done | bytes 32800 | tf_op jit(solution)/shard_map/ppermute | solution.py:26
  6.9 2.1 %collective-permute-start.2 = (f32[8,2048]{1,0:T(8,128)S(1)}, f32[8,2048]{1,0:T(8,128)S(1)}, u32[]{:S(2)}, u32[]{:S(2)}) collective-permute-start(f32[8,2048]{1,0:T(8,128)S(1)} %get-tuple-element.19), channel_id=1, source_target_pairs={{0,2},{1,3},{2,0},{3,1},{4,6},{5,7},{6,4},{7,5},{8,10},{9,11},{10,... | collective-permute-start | bytes 196616 | tf_op jit(solution)/shard_map/ppermute | solution.py:26
  9.0 0.7 %fusion.10 = s32[5,3]{0,1:T(4,128)S(1)} fusion(s32[1,5,3]{1,0,2:T(1,128)} %param.9, s32[]{:T(128)S(6)} %axis_index.22), kind=kLoop, calls=%fused_computation.47 | loop fusion | flops 330 | bytes 124 | tf_op jit(solution)/shard_map/add | solution.py:101
  9.7 0.7 %fusion.12 = f32[5,3]{0,1:T(4,128)S(1)} fusion(s32[5]{0:T(128)} %bitcast.79), kind=kLoop, calls=%fused_computation.52 | loop fusion | flops 30 | bytes 80 | tf_op jit(solution)/shard_map/convert_element_type | solution.py:131
  10.3 0.9 %collective-permute-done.2 = f32[8,2048]{1,0:T(8,128)S(1)} collective-permute-done((f32[8,2048]{1,0:T(8,128)S(1)}, f32[8,2048]{1,0:T(8,128)S(1)}, u32[]{:S(2)}, u32[]{:S(2)}) %collective-permute-start.2) | collective-permute-done | bytes 65568 | tf_op jit(solution)/shard_map/ppermute | solution.py:26
  11.2 4.0 %collective-permute-start.3 = (f32[8,4096]{1,0:T(8,128)S(1)}, f32[8,4096]{1,0:T(8,128)S(1)}, u32[]{:S(2)}, u32[]{:S(2)}) collective-permute-start(f32[8,4096]{1,0:T(8,128)S(1)} %constant_dynamic-update-slice_fusion.5), channel_id=1, source_target_pairs={{0,8},{8,16},{16,24},{12,4},{20,12},{28,20},{1,9},{9,17},{17,25},{... | collective-permute-start | bytes 393224 | tf_op jit(solution)/shard_map/ppermute | solution.py:119
  15.2 0.7 %fusion.20 = s32[5]{0:T(128)S(1)} fusion(s32[5]{0:T(128)} %constant.71.clone, s32[5]{0:T(128)} %constant.72.clone, pred[]{:T(512)S(6)} %eq.24), kind=kLoop, calls=%fused_computation.62 | loop fusion | flops 30 | bytes 61 | tf_op jit(solution)/shard_map/concatenate | solution.py:139
  15.9 0.7 %fusion.18 = s32[5,3,1]{0,2,1:T(1,128)S(1)} fusion(s32[1,5,3]{1,0,2:T(1,128)} %param.10, s32[5]{0:T(128)S(1)} %fusion.20, s32[]{:T(128)S(6)} %axis_index.22), kind=kLoop, calls=%fused_computation.58 | loop fusion | flops 420 | bytes 144 | tf_op jit(solution)/shard_map/concatenate | solution.py:139
  16.6 0.1 copy.23
  16.7 0.1 reshape.229
  16.8 0.9 %collective-permute-done.3 = f32[8,4096]{1,0:T(8,128)S(1)} collective-permute-done((f32[8,4096]{1,0:T(8,128)S(1)}, f32[8,4096]{1,0:T(8,128)S(1)}, u32[]{:S(2)}, u32[]{:S(2)}) %collective-permute-start.3) | collective-permute-done | bytes 131104 | tf_op jit(solution)/shard_map/ppermute | solution.py:119
  17.7 0.1 collective-permute-start.4
  17.8 1.3 %collective-permute-done.4 = f32[8,4096]{1,0:T(8,128)S(1)} collective-permute-done((f32[8,4096]{1,0:T(8,128)S(1)}, f32[8,4096]{1,0:T(8,128)S(1)}, u32[]{:S(2)}, u32[]{:S(2)}) %collective-permute-start.4) | collective-permute-done | bytes 131104 | tf_op jit(solution)/shard_map/ppermute | solution.py:26
  19.2 0.6 %gather_fusion = f32[15,8,256]{2,1,0:T(8,128)S(1)} fusion(f32[6,8,8,256]{3,2,1,0:T(8,128)S(1)} %bitcast.78, s32[15]{0:T(128)S(1)} %reshape.229), kind=kCustom, calls=%fused_computation | custom fusion | bytes 245880 | tf_op jit(solution)/shard_map/gather | solution.py:139
  19.8 3.2 %fusion = f32[5,3,8,256]{3,2,1,0:T(8,128)S(1)} fusion(f32[5,3,8,256]{3,2,1,0:T(8,128)S(1)} %bitcast.69, f32[1,5,3,256,256]{4,3,2,1,0:T(8,128)} %param.8), kind=kOutput, calls=%fused_computation.1 | convolution fusion | flops 47185920 | bytes 4177920 | tf_op jit(solution)/shard_map/osit,ostu->osiu/dot_general | solution.py:140
  23.0 0.4 convolution_bitcast_fusion
  23.5 0.1 fusion.26
  23.6 0.1 maximum_multiply_fusion
  23.7 1.5 %collective-permute-start.5 = (f32[8,1152]{1,0:T(8,128)S(1)}, f32[8,1152]{1,0:T(8,128)S(1)}, u32[]{:S(2)}, u32[]{:S(2)}) collective-permute-start(f32[8,1152]{1,0:T(8,128)S(1)} %pad_maximum_fusion), channel_id=1, source_target_pairs={{0,2},{1,3},{2,0},{3,1},{4,6},{5,7},{6,4},{7,5},{8,10},{9,11},{10,... | collective-permute-start | bytes 110600 | tf_op jit(solution)/shard_map/ppermute | solution.py:26
  25.3 2.4 %collective-permute-done.5 = f32[8,1152]{1,0:T(8,128)S(1)} collective-permute-done((f32[8,1152]{1,0:T(8,128)S(1)}, f32[8,1152]{1,0:T(8,128)S(1)}, u32[]{:S(2)}, u32[]{:S(2)}) %collective-permute-start.5) | collective-permute-done | bytes 36896 | tf_op jit(solution)/shard_map/ppermute | solution.py:26
  27.7 0.1 slice_add_fusion.3
  27.8 1.5 %collective-permute-start.6 = (f32[8,640]{1,0:T(8,128)S(1)}, f32[8,640]{1,0:T(8,128)S(1)}, u32[]{:S(2)}, u32[]{:S(2)}) collective-permute-start(f32[8,640]{1,0:T(8,128)S(1)} %pad_maximum_fusion.1), channel_id=1, source_target_pairs={{0,1},{1,0},{2,3},{3,2},{4,5},{5,4},{6,7},{7,6},{8,9},{9,8},{10,11... | collective-permute-start | bytes 61448 | tf_op jit(solution)/shard_map/ppermute | solution.py:26
  29.3 2.3 %collective-permute-done.6 = f32[8,640]{1,0:T(8,128)S(1)} collective-permute-done((f32[8,640]{1,0:T(8,128)S(1)}, f32[8,640]{1,0:T(8,128)S(1)}, u32[]{:S(2)}, u32[]{:S(2)}) %collective-permute-start.6) | collective-permute-done | bytes 20512 | tf_op jit(solution)/shard_map/ppermute | solution.py:26
  31.6 0.0 collective-permute-start.7
  31.6 1.2 %collective-permute-done.7 = f32[8,128]{1,0:T(8,128)S(1)} collective-permute-done((f32[8,128]{1,0:T(8,128)S(1)}, f32[8,128]{1,0:T(8,128)S(1)}, u32[]{:S(2)}, u32[]{:S(2)}) %collective-permute-start.7) | collective-permute-done | bytes 4128 | tf_op jit(solution)/shard_map/ppermute | solution.py:26
  32.8 2.4 %collective-permute-start.8 = (f32[8,128]{1,0:T(8,128)S(1)}, f32[8,128]{1,0:T(8,128)S(1)}, u32[]{:S(2)}, u32[]{:S(2)}) collective-permute-start(f32[8,128]{1,0:T(8,128)S(1)} %add.101), channel_id=1, source_target_pairs={{0,8},{4,12},{8,0},{12,4},{16,24},{20,28},{24,16},{28,20},{1,9},{5... | collective-permute-start | bytes 12296 | tf_op jit(solution)/shard_map/ppermute | solution.py:26
  35.2 1.6 %collective-permute-done.8 = f32[8,128]{1,0:T(8,128)S(1)} collective-permute-done((f32[8,128]{1,0:T(8,128)S(1)}, f32[8,128]{1,0:T(8,128)S(1)}, u32[]{:S(2)}, u32[]{:S(2)}) %collective-permute-start.8) | collective-permute-done | bytes 4128 | tf_op jit(solution)/shard_map/ppermute | solution.py:26
  36.8 3.0 %collective-permute-start.9 = (f32[8,128]{1,0:T(8,128)S(1)}, f32[8,128]{1,0:T(8,128)S(1)}, u32[]{:S(2)}, u32[]{:S(2)}) collective-permute-start(f32[8,128]{1,0:T(8,128)S(1)} %add.102), channel_id=1, source_target_pairs={{0,16},{4,20},{8,24},{12,28},{16,0},{20,4},{24,8},{28,12},{1,17},{... | collective-permute-start | bytes 12296 | tf_op jit(solution)/shard_map/ppermute | solution.py:26
  39.8 0.6 %slice_add_fusion.1 = f32[8,512]{1,0:T(8,128)} fusion(f32[8,640]{1,0:T(8,128)S(1)} %collective-permute-done.6, f32[8,1024]{1,0:T(8,128)S(1)} %slice_add_fusion), kind=kLoop, calls=%fused_computation.23 | loop fusion | flops 4096 | bytes 49152 | tf_op jit(solution)/shard_map/add | solution.py:60
  40.4 1.0 %collective-permute-done.9 = f32[8,128]{1,0:T(8,128)S(1)} collective-permute-done((f32[8,128]{1,0:T(8,128)S(1)}, f32[8,128]{1,0:T(8,128)S(1)}, u32[]{:S(2)}, u32[]{:S(2)}) %collective-permute-start.9) | collective-permute-done | bytes 4128 | tf_op jit(solution)/shard_map/ppermute | solution.py:26
  41.4 0.7 %fusion.25 = (f32[8,8]{1,0:T(8,128)}, f32[8,8]{1,0:T(8,128)}) fusion(f32[8,128]{1,0:T(8,128)S(1)} %add.103), kind=kLoop, calls=%fused_computation.67 | loop fusion | bytes 1024 | tf_op jit(solution)/shard_map/slice | solution.py:180
  (23 shorter events, 0.2 us)
Async XLA Ops:
  0.6 1.6 %collective-permute-start = (f32[8,512]{1,0:T(8,128)}, f32[8,512]{1,0:T(8,128)S(1)}, u32[]{:S(2)}, u32[]{:S(2)}) collective-permute-start(f32[8,512]{1,0:T(8,128)} %param.7), channel_id=1, source_target_pairs={{0,4},{4,0},{8,12},{12,8},{16,20},{20,16},{24,28},{28,24},{1,5},{5... | collective-permute-start | bytes 49160 | tf_op jit(solution)/shard_map/ppermute | solution.py:26
  2.2 4.7 %collective-permute-start.1 = (f32[8,1024]{1,0:T(8,128)S(1)}, f32[8,1024]{1,0:T(8,128)S(1)}, u32[]{:S(2)}, u32[]{:S(2)}) collective-permute-start(f32[8,1024]{1,0:T(8,128)S(1)} %get-tuple-element.23), channel_id=1, source_target_pairs={{0,1},{1,0},{2,3},{3,2},{4,5},{5,4},{6,7},{7,6},{8,9},{9,8},{10,11... | collective-permute-start | bytes 98312 | tf_op jit(solution)/shard_map/ppermute | solution.py:26
  6.9 4.3 %collective-permute-start.2 = (f32[8,2048]{1,0:T(8,128)S(1)}, f32[8,2048]{1,0:T(8,128)S(1)}, u32[]{:S(2)}, u32[]{:S(2)}) collective-permute-start(f32[8,2048]{1,0:T(8,128)S(1)} %get-tuple-element.19), channel_id=1, source_target_pairs={{0,2},{1,3},{2,0},{3,1},{4,6},{5,7},{6,4},{7,5},{8,10},{9,11},{10,... | collective-permute-start | bytes 196616 | tf_op jit(solution)/shard_map/ppermute | solution.py:26
  11.2 6.5 %collective-permute-start.3 = (f32[8,4096]{1,0:T(8,128)S(1)}, f32[8,4096]{1,0:T(8,128)S(1)}, u32[]{:S(2)}, u32[]{:S(2)}) collective-permute-start(f32[8,4096]{1,0:T(8,128)S(1)} %constant_dynamic-update-slice_fusion.5), channel_id=1, source_target_pairs={{0,8},{8,16},{16,24},{12,4},{20,12},{28,20},{1,9},{9,17},{17,25},{... | collective-permute-start | bytes 393224 | tf_op jit(solution)/shard_map/ppermute | solution.py:119
  17.7 1.4 %collective-permute-start.4 = (f32[8,4096]{1,0:T(8,128)S(1)}, f32[8,4096]{1,0:T(8,128)S(1)}, u32[]{:S(2)}, u32[]{:S(2)}) collective-permute-start(f32[8,4096]{1,0:T(8,128)S(1)} %collective-permute-done.3), channel_id=1, source_target_pairs={{0,4},{4,0},{8,12},{12,8},{16,20},{20,16},{24,28},{28,24},{1,5},{5... | collective-permute-start | bytes 393224 | tf_op jit(solution)/shard_map/ppermute | solution.py:26
  23.7 4.0 %collective-permute-start.5 = (f32[8,1152]{1,0:T(8,128)S(1)}, f32[8,1152]{1,0:T(8,128)S(1)}, u32[]{:S(2)}, u32[]{:S(2)}) collective-permute-start(f32[8,1152]{1,0:T(8,128)S(1)} %pad_maximum_fusion), channel_id=1, source_target_pairs={{0,2},{1,3},{2,0},{3,1},{4,6},{5,7},{6,4},{7,5},{8,10},{9,11},{10,... | collective-permute-start | bytes 110600 | tf_op jit(solution)/shard_map/ppermute | solution.py:26
  27.8 3.8 %collective-permute-start.6 = (f32[8,640]{1,0:T(8,128)S(1)}, f32[8,640]{1,0:T(8,128)S(1)}, u32[]{:S(2)}, u32[]{:S(2)}) collective-permute-start(f32[8,640]{1,0:T(8,128)S(1)} %pad_maximum_fusion.1), channel_id=1, source_target_pairs={{0,1},{1,0},{2,3},{3,2},{4,5},{5,4},{6,7},{7,6},{8,9},{9,8},{10,11... | collective-permute-start | bytes 61448 | tf_op jit(solution)/shard_map/ppermute | solution.py:26
  31.6 1.2 %collective-permute-start.7 = (f32[8,128]{1,0:T(8,128)S(1)}, f32[8,128]{1,0:T(8,128)S(1)}, u32[]{:S(2)}, u32[]{:S(2)}) collective-permute-start(f32[8,128]{1,0:T(8,128)S(1)} %slice_add_fusion.2), channel_id=1, source_target_pairs={{0,4},{4,0},{8,12},{12,8},{16,20},{20,16},{24,28},{28,24},{1,5},{5... | collective-permute-start | bytes 12296 | tf_op jit(solution)/shard_map/ppermute | solution.py:26
  32.8 4.0 %collective-permute-start.8 = (f32[8,128]{1,0:T(8,128)S(1)}, f32[8,128]{1,0:T(8,128)S(1)}, u32[]{:S(2)}, u32[]{:S(2)}) collective-permute-start(f32[8,128]{1,0:T(8,128)S(1)} %add.101), channel_id=1, source_target_pairs={{0,8},{4,12},{8,0},{12,4},{16,24},{20,28},{24,16},{28,20},{1,9},{5... | collective-permute-start | bytes 12296 | tf_op jit(solution)/shard_map/ppermute | solution.py:26
  36.8 4.6 %collective-permute-start.9 = (f32[8,128]{1,0:T(8,128)S(1)}, f32[8,128]{1,0:T(8,128)S(1)}, u32[]{:S(2)}, u32[]{:S(2)}) collective-permute-start(f32[8,128]{1,0:T(8,128)S(1)} %add.102), channel_id=1, source_target_pairs={{0,16},{4,20},{8,24},{12,28},{16,0},{20,4},{24,8},{28,12},{1,17},{... | collective-permute-start | bytes 12296 | tf_op jit(solution)/shard_map/ppermute | solution.py:26

commit v20 on v19

--- a/solution.py
+++ b/solution.py
@@ -93,7 +93,7 @@
     piece_width = vectors.shape[1]
     group_width = piece_width * lax.axis_size("help")
     group_rows = group_width // TILE
-    paired = groups % 2 == 0 and is_power_of_two(lax.axis_size("help"))
+    paired = groups % 2 == 0 and lax.axis_size("help") > 1 and is_power_of_two(lax.axis_size("help"))
     tiles_per_piece = piece_width // TILE
     order = help_order()
 
@@ -103,9 +103,9 @@
     core = lax.axis_index("blk") % 2
     if paired:
         helpers = lax.axis_size("help")
-        own_pair = jnp.concatenate([vectors, exchanged(vectors, "blk", 1)], axis=1)
+        own_pair = jnp.concatenate([vectors, exchanged(vectors, "help", 1)], axis=1)
         vectors, _ = lax.optimization_barrier((vectors, own_pair))
-        own_pair = jnp.concatenate([own_pair, exchanged(own_pair, "help", 1)], axis=1)
+        own_pair = jnp.concatenate([own_pair, exchanged(own_pair, "blk", 1)], axis=1)
         tile_row, tile_col, counts, _ = lax.optimization_barrier(
             (tile_row, tile_col, counts, own_pair)
         )
@@ -120,7 +120,7 @@
         partner_remote = exchanged(remote, "blk", 1)
         sources = []
         for pair in (own_pair, remote, partner_remote):
-            halves = pair.reshape(VEC, helpers, 2, piece_width)
+            halves = pair.reshape(VEC, helpers // 2, 2, 2 * piece_width)
             sources += [halves[:, :, side].reshape(VEC, group_width) for side in range(2)]
         full_panel = sources[0]
     else:

time: 42.6 us -> 42.5 us (level)
  starting transfers between devices: 18 us -> 17.3 us
    ppermute x9, waiting for transfers between devices: 11.9 us -> 12.3 us  [exchanged(): lax.ppermute(value, axis, [(source, source ^ mask) for source in range(co...]
where the time goes in v20:
time: 42.5 us; the launch traced here: 42 us
  starting transfers between devices  17.3 us (41%)
  waiting for transfers between devices  13.2 us (31%)
  matrix products  4.63 us (11%)
  other arithmetic  3.58 us (8%)
  local copies, waits for them, and re-layouts  2.43 us (6%)
  between operations  0.76 us (2%)
    ppermute x9, starting transfers between devices, exchanged(): lax.ppermute(value, axis, [(source, source ^ mask) for source in range(co...  13.6 us
    ppermute x9, waiting for transfers between devices, exchanged(): lax.ppermute(value, axis, [(source, source ^ mask) for source in range(co...  12.3 us
    ppermute x1, starting transfers between devices, local(): remote = lax.ppermute(own_pair, 'blk', crossing)  3.7 us
    dot_general x1, matrix products, batch_product(): jnp.einsum('osit,ostu->osiu', pieces, tile_blocks[0, first:last:step], pr...  3.18 us
    concatenate x2, other arithmetic, batch_product(): pieces = stacked[panel_ids[:, None], column_place[first:last:step]]  1.38 us
    dot_general x1, matrix products, local(): jnp.dot(vectors, vectors.T, precision=lax.Precision.HIGHEST, preferred_el...  0.92 us
    ppermute x1, waiting for transfers between devices, local(): remote = lax.ppermute(own_pair, 'blk', crossing)  0.9 us
  transfers between devices with their start and end apart: 10, of which 10 were waited for; matrix products, arithmetic and copies ran while one was open for 13% of the time, Pallas kernels for 0%

profile of v20, /device:TPU:0, one launch (start us, length us, event | category | flops | bytes accessed | tf_op | source)
XLA Modules:
  0.0 42.0 jit_solution(16055094708399766652)
XLA Ops:
  0.6 3.0 %collective-permute-start = (f32[8,512]{1,0:T(8,128)}, f32[8,512]{1,0:T(8,128)S(1)}, u32[]{:S(2)}, u32[]{:S(2)}) collective-permute-start(f32[8,512]{1,0:T(8,128)} %param.7), channel_id=1, source_target_pairs={{0,1},{1,0},{2,3},{3,2},{4,5},{5,4},{6,7},{7,6},{8,9},{9,8},{10,11... | collective-permute-start | bytes 49160 | tf_op jit(solution)/shard_map/ppermute | solution.py:26
  3.6 0.8 %constant_dynamic-update-slice_fusion.4 = (f32[8,2048]{1,0:T(8,128)S(1)}, f32[8,1024]{1,0:T(8,128)S(1)}, f32[8,4096]{1,0:T(8,128)S(1)}) fusion(f32[8,512]{1,0:T(8,128)} %param.7), kind=kLoop, calls=%fused_computation.11 | loop fusion | bytes 65536
  4.4 0.1 pad.6.clone
  4.5 1.1 %collective-permute-done = f32[8,512]{1,0:T(8,128)S(1)} collective-permute-done((f32[8,512]{1,0:T(8,128)}, f32[8,512]{1,0:T(8,128)S(1)}, u32[]{:S(2)}, u32[]{:S(2)}) %collective-permute-start) | collective-permute-done | bytes 16416 | tf_op jit(solution)/shard_map/ppermute | solution.py:26
  5.6 0.0 collective-permute-start.1
  5.6 0.9 %fusion.27 = f32[8,8]{1,0:T(8,128)S(1)} fusion(f32[8,512]{1,0:T(8,128)} %param.7), kind=kOutput, calls=%fused_computation.69 | convolution fusion | flops 393216 | bytes 16640 | tf_op jit(solution)/shard_map/dot_general | solution.py:164
  6.5 0.3 collective-permute-done.1
  6.8 2.0 %collective-permute-start.2 = (f32[8,2048]{1,0:T(8,128)S(1)}, f32[8,2048]{1,0:T(8,128)S(1)}, u32[]{:S(2)}, u32[]{:S(2)}) collective-permute-start(f32[8,2048]{1,0:T(8,128)S(1)} %get-tuple-element.19), channel_id=1, source_target_pairs={{0,2},{1,3},{2,0},{3,1},{4,6},{5,7},{6,4},{7,5},{8,10},{9,11},{10,... | collective-permute-start | bytes 196616 | tf_op jit(solution)/shard_map/ppermute | solution.py:26
  8.8 0.7 %fusion.10 = s32[5,3]{0,1:T(4,128)S(1)} fusion(s32[1,5,3]{1,0,2:T(1,128)} %param.9, s32[]{:T(128)S(6)} %axis_index.22), kind=kLoop, calls=%fused_computation.47 | loop fusion | flops 330 | bytes 124 | tf_op jit(solution)/shard_map/add | solution.py:101
  9.5 0.7 %fusion.12 = f32[5,3]{0,1:T(4,128)S(1)} fusion(s32[5]{0:T(128)} %bitcast.79), kind=kLoop, calls=%fused_computation.52 | loop fusion | flops 30 | bytes 80 | tf_op jit(solution)/shard_map/convert_element_type | solution.py:131
  10.2 1.2 %collective-permute-done.2 = f32[8,2048]{1,0:T(8,128)S(1)} collective-permute-done((f32[8,2048]{1,0:T(8,128)S(1)}, f32[8,2048]{1,0:T(8,128)S(1)}, u32[]{:S(2)}, u32[]{:S(2)}) %collective-permute-start.2) | collective-permute-done | bytes 65568 | tf_op jit(solution)/shard_map/ppermute | solution.py:26
  11.4 3.7 %collective-permute-start.3 = (f32[8,4096]{1,0:T(8,128)S(1)}, f32[8,4096]{1,0:T(8,128)S(1)}, u32[]{:S(2)}, u32[]{:S(2)}) collective-permute-start(f32[8,4096]{1,0:T(8,128)S(1)} %constant_dynamic-update-slice_fusion.5), channel_id=1, source_target_pairs={{0,8},{8,16},{16,24},{12,4},{20,12},{28,20},{1,9},{9,17},{17,25},{... | collective-permute-start | bytes 393224 | tf_op jit(solution)/shard_map/ppermute | solution.py:119
  15.1 0.7 %fusion.20 = s32[5]{0:T(128)S(1)} fusion(s32[5]{0:T(128)} %constant.71.clone, s32[5]{0:T(128)} %constant.72.clone, pred[]{:T(512)S(6)} %eq.24), kind=kLoop, calls=%fused_computation.62 | loop fusion | flops 30 | bytes 61 | tf_op jit(solution)/shard_map/concatenate | solution.py:139
  15.8 0.7 %fusion.18 = s32[5,3,1]{0,2,1:T(1,128)S(1)} fusion(s32[1,5,3]{1,0,2:T(1,128)} %param.10, s32[5]{0:T(128)S(1)} %fusion.20, s32[]{:T(128)S(6)} %axis_index.22), kind=kLoop, calls=%fused_computation.58 | loop fusion | flops 420 | bytes 144 | tf_op jit(solution)/shard_map/concatenate | solution.py:139
  16.5 0.1 copy.23
  16.6 0.1 reshape.229
  16.7 0.9 %collective-permute-done.3 = f32[8,4096]{1,0:T(8,128)S(1)} collective-permute-done((f32[8,4096]{1,0:T(8,128)S(1)}, f32[8,4096]{1,0:T(8,128)S(1)}, u32[]{:S(2)}, u32[]{:S(2)}) %collective-permute-start.3) | collective-permute-done | bytes 131104 | tf_op jit(solution)/shard_map/ppermute | solution.py:119
  17.6 0.1 collective-permute-start.4
  17.7 1.3 %collective-permute-done.4 = f32[8,4096]{1,0:T(8,128)S(1)} collective-permute-done((f32[8,4096]{1,0:T(8,128)S(1)}, f32[8,4096]{1,0:T(8,128)S(1)}, u32[]{:S(2)}, u32[]{:S(2)}) %collective-permute-start.4) | collective-permute-done | bytes 131104 | tf_op jit(solution)/shard_map/ppermute | solution.py:26
  19.1 0.6 %gather_fusion = f32[15,8,256]{2,1,0:T(8,128)S(1)} fusion(f32[6,8,8,256]{3,2,1,0:T(8,128)S(1)} %bitcast.78, s32[15]{0:T(128)S(1)} %reshape.229), kind=kCustom, calls=%fused_computation | custom fusion | bytes 245880 | tf_op jit(solution)/shard_map/gather | solution.py:139
  19.7 3.2 %fusion = f32[5,3,8,256]{3,2,1,0:T(8,128)S(1)} fusion(f32[5,3,8,256]{3,2,1,0:T(8,128)S(1)} %bitcast.69, f32[1,5,3,256,256]{4,3,2,1,0:T(8,128)} %param.8), kind=kOutput, calls=%fused_computation.1 | convolution fusion | flops 47185920 | bytes 4177920 | tf_op jit(solution)/shard_map/osit,ostu->osiu/dot_general | solution.py:140
  22.9 0.4 convolution_bitcast_fusion
  23.3 0.1 fusion.26
  23.5 0.1 maximum_multiply_fusion
  23.6 1.5 %collective-permute-start.5 = (f32[8,1152]{1,0:T(8,128)S(1)}, f32[8,1152]{1,0:T(8,128)S(1)}, u32[]{:S(2)}, u32[]{:S(2)}) collective-permute-start(f32[8,1152]{1,0:T(8,128)S(1)} %pad_maximum_fusion), channel_id=1, source_target_pairs={{0,2},{1,3},{2,0},{3,1},{4,6},{5,7},{6,4},{7,5},{8,10},{9,11},{10,... | collective-permute-start | bytes 110600 | tf_op jit(solution)/shard_map/ppermute | solution.py:26
  25.1 2.4 %collective-permute-done.5 = f32[8,1152]{1,0:T(8,128)S(1)} collective-permute-done((f32[8,1152]{1,0:T(8,128)S(1)}, f32[8,1152]{1,0:T(8,128)S(1)}, u32[]{:S(2)}, u32[]{:S(2)}) %collective-permute-start.5) | collective-permute-done | bytes 36896 | tf_op jit(solution)/shard_map/ppermute | solution.py:26
  27.6 0.1 slice_add_fusion.3
  27.7 1.5 %collective-permute-start.6 = (f32[8,640]{1,0:T(8,128)S(1)}, f32[8,640]{1,0:T(8,128)S(1)}, u32[]{:S(2)}, u32[]{:S(2)}) collective-permute-start(f32[8,640]{1,0:T(8,128)S(1)} %pad_maximum_fusion.1), channel_id=1, source_target_pairs={{0,1},{1,0},{2,3},{3,2},{4,5},{5,4},{6,7},{7,6},{8,9},{9,8},{10,11... | collective-permute-start | bytes 61448 | tf_op jit(solution)/shard_map/ppermute | solution.py:26
  29.2 2.3 %collective-permute-done.6 = f32[8,640]{1,0:T(8,128)S(1)} collective-permute-done((f32[8,640]{1,0:T(8,128)S(1)}, f32[8,640]{1,0:T(8,128)S(1)}, u32[]{:S(2)}, u32[]{:S(2)}) %collective-permute-start.6) | collective-permute-done | bytes 20512 | tf_op jit(solution)/shard_map/ppermute | solution.py:26
  31.5 0.0 collective-permute-start.7
  31.5 1.2 %collective-permute-done.7 = f32[8,128]{1,0:T(8,128)S(1)} collective-permute-done((f32[8,128]{1,0:T(8,128)S(1)}, f32[8,128]{1,0:T(8,128)S(1)}, u32[]{:S(2)}, u32[]{:S(2)}) %collective-permute-start.7) | collective-permute-done | bytes 4128 | tf_op jit(solution)/shard_map/ppermute | solution.py:26
  32.6 2.4 %collective-permute-start.8 = (f32[8,128]{1,0:T(8,128)S(1)}, f32[8,128]{1,0:T(8,128)S(1)}, u32[]{:S(2)}, u32[]{:S(2)}) collective-permute-start(f32[8,128]{1,0:T(8,128)S(1)} %add.101), channel_id=1, source_target_pairs={{0,8},{4,12},{8,0},{12,4},{16,24},{20,28},{24,16},{28,20},{1,9},{5... | collective-permute-start | bytes 12296 | tf_op jit(solution)/shard_map/ppermute | solution.py:26
  35.1 1.6 %collective-permute-done.8 = f32[8,128]{1,0:T(8,128)S(1)} collective-permute-done((f32[8,128]{1,0:T(8,128)S(1)}, f32[8,128]{1,0:T(8,128)S(1)}, u32[]{:S(2)}, u32[]{:S(2)}) %collective-permute-start.8) | collective-permute-done | bytes 4128 | tf_op jit(solution)/shard_map/ppermute | solution.py:26
  36.7 3.0 %collective-permute-start.9 = (f32[8,128]{1,0:T(8,128)S(1)}, f32[8,128]{1,0:T(8,128)S(1)}, u32[]{:S(2)}, u32[]{:S(2)}) collective-permute-start(f32[8,128]{1,0:T(8,128)S(1)} %add.102), channel_id=1, source_target_pairs={{0,16},{4,20},{8,24},{12,28},{16,0},{20,4},{24,8},{28,12},{1,17},{... | collective-permute-start | bytes 12296 | tf_op jit(solution)/shard_map/ppermute | solution.py:26
  39.7 0.6 %slice_add_fusion.1 = f32[8,512]{1,0:T(8,128)} fusion(f32[8,640]{1,0:T(8,128)S(1)} %collective-permute-done.6, f32[8,1024]{1,0:T(8,128)S(1)} %slice_add_fusion), kind=kLoop, calls=%fused_computation.23 | loop fusion | flops 4096 | bytes 49152 | tf_op jit(solution)/shard_map/add | solution.py:60
  40.3 1.0 %collective-permute-done.9 = f32[8,128]{1,0:T(8,128)S(1)} collective-permute-done((f32[8,128]{1,0:T(8,128)S(1)}, f32[8,128]{1,0:T(8,128)S(1)}, u32[]{:S(2)}, u32[]{:S(2)}) %collective-permute-start.9) | collective-permute-done | bytes 4128 | tf_op jit(solution)/shard_map/ppermute | solution.py:26
  41.3 0.7 %fusion.25 = (f32[8,8]{1,0:T(8,128)}, f32[8,8]{1,0:T(8,128)}) fusion(f32[8,128]{1,0:T(8,128)S(1)} %add.103), kind=kLoop, calls=%fused_computation.67 | loop fusion | bytes 1024 | tf_op jit(solution)/shard_map/slice | solution.py:180
  (23 shorter events, 0.2 us)
Async XLA Ops:
  0.6 4.9 %collective-permute-start = (f32[8,512]{1,0:T(8,128)}, f32[8,512]{1,0:T(8,128)S(1)}, u32[]{:S(2)}, u32[]{:S(2)}) collective-permute-start(f32[8,512]{1,0:T(8,128)} %param.7), channel_id=1, source_target_pairs={{0,1},{1,0},{2,3},{3,2},{4,5},{5,4},{6,7},{7,6},{8,9},{9,8},{10,11... | collective-permute-start | bytes 49160 | tf_op jit(solution)/shard_map/ppermute | solution.py:26
  5.6 1.2 %collective-permute-start.1 = (f32[8,1024]{1,0:T(8,128)S(1)}, f32[8,1024]{1,0:T(8,128)S(1)}, u32[]{:S(2)}, u32[]{:S(2)}) collective-permute-start(f32[8,1024]{1,0:T(8,128)S(1)} %get-tuple-element.23), channel_id=1, source_target_pairs={{0,4},{4,0},{8,12},{12,8},{16,20},{20,16},{24,28},{28,24},{1,5},{5... | collective-permute-start | bytes 98312 | tf_op jit(solution)/shard_map/ppermute | solution.py:26
  6.8 4.6 %collective-permute-start.2 = (f32[8,2048]{1,0:T(8,128)S(1)}, f32[8,2048]{1,0:T(8,128)S(1)}, u32[]{:S(2)}, u32[]{:S(2)}) collective-permute-start(f32[8,2048]{1,0:T(8,128)S(1)} %get-tuple-element.19), channel_id=1, source_target_pairs={{0,2},{1,3},{2,0},{3,1},{4,6},{5,7},{6,4},{7,5},{8,10},{9,11},{10,... | collective-permute-start | bytes 196616 | tf_op jit(solution)/shard_map/ppermute | solution.py:26
  11.4 6.2 %collective-permute-start.3 = (f32[8,4096]{1,0:T(8,128)S(1)}, f32[8,4096]{1,0:T(8,128)S(1)}, u32[]{:S(2)}, u32[]{:S(2)}) collective-permute-start(f32[8,4096]{1,0:T(8,128)S(1)} %constant_dynamic-update-slice_fusion.5), channel_id=1, source_target_pairs={{0,8},{8,16},{16,24},{12,4},{20,12},{28,20},{1,9},{9,17},{17,25},{... | collective-permute-start | bytes 393224 | tf_op jit(solution)/shard_map/ppermute | solution.py:119
  17.6 1.4 %collective-permute-start.4 = (f32[8,4096]{1,0:T(8,128)S(1)}, f32[8,4096]{1,0:T(8,128)S(1)}, u32[]{:S(2)}, u32[]{:S(2)}) collective-permute-start(f32[8,4096]{1,0:T(8,128)S(1)} %collective-permute-done.3), channel_id=1, source_target_pairs={{0,4},{4,0},{8,12},{12,8},{16,20},{20,16},{24,28},{28,24},{1,5},{5... | collective-permute-start | bytes 393224 | tf_op jit(solution)/shard_map/ppermute | solution.py:26
  23.6 4.0 %collective-permute-start.5 = (f32[8,1152]{1,0:T(8,128)S(1)}, f32[8,1152]{1,0:T(8,128)S(1)}, u32[]{:S(2)}, u32[]{:S(2)}) collective-permute-start(f32[8,1152]{1,0:T(8,128)S(1)} %pad_maximum_fusion), channel_id=1, source_target_pairs={{0,2},{1,3},{2,0},{3,1},{4,6},{5,7},{6,4},{7,5},{8,10},{9,11},{10,... | collective-permute-start | bytes 110600 | tf_op jit(solution)/shard_map/ppermute | solution.py:26
  27.7 3.8 %collective-permute-start.6 = (f32[8,640]{1,0:T(8,128)S(1)}, f32[8,640]{1,0:T(8,128)S(1)}, u32[]{:S(2)}, u32[]{:S(2)}) collective-permute-start(f32[8,640]{1,0:T(8,128)S(1)} %pad_maximum_fusion.1), channel_id=1, source_target_pairs={{0,1},{1,0},{2,3},{3,2},{4,5},{5,4},{6,7},{7,6},{8,9},{9,8},{10,11... | collective-permute-start | bytes 61448 | tf_op jit(solution)/shard_map/ppermute | solution.py:26
  31.5 1.2 %collective-permute-start.7 = (f32[8,128]{1,0:T(8,128)S(1)}, f32[8,128]{1,0:T(8,128)S(1)}, u32[]{:S(2)}, u32[]{:S(2)}) collective-permute-start(f32[8,128]{1,0:T(8,128)S(1)} %slice_add_fusion.2), channel_id=1, source_target_pairs={{0,4},{4,0},{8,12},{12,8},{16,20},{20,16},{24,28},{28,24},{1,5},{5... | collective-permute-start | bytes 12296 | tf_op jit(solution)/shard_map/ppermute | solution.py:26
  32.6 4.0 %collective-permute-start.8 = (f32[8,128]{1,0:T(8,128)S(1)}, f32[8,128]{1,0:T(8,128)S(1)}, u32[]{:S(2)}, u32[]{:S(2)}) collective-permute-start(f32[8,128]{1,0:T(8,128)S(1)} %add.101), channel_id=1, source_target_pairs={{0,8},{4,12},{8,0},{12,4},{16,24},{20,28},{24,16},{28,20},{1,9},{5... | collective-permute-start | bytes 12296 | tf_op jit(solution)/shard_map/ppermute | solution.py:26
  36.7 4.6 %collective-permute-start.9 = (f32[8,128]{1,0:T(8,128)S(1)}, f32[8,128]{1,0:T(8,128)S(1)}, u32[]{:S(2)}, u32[]{:S(2)}) collective-permute-start(f32[8,128]{1,0:T(8,128)S(1)} %add.102), channel_id=1, source_target_pairs={{0,16},{4,20},{8,24},{12,28},{16,0},{20,4},{24,8},{28,12},{1,17},{... | collective-permute-start | bytes 12296 | tf_op jit(solution)/shard_map/ppermute | solution.py:26

commit v21 on v20

--- a/solution.py
+++ b/solution.py
@@ -104,10 +104,9 @@
     if paired:
         helpers = lax.axis_size("help")
         own_pair = jnp.concatenate([vectors, exchanged(vectors, "help", 1)], axis=1)
-        vectors, _ = lax.optimization_barrier((vectors, own_pair))
         own_pair = jnp.concatenate([own_pair, exchanged(own_pair, "blk", 1)], axis=1)
-        tile_row, tile_col, counts, _ = lax.optimization_barrier(
-            (tile_row, tile_col, counts, own_pair)
+        tile_row, tile_col, counts, vectors, _ = lax.optimization_barrier(
+            (tile_row, tile_col, counts, vectors, own_pair)
         )
         mask = 2
         while mask < helpers:

time: 42.5 us -> 43.2 us (1.016)
  other arithmetic: 3.58 us -> 4.32 us
    concatenate x0 -> x1, other arithmetic: none -> 0.72 us  [local(): own_pair = jnp.concatenate([vectors, exchanged(vectors, 'help', 1)], axis=1)]
  transfers between devices with their start and end apart: 10 -> 10, of which waited for: 10 -> 10; matrix products, arithmetic and copies ran while one was open for 13% -> 12% of each run, Pallas kernels for 0% -> 0%
where the time goes in v21:
time: 43.2 us; the launch traced here: 42.6 us
  starting transfers between devices  17.4 us (40%)
  waiting for transfers between devices  13.1 us (30%)
  matrix products  4.62 us (11%)
  other arithmetic  4.32 us (10%)
  local copies, waits for them, and re-layouts  2.43 us (6%)
  between operations  0.76 us (2%)
    ppermute x9, starting transfers between devices, exchanged(): lax.ppermute(value, axis, [(source, source ^ mask) for source in range(co...  13.6 us
    ppermute x9, waiting for transfers between devices, exchanged(): lax.ppermute(value, axis, [(source, source ^ mask) for source in range(co...  12.2 us
    ppermute x1, starting transfers between devices, local(): remote = lax.ppermute(own_pair, 'blk', crossing)  3.81 us
    dot_general x1, matrix products, batch_product(): jnp.einsum('osit,ostu->osiu', pieces, tile_blocks[0, first:last:step], pr...  3.18 us
    concatenate x2, other arithmetic, batch_product(): pieces = stacked[panel_ids[:, None], column_place[first:last:step]]  1.38 us
    dot_general x1, matrix products, local(): jnp.dot(vectors, vectors.T, precision=lax.Precision.HIGHEST, preferred_el...  0.92 us
    ppermute x1, waiting for transfers between devices, local(): remote = lax.ppermute(own_pair, 'blk', crossing)  0.9 us
  transfers between devices with their start and end apart: 10, of which 10 were waited for; matrix products, arithmetic and copies ran while one was open for 12% of the time, Pallas kernels for 0%

profile of v21, /device:TPU:0, one launch (start us, length us, event | category | flops | bytes accessed | tf_op | source)
XLA Modules:
  0.0 42.6 jit_solution(582759059275548425)
XLA Ops:
  0.6 3.0 %collective-permute-start = (f32[8,512]{1,0:T(8,128)}, f32[8,512]{1,0:T(8,128)S(1)}, u32[]{:S(2)}, u32[]{:S(2)}) collective-permute-start(f32[8,512]{1,0:T(8,128)} %param.7), channel_id=1, source_target_pairs={{0,1},{1,0},{2,3},{3,2},{4,5},{5,4},{6,7},{7,6},{8,9},{9,8},{10,11... | collective-permute-start | bytes 49160 | tf_op jit(solution)/shard_map/ppermute | solution.py:26
  3.6 0.8 %constant_dynamic-update-slice_fusion.6 = (f32[8,4096]{1,0:T(8,128)S(1)}, f32[8,2048]{1,0:T(8,128)S(1)}) fusion(f32[8,512]{1,0:T(8,128)} %param.7), kind=kLoop, calls=%fused_computation.14 | loop fusion | bytes 49152
  4.4 0.1 pad.6.clone
  4.5 1.1 %collective-permute-done = f32[8,512]{1,0:T(8,128)S(1)} collective-permute-done((f32[8,512]{1,0:T(8,128)}, f32[8,512]{1,0:T(8,128)S(1)}, u32[]{:S(2)}, u32[]{:S(2)}) %collective-permute-start) | collective-permute-done | bytes 16416 | tf_op jit(solution)/shard_map/ppermute | solution.py:26
  5.6 0.7 %pad_maximum_fusion.1 = f32[8,1024]{1,0:T(8,128)S(1)} fusion(f32[8,512]{1,0:T(8,128)S(1)} %collective-permute-done, f32[8,512]{1,0:T(8,128)} %param.7), kind=kLoop, calls=%fused_computation.7 | loop fusion | flops 8192 | bytes 65536 | tf_op jit(solution)/shard_map/concatenate | solution.py:106
  6.3 0.0 collective-permute-start.1
  6.3 1.2 %collective-permute-done.1 = f32[8,1024]{1,0:T(8,128)S(1)} collective-permute-done((f32[8,1024]{1,0:T(8,128)S(1)}, f32[8,1024]{1,0:T(8,128)S(1)}, u32[]{:S(2)}, u32[]{:S(2)}) %collective-permute-start.1) | collective-permute-done | bytes 32800 | tf_op jit(solution)/shard_map/ppermute | solution.py:26
  7.5 2.0 %collective-permute-start.2 = (f32[8,2048]{1,0:T(8,128)S(1)}, f32[8,2048]{1,0:T(8,128)S(1)}, u32[]{:S(2)}, u32[]{:S(2)}) collective-permute-start(f32[8,2048]{1,0:T(8,128)S(1)} %get-tuple-element.20), channel_id=1, source_target_pairs={{0,2},{1,3},{2,0},{3,1},{4,6},{5,7},{6,4},{7,5},{8,10},{9,11},{10,... | collective-permute-start | bytes 196616 | tf_op jit(solution)/shard_map/ppermute | solution.py:26
  9.5 0.9 %fusion.27 = f32[8,8]{1,0:T(8,128)S(1)} fusion(f32[8,512]{1,0:T(8,128)} %param.7), kind=kOutput, calls=%fused_computation.68 | convolution fusion | flops 393216 | bytes 16640 | tf_op jit(solution)/shard_map/dot_general | solution.py:163
  10.5 0.7 %fusion.10 = s32[5,3]{0,1:T(4,128)S(1)} fusion(s32[1,5,3]{1,0,2:T(1,128)} %param.9, s32[]{:T(128)S(6)} %axis_index.22), kind=kLoop, calls=%fused_computation.46 | loop fusion | flops 330 | bytes 124 | tf_op jit(solution)/shard_map/add | solution.py:101
  11.2 0.7 %fusion.12 = f32[5,3]{0,1:T(4,128)S(1)} fusion(s32[5]{0:T(128)} %bitcast.79), kind=kLoop, calls=%fused_computation.51 | loop fusion | flops 30 | bytes 80 | tf_op jit(solution)/shard_map/convert_element_type | solution.py:130
  11.8 0.1 collective-permute-done.2
  12.0 3.8 %collective-permute-start.3 = (f32[8,4096]{1,0:T(8,128)S(1)}, f32[8,4096]{1,0:T(8,128)S(1)}, u32[]{:S(2)}, u32[]{:S(2)}) collective-permute-start(f32[8,4096]{1,0:T(8,128)S(1)} %constant_dynamic-update-slice_fusion.3), channel_id=1, source_target_pairs={{0,8},{8,16},{16,24},{12,4},{20,12},{28,20},{1,9},{9,17},{17,25},{... | collective-permute-start | bytes 393224 | tf_op jit(solution)/shard_map/ppermute | solution.py:118
  15.8 0.7 %fusion.20 = s32[5]{0:T(128)S(1)} fusion(s32[5]{0:T(128)} %constant.71.clone, s32[5]{0:T(128)} %constant.72.clone, pred[]{:T(512)S(6)} %eq.24), kind=kLoop, calls=%fused_computation.61 | loop fusion | flops 30 | bytes 61 | tf_op jit(solution)/shard_map/concatenate | solution.py:138
  16.5 0.7 %fusion.18 = s32[5,3,1]{0,2,1:T(1,128)S(1)} fusion(s32[1,5,3]{1,0,2:T(1,128)} %param.10, s32[5]{0:T(128)S(1)} %fusion.20, s32[]{:T(128)S(6)} %axis_index.22), kind=kLoop, calls=%fused_computation.57 | loop fusion | flops 420 | bytes 144 | tf_op jit(solution)/shard_map/concatenate | solution.py:138
  17.2 0.1 copy.23
  17.3 0.1 reshape.229
  17.4 0.9 %collective-permute-done.3 = f32[8,4096]{1,0:T(8,128)S(1)} collective-permute-done((f32[8,4096]{1,0:T(8,128)S(1)}, f32[8,4096]{1,0:T(8,128)S(1)}, u32[]{:S(2)}, u32[]{:S(2)}) %collective-permute-start.3) | collective-permute-done | bytes 131104 | tf_op jit(solution)/shard_map/ppermute | solution.py:118
  18.3 0.1 collective-permute-start.4
  18.4 1.3 %collective-permute-done.4 = f32[8,4096]{1,0:T(8,128)S(1)} collective-permute-done((f32[8,4096]{1,0:T(8,128)S(1)}, f32[8,4096]{1,0:T(8,128)S(1)}, u32[]{:S(2)}, u32[]{:S(2)}) %collective-permute-start.4) | collective-permute-done | bytes 131104 | tf_op jit(solution)/shard_map/ppermute | solution.py:26
  19.8 0.6 %gather_fusion = f32[15,8,256]{2,1,0:T(8,128)S(1)} fusion(f32[6,8,8,256]{3,2,1,0:T(8,128)S(1)} %bitcast.78, s32[15]{0:T(128)S(1)} %reshape.229), kind=kCustom, calls=%fused_computation | custom fusion | bytes 245880 | tf_op jit(solution)/shard_map/gather | solution.py:138
  20.4 3.2 %fusion = f32[5,3,8,256]{3,2,1,0:T(8,128)S(1)} fusion(f32[5,3,8,256]{3,2,1,0:T(8,128)S(1)} %bitcast.69, f32[1,5,3,256,256]{4,3,2,1,0:T(8,128)} %param.8), kind=kOutput, calls=%fused_computation.1 | convolution fusion | flops 47185920 | bytes 4177920 | tf_op jit(solution)/shard_map/osit,ostu->osiu/dot_general | solution.py:139
  23.6 0.4 convolution_bitcast_fusion
  24.0 0.1 fusion.26
  24.1 0.1 maximum_multiply_fusion
  24.3 1.5 %collective-permute-start.5 = (f32[8,1152]{1,0:T(8,128)S(1)}, f32[8,1152]{1,0:T(8,128)S(1)}, u32[]{:S(2)}, u32[]{:S(2)}) collective-permute-start(f32[8,1152]{1,0:T(8,128)S(1)} %pad_maximum_fusion), channel_id=1, source_target_pairs={{0,2},{1,3},{2,0},{3,1},{4,6},{5,7},{6,4},{7,5},{8,10},{9,11},{10,... | collective-permute-start | bytes 110600 | tf_op jit(solution)/shard_map/ppermute | solution.py:26
  25.8 2.4 %collective-permute-done.5 = f32[8,1152]{1,0:T(8,128)S(1)} collective-permute-done((f32[8,1152]{1,0:T(8,128)S(1)}, f32[8,1152]{1,0:T(8,128)S(1)}, u32[]{:S(2)}, u32[]{:S(2)}) %collective-permute-start.5) | collective-permute-done | bytes 36896 | tf_op jit(solution)/shard_map/ppermute | solution.py:26
  28.3 0.1 slice_add_fusion.3
  28.4 1.5 %collective-permute-start.6 = (f32[8,640]{1,0:T(8,128)S(1)}, f32[8,640]{1,0:T(8,128)S(1)}, u32[]{:S(2)}, u32[]{:S(2)}) collective-permute-start(f32[8,640]{1,0:T(8,128)S(1)} %pad_maximum_fusion.2), channel_id=1, source_target_pairs={{0,1},{1,0},{2,3},{3,2},{4,5},{5,4},{6,7},{7,6},{8,9},{9,8},{10,11... | collective-permute-start | bytes 61448 | tf_op jit(solution)/shard_map/ppermute | solution.py:26
  29.9 2.3 %collective-permute-done.6 = f32[8,640]{1,0:T(8,128)S(1)} collective-permute-done((f32[8,640]{1,0:T(8,128)S(1)}, f32[8,640]{1,0:T(8,128)S(1)}, u32[]{:S(2)}, u32[]{:S(2)}) %collective-permute-start.6) | collective-permute-done | bytes 20512 | tf_op jit(solution)/shard_map/ppermute | solution.py:26
  32.1 0.0 collective-permute-start.7
  32.1 1.2 %collective-permute-done.7 = f32[8,128]{1,0:T(8,128)S(1)} collective-permute-done((f32[8,128]{1,0:T(8,128)S(1)}, f32[8,128]{1,0:T(8,128)S(1)}, u32[]{:S(2)}, u32[]{:S(2)}) %collective-permute-start.7) | collective-permute-done | bytes 4128 | tf_op jit(solution)/shard_map/ppermute | solution.py:26
  33.3 2.4 %collective-permute-start.8 = (f32[8,128]{1,0:T(8,128)S(1)}, f32[8,128]{1,0:T(8,128)S(1)}, u32[]{:S(2)}, u32[]{:S(2)}) collective-permute-start(f32[8,128]{1,0:T(8,128)S(1)} %add.101), channel_id=1, source_target_pairs={{0,8},{4,12},{8,0},{12,4},{16,24},{20,28},{24,16},{28,20},{1,9},{5... | collective-permute-start | bytes 12296 | tf_op jit(solution)/shard_map/ppermute | solution.py:26
  35.8 1.6 %collective-permute-done.8 = f32[8,128]{1,0:T(8,128)S(1)} collective-permute-done((f32[8,128]{1,0:T(8,128)S(1)}, f32[8,128]{1,0:T(8,128)S(1)}, u32[]{:S(2)}, u32[]{:S(2)}) %collective-permute-start.8) | collective-permute-done | bytes 4128 | tf_op jit(solution)/shard_map/ppermute | solution.py:26
  37.4 3.0 %collective-permute-start.9 = (f32[8,128]{1,0:T(8,128)S(1)}, f32[8,128]{1,0:T(8,128)S(1)}, u32[]{:S(2)}, u32[]{:S(2)}) collective-permute-start(f32[8,128]{1,0:T(8,128)S(1)} %add.102), channel_id=1, source_target_pairs={{0,16},{4,20},{8,24},{12,28},{16,0},{20,4},{24,8},{28,12},{1,17},{... | collective-permute-start | bytes 12296 | tf_op jit(solution)/shard_map/ppermute | solution.py:26
  40.4 0.6 %slice_add_fusion.1 = f32[8,512]{1,0:T(8,128)} fusion(f32[8,640]{1,0:T(8,128)S(1)} %collective-permute-done.6, f32[8,1024]{1,0:T(8,128)S(1)} %slice_add_fusion), kind=kLoop, calls=%fused_computation.22 | loop fusion | flops 4096 | bytes 49152 | tf_op jit(solution)/shard_map/add | solution.py:60
  41.0 1.0 %collective-permute-done.9 = f32[8,128]{1,0:T(8,128)S(1)} collective-permute-done((f32[8,128]{1,0:T(8,128)S(1)}, f32[8,128]{1,0:T(8,128)S(1)}, u32[]{:S(2)}, u32[]{:S(2)}) %collective-permute-start.9) | collective-permute-done | bytes 4128 | tf_op jit(solution)/shard_map/ppermute | solution.py:26
  42.0 0.7 %fusion.25 = (f32[8,8]{1,0:T(8,128)}, f32[8,8]{1,0:T(8,128)}) fusion(f32[8,128]{1,0:T(8,128)S(1)} %add.103), kind=kLoop, calls=%fused_computation.66 | loop fusion | bytes 1024 | tf_op jit(solution)/shard_map/slice | solution.py:179
  (23 shorter events, 0.2 us)
Async XLA Ops:
  0.6 4.9 %collective-permute-start = (f32[8,512]{1,0:T(8,128)}, f32[8,512]{1,0:T(8,128)S(1)}, u32[]{:S(2)}, u32[]{:S(2)}) collective-permute-start(f32[8,512]{1,0:T(8,128)} %param.7), channel_id=1, source_target_pairs={{0,1},{1,0},{2,3},{3,2},{4,5},{5,4},{6,7},{7,6},{8,9},{9,8},{10,11... | collective-permute-start | bytes 49160 | tf_op jit(solution)/shard_map/ppermute | solution.py:26
  6.3 1.2 %collective-permute-start.1 = (f32[8,1024]{1,0:T(8,128)S(1)}, f32[8,1024]{1,0:T(8,128)S(1)}, u32[]{:S(2)}, u32[]{:S(2)}) collective-permute-start(f32[8,1024]{1,0:T(8,128)S(1)} %pad_maximum_fusion.1), channel_id=1, source_target_pairs={{0,4},{4,0},{8,12},{12,8},{16,20},{20,16},{24,28},{28,24},{1,5},{5... | collective-permute-start | bytes 98312 | tf_op jit(solution)/shard_map/ppermute | solution.py:26
  7.5 4.5 %collective-permute-start.2 = (f32[8,2048]{1,0:T(8,128)S(1)}, f32[8,2048]{1,0:T(8,128)S(1)}, u32[]{:S(2)}, u32[]{:S(2)}) collective-permute-start(f32[8,2048]{1,0:T(8,128)S(1)} %get-tuple-element.20), channel_id=1, source_target_pairs={{0,2},{1,3},{2,0},{3,1},{4,6},{5,7},{6,4},{7,5},{8,10},{9,11},{10,... | collective-permute-start | bytes 196616 | tf_op jit(solution)/shard_map/ppermute | solution.py:26
  12.0 6.3 %collective-permute-start.3 = (f32[8,4096]{1,0:T(8,128)S(1)}, f32[8,4096]{1,0:T(8,128)S(1)}, u32[]{:S(2)}, u32[]{:S(2)}) collective-permute-start(f32[8,4096]{1,0:T(8,128)S(1)} %constant_dynamic-update-slice_fusion.3), channel_id=1, source_target_pairs={{0,8},{8,16},{16,24},{12,4},{20,12},{28,20},{1,9},{9,17},{17,25},{... | collective-permute-start | bytes 393224 | tf_op jit(solution)/shard_map/ppermute | solution.py:118
  18.3 1.4 %collective-permute-start.4 = (f32[8,4096]{1,0:T(8,128)S(1)}, f32[8,4096]{1,0:T(8,128)S(1)}, u32[]{:S(2)}, u32[]{:S(2)}) collective-permute-start(f32[8,4096]{1,0:T(8,128)S(1)} %collective-permute-done.3), channel_id=1, source_target_pairs={{0,4},{4,0},{8,12},{12,8},{16,20},{20,16},{24,28},{28,24},{1,5},{5... | collective-permute-start | bytes 393224 | tf_op jit(solution)/shard_map/ppermute | solution.py:26
  24.3 4.0 %collective-permute-start.5 = (f32[8,1152]{1,0:T(8,128)S(1)}, f32[8,1152]{1,0:T(8,128)S(1)}, u32[]{:S(2)}, u32[]{:S(2)}) collective-permute-start(f32[8,1152]{1,0:T(8,128)S(1)} %pad_maximum_fusion), channel_id=1, source_target_pairs={{0,2},{1,3},{2,0},{3,1},{4,6},{5,7},{6,4},{7,5},{8,10},{9,11},{10,... | collective-permute-start | bytes 110600 | tf_op jit(solution)/shard_map/ppermute | solution.py:26
  28.4 3.8 %collective-permute-start.6 = (f32[8,640]{1,0:T(8,128)S(1)}, f32[8,640]{1,0:T(8,128)S(1)}, u32[]{:S(2)}, u32[]{:S(2)}) collective-permute-start(f32[8,640]{1,0:T(8,128)S(1)} %pad_maximum_fusion.2), channel_id=1, source_target_pairs={{0,1},{1,0},{2,3},{3,2},{4,5},{5,4},{6,7},{7,6},{8,9},{9,8},{10,11... | collective-permute-start | bytes 61448 | tf_op jit(solution)/shard_map/ppermute | solution.py:26
  32.1 1.2 %collective-permute-start.7 = (f32[8,128]{1,0:T(8,128)S(1)}, f32[8,128]{1,0:T(8,128)S(1)}, u32[]{:S(2)}, u32[]{:S(2)}) collective-permute-start(f32[8,128]{1,0:T(8,128)S(1)} %slice_add_fusion.2), channel_id=1, source_target_pairs={{0,4},{4,0},{8,12},{12,8},{16,20},{20,16},{24,28},{28,24},{1,5},{5... | collective-permute-start | bytes 12296 | tf_op jit(solution)/shard_map/ppermute | solution.py:26
  33.3 4.0 %collective-permute-start.8 = (f32[8,128]{1,0:T(8,128)S(1)}, f32[8,128]{1,0:T(8,128)S(1)}, u32[]{:S(2)}, u32[]{:S(2)}) collective-permute-start(f32[8,128]{1,0:T(8,128)S(1)} %add.101), channel_id=1, source_target_pairs={{0,8},{4,12},{8,0},{12,4},{16,24},{20,28},{24,16},{28,20},{1,9},{5... | collective-permute-start | bytes 12296 | tf_op jit(solution)/shard_map/ppermute | solution.py:26
  37.4 4.6 %collective-permute-start.9 = (f32[8,128]{1,0:T(8,128)S(1)}, f32[8,128]{1,0:T(8,128)S(1)}, u32[]{:S(2)}, u32[]{:S(2)}) collective-permute-start(f32[8,128]{1,0:T(8,128)S(1)} %add.102), channel_id=1, source_target_pairs={{0,16},{4,20},{8,24},{12,28},{16,0},{20,4},{24,8},{28,12},{1,17},{... | collective-permute-start | bytes 12296 | tf_op jit(solution)/shard_map/ppermute | solution.py:26

commit v22 on v20

--- a/solution.py
+++ b/solution.py
@@ -104,7 +104,6 @@
     if paired:
         helpers = lax.axis_size("help")
         own_pair = jnp.concatenate([vectors, exchanged(vectors, "help", 1)], axis=1)
-        vectors, _ = lax.optimization_barrier((vectors, own_pair))
         own_pair = jnp.concatenate([own_pair, exchanged(own_pair, "blk", 1)], axis=1)
         tile_row, tile_col, counts, _ = lax.optimization_barrier(
             (tile_row, tile_col, counts, own_pair)

time: 42.5 us -> 43.2 us (1.016)
  other arithmetic: 3.58 us -> 4.3 us
    concatenate x0 -> x1, other arithmetic: none -> 0.72 us  [local(): own_pair = jnp.concatenate([vectors, exchanged(vectors, 'help', 1)], axis=1)]
  transfers between devices with their start and end apart: 10 -> 10, of which waited for: 10 -> 10; matrix products, arithmetic and copies ran while one was open for 13% -> 12% of each run, Pallas kernels for 0% -> 0%
where the time goes in v22:
time: 43.2 us; the launch traced here: 42.6 us
  starting transfers between devices  17.4 us (40%)
  waiting for transfers between devices  13.1 us (30%)
  matrix products  4.62 us (11%)
  other arithmetic  4.3 us (10%)
  local copies, waits for them, and re-layouts  2.42 us (6%)
  between operations  0.76 us (2%)
    ppermute x9, starting transfers between devices, exchanged(): lax.ppermute(value, axis, [(source, source ^ mask) for source in range(co...  13.6 us
    ppermute x9, waiting for transfers between devices, exchanged(): lax.ppermute(value, axis, [(source, source ^ mask) for source in range(co...  12.2 us
    ppermute x1, starting transfers between devices, local(): remote = lax.ppermute(own_pair, 'blk', crossing)  3.81 us
    dot_general x1, matrix products, batch_product(): jnp.einsum('osit,ostu->osiu', pieces, tile_blocks[0, first:last:step], pr...  3.18 us
    concatenate x2, other arithmetic, batch_product(): pieces = stacked[panel_ids[:, None], column_place[first:last:step]]  1.38 us
    dot_general x1, matrix products, local(): jnp.dot(vectors, vectors.T, precision=lax.Precision.HIGHEST, preferred_el...  0.91 us
    ppermute x1, waiting for transfers between devices, local(): remote = lax.ppermute(own_pair, 'blk', crossing)  0.9 us
  transfers between devices with their start and end apart: 10, of which 10 were waited for; matrix products, arithmetic and copies ran while one was open for 12% of the time, Pallas kernels for 0%

profile of v22, /device:TPU:0, one launch (start us, length us, event | category | flops | bytes accessed | tf_op | source)
XLA Modules:
  0.0 42.6 jit_solution(11455734629437099708)
XLA Ops:
  0.6 3.0 %collective-permute-start = (f32[8,512]{1,0:T(8,128)}, f32[8,512]{1,0:T(8,128)S(1)}, u32[]{:S(2)}, u32[]{:S(2)}) collective-permute-start(f32[8,512]{1,0:T(8,128)} %param.7), channel_id=1, source_target_pairs={{0,1},{1,0},{2,3},{3,2},{4,5},{5,4},{6,7},{7,6},{8,9},{9,8},{10,11... | collective-permute-start | bytes 49160 | tf_op jit(solution)/shard_map/ppermute | solution.py:26
  3.6 0.9 %fusion.27 = f32[8,8]{1,0:T(8,128)S(1)} fusion(f32[8,512]{1,0:T(8,128)} %param.7), kind=kOutput, calls=%fused_computation.68 | convolution fusion | flops 393216 | bytes 16640 | tf_op jit(solution)/shard_map/dot_general | solution.py:163
  4.5 0.7 %constant_dynamic-update-slice_fusion.2 = (f32[8,2048]{1,0:T(8,128)S(1)}, f32[8,4096]{1,0:T(8,128)S(1)}) fusion(f32[8,512]{1,0:T(8,128)} %param.7), kind=kLoop, calls=%fused_computation.10 | loop fusion | bytes 49152
  5.3 0.1 pad.6.clone
  5.4 0.2 collective-permute-done
  5.6 0.7 %pad_maximum_fusion.1 = f32[8,1024]{1,0:T(8,128)S(1)} fusion(f32[8,512]{1,0:T(8,128)S(1)} %collective-permute-done, f32[8,512]{1,0:T(8,128)} %param.7), kind=kLoop, calls=%fused_computation.7 | loop fusion | flops 8192 | bytes 65536 | tf_op jit(solution)/shard_map/concatenate | solution.py:106
  6.3 0.0 collective-permute-start.1
  6.3 1.2 %collective-permute-done.1 = f32[8,1024]{1,0:T(8,128)S(1)} collective-permute-done((f32[8,1024]{1,0:T(8,128)S(1)}, f32[8,1024]{1,0:T(8,128)S(1)}, u32[]{:S(2)}, u32[]{:S(2)}) %collective-permute-start.1) | collective-permute-done | bytes 32800 | tf_op jit(solution)/shard_map/ppermute | solution.py:26
  7.5 2.0 %collective-permute-start.2 = (f32[8,2048]{1,0:T(8,128)S(1)}, f32[8,2048]{1,0:T(8,128)S(1)}, u32[]{:S(2)}, u32[]{:S(2)}) collective-permute-start(f32[8,2048]{1,0:T(8,128)S(1)} %get-tuple-element.17), channel_id=1, source_target_pairs={{0,2},{1,3},{2,0},{3,1},{4,6},{5,7},{6,4},{7,5},{8,10},{9,11},{10,... | collective-permute-start | bytes 196616 | tf_op jit(solution)/shard_map/ppermute | solution.py:26
  9.5 0.7 %fusion.10 = s32[5,3]{0,1:T(4,128)S(1)} fusion(s32[1,5,3]{1,0,2:T(1,128)} %param.9, s32[]{:T(128)S(6)} %axis_index.22), kind=kLoop, calls=%fused_computation.46 | loop fusion | flops 330 | bytes 124 | tf_op jit(solution)/shard_map/add | solution.py:101
  10.2 0.7 %fusion.12 = f32[5,3]{0,1:T(4,128)S(1)} fusion(s32[5]{0:T(128)} %bitcast.79), kind=kLoop, calls=%fused_computation.51 | loop fusion | flops 30 | bytes 80 | tf_op jit(solution)/shard_map/convert_element_type | solution.py:130
  10.9 1.1 %collective-permute-done.2 = f32[8,2048]{1,0:T(8,128)S(1)} collective-permute-done((f32[8,2048]{1,0:T(8,128)S(1)}, f32[8,2048]{1,0:T(8,128)S(1)}, u32[]{:S(2)}, u32[]{:S(2)}) %collective-permute-start.2) | collective-permute-done | bytes 65568 | tf_op jit(solution)/shard_map/ppermute | solution.py:26
  12.0 3.8 %collective-permute-start.3 = (f32[8,4096]{1,0:T(8,128)S(1)}, f32[8,4096]{1,0:T(8,128)S(1)}, u32[]{:S(2)}, u32[]{:S(2)}) collective-permute-start(f32[8,4096]{1,0:T(8,128)S(1)} %constant_dynamic-update-slice_fusion.3), channel_id=1, source_target_pairs={{0,8},{8,16},{16,24},{12,4},{20,12},{28,20},{1,9},{9,17},{17,25},{... | collective-permute-start | bytes 393224 | tf_op jit(solution)/shard_map/ppermute | solution.py:118
  15.8 0.7 %fusion.20 = s32[5]{0:T(128)S(1)} fusion(s32[5]{0:T(128)} %constant.71.clone, s32[5]{0:T(128)} %constant.72.clone, pred[]{:T(512)S(6)} %eq.24), kind=kLoop, calls=%fused_computation.61 | loop fusion | flops 30 | bytes 61 | tf_op jit(solution)/shard_map/concatenate | solution.py:138
  16.5 0.7 %fusion.18 = s32[5,3,1]{0,2,1:T(1,128)S(1)} fusion(s32[1,5,3]{1,0,2:T(1,128)} %param.10, s32[5]{0:T(128)S(1)} %fusion.20, s32[]{:T(128)S(6)} %axis_index.22), kind=kLoop, calls=%fused_computation.57 | loop fusion | flops 420 | bytes 144 | tf_op jit(solution)/shard_map/concatenate | solution.py:138
  17.2 0.1 copy.23
  17.3 0.1 reshape.229
  17.4 0.9 %collective-permute-done.3 = f32[8,4096]{1,0:T(8,128)S(1)} collective-permute-done((f32[8,4096]{1,0:T(8,128)S(1)}, f32[8,4096]{1,0:T(8,128)S(1)}, u32[]{:S(2)}, u32[]{:S(2)}) %collective-permute-start.3) | collective-permute-done | bytes 131104 | tf_op jit(solution)/shard_map/ppermute | solution.py:118
  18.3 0.1 collective-permute-start.4
  18.4 1.3 %collective-permute-done.4 = f32[8,4096]{1,0:T(8,128)S(1)} collective-permute-done((f32[8,4096]{1,0:T(8,128)S(1)}, f32[8,4096]{1,0:T(8,128)S(1)}, u32[]{:S(2)}, u32[]{:S(2)}) %collective-permute-start.4) | collective-permute-done | bytes 131104 | tf_op jit(solution)/shard_map/ppermute | solution.py:26
  19.8 0.6 %gather_fusion = f32[15,8,256]{2,1,0:T(8,128)S(1)} fusion(f32[6,8,8,256]{3,2,1,0:T(8,128)S(1)} %bitcast.78, s32[15]{0:T(128)S(1)} %reshape.229), kind=kCustom, calls=%fused_computation | custom fusion | bytes 245880 | tf_op jit(solution)/shard_map/gather | solution.py:138
  20.4 3.2 %fusion = f32[5,3,8,256]{3,2,1,0:T(8,128)S(1)} fusion(f32[5,3,8,256]{3,2,1,0:T(8,128)S(1)} %bitcast.69, f32[1,5,3,256,256]{4,3,2,1,0:T(8,128)} %param.8), kind=kOutput, calls=%fused_computation.1 | convolution fusion | flops 47185920 | bytes 4177920 | tf_op jit(solution)/shard_map/osit,ostu->osiu/dot_general | solution.py:139
  23.6 0.4 convolution_bitcast_fusion
  24.0 0.1 fusion.26
  24.1 0.1 maximum_multiply_fusion
  24.3 1.5 %collective-permute-start.5 = (f32[8,1152]{1,0:T(8,128)S(1)}, f32[8,1152]{1,0:T(8,128)S(1)}, u32[]{:S(2)}, u32[]{:S(2)}) collective-permute-start(f32[8,1152]{1,0:T(8,128)S(1)} %pad_maximum_fusion), channel_id=1, source_target_pairs={{0,2},{1,3},{2,0},{3,1},{4,6},{5,7},{6,4},{7,5},{8,10},{9,11},{10,... | collective-permute-start | bytes 110600 | tf_op jit(solution)/shard_map/ppermute | solution.py:26
  25.8 2.4 %collective-permute-done.5 = f32[8,1152]{1,0:T(8,128)S(1)} collective-permute-done((f32[8,1152]{1,0:T(8,128)S(1)}, f32[8,1152]{1,0:T(8,128)S(1)}, u32[]{:S(2)}, u32[]{:S(2)}) %collective-permute-start.5) | collective-permute-done | bytes 36896 | tf_op jit(solution)/shard_map/ppermute | solution.py:26
  28.3 0.1 slice_add_fusion.3
  28.4 1.5 %collective-permute-start.6 = (f32[8,640]{1,0:T(8,128)S(1)}, f32[8,640]{1,0:T(8,128)S(1)}, u32[]{:S(2)}, u32[]{:S(2)}) collective-permute-start(f32[8,640]{1,0:T(8,128)S(1)} %pad_maximum_fusion.2), channel_id=1, source_target_pairs={{0,1},{1,0},{2,3},{3,2},{4,5},{5,4},{6,7},{7,6},{8,9},{9,8},{10,11... | collective-permute-start | bytes 61448 | tf_op jit(solution)/shard_map/ppermute | solution.py:26
  29.9 2.3 %collective-permute-done.6 = f32[8,640]{1,0:T(8,128)S(1)} collective-permute-done((f32[8,640]{1,0:T(8,128)S(1)}, f32[8,640]{1,0:T(8,128)S(1)}, u32[]{:S(2)}, u32[]{:S(2)}) %collective-permute-start.6) | collective-permute-done | bytes 20512 | tf_op jit(solution)/shard_map/ppermute | solution.py:26
  32.1 0.0 collective-permute-start.7
  32.1 1.2 %collective-permute-done.7 = f32[8,128]{1,0:T(8,128)S(1)} collective-permute-done((f32[8,128]{1,0:T(8,128)S(1)}, f32[8,128]{1,0:T(8,128)S(1)}, u32[]{:S(2)}, u32[]{:S(2)}) %collective-permute-start.7) | collective-permute-done | bytes 4128 | tf_op jit(solution)/shard_map/ppermute | solution.py:26
  33.3 2.4 %collective-permute-start.8 = (f32[8,128]{1,0:T(8,128)S(1)}, f32[8,128]{1,0:T(8,128)S(1)}, u32[]{:S(2)}, u32[]{:S(2)}) collective-permute-start(f32[8,128]{1,0:T(8,128)S(1)} %add.101), channel_id=1, source_target_pairs={{0,8},{4,12},{8,0},{12,4},{16,24},{20,28},{24,16},{28,20},{1,9},{5... | collective-permute-start | bytes 12296 | tf_op jit(solution)/shard_map/ppermute | solution.py:26
  35.8 1.6 %collective-permute-done.8 = f32[8,128]{1,0:T(8,128)S(1)} collective-permute-done((f32[8,128]{1,0:T(8,128)S(1)}, f32[8,128]{1,0:T(8,128)S(1)}, u32[]{:S(2)}, u32[]{:S(2)}) %collective-permute-start.8) | collective-permute-done | bytes 4128 | tf_op jit(solution)/shard_map/ppermute | solution.py:26
  37.4 3.0 %collective-permute-start.9 = (f32[8,128]{1,0:T(8,128)S(1)}, f32[8,128]{1,0:T(8,128)S(1)}, u32[]{:S(2)}, u32[]{:S(2)}) collective-permute-start(f32[8,128]{1,0:T(8,128)S(1)} %add.102), channel_id=1, source_target_pairs={{0,16},{4,20},{8,24},{12,28},{16,0},{20,4},{24,8},{28,12},{1,17},{... | collective-permute-start | bytes 12296 | tf_op jit(solution)/shard_map/ppermute | solution.py:26
  40.4 0.6 %slice_add_fusion.1 = f32[8,512]{1,0:T(8,128)} fusion(f32[8,640]{1,0:T(8,128)S(1)} %collective-permute-done.6, f32[8,1024]{1,0:T(8,128)S(1)} %slice_add_fusion), kind=kLoop, calls=%fused_computation.22 | loop fusion | flops 4096 | bytes 49152 | tf_op jit(solution)/shard_map/add | solution.py:60
  41.0 1.0 %collective-permute-done.9 = f32[8,128]{1,0:T(8,128)S(1)} collective-permute-done((f32[8,128]{1,0:T(8,128)S(1)}, f32[8,128]{1,0:T(8,128)S(1)}, u32[]{:S(2)}, u32[]{:S(2)}) %collective-permute-start.9) | collective-permute-done | bytes 4128 | tf_op jit(solution)/shard_map/ppermute | solution.py:26
  42.0 0.7 %fusion.25 = (f32[8,8]{1,0:T(8,128)}, f32[8,8]{1,0:T(8,128)}) fusion(f32[8,128]{1,0:T(8,128)S(1)} %add.103), kind=kLoop, calls=%fused_computation.66 | loop fusion | bytes 1024 | tf_op jit(solution)/shard_map/slice | solution.py:179
  (23 shorter events, 0.2 us)
Async XLA Ops:
  0.6 4.9 %collective-permute-start = (f32[8,512]{1,0:T(8,128)}, f32[8,512]{1,0:T(8,128)S(1)}, u32[]{:S(2)}, u32[]{:S(2)}) collective-permute-start(f32[8,512]{1,0:T(8,128)} %param.7), channel_id=1, source_target_pairs={{0,1},{1,0},{2,3},{3,2},{4,5},{5,4},{6,7},{7,6},{8,9},{9,8},{10,11... | collective-permute-start | bytes 49160 | tf_op jit(solution)/shard_map/ppermute | solution.py:26
  6.3 1.2 %collective-permute-start.1 = (f32[8,1024]{1,0:T(8,128)S(1)}, f32[8,1024]{1,0:T(8,128)S(1)}, u32[]{:S(2)}, u32[]{:S(2)}) collective-permute-start(f32[8,1024]{1,0:T(8,128)S(1)} %pad_maximum_fusion.1), channel_id=1, source_target_pairs={{0,4},{4,0},{8,12},{12,8},{16,20},{20,16},{24,28},{28,24},{1,5},{5... | collective-permute-start | bytes 98312 | tf_op jit(solution)/shard_map/ppermute | solution.py:26
  7.5 4.5 %collective-permute-start.2 = (f32[8,2048]{1,0:T(8,128)S(1)}, f32[8,2048]{1,0:T(8,128)S(1)}, u32[]{:S(2)}, u32[]{:S(2)}) collective-permute-start(f32[8,2048]{1,0:T(8,128)S(1)} %get-tuple-element.17), channel_id=1, source_target_pairs={{0,2},{1,3},{2,0},{3,1},{4,6},{5,7},{6,4},{7,5},{8,10},{9,11},{10,... | collective-permute-start | bytes 196616 | tf_op jit(solution)/shard_map/ppermute | solution.py:26
  12.0 6.3 %collective-permute-start.3 = (f32[8,4096]{1,0:T(8,128)S(1)}, f32[8,4096]{1,0:T(8,128)S(1)}, u32[]{:S(2)}, u32[]{:S(2)}) collective-permute-start(f32[8,4096]{1,0:T(8,128)S(1)} %constant_dynamic-update-slice_fusion.3), channel_id=1, source_target_pairs={{0,8},{8,16},{16,24},{12,4},{20,12},{28,20},{1,9},{9,17},{17,25},{... | collective-permute-start | bytes 393224 | tf_op jit(solution)/shard_map/ppermute | solution.py:118
  18.3 1.4 %collective-permute-start.4 = (f32[8,4096]{1,0:T(8,128)S(1)}, f32[8,4096]{1,0:T(8,128)S(1)}, u32[]{:S(2)}, u32[]{:S(2)}) collective-permute-start(f32[8,4096]{1,0:T(8,128)S(1)} %collective-permute-done.3), channel_id=1, source_target_pairs={{0,4},{4,0},{8,12},{12,8},{16,20},{20,16},{24,28},{28,24},{1,5},{5... | collective-permute-start | bytes 393224 | tf_op jit(solution)/shard_map/ppermute | solution.py:26
  24.3 4.0 %collective-permute-start.5 = (f32[8,1152]{1,0:T(8,128)S(1)}, f32[8,1152]{1,0:T(8,128)S(1)}, u32[]{:S(2)}, u32[]{:S(2)}) collective-permute-start(f32[8,1152]{1,0:T(8,128)S(1)} %pad_maximum_fusion), channel_id=1, source_target_pairs={{0,2},{1,3},{2,0},{3,1},{4,6},{5,7},{6,4},{7,5},{8,10},{9,11},{10,... | collective-permute-start | bytes 110600 | tf_op jit(solution)/shard_map/ppermute | solution.py:26
  28.4 3.8 %collective-permute-start.6 = (f32[8,640]{1,0:T(8,128)S(1)}, f32[8,640]{1,0:T(8,128)S(1)}, u32[]{:S(2)}, u32[]{:S(2)}) collective-permute-start(f32[8,640]{1,0:T(8,128)S(1)} %pad_maximum_fusion.2), channel_id=1, source_target_pairs={{0,1},{1,0},{2,3},{3,2},{4,5},{5,4},{6,7},{7,6},{8,9},{9,8},{10,11... | collective-permute-start | bytes 61448 | tf_op jit(solution)/shard_map/ppermute | solution.py:26
  32.1 1.2 %collective-permute-start.7 = (f32[8,128]{1,0:T(8,128)S(1)}, f32[8,128]{1,0:T(8,128)S(1)}, u32[]{:S(2)}, u32[]{:S(2)}) collective-permute-start(f32[8,128]{1,0:T(8,128)S(1)} %slice_add_fusion.2), channel_id=1, source_target_pairs={{0,4},{4,0},{8,12},{12,8},{16,20},{20,16},{24,28},{28,24},{1,5},{5... | collective-permute-start | bytes 12296 | tf_op jit(solution)/shard_map/ppermute | solution.py:26
  33.3 4.0 %collective-permute-start.8 = (f32[8,128]{1,0:T(8,128)S(1)}, f32[8,128]{1,0:T(8,128)S(1)}, u32[]{:S(2)}, u32[]{:S(2)}) collective-permute-start(f32[8,128]{1,0:T(8,128)S(1)} %add.101), channel_id=1, source_target_pairs={{0,8},{4,12},{8,0},{12,4},{16,24},{20,28},{24,16},{28,20},{1,9},{5... | collective-permute-start | bytes 12296 | tf_op jit(solution)/shard_map/ppermute | solution.py:26
  37.4 4.6 %collective-permute-start.9 = (f32[8,128]{1,0:T(8,128)S(1)}, f32[8,128]{1,0:T(8,128)S(1)}, u32[]{:S(2)}, u32[]{:S(2)}) collective-permute-start(f32[8,128]{1,0:T(8,128)S(1)} %add.102), channel_id=1, source_target_pairs={{0,16},{4,20},{8,24},{12,28},{16,0},{20,4},{24,8},{28,12},{1,17},{... | collective-permute-start | bytes 12296 | tf_op jit(solution)/shard_map/ppermute | solution.py:26

commit v23 on v20

--- a/solution.py
+++ b/solution.py
@@ -143,12 +143,11 @@
             tile_blocks[0, first:last:step],
             precision=lax.Precision.HIGH,
         )
-        return jnp.einsum(
-            "osiu,osr->iru",
-            contribution,
-            one_hot[first:last:step],
-            precision=lax.Precision.HIGH,
-        )
+        placed_rows = row_place[first:last:step].reshape(-1)
+        weighted = contribution * live[first:last:step][:, :, None, None]
+        rows = jnp.zeros((group_rows, VEC, TILE), jnp.float32)
+        rows = rows.at[placed_rows].add(weighted.reshape(-1, VEC, TILE))
+        return rows.transpose(1, 0, 2)
 
     if paired:
         panel_ids = jnp.where(

time: 42.5 us -> 43.2 us (1.016)
  local copies, waits for them, and re-layouts: 2.43 us -> 3.26 us
  other arithmetic: 3.58 us -> 4.07 us
    scatter-add x0 -> x1, other arithmetic: none -> 1.11 us  [batch_product(): rows = rows.at[placed_rows].add(weighted.reshape(-1, VEC, TILE))]
    optimization_barrier x0 -> x1, local copies, waits for them, and re-layouts: none -> 0.77 us  [local(): lax.optimization_barrier((tile_row, tile_col, counts, own_pair))]
    add x1 -> x0, other arithmetic: 0.69 us -> none  [placed(): (tile_index // tiles_per_piece ^ order) * tiles_per_piece]
where the time goes in v23:
time: 43.2 us; the launch traced here: 42.7 us
  starting transfers between devices  17.3 us (40%)
  waiting for transfers between devices  13 us (30%)
  matrix products  4.23 us (10%)
  other arithmetic  4.07 us (9%)
  local copies, waits for them, and re-layouts  3.26 us (8%)
  between operations  0.77 us (2%)
    ppermute x9, starting transfers between devices, exchanged(): lax.ppermute(value, axis, [(source, source ^ mask) for source in range(co...  13.6 us
    ppermute x9, waiting for transfers between devices, exchanged(): lax.ppermute(value, axis, [(source, source ^ mask) for source in range(co...  12.1 us
    ppermute x1, starting transfers between devices, local(): remote = lax.ppermute(own_pair, 'blk', crossing)  3.7 us
    dot_general x1, matrix products, batch_product(): jnp.einsum('osit,ostu->osiu', pieces, tile_blocks[0, first:last:step], pr...  3.18 us
    concatenate x2, other arithmetic, batch_product(): pieces = stacked[panel_ids[:, None], column_place[first:last:step]]  1.38 us
    scatter-add x1, other arithmetic, batch_product(): rows = rows.at[placed_rows].add(weighted.reshape(-1, VEC, TILE))  1.11 us
    dot_general x1, matrix products, local(): jnp.dot(vectors, vectors.T, precision=lax.Precision.HIGHEST, preferred_el...  0.92 us
    ppermute x1, waiting for transfers between devices, local(): remote = lax.ppermute(own_pair, 'blk', crossing)  0.9 us
  transfers between devices with their start and end apart: 10, of which 10 were waited for; matrix products, arithmetic and copies ran while one was open for 13% of the time, Pallas kernels for 0%

profile of v23, /device:TPU:0, one launch (start us, length us, event | category | flops | bytes accessed | tf_op | source)
XLA Modules:
  0.0 42.7 jit_solution(4835839660888935480)
XLA Ops:
  0.6 3.0 %collective-permute-start = (f32[8,512]{1,0:T(8,128)}, f32[8,512]{1,0:T(8,128)S(1)}, u32[]{:S(2)}, u32[]{:S(2)}) collective-permute-start(f32[8,512]{1,0:T(8,128)} %param.7), channel_id=1, source_target_pairs={{0,1},{1,0},{2,3},{3,2},{4,5},{5,4},{6,7},{7,6},{8,9},{9,8},{10,11... | collective-permute-start | bytes 49160 | tf_op jit(solution)/shard_map/ppermute | solution.py:26
  3.6 0.8 %constant_dynamic-update-slice_fusion.4 = (f32[8,2048]{1,0:T(8,128)S(1)}, f32[8,1024]{1,0:T(8,128)S(1)}, f32[8,4096]{1,0:T(8,128)S(1)}) fusion(f32[8,512]{1,0:T(8,128)} %param.7), kind=kLoop, calls=%fused_computation.11 | loop fusion | bytes 65536
  4.4 0.1 pad.6.clone
  4.5 1.1 %collective-permute-done = f32[8,512]{1,0:T(8,128)S(1)} collective-permute-done((f32[8,512]{1,0:T(8,128)}, f32[8,512]{1,0:T(8,128)S(1)}, u32[]{:S(2)}, u32[]{:S(2)}) %collective-permute-start) | collective-permute-done | bytes 16416 | tf_op jit(solution)/shard_map/ppermute | solution.py:26
  5.6 0.0 collective-permute-start.1
  5.6 0.9 %fusion.19 = f32[8,8]{1,0:T(8,128)S(1)} fusion(f32[8,512]{1,0:T(8,128)} %param.7), kind=kOutput, calls=%fused_computation.57 | convolution fusion | flops 393216 | bytes 16640 | tf_op jit(solution)/shard_map/dot_general | solution.py:163
  6.5 0.3 collective-permute-done.1
  6.8 2.0 %collective-permute-start.2 = (f32[8,2048]{1,0:T(8,128)S(1)}, f32[8,2048]{1,0:T(8,128)S(1)}, u32[]{:S(2)}, u32[]{:S(2)}) collective-permute-start(f32[8,2048]{1,0:T(8,128)S(1)} %get-tuple-element.19), channel_id=1, source_target_pairs={{0,2},{1,3},{2,0},{3,1},{4,6},{5,7},{6,4},{7,5},{8,10},{9,11},{10,... | collective-permute-start | bytes 196616 | tf_op jit(solution)/shard_map/ppermute | solution.py:26
  8.8 0.8 %copy.12 = s32[1,5,3]{2,1,0:T(8,128)S(1)} copy(s32[1,5,3]{1,0,2:T(1,128)} %param.9) | data formatting | bytes 120 | tf_op jit(solution)/shard_map/optimization_barrier | solution.py:109
  9.6 0.1 squeeze.9
  9.7 0.7 %fusion.5 = f32[5,3]{1,0:T(8,128)S(1)} fusion(s32[5]{0:T(128)} %bitcast.62), kind=kLoop, calls=%fused_computation.31 | loop fusion | flops 30 | bytes 80 | tf_op jit(solution)/shard_map/convert_element_type | solution.py:131
  10.4 1.0 %collective-permute-done.2 = f32[8,2048]{1,0:T(8,128)S(1)} collective-permute-done((f32[8,2048]{1,0:T(8,128)S(1)}, f32[8,2048]{1,0:T(8,128)S(1)}, u32[]{:S(2)}, u32[]{:S(2)}) %collective-permute-start.2) | collective-permute-done | bytes 65568 | tf_op jit(solution)/shard_map/ppermute | solution.py:26
  11.4 3.7 %collective-permute-start.3 = (f32[8,4096]{1,0:T(8,128)S(1)}, f32[8,4096]{1,0:T(8,128)S(1)}, u32[]{:S(2)}, u32[]{:S(2)}) collective-permute-start(f32[8,4096]{1,0:T(8,128)S(1)} %constant_dynamic-update-slice_fusion.5), channel_id=1, source_target_pairs={{0,8},{8,16},{16,24},{12,4},{20,12},{28,20},{1,9},{9,17},{17,25},{... | collective-permute-start | bytes 393224 | tf_op jit(solution)/shard_map/ppermute | solution.py:119
  15.1 0.7 %fusion.13 = s32[5]{0:T(128)S(1)} fusion(s32[5]{0:T(128)} %constant.73.clone, s32[5]{0:T(128)} %constant.74.clone, pred[]{:T(512)S(6)} %eq.8), kind=kLoop, calls=%fused_computation.51 | loop fusion | flops 30 | bytes 61 | tf_op jit(solution)/shard_map/concatenate | solution.py:139
  15.8 0.7 %fusion.9 = s32[5,3,1]{0,2,1:T(1,128)S(1)} fusion(s32[1,5,3]{1,0,2:T(1,128)} %param.10, s32[5]{0:T(128)S(1)} %fusion.13, s32[]{:T(128)S(6)} %axis_index.22), kind=kLoop, calls=%fused_computation.42 | loop fusion | flops 420 | bytes 144 | tf_op jit(solution)/shard_map/concatenate | solution.py:139
  16.5 0.1 copy.25
  16.6 0.1 reshape.297
  16.7 0.9 %collective-permute-done.3 = f32[8,4096]{1,0:T(8,128)S(1)} collective-permute-done((f32[8,4096]{1,0:T(8,128)S(1)}, f32[8,4096]{1,0:T(8,128)S(1)}, u32[]{:S(2)}, u32[]{:S(2)}) %collective-permute-start.3) | collective-permute-done | bytes 131104 | tf_op jit(solution)/shard_map/ppermute | solution.py:119
  17.6 0.1 collective-permute-start.4
  17.7 1.3 %collective-permute-done.4 = f32[8,4096]{1,0:T(8,128)S(1)} collective-permute-done((f32[8,4096]{1,0:T(8,128)S(1)}, f32[8,4096]{1,0:T(8,128)S(1)}, u32[]{:S(2)}, u32[]{:S(2)}) %collective-permute-start.4) | collective-permute-done | bytes 131104 | tf_op jit(solution)/shard_map/ppermute | solution.py:26
  19.1 0.6 %gather_fusion = f32[15,8,256]{2,1,0:T(8,128)S(1)} fusion(f32[6,8,8,256]{3,2,1,0:T(8,128)S(1)} %bitcast.61, s32[15]{0:T(128)S(1)} %reshape.297), kind=kCustom, calls=%fused_computation | custom fusion | bytes 245880 | tf_op jit(solution)/shard_map/gather | solution.py:139
  19.7 3.2 %fusion.2 = f32[5,3,8,256]{3,2,1,0:T(8,128)S(1)} fusion(f32[5,3,8,256]{3,2,1,0:T(8,128)S(1)} %bitcast.52, f32[1,5,3,256,256]{4,3,2,1,0:T(8,128)} %param.8, f32[5,3]{1,0:T(8,128)S(1)} %fusion.5), kind=kOutput, calls=%fused_computation.4 | convolution fusion | flops 47216640 | bytes 4177980 | tf_op jit(solution)/shard_map/osit,ostu->osiu/dot_general | solution.py:140
  22.9 1.1 %scatter_fusion = f32[8,8,256]{2,1,0:T(8,128)S(1)} fusion(f32[8,8,256]{2,1,0:T(8,128)S(1)} %broadcast_in_dim.6, s32[15]{0:T(128)S(1)} %fusion.11, f32[15,8,256]{2,1,0:T(8,128)S(1)} %bitcast.51), kind=kCustom, calls=%fused_computation.1 | custom fusion | flops 30720 | bytes 368700 | tf_op jit(solution)/shard_map/scatter-add | solution.py:149
  24.1 0.1 fusion.18
  24.2 0.1 maximum_multiply_fusion
  24.3 1.5 %collective-permute-start.5 = (f32[8,1152]{1,0:T(8,128)S(1)}, f32[8,1152]{1,0:T(8,128)S(1)}, u32[]{:S(2)}, u32[]{:S(2)}) collective-permute-start(f32[8,1152]{1,0:T(8,128)S(1)} %pad_maximum_fusion), channel_id=1, source_target_pairs={{0,2},{1,3},{2,0},{3,1},{4,6},{5,7},{6,4},{7,5},{8,10},{9,11},{10,... | collective-permute-start | bytes 110600 | tf_op jit(solution)/shard_map/ppermute | solution.py:26
  25.9 2.4 %collective-permute-done.5 = f32[8,1152]{1,0:T(8,128)S(1)} collective-permute-done((f32[8,1152]{1,0:T(8,128)S(1)}, f32[8,1152]{1,0:T(8,128)S(1)}, u32[]{:S(2)}, u32[]{:S(2)}) %collective-permute-start.5) | collective-permute-done | bytes 36896 | tf_op jit(solution)/shard_map/ppermute | solution.py:26
  28.3 0.1 slice_add_fusion.3
  28.4 1.5 %collective-permute-start.6 = (f32[8,640]{1,0:T(8,128)S(1)}, f32[8,640]{1,0:T(8,128)S(1)}, u32[]{:S(2)}, u32[]{:S(2)}) collective-permute-start(f32[8,640]{1,0:T(8,128)S(1)} %pad_maximum_fusion.1), channel_id=1, source_target_pairs={{0,1},{1,0},{2,3},{3,2},{4,5},{5,4},{6,7},{7,6},{8,9},{9,8},{10,11... | collective-permute-start | bytes 61448 | tf_op jit(solution)/shard_map/ppermute | solution.py:26
  29.9 2.3 %collective-permute-done.6 = f32[8,640]{1,0:T(8,128)S(1)} collective-permute-done((f32[8,640]{1,0:T(8,128)S(1)}, f32[8,640]{1,0:T(8,128)S(1)}, u32[]{:S(2)}, u32[]{:S(2)}) %collective-permute-start.6) | collective-permute-done | bytes 20512 | tf_op jit(solution)/shard_map/ppermute | solution.py:26
  32.2 0.0 collective-permute-start.7
  32.2 1.2 %collective-permute-done.7 = f32[8,128]{1,0:T(8,128)S(1)} collective-permute-done((f32[8,128]{1,0:T(8,128)S(1)}, f32[8,128]{1,0:T(8,128)S(1)}, u32[]{:S(2)}, u32[]{:S(2)}) %collective-permute-start.7) | collective-permute-done | bytes 4128 | tf_op jit(solution)/shard_map/ppermute | solution.py:26
  33.4 2.5 %collective-permute-start.8 = (f32[8,128]{1,0:T(8,128)S(1)}, f32[8,128]{1,0:T(8,128)S(1)}, u32[]{:S(2)}, u32[]{:S(2)}) collective-permute-start(f32[8,128]{1,0:T(8,128)S(1)} %add.126), channel_id=1, source_target_pairs={{0,8},{4,12},{8,0},{12,4},{16,24},{20,28},{24,16},{28,20},{1,9},{5... | collective-permute-start | bytes 12296 | tf_op jit(solution)/shard_map/ppermute | solution.py:26
  35.8 1.6 %collective-permute-done.8 = f32[8,128]{1,0:T(8,128)S(1)} collective-permute-done((f32[8,128]{1,0:T(8,128)S(1)}, f32[8,128]{1,0:T(8,128)S(1)}, u32[]{:S(2)}, u32[]{:S(2)}) %collective-permute-start.8) | collective-permute-done | bytes 4128 | tf_op jit(solution)/shard_map/ppermute | solution.py:26
  37.4 3.0 %collective-permute-start.9 = (f32[8,128]{1,0:T(8,128)S(1)}, f32[8,128]{1,0:T(8,128)S(1)}, u32[]{:S(2)}, u32[]{:S(2)}) collective-permute-start(f32[8,128]{1,0:T(8,128)S(1)} %add.127), channel_id=1, source_target_pairs={{0,16},{4,20},{8,24},{12,28},{16,0},{20,4},{24,8},{28,12},{1,17},{... | collective-permute-start | bytes 12296 | tf_op jit(solution)/shard_map/ppermute | solution.py:26
  40.4 0.6 %slice_add_fusion.1 = f32[8,512]{1,0:T(8,128)} fusion(f32[8,640]{1,0:T(8,128)S(1)} %collective-permute-done.6, f32[8,1024]{1,0:T(8,128)S(1)} %slice_add_fusion), kind=kLoop, calls=%fused_computation.23 | loop fusion | flops 4096 | bytes 49152 | tf_op jit(solution)/shard_map/add | solution.py:60
  41.0 1.0 %collective-permute-done.9 = f32[8,128]{1,0:T(8,128)S(1)} collective-permute-done((f32[8,128]{1,0:T(8,128)S(1)}, f32[8,128]{1,0:T(8,128)S(1)}, u32[]{:S(2)}, u32[]{:S(2)}) %collective-permute-start.9) | collective-permute-done | bytes 4128 | tf_op jit(solution)/shard_map/ppermute | solution.py:26
  42.0 0.7 %fusion.17 = (f32[8,8]{1,0:T(8,128)}, f32[8,8]{1,0:T(8,128)}) fusion(f32[8,128]{1,0:T(8,128)S(1)} %add.128), kind=kLoop, calls=%fused_computation.55 | loop fusion | bytes 1024 | tf_op jit(solution)/shard_map/slice | solution.py:179
  (24 shorter events, 0.2 us)
Async XLA Ops:
  0.6 4.9 %collective-permute-start = (f32[8,512]{1,0:T(8,128)}, f32[8,512]{1,0:T(8,128)S(1)}, u32[]{:S(2)}, u32[]{:S(2)}) collective-permute-start(f32[8,512]{1,0:T(8,128)} %param.7), channel_id=1, source_target_pairs={{0,1},{1,0},{2,3},{3,2},{4,5},{5,4},{6,7},{7,6},{8,9},{9,8},{10,11... | collective-permute-start | bytes 49160 | tf_op jit(solution)/shard_map/ppermute | solution.py:26
  5.6 1.2 %collective-permute-start.1 = (f32[8,1024]{1,0:T(8,128)S(1)}, f32[8,1024]{1,0:T(8,128)S(1)}, u32[]{:S(2)}, u32[]{:S(2)}) collective-permute-start(f32[8,1024]{1,0:T(8,128)S(1)} %get-tuple-element.23), channel_id=1, source_target_pairs={{0,4},{4,0},{8,12},{12,8},{16,20},{20,16},{24,28},{28,24},{1,5},{5... | collective-permute-start | bytes 98312 | tf_op jit(solution)/shard_map/ppermute | solution.py:26
  6.8 4.6 %collective-permute-start.2 = (f32[8,2048]{1,0:T(8,128)S(1)}, f32[8,2048]{1,0:T(8,128)S(1)}, u32[]{:S(2)}, u32[]{:S(2)}) collective-permute-start(f32[8,2048]{1,0:T(8,128)S(1)} %get-tuple-element.19), channel_id=1, source_target_pairs={{0,2},{1,3},{2,0},{3,1},{4,6},{5,7},{6,4},{7,5},{8,10},{9,11},{10,... | collective-permute-start | bytes 196616 | tf_op jit(solution)/shard_map/ppermute | solution.py:26
  11.4 6.2 %collective-permute-start.3 = (f32[8,4096]{1,0:T(8,128)S(1)}, f32[8,4096]{1,0:T(8,128)S(1)}, u32[]{:S(2)}, u32[]{:S(2)}) collective-permute-start(f32[8,4096]{1,0:T(8,128)S(1)} %constant_dynamic-update-slice_fusion.5), channel_id=1, source_target_pairs={{0,8},{8,16},{16,24},{12,4},{20,12},{28,20},{1,9},{9,17},{17,25},{... | collective-permute-start | bytes 393224 | tf_op jit(solution)/shard_map/ppermute | solution.py:119
  17.6 1.4 %collective-permute-start.4 = (f32[8,4096]{1,0:T(8,128)S(1)}, f32[8,4096]{1,0:T(8,128)S(1)}, u32[]{:S(2)}, u32[]{:S(2)}) collective-permute-start(f32[8,4096]{1,0:T(8,128)S(1)} %collective-permute-done.3), channel_id=1, source_target_pairs={{0,4},{4,0},{8,12},{12,8},{16,20},{20,16},{24,28},{28,24},{1,5},{5... | collective-permute-start | bytes 393224 | tf_op jit(solution)/shard_map/ppermute | solution.py:26
  24.3 4.0 %collective-permute-start.5 = (f32[8,1152]{1,0:T(8,128)S(1)}, f32[8,1152]{1,0:T(8,128)S(1)}, u32[]{:S(2)}, u32[]{:S(2)}) collective-permute-start(f32[8,1152]{1,0:T(8,128)S(1)} %pad_maximum_fusion), channel_id=1, source_target_pairs={{0,2},{1,3},{2,0},{3,1},{4,6},{5,7},{6,4},{7,5},{8,10},{9,11},{10,... | collective-permute-start | bytes 110600 | tf_op jit(solution)/shard_map/ppermute | solution.py:26
  28.4 3.8 %collective-permute-start.6 = (f32[8,640]{1,0:T(8,128)S(1)}, f32[8,640]{1,0:T(8,128)S(1)}, u32[]{:S(2)}, u32[]{:S(2)}) collective-permute-start(f32[8,640]{1,0:T(8,128)S(1)} %pad_maximum_fusion.1), channel_id=1, source_target_pairs={{0,1},{1,0},{2,3},{3,2},{4,5},{5,4},{6,7},{7,6},{8,9},{9,8},{10,11... | collective-permute-start | bytes 61448 | tf_op jit(solution)/shard_map/ppermute | solution.py:26
  32.2 1.2 %collective-permute-start.7 = (f32[8,128]{1,0:T(8,128)S(1)}, f32[8,128]{1,0:T(8,128)S(1)}, u32[]{:S(2)}, u32[]{:S(2)}) collective-permute-start(f32[8,128]{1,0:T(8,128)S(1)} %slice_add_fusion.2), channel_id=1, source_target_pairs={{0,4},{4,0},{8,12},{12,8},{16,20},{20,16},{24,28},{28,24},{1,5},{5... | collective-permute-start | bytes 12296 | tf_op jit(solution)/shard_map/ppermute | solution.py:26
  33.4 4.0 %collective-permute-start.8 = (f32[8,128]{1,0:T(8,128)S(1)}, f32[8,128]{1,0:T(8,128)S(1)}, u32[]{:S(2)}, u32[]{:S(2)}) collective-permute-start(f32[8,128]{1,0:T(8,128)S(1)} %add.126), channel_id=1, source_target_pairs={{0,8},{4,12},{8,0},{12,4},{16,24},{20,28},{24,16},{28,20},{1,9},{5... | collective-permute-start | bytes 12296 | tf_op jit(solution)/shard_map/ppermute | solution.py:26
  37.4 4.6 %collective-permute-start.9 = (f32[8,128]{1,0:T(8,128)S(1)}, f32[8,128]{1,0:T(8,128)S(1)}, u32[]{:S(2)}, u32[]{:S(2)}) collective-permute-start(f32[8,128]{1,0:T(8,128)S(1)} %add.127), channel_id=1, source_target_pairs={{0,16},{4,20},{8,24},{12,28},{16,0},{20,4},{24,8},{28,12},{1,17},{... | collective-permute-start | bytes 12296 | tf_op jit(solution)/shard_map/ppermute | solution.py:26
